TPU v7x, 32 devices: a whole 2x2x4 slice. The times are simulated.
32 devices in a mesh: section: 2 (over x), tm: 4 (over z), space: 4 (over y, core).
Axes of the slice: x: 2, y: 2, z: 4, core: 2. Of those that a mesh axis runs over, the one named last changes fastest.
Arguments:
- video: bfloat16 [2, 8, 16, 512, 128], P('section', 'tm', 'space'), may hold values from -6 to 6
- weights: bfloat16 [2, 9, 384, 128], P('section'), may hold values from -0.109375 to 0.109375
Outputs:
- decoded: bfloat16 [2, 8, 16, 512, 128], P('section', 'tm', 'space')
All inputs are finite; a program needn't handle non-finite values.
Results may differ from a plain program's by a relative error of at most 0.0095.
Values may be sent and summed in bfloat16 or wider, within the bound.
No kernel may reach another device: no remote copies, remote signals or barrier semaphores. Data moves between devices by JAX's collectives and lax.ppermute only.
A program may use at most 128 MiB of HBM per device.

v0:
```python
import jax
import jax.numpy as jnp
from jax import lax
from jax.experimental import pallas as pl
from jax.experimental.pallas import tpu as pltpu
from jax.sharding import PartitionSpec as P


def shift_tm(x):
    n = lax.axis_size("tm")
    return lax.ppermute(x, "tm", [(i, i + 1) for i in range(n - 1)])


def silu(x):
    return jax.nn.silu(x.astype(jnp.float32)).astype(jnp.bfloat16)


def conv_kernel(carried_ref, act_ref, top_ref, bottom_ref, clip_ref, w_ref, out_ref):
    frames, rows, width, chans = clip_ref.shape
    back = carried_ref.shape[0]

    def slab(f, j):
        if j == 0:
            return top_ref[f, 0]
        if j == rows + 1:
            return bottom_ref[f, 0]
        if f < back:
            return carried_ref[f, j - 1]
        return act_ref[f - back, j - 1]

    column = lax.broadcasted_iota(jnp.int32, (width, chans), 0)
    for t in range(frames):
        for h in range(rows):
            lhs = jnp.concatenate(
                [slab(t + back - 2 + a, h + r) for a in range(3) for r in range(3)], axis=-1
            )
            z = jnp.dot(lhs, w_ref[...], preferred_element_type=jnp.float32)
            left = pltpu.roll(z[:, :chans], 1, 0)
            right = pltpu.roll(z[:, 2 * chans :], width - 1, 0)
            left = jnp.where(column == 0, 0.0, left)
            right = jnp.where(column == width - 1, 0.0, right)
            total = z[:, chans : 2 * chans] + left + right
            out_ref[t, h] = (clip_ref[t, h].astype(jnp.float32) + total).astype(out_ref.dtype)


def tap_matrix(taps):
    nine, three_c, chans = taps.shape
    return (
        taps.reshape(nine, 3, chans, chans)
        .transpose(0, 2, 1, 3)
        .reshape(nine * chans, 3 * chans)
    )


def fused_conv(carried, act, top, bottom, clip, w_mat):
    frames, rows, width, chans = clip.shape
    flops = 2 * frames * rows * width * w_mat.shape[0] * w_mat.shape[1]
    nbytes = 2 * (carried.size + act.size + top.size + bottom.size + 2 * clip.size + w_mat.size)
    return pl.pallas_call(
        conv_kernel,
        out_shape=jax.ShapeDtypeStruct(clip.shape, clip.dtype),
        cost_estimate=pl.CostEstimate(flops=flops, bytes_accessed=nbytes, transcendentals=0),
    )(carried, act, top, bottom, clip, w_mat)


def conv_block(clip, w_mat):
    frames = clip.shape[0]
    assert frames == 2
    act = silu(clip)
    carried = shift_tm(act)
    n = lax.axis_size("space")
    last_rows = jnp.concatenate([carried[:, -1:], act[:, -1:]], axis=0)
    first_rows = jnp.concatenate([carried[:, :1], act[:, :1]], axis=0)
    top = lax.ppermute(last_rows, "space", [(i, i + 1) for i in range(n - 1)])
    bottom = lax.ppermute(first_rows, "space", [(i + 1, i) for i in range(n - 1)])
    return fused_conv(carried, act, top, bottom, clip, w_mat)


def body(video, weights):
    all_taps = lax.all_gather(weights, "section", axis=0, tiled=True)
    hidden = conv_block(video[0], tap_matrix(all_taps[0]))
    finished = conv_block(hidden, tap_matrix(all_taps[1]))
    return finished[None]


def solution(mesh):
    return jax.shard_map(
        body,
        mesh=mesh,
        in_specs=(P("section", "tm", "space", None, None), P("section", None, None, None)),
        out_specs=P("section", "tm", "space", None, None),
        check_vma=False,
    )
```

profile of v0, /device:TPU:1, one launch (start us, length us, event | category | flops | bytes accessed | tf_op | source)
XLA Modules:
  0.0 112.9 jit_solution(4998872391325817410)
XLA Ops:
  6.5 0.0 all-gather.2.cloned.1.call-start
  6.5 1.8 %fusion.3.act_ref = bf16[2,4,512,128]{3,2,1,0:T(8,128)(2,1)S(1)} fusion(bf16[1,2,4,512,128]{4,3,2,1,0:T(8,128)(2,1)} %param.2), kind=kLoop, calls=%fused_computation.7 | loop fusion | flops 3145728 | bytes 2097152 | tf_op jit(solution)/shard_map/convert_element_type | solution.py:15
  8.3 0.0 copy-start
  8.3 4.1 %collective-permute-start = (bf16[2,4,512,128]{3,2,1,0:T(8,128)(2,1)S(1)}, bf16[2,4,512,128]{3,2,1,0:T(8,128)(2,1)S(1)}, u32[]{:S(2)}, u32[]{:S(2)}) collective-permute-start(bf16[2,4,512,128]{3,2,1,0:T(8,128)(2,1)S(1)} %fusion.3.act_ref), channel_id=1, source_target_pairs={{0,4},{4,8},{8,12},{1,5},{5,9},{9,13},{2,6},{6,10},{10,14},{3,7},{... | collective-permute-start | bytes 3145736 | tf_op jit(solution)/shard_map/ppermute | solution.py:11
  12.4 0.0 all-gather.2.cloned.1.call-update
  12.5 21.7 %collective-permute-done.carried_ref = bf16[2,4,512,128]{3,2,1,0:T(8,128)(2,1)S(1)} collective-permute-done((bf16[2,4,512,128]{3,2,1,0:T(8,128)(2,1)S(1)}, bf16[2,4,512,128]{3,2,1,0:T(8,128)(2,1)S(1)}, u32[]{:S(2)}, u32[]{:S(2)}) %collective-permute-start) | collective-permute-done | bytes 1048608 | tf_op jit(solution)/shard_map/ppermute | solution.py:11
  34.2 0.0 copy-start.2
  34.3 0.0 copy-done
  34.3 4.6 %collective-permute-start.1 = (bf16[4,1,512,128]{3,2,1,0:T(8,128)(2,1)S(1)}, bf16[4,1,512,128]{3,2,1,0:T(8,128)(2,1)}, u32[]{:S(2)}, u32[]{:S(2)}) collective-permute-start(bf16[4,1,512,128]{3,2,1,0:T(8,128)(2,1)S(1)} %pad_maximum_fusion), channel_id=1, source_target_pairs={{0,1},{1,2},{2,3},{4,5},{5,6},{6,7},{8,9},{9,10},{10,11},{12,13},{... | collective-permute-start | bytes 1572872 | tf_op jit(solution)/shard_map/ppermute | solution.py:74
  38.9 1.9 %collective-permute-start.2 = (bf16[4,1,512,128]{3,2,1,0:T(8,128)(2,1)S(1)}, bf16[4,1,512,128]{3,2,1,0:T(8,128)(2,1)}, u32[]{:S(2)}, u32[]{:S(2)}) collective-permute-start(bf16[4,1,512,128]{3,2,1,0:T(8,128)(2,1)S(1)} %pad_maximum_fusion.1), channel_id=1, source_target_pairs={{1,0},{2,1},{3,2},{5,4},{6,5},{7,6},{9,8},{10,9},{11,10},{13,12},{... | collective-permute-start | bytes 1572872 | tf_op jit(solution)/shard_map/ppermute | solution.py:75
  40.9 1.6 %all-gather.2.cloned.1.call-done = bf16[2,9,384,128]{3,2,1,0:T(8,128)(2,1)} async-done(((bf16[1,9,384,128]{3,2,1,0:T(8,128)(2,1)}), bf16[2,9,384,128]{3,2,1,0:T(8,128)(2,1)}) %all-gather.2.cloned.1.call-update) | async-done | bytes 1769488 | tf_op jit(solution)/shard_map/all_gather | solution.py:80
  42.5 1.6 %fusion.8 = (bf16[1,9,384,128]{3,2,1,0:T(8,128)(2,1)S(1)}, bf16[1,9,384,128]{3,2,1,0:T(8,128)(2,1)S(1)}) fusion(bf16[2,9,384,128]{3,2,1,0:T(8,128)(2,1)} %all-gather.2.cloned.1.call-done), kind=kLoop, calls=%fused_computation.18 | loop fusion | bytes 3538944 | tf_op jit(solution)/shard_map/slice | solution.py:82
  44.1 0.0 copy-done.2
  44.1 0.8 copy.7
  44.8 1.0 copy.14
  45.9 0.0 collective-permute-done.1.top_ref
  45.9 3.6 %collective-permute-done.2.bottom_ref = bf16[4,1,512,128]{3,2,1,0:T(8,128)(2,1)} collective-permute-done((bf16[4,1,512,128]{3,2,1,0:T(8,128)(2,1)S(1)}, bf16[4,1,512,128]{3,2,1,0:T(8,128)(2,1)}, u32[]{:S(2)}, u32[]{:S(2)}) %collective-permute-start.2) | collective-permute-done | bytes 524320 | tf_op jit(solution)/shard_map/ppermute | solution.py:75
  49.5 8.7 %shard_map.28.clip_ref = bf16[2,4,512,128]{3,2,1,0:T(8,128)(2,1)} custom-call(bf16[2,4,512,128]{3,2,1,0:T(8,128)(2,1)} %copy-done.2, bf16[2,4,512,128]{3,2,1,0:T(8,128)(2,1)} %copy-done, bf16[4,1,512,128]{3,2,1,0:T(8,128)(2,1)} %collective-permute-done.1.top_ref, bf16[4,1,512,128]{3,2,1,0:T(8,128)(2,1)} %collective-permute-done.2.bottom_ref, ...), custom_call_target="tpu_custom_call" | custom-call | flops 3623878656 | bytes 6127616 | tf_op jit(solution)/shard_map/pallas_call | solution.py:59
  58.3 1.8 %fusion.7.act_ref = bf16[2,4,512,128]{3,2,1,0:T(8,128)(2,1)S(1)} fusion(bf16[2,4,512,128]{3,2,1,0:T(8,128)(2,1)} %shard_map.28.clip_ref), kind=kLoop, calls=%fused_computation.11 | loop fusion | flops 3145728 | bytes 2097152 | tf_op jit(solution)/shard_map/convert_element_type | solution.py:15
  60.0 0.0 copy-start.1
  60.1 4.2 %collective-permute-start.3 = (bf16[2,4,512,128]{3,2,1,0:T(8,128)(2,1)S(1)}, bf16[2,4,512,128]{3,2,1,0:T(8,128)(2,1)S(1)}, u32[]{:S(2)}, u32[]{:S(2)}) collective-permute-start(bf16[2,4,512,128]{3,2,1,0:T(8,128)(2,1)S(1)} %fusion.7.act_ref), channel_id=1, source_target_pairs={{0,4},{4,8},{8,12},{1,5},{5,9},{9,13},{2,6},{6,10},{10,14},{3,7},{... | collective-permute-start | bytes 3145736 | tf_op jit(solution)/shard_map/ppermute | solution.py:11
  64.3 19.3 %collective-permute-done.3.carried_ref = bf16[2,4,512,128]{3,2,1,0:T(8,128)(2,1)S(1)} collective-permute-done((bf16[2,4,512,128]{3,2,1,0:T(8,128)(2,1)S(1)}, bf16[2,4,512,128]{3,2,1,0:T(8,128)(2,1)S(1)}, u32[]{:S(2)}, u32[]{:S(2)}) %collective-permute-start.3) | collective-permute-done | bytes 1048608 | tf_op jit(solution)/shard_map/ppermute | solution.py:11
  83.6 0.0 copy-start.3
  83.7 2.2 %collective-permute-start.4 = (bf16[4,1,512,128]{3,2,1,0:T(8,128)(2,1)S(1)}, bf16[4,1,512,128]{3,2,1,0:T(8,128)(2,1)S(1)}, u32[]{:S(2)}, u32[]{:S(2)}) collective-permute-start(bf16[4,1,512,128]{3,2,1,0:T(8,128)(2,1)S(1)} %pad_maximum_fusion.2), channel_id=1, source_target_pairs={{0,1},{1,2},{2,3},{4,5},{5,6},{6,7},{8,9},{9,10},{10,11},{12,13},{... | collective-permute-start | bytes 1572872 | tf_op jit(solution)/shard_map/ppermute | solution.py:74
  86.0 0.0 copy-done.1
  86.0 2.3 %collective-permute-start.5 = (bf16[4,1,512,128]{3,2,1,0:T(8,128)(2,1)S(1)}, bf16[4,1,512,128]{3,2,1,0:T(8,128)(2,1)S(1)}, u32[]{:S(2)}, u32[]{:S(2)}) collective-permute-start(bf16[4,1,512,128]{3,2,1,0:T(8,128)(2,1)S(1)} %pad_maximum_fusion.3), channel_id=1, source_target_pairs={{1,0},{2,1},{3,2},{5,4},{6,5},{7,6},{9,8},{10,9},{11,10},{13,12},{... | collective-permute-start | bytes 1572872 | tf_op jit(solution)/shard_map/ppermute | solution.py:75
  88.3 0.8 copy.8
  89.1 0.0 copy-done.3
  89.1 1.1 copy.13
  90.2 1.9 %collective-permute-done.4.top_ref = bf16[4,1,512,128]{3,2,1,0:T(8,128)(2,1)S(1)} collective-permute-done((bf16[4,1,512,128]{3,2,1,0:T(8,128)(2,1)S(1)}, bf16[4,1,512,128]{3,2,1,0:T(8,128)(2,1)S(1)}, u32[]{:S(2)}, u32[]{:S(2)}) %collective-permute-start.4) | collective-permute-done | bytes 524320 | tf_op jit(solution)/shard_map/ppermute | solution.py:74
  92.1 0.0 copy-start.4
  92.1 4.5 %collective-permute-done.5.bottom_ref = bf16[4,1,512,128]{3,2,1,0:T(8,128)(2,1)S(1)} collective-permute-done((bf16[4,1,512,128]{3,2,1,0:T(8,128)(2,1)S(1)}, bf16[4,1,512,128]{3,2,1,0:T(8,128)(2,1)S(1)}, u32[]{:S(2)}, u32[]{:S(2)}) %collective-permute-start.5) | collective-permute-done | bytes 524320 | tf_op jit(solution)/shard_map/ppermute | solution.py:75
  96.5 0.0 copy-start.5
  96.5 0.0 copy-done.4
  96.6 0.8 copy-done.5
  97.3 8.7 %shard_map.29 = bf16[2,4,512,128]{3,2,1,0:T(8,128)(2,1)} custom-call(bf16[2,4,512,128]{3,2,1,0:T(8,128)(2,1)} %copy-done.3, bf16[2,4,512,128]{3,2,1,0:T(8,128)(2,1)} %copy-done.1, bf16[4,1,512,128]{3,2,1,0:T(8,128)(2,1)} %copy-done.4, bf16[4,1,512,128]{3,2,1,0:T(8,128)(2,1)} %copy-done.5, bf16[2,4,512,128]{3,2,1,0:T(8,128)(2,1)} %shard_map.28.clip_ref, ...), custom_call_target="tpu_custom_call" | custom-call | flops 3623878656 | bytes 6127616 | tf_op jit(solution)/shard_map/pallas_call | solution.py:59
  (8 shorter events, 0.3 us)
Async XLA Ops:
  6.5 36.0 %all-gather.2.cloned.1.call-start = ((), (), s32[]{:S(2)}) async-start(), calls=%async_computation | async-start | bytes 2654208 | tf_op jit(solution)/shard_map/all_gather | solution.py:80
  8.3 26.0 %copy-start = (bf16[2,4,512,128]{3,2,1,0:T(8,128)(2,1)}, bf16[2,4,512,128]{3,2,1,0:T(8,128)(2,1)S(1)}, u32[]{:S(2)}) copy-start(bf16[2,4,512,128]{3,2,1,0:T(8,128)(2,1)S(1)} %fusion.3.act_ref) | copy-start | bytes 3145732
  8.3 25.8 %collective-permute-start = (bf16[2,4,512,128]{3,2,1,0:T(8,128)(2,1)S(1)}, bf16[2,4,512,128]{3,2,1,0:T(8,128)(2,1)S(1)}, u32[]{:S(2)}, u32[]{:S(2)}) collective-permute-start(bf16[2,4,512,128]{3,2,1,0:T(8,128)(2,1)S(1)} %fusion.3.act_ref), channel_id=1, source_target_pairs={{0,4},{4,8},{8,12},{1,5},{5,9},{9,13},{2,6},{6,10},{10,14},{3,7},{... | collective-permute-start | bytes 3145736 | tf_op jit(solution)/shard_map/ppermute | solution.py:11
  34.2 9.9 %copy-start.2 = (bf16[2,4,512,128]{3,2,1,0:T(8,128)(2,1)}, bf16[2,4,512,128]{3,2,1,0:T(8,128)(2,1)S(1)}, u32[]{:S(2)}) copy-start(bf16[2,4,512,128]{3,2,1,0:T(8,128)(2,1)S(1)} %collective-permute-done.carried_ref) | copy-start | bytes 3145732
  34.3 11.6 %collective-permute-start.1 = (bf16[4,1,512,128]{3,2,1,0:T(8,128)(2,1)S(1)}, bf16[4,1,512,128]{3,2,1,0:T(8,128)(2,1)}, u32[]{:S(2)}, u32[]{:S(2)}) collective-permute-start(bf16[4,1,512,128]{3,2,1,0:T(8,128)(2,1)S(1)} %pad_maximum_fusion), channel_id=1, source_target_pairs={{0,1},{1,2},{2,3},{4,5},{5,6},{6,7},{8,9},{9,10},{10,11},{12,13},{... | collective-permute-start | bytes 1572872 | tf_op jit(solution)/shard_map/ppermute | solution.py:74
  38.9 10.6 %collective-permute-start.2 = (bf16[4,1,512,128]{3,2,1,0:T(8,128)(2,1)S(1)}, bf16[4,1,512,128]{3,2,1,0:T(8,128)(2,1)}, u32[]{:S(2)}, u32[]{:S(2)}) collective-permute-start(bf16[4,1,512,128]{3,2,1,0:T(8,128)(2,1)S(1)} %pad_maximum_fusion.1), channel_id=1, source_target_pairs={{1,0},{2,1},{3,2},{5,4},{6,5},{7,6},{9,8},{10,9},{11,10},{13,12},{... | collective-permute-start | bytes 1572872 | tf_op jit(solution)/shard_map/ppermute | solution.py:75
  60.0 26.0 %copy-start.1 = (bf16[2,4,512,128]{3,2,1,0:T(8,128)(2,1)}, bf16[2,4,512,128]{3,2,1,0:T(8,128)(2,1)S(1)}, u32[]{:S(2)}) copy-start(bf16[2,4,512,128]{3,2,1,0:T(8,128)(2,1)S(1)} %fusion.7.act_ref) | copy-start | bytes 3145732
  60.1 23.6 %collective-permute-start.3 = (bf16[2,4,512,128]{3,2,1,0:T(8,128)(2,1)S(1)}, bf16[2,4,512,128]{3,2,1,0:T(8,128)(2,1)S(1)}, u32[]{:S(2)}, u32[]{:S(2)}) collective-permute-start(bf16[2,4,512,128]{3,2,1,0:T(8,128)(2,1)S(1)} %fusion.7.act_ref), channel_id=1, source_target_pairs={{0,4},{4,8},{8,12},{1,5},{5,9},{9,13},{2,6},{6,10},{10,14},{3,7},{... | collective-permute-start | bytes 3145736 | tf_op jit(solution)/shard_map/ppermute | solution.py:11
  83.6 5.5 %copy-start.3 = (bf16[2,4,512,128]{3,2,1,0:T(8,128)(2,1)}, bf16[2,4,512,128]{3,2,1,0:T(8,128)(2,1)S(1)}, u32[]{:S(2)}) copy-start(bf16[2,4,512,128]{3,2,1,0:T(8,128)(2,1)S(1)} %collective-permute-done.3.carried_ref) | copy-start | bytes 3145732
  83.7 8.4 %collective-permute-start.4 = (bf16[4,1,512,128]{3,2,1,0:T(8,128)(2,1)S(1)}, bf16[4,1,512,128]{3,2,1,0:T(8,128)(2,1)S(1)}, u32[]{:S(2)}, u32[]{:S(2)}) collective-permute-start(bf16[4,1,512,128]{3,2,1,0:T(8,128)(2,1)S(1)} %pad_maximum_fusion.2), channel_id=1, source_target_pairs={{0,1},{1,2},{2,3},{4,5},{5,6},{6,7},{8,9},{9,10},{10,11},{12,13},{... | collective-permute-start | bytes 1572872 | tf_op jit(solution)/shard_map/ppermute | solution.py:74
  86.0 10.5 %collective-permute-start.5 = (bf16[4,1,512,128]{3,2,1,0:T(8,128)(2,1)S(1)}, bf16[4,1,512,128]{3,2,1,0:T(8,128)(2,1)S(1)}, u32[]{:S(2)}, u32[]{:S(2)}) collective-permute-start(bf16[4,1,512,128]{3,2,1,0:T(8,128)(2,1)S(1)} %pad_maximum_fusion.3), channel_id=1, source_target_pairs={{1,0},{2,1},{3,2},{5,4},{6,5},{7,6},{9,8},{10,9},{11,10},{13,12},{... | collective-permute-start | bytes 1572872 | tf_op jit(solution)/shard_map/ppermute | solution.py:75
  92.1 4.5 %copy-start.4 = (bf16[4,1,512,128]{3,2,1,0:T(8,128)(2,1)}, bf16[4,1,512,128]{3,2,1,0:T(8,128)(2,1)S(1)}, u32[]{:S(2)}) copy-start(bf16[4,1,512,128]{3,2,1,0:T(8,128)(2,1)S(1)} %collective-permute-done.4.top_ref) | copy-start | bytes 1572868
  96.5 0.8 copy-start.5
Sparse Core Ops, SparseCore 0:
  12.6 29.8 all-gather.1
where the time goes:
time: 113 us
  waiting for transfers between devices  52.7 us (47%)
  starting transfers between devices  19.3 us (17%)
  Pallas kernels  17.5 us (15%)
  between operations  13.6 us (12%)
  local copies, waits for them, and re-layouts  6.18 us (5%)
  other arithmetic  3.75 us (3%)
    ppermute x2, waiting for transfers between devices, shift_tm(): return lax.ppermute(x, 'tm', [(i, i + 1) for i in range(n - 1)])  41 us
    pallas_call x2, Pallas kernels, fused_conv(): pl.pallas_call(conv_kernel, out_shape=jax.ShapeDtypeStruct(clip.shape, cl...  17.5 us
    ppermute x2, starting transfers between devices, shift_tm(): return lax.ppermute(x, 'tm', [(i, i + 1) for i in range(n - 1)])  8.27 us
    ppermute x2, waiting for transfers between devices, conv_block(): lax.ppermute(first_rows, 'space', [(i + 1, i) for i in range(n - 1)])  8.11 us
    ppermute x2, starting transfers between devices, conv_block(): top = lax.ppermute(last_rows, 'space', [(i, i + 1) for i in range(n - 1)])  6.83 us
    ppermute x2, starting transfers between devices, conv_block(): lax.ppermute(first_rows, 'space', [(i + 1, i) for i in range(n - 1)])  4.21 us
    convert_element_type x2, other arithmetic, silu(): return jax.nn.silu(x.astype(jnp.float32)).astype(jnp.bfloat16)  3.55 us
    unnamed x14, local copies, waits for them, and re-layouts  2.95 us
  transfers between devices with their start and end apart: 7, of which 6 were waited for; matrix products, arithmetic and copies ran while one was open for 5% of the time, Pallas kernels for 0%

commit v1 on v0

--- a/solution.py
+++ b/solution.py
@@ -15,9 +15,18 @@
     return jax.nn.silu(x.astype(jnp.float32)).astype(jnp.bfloat16)
 
 
-def conv_kernel(carried_ref, act_ref, top_ref, bottom_ref, clip_ref, w_ref, out_ref):
-    frames, rows, width, chans = clip_ref.shape
-    back = carried_ref.shape[0]
+def own_kernel(act_ref, base_ref, w_ref, out_ref):
+    conv_kernel("own", None, act_ref, None, None, base_ref, w_ref, out_ref)
+
+
+def rest_kernel(carried_ref, act_ref, top_ref, bottom_ref, base_ref, w_ref, out_ref):
+    conv_kernel("rest", carried_ref, act_ref, top_ref, bottom_ref, base_ref, w_ref, out_ref)
+
+
+def conv_kernel(part, carried_ref, act_ref, top_ref, bottom_ref, base_ref, w_ref, out_ref):
+    frames, rows, width, chans = base_ref.shape
+    back = act_ref.shape[0]
+    group = 3 * chans
 
     def slab(f, j):
         if j == 0:
@@ -31,16 +40,30 @@
     column = lax.broadcasted_iota(jnp.int32, (width, chans), 0)
     for t in range(frames):
         for h in range(rows):
-            lhs = jnp.concatenate(
-                [slab(t + back - 2 + a, h + r) for a in range(3) for r in range(3)], axis=-1
-            )
-            z = jnp.dot(lhs, w_ref[...], preferred_element_type=jnp.float32)
+            z = None
+            for a in range(3):
+                f = t + back - 2 + a
+                if part == "own" and f >= back:
+                    taps = [r for r in range(3) if 1 <= h + r <= rows]
+                elif part == "rest" and f < back:
+                    taps = [0, 1, 2]
+                elif part == "rest":
+                    taps = [r for r in range(3) if not 1 <= h + r <= rows]
+                else:
+                    taps = []
+                if not taps:
+                    continue
+                lhs = jnp.concatenate([slab(f, h + r) for r in taps], axis=-1)
+                lo = a * group + taps[0] * chans
+                w = w_ref[lo : lo + len(taps) * chans, :]
+                term = jnp.dot(lhs, w, preferred_element_type=jnp.float32)
+                z = term if z is None else z + term
             left = pltpu.roll(z[:, :chans], 1, 0)
             right = pltpu.roll(z[:, 2 * chans :], width - 1, 0)
             left = jnp.where(column == 0, 0.0, left)
             right = jnp.where(column == width - 1, 0.0, right)
             total = z[:, chans : 2 * chans] + left + right
-            out_ref[t, h] = (clip_ref[t, h].astype(jnp.float32) + total).astype(out_ref.dtype)
+            out_ref[t, h] = (base_ref[t, h].astype(jnp.float32) + total).astype(out_ref.dtype)
 
 
 def tap_matrix(taps):
@@ -52,15 +75,15 @@
     )
 
 
-def fused_conv(carried, act, top, bottom, clip, w_mat):
-    frames, rows, width, chans = clip.shape
-    flops = 2 * frames * rows * width * w_mat.shape[0] * w_mat.shape[1]
-    nbytes = 2 * (carried.size + act.size + top.size + bottom.size + 2 * clip.size + w_mat.size)
+def conv_part(kernel, operands, base, w_mat, out_dtype):
+    frames, rows, width, chans = base.shape
+    flops = frames * rows * width * w_mat.shape[0] * w_mat.shape[1]
+    nbytes = sum(x.size * x.dtype.itemsize for x in operands) + 2 * base.size * 4 + w_mat.size * 2
     return pl.pallas_call(
-        conv_kernel,
-        out_shape=jax.ShapeDtypeStruct(clip.shape, clip.dtype),
+        kernel,
+        out_shape=jax.ShapeDtypeStruct(base.shape, out_dtype),
         cost_estimate=pl.CostEstimate(flops=flops, bytes_accessed=nbytes, transcendentals=0),
-    )(carried, act, top, bottom, clip, w_mat)
+    )(*operands, base, w_mat)
 
 
 def conv_block(clip, w_mat):
@@ -68,12 +91,14 @@
     assert frames == 2
     act = silu(clip)
     carried = shift_tm(act)
+    partial = conv_part(own_kernel, (act,), clip, w_mat, jnp.float32)
+    carried, partial = lax.optimization_barrier((carried, partial))
     n = lax.axis_size("space")
     last_rows = jnp.concatenate([carried[:, -1:], act[:, -1:]], axis=0)
     first_rows = jnp.concatenate([carried[:, :1], act[:, :1]], axis=0)
     top = lax.ppermute(last_rows, "space", [(i, i + 1) for i in range(n - 1)])
     bottom = lax.ppermute(first_rows, "space", [(i + 1, i) for i in range(n - 1)])
-    return fused_conv(carried, act, top, bottom, clip, w_mat)
+    return conv_part(rest_kernel, (carried, act, top, bottom), partial, w_mat, clip.dtype)
 
 
 def body(video, weights):

time: 113 us -> 122 us (1.080)
  Pallas kernels: 17.5 us -> 25.8 us
  starting transfers between devices: 19.3 us -> 17.4 us
  local copies, waits for them, and re-layouts: 6.18 us -> 7.98 us
    ppermute x2, waiting for transfers between devices: 41 us -> 8.03 us  [shift_tm(): return lax.ppermute(x, 'tm', [(i, i + 1) for i in range(n - 1)])]
    all_gather x1, waiting for transfers between devices: 1.63 us -> 27.2 us  [body(): all_taps = lax.all_gather(weights, 'section', axis=0, tiled=True)]
    pallas_call x2 -> x4, Pallas kernels: 17.5 us -> 25.8 us  [conv_part(): pl.pallas_call(kernel, out_shape=jax.ShapeDtypeStruct(base.shape, out_dty...]
    ppermute x2, waiting for transfers between devices: 1.87 us -> 7.72 us  [conv_block(): top = lax.ppermute(last_rows, 'space', [(i, i + 1) for i in range(n - 1)])]
    ppermute x2, starting transfers between devices: 6.83 us -> 5.58 us  [conv_block(): top = lax.ppermute(last_rows, 'space', [(i, i + 1) for i in range(n - 1)])]
    unnamed x14 -> x18, local copies, waits for them, and re-layouts: 2.95 us -> 3.72 us
  transfers between devices with their start and end apart: 7 -> 7, of which waited for: 6 -> 6; matrix products, arithmetic and copies ran while one was open for 5% -> 7% of each run, Pallas kernels for 0% -> 9%
where the time goes in v1:
time: 122 us; the launch traced here: 121 us
  waiting for transfers between devices  52.6 us (43%)
  Pallas kernels  25.8 us (21%)
  starting transfers between devices  17.4 us (14%)
  between operations  13.6 us (11%)
  local copies, waits for them, and re-layouts  7.98 us (7%)
  other arithmetic  3.75 us (3%)
    all_gather x1, waiting for transfers between devices, body(): all_taps = lax.all_gather(weights, 'section', axis=0, tiled=True)  27.2 us
    pallas_call x4, Pallas kernels, conv_part(): pl.pallas_call(kernel, out_shape=jax.ShapeDtypeStruct(base.shape, out_dty...  25.8 us
    ppermute x2, waiting for transfers between devices, conv_block(): lax.ppermute(first_rows, 'space', [(i + 1, i) for i in range(n - 1)])  8.9 us
    ppermute x2, waiting for transfers between devices, shift_tm(): return lax.ppermute(x, 'tm', [(i, i + 1) for i in range(n - 1)])  8.03 us
    ppermute x2, waiting for transfers between devices, conv_block(): top = lax.ppermute(last_rows, 'space', [(i, i + 1) for i in range(n - 1)])  7.72 us
    ppermute x2, starting transfers between devices, shift_tm(): return lax.ppermute(x, 'tm', [(i, i + 1) for i in range(n - 1)])  7.46 us
    ppermute x2, starting transfers between devices, conv_block(): top = lax.ppermute(last_rows, 'space', [(i, i + 1) for i in range(n - 1)])  5.58 us
    ppermute x2, starting transfers between devices, conv_block(): lax.ppermute(first_rows, 'space', [(i + 1, i) for i in range(n - 1)])  4.36 us
  transfers between devices with their start and end apart: 7, of which 6 were waited for; matrix products, arithmetic and copies ran while one was open for 7% of the time, Pallas kernels for 9%

profile of v1, /device:TPU:1, one launch (start us, length us, event | category | flops | bytes accessed | tf_op | source)
XLA Modules:
  0.0 121.1 jit_solution(78513751122838457)
XLA Ops:
  6.5 0.0 all-gather.2.cloned.1.call-start
  6.5 0.7 all-gather.2.cloned.1.call-update
  7.3 1.8 %fusion.3.act_ref = bf16[2,4,512,128]{3,2,1,0:T(8,128)(2,1)S(1)} fusion(bf16[1,2,4,512,128]{4,3,2,1,0:T(8,128)(2,1)} %param.2), kind=kLoop, calls=%fused_computation.7 | loop fusion | flops 3145728 | bytes 2097152 | tf_op jit(solution)/shard_map/convert_element_type | solution.py:15
  9.0 0.0 copy-start
  9.0 4.1 %collective-permute-start = (bf16[2,4,512,128]{3,2,1,0:T(8,128)(2,1)S(1)}, bf16[2,4,512,128]{3,2,1,0:T(8,128)(2,1)S(1)}, u32[]{:S(2)}, u32[]{:S(2)}) collective-permute-start(bf16[2,4,512,128]{3,2,1,0:T(8,128)(2,1)S(1)} %fusion.3.act_ref), channel_id=1, source_target_pairs={{0,4},{4,8},{8,12},{1,5},{5,9},{9,13},{2,6},{6,10},{10,14},{3,7},{... | collective-permute-start | bytes 3145736 | tf_op jit(solution)/shard_map/ppermute | solution.py:11
  13.2 27.2 %all-gather.2.cloned.1.call-done = bf16[2,9,384,128]{3,2,1,0:T(8,128)(2,1)} async-done(((bf16[1,9,384,128]{3,2,1,0:T(8,128)(2,1)}), bf16[2,9,384,128]{3,2,1,0:T(8,128)(2,1)}) %all-gather.2.cloned.1.call-update) | async-done | bytes 1769488 | tf_op jit(solution)/shard_map/all_gather | solution.py:105
  40.4 1.6 %fusion.8 = (bf16[1,9,384,128]{3,2,1,0:T(8,128)(2,1)S(1)}, bf16[1,9,384,128]{3,2,1,0:T(8,128)(2,1)S(1)}) fusion(bf16[2,9,384,128]{3,2,1,0:T(8,128)(2,1)} %all-gather.2.cloned.1.call-done), kind=kLoop, calls=%fused_computation.18 | loop fusion | bytes 3538944 | tf_op jit(solution)/shard_map/slice | solution.py:107
  42.0 0.0 copy-done
  42.0 0.8 copy.7
  42.8 1.1 copy.14
  43.9 5.6 %shard_map.28.base_ref = f32[2,4,512,128]{3,2,1,0:T(8,128)} custom-call(bf16[2,4,512,128]{3,2,1,0:T(8,128)(2,1)} %copy-done, bf16[2,4,512,128]{3,2,1,0:T(8,128)(2,1)} %bitcast.25, bf16[1152,384]{1,0:T(8,128)(2,1)} %bitcast.23), custom_call_target="tpu_custom_call" | custom-call | flops 1811939328 | bytes 6127616 | tf_op jit(solution)/shard_map/pallas_call | solution.py:82
  49.4 0.0 collective-permute-done.carried_ref
  49.4 0.0 copy-start.2
  49.5 3.7 %collective-permute-start.1 = (bf16[4,1,512,128]{3,2,1,0:T(8,128)(2,1)S(1)}, bf16[4,1,512,128]{3,2,1,0:T(8,128)(2,1)S(1)}, u32[]{:S(2)}, u32[]{:S(2)}) collective-permute-start(bf16[4,1,512,128]{3,2,1,0:T(8,128)(2,1)S(1)} %pad_maximum_fusion), channel_id=1, source_target_pairs={{0,1},{1,2},{2,3},{4,5},{5,6},{6,7},{8,9},{9,10},{10,11},{12,13},{... | collective-permute-start | bytes 1572872 | tf_op jit(solution)/shard_map/ppermute | solution.py:99
  53.2 1.9 %collective-permute-start.2 = (bf16[4,1,512,128]{3,2,1,0:T(8,128)(2,1)S(1)}, bf16[4,1,512,128]{3,2,1,0:T(8,128)(2,1)S(1)}, u32[]{:S(2)}, u32[]{:S(2)}) collective-permute-start(bf16[4,1,512,128]{3,2,1,0:T(8,128)(2,1)S(1)} %pad_maximum_fusion.1), channel_id=1, source_target_pairs={{1,0},{2,1},{3,2},{5,4},{6,5},{7,6},{9,8},{10,9},{11,10},{13,12},{... | collective-permute-start | bytes 1572872 | tf_op jit(solution)/shard_map/ppermute | solution.py:100
  55.2 4.1 %collective-permute-done.1.top_ref = bf16[4,1,512,128]{3,2,1,0:T(8,128)(2,1)S(1)} collective-permute-done((bf16[4,1,512,128]{3,2,1,0:T(8,128)(2,1)S(1)}, bf16[4,1,512,128]{3,2,1,0:T(8,128)(2,1)S(1)}, u32[]{:S(2)}, u32[]{:S(2)}) %collective-permute-start.1) | collective-permute-done | bytes 524320 | tf_op jit(solution)/shard_map/ppermute | solution.py:99
  59.3 0.0 copy-start.4
  59.3 4.5 %collective-permute-done.2.bottom_ref = bf16[4,1,512,128]{3,2,1,0:T(8,128)(2,1)S(1)} collective-permute-done((bf16[4,1,512,128]{3,2,1,0:T(8,128)(2,1)S(1)}, bf16[4,1,512,128]{3,2,1,0:T(8,128)(2,1)S(1)}, u32[]{:S(2)}, u32[]{:S(2)}) %collective-permute-start.2) | collective-permute-done | bytes 524320 | tf_op jit(solution)/shard_map/ppermute | solution.py:100
  63.7 0.0 copy-done.2
  63.7 0.0 copy-done.4
  63.7 0.0 copy-start.6
  63.7 0.8 copy-done.6
  64.5 7.4 %shard_map.29.base_ref = bf16[2,4,512,128]{3,2,1,0:T(8,128)(2,1)} custom-call(bf16[2,4,512,128]{3,2,1,0:T(8,128)(2,1)} %copy-done.2, bf16[2,4,512,128]{3,2,1,0:T(8,128)(2,1)} %copy-done, bf16[4,1,512,128]{3,2,1,0:T(8,128)(2,1)} %copy-done.4, bf16[4,1,512,128]{3,2,1,0:T(8,128)(2,1)} %copy-done.6, f32[2,4,512,128]{3,2,1,0:T(8,128)} %shard_map.28.base_ref, ...), custom_call_target="tpu_custom_call" | custom-call | flops 1811939328 | bytes 8224768 | tf_op jit(solution)/shard_map/pallas_call | solution.py:82
  71.9 1.8 %fusion.7.act_ref = bf16[2,4,512,128]{3,2,1,0:T(8,128)(2,1)S(1)} fusion(bf16[2,4,512,128]{3,2,1,0:T(8,128)(2,1)} %shard_map.29.base_ref), kind=kLoop, calls=%fused_computation.11 | loop fusion | flops 3145728 | bytes 2097152 | tf_op jit(solution)/shard_map/convert_element_type | solution.py:15
  73.7 0.0 copy-start.1
  73.7 3.4 %collective-permute-start.3 = (bf16[2,4,512,128]{3,2,1,0:T(8,128)(2,1)S(1)}, bf16[2,4,512,128]{3,2,1,0:T(8,128)(2,1)S(1)}, u32[]{:S(2)}, u32[]{:S(2)}) collective-permute-start(bf16[2,4,512,128]{3,2,1,0:T(8,128)(2,1)S(1)} %fusion.7.act_ref), channel_id=1, source_target_pairs={{0,4},{4,8},{8,12},{1,5},{5,9},{9,13},{2,6},{6,10},{10,14},{3,7},{... | collective-permute-start | bytes 3145736 | tf_op jit(solution)/shard_map/ppermute | solution.py:11
  77.0 0.8 copy.8
  77.8 1.1 copy.13
  78.9 0.0 copy-done.1
  78.9 5.6 %shard_map.30.base_ref = f32[2,4,512,128]{3,2,1,0:T(8,128)} custom-call(bf16[2,4,512,128]{3,2,1,0:T(8,128)(2,1)} %copy-done.1, bf16[2,4,512,128]{3,2,1,0:T(8,128)(2,1)} %shard_map.29.base_ref, bf16[1152,384]{1,0:T(8,128)(2,1)} %bitcast.21), custom_call_target="tpu_custom_call" | custom-call | flops 1811939328 | bytes 6127616 | tf_op jit(solution)/shard_map/pallas_call | solution.py:82
  84.4 1.1 fusion.10
  85.5 8.0 %collective-permute-done.3.carried_ref = bf16[2,4,512,128]{3,2,1,0:T(8,128)(2,1)S(1)} collective-permute-done((bf16[2,4,512,128]{3,2,1,0:T(8,128)(2,1)S(1)}, bf16[2,4,512,128]{3,2,1,0:T(8,128)(2,1)S(1)}, u32[]{:S(2)}, u32[]{:S(2)}) %collective-permute-start.3) | collective-permute-done | bytes 1048608 | tf_op jit(solution)/shard_map/ppermute | solution.py:11
  93.5 0.0 copy-start.3
  93.6 1.9 %collective-permute-start.4 = (bf16[4,1,512,128]{3,2,1,0:T(8,128)(2,1)S(1)}, bf16[4,1,512,128]{3,2,1,0:T(8,128)(2,1)S(1)}, u32[]{:S(2)}, u32[]{:S(2)}) collective-permute-start(bf16[4,1,512,128]{3,2,1,0:T(8,128)(2,1)S(1)} %pad_maximum_fusion.2), channel_id=1, source_target_pairs={{0,1},{1,2},{2,3},{4,5},{5,6},{6,7},{8,9},{9,10},{10,11},{12,13},{... | collective-permute-start | bytes 1572872 | tf_op jit(solution)/shard_map/ppermute | solution.py:99
  95.6 2.4 %collective-permute-start.5 = (bf16[4,1,512,128]{3,2,1,0:T(8,128)(2,1)S(1)}, bf16[4,1,512,128]{3,2,1,0:T(8,128)(2,1)S(1)}, u32[]{:S(2)}, u32[]{:S(2)}) collective-permute-start(bf16[4,1,512,128]{3,2,1,0:T(8,128)(2,1)S(1)} %pad_maximum_fusion.3), channel_id=1, source_target_pairs={{1,0},{2,1},{3,2},{5,4},{6,5},{7,6},{9,8},{10,9},{11,10},{13,12},{... | collective-permute-start | bytes 1572872 | tf_op jit(solution)/shard_map/ppermute | solution.py:100
  98.1 3.6 %collective-permute-done.4.top_ref = bf16[4,1,512,128]{3,2,1,0:T(8,128)(2,1)S(1)} collective-permute-done((bf16[4,1,512,128]{3,2,1,0:T(8,128)(2,1)S(1)}, bf16[4,1,512,128]{3,2,1,0:T(8,128)(2,1)S(1)}, u32[]{:S(2)}, u32[]{:S(2)}) %collective-permute-start.4) | collective-permute-done | bytes 524320 | tf_op jit(solution)/shard_map/ppermute | solution.py:99
  101.7 0.0 copy-start.5
  101.7 4.5 %collective-permute-done.5.bottom_ref = bf16[4,1,512,128]{3,2,1,0:T(8,128)(2,1)S(1)} collective-permute-done((bf16[4,1,512,128]{3,2,1,0:T(8,128)(2,1)S(1)}, bf16[4,1,512,128]{3,2,1,0:T(8,128)(2,1)S(1)}, u32[]{:S(2)}, u32[]{:S(2)}) %collective-permute-start.5) | collective-permute-done | bytes 524320 | tf_op jit(solution)/shard_map/ppermute | solution.py:100
  106.1 0.0 copy-done.3
  106.1 0.0 copy-done.5
  106.1 0.0 copy-start.7
  106.1 0.8 copy-done.7
  106.9 7.4 %shard_map.31 = bf16[2,4,512,128]{3,2,1,0:T(8,128)(2,1)} custom-call(bf16[2,4,512,128]{3,2,1,0:T(8,128)(2,1)} %copy-done.3, bf16[2,4,512,128]{3,2,1,0:T(8,128)(2,1)} %copy-done.1, bf16[4,1,512,128]{3,2,1,0:T(8,128)(2,1)} %copy-done.5, bf16[4,1,512,128]{3,2,1,0:T(8,128)(2,1)} %copy-done.7, f32[2,4,512,128]{3,2,1,0:T(8,128)} %shard_map.30.base_ref, ...), custom_call_target="tpu_custom_call" | custom-call | flops 1811939328 | bytes 8224768 | tf_op jit(solution)/shard_map/pallas_call | solution.py:82
  (7 shorter events, 0.3 us)
Async XLA Ops:
  6.5 33.9 %all-gather.2.cloned.1.call-start = ((), (), s32[]{:S(2)}) async-start(), calls=%async_computation | async-start | bytes 2654208 | tf_op jit(solution)/shard_map/all_gather | solution.py:105
  9.0 33.0 %copy-start = (bf16[2,4,512,128]{3,2,1,0:T(8,128)(2,1)}, bf16[2,4,512,128]{3,2,1,0:T(8,128)(2,1)S(1)}, u32[]{:S(2)}) copy-start(bf16[2,4,512,128]{3,2,1,0:T(8,128)(2,1)S(1)} %fusion.3.act_ref) | copy-start | bytes 3145732
  9.0 40.4 %collective-permute-start = (bf16[2,4,512,128]{3,2,1,0:T(8,128)(2,1)S(1)}, bf16[2,4,512,128]{3,2,1,0:T(8,128)(2,1)S(1)}, u32[]{:S(2)}, u32[]{:S(2)}) collective-permute-start(bf16[2,4,512,128]{3,2,1,0:T(8,128)(2,1)S(1)} %fusion.3.act_ref), channel_id=1, source_target_pairs={{0,4},{4,8},{8,12},{1,5},{5,9},{9,13},{2,6},{6,10},{10,14},{3,7},{... | collective-permute-start | bytes 3145736 | tf_op jit(solution)/shard_map/ppermute | solution.py:11
  49.4 14.3 %copy-start.2 = (bf16[2,4,512,128]{3,2,1,0:T(8,128)(2,1)}, bf16[2,4,512,128]{3,2,1,0:T(8,128)(2,1)S(1)}, u32[]{:S(2)}) copy-start(bf16[2,4,512,128]{3,2,1,0:T(8,128)(2,1)S(1)} %collective-permute-done.carried_ref) | copy-start | bytes 3145732
  49.5 9.8 %collective-permute-start.1 = (bf16[4,1,512,128]{3,2,1,0:T(8,128)(2,1)S(1)}, bf16[4,1,512,128]{3,2,1,0:T(8,128)(2,1)S(1)}, u32[]{:S(2)}, u32[]{:S(2)}) collective-permute-start(bf16[4,1,512,128]{3,2,1,0:T(8,128)(2,1)S(1)} %pad_maximum_fusion), channel_id=1, source_target_pairs={{0,1},{1,2},{2,3},{4,5},{5,6},{6,7},{8,9},{9,10},{10,11},{12,13},{... | collective-permute-start | bytes 1572872 | tf_op jit(solution)/shard_map/ppermute | solution.py:99
  53.2 10.5 %collective-permute-start.2 = (bf16[4,1,512,128]{3,2,1,0:T(8,128)(2,1)S(1)}, bf16[4,1,512,128]{3,2,1,0:T(8,128)(2,1)S(1)}, u32[]{:S(2)}, u32[]{:S(2)}) collective-permute-start(bf16[4,1,512,128]{3,2,1,0:T(8,128)(2,1)S(1)} %pad_maximum_fusion.1), channel_id=1, source_target_pairs={{1,0},{2,1},{3,2},{5,4},{6,5},{7,6},{9,8},{10,9},{11,10},{13,12},{... | collective-permute-start | bytes 1572872 | tf_op jit(solution)/shard_map/ppermute | solution.py:100
  59.3 4.5 %copy-start.4 = (bf16[4,1,512,128]{3,2,1,0:T(8,128)(2,1)}, bf16[4,1,512,128]{3,2,1,0:T(8,128)(2,1)S(1)}, u32[]{:S(2)}) copy-start(bf16[4,1,512,128]{3,2,1,0:T(8,128)(2,1)S(1)} %collective-permute-done.1.top_ref) | copy-start | bytes 1572868
  63.7 0.8 copy-start.6
  73.7 5.2 %copy-start.1 = (bf16[2,4,512,128]{3,2,1,0:T(8,128)(2,1)}, bf16[2,4,512,128]{3,2,1,0:T(8,128)(2,1)S(1)}, u32[]{:S(2)}) copy-start(bf16[2,4,512,128]{3,2,1,0:T(8,128)(2,1)S(1)} %fusion.7.act_ref) | copy-start | bytes 3145732
  73.7 19.9 %collective-permute-start.3 = (bf16[2,4,512,128]{3,2,1,0:T(8,128)(2,1)S(1)}, bf16[2,4,512,128]{3,2,1,0:T(8,128)(2,1)S(1)}, u32[]{:S(2)}, u32[]{:S(2)}) collective-permute-start(bf16[2,4,512,128]{3,2,1,0:T(8,128)(2,1)S(1)} %fusion.7.act_ref), channel_id=1, source_target_pairs={{0,4},{4,8},{8,12},{1,5},{5,9},{9,13},{2,6},{6,10},{10,14},{3,7},{... | collective-permute-start | bytes 3145736 | tf_op jit(solution)/shard_map/ppermute | solution.py:11
  93.5 12.6 %copy-start.3 = (bf16[2,4,512,128]{3,2,1,0:T(8,128)(2,1)}, bf16[2,4,512,128]{3,2,1,0:T(8,128)(2,1)S(1)}, u32[]{:S(2)}) copy-start(bf16[2,4,512,128]{3,2,1,0:T(8,128)(2,1)S(1)} %collective-permute-done.3.carried_ref) | copy-start | bytes 3145732
  93.6 8.0 %collective-permute-start.4 = (bf16[4,1,512,128]{3,2,1,0:T(8,128)(2,1)S(1)}, bf16[4,1,512,128]{3,2,1,0:T(8,128)(2,1)S(1)}, u32[]{:S(2)}, u32[]{:S(2)}) collective-permute-start(bf16[4,1,512,128]{3,2,1,0:T(8,128)(2,1)S(1)} %pad_maximum_fusion.2), channel_id=1, source_target_pairs={{0,1},{1,2},{2,3},{4,5},{5,6},{6,7},{8,9},{9,10},{10,11},{12,13},{... | collective-permute-start | bytes 1572872 | tf_op jit(solution)/shard_map/ppermute | solution.py:99
  95.6 10.5 %collective-permute-start.5 = (bf16[4,1,512,128]{3,2,1,0:T(8,128)(2,1)S(1)}, bf16[4,1,512,128]{3,2,1,0:T(8,128)(2,1)S(1)}, u32[]{:S(2)}, u32[]{:S(2)}) collective-permute-start(bf16[4,1,512,128]{3,2,1,0:T(8,128)(2,1)S(1)} %pad_maximum_fusion.3), channel_id=1, source_target_pairs={{1,0},{2,1},{3,2},{5,4},{6,5},{7,6},{9,8},{10,9},{11,10},{13,12},{... | collective-permute-start | bytes 1572872 | tf_op jit(solution)/shard_map/ppermute | solution.py:100
  101.7 4.5 %copy-start.5 = (bf16[4,1,512,128]{3,2,1,0:T(8,128)(2,1)}, bf16[4,1,512,128]{3,2,1,0:T(8,128)(2,1)S(1)}, u32[]{:S(2)}) copy-start(bf16[4,1,512,128]{3,2,1,0:T(8,128)(2,1)S(1)} %collective-permute-done.4.top_ref) | copy-start | bytes 1572868
  106.1 0.8 copy-start.7
Sparse Core Ops, SparseCore 0:
  8.9 31.4 all-gather.1

commit v2 on v0

--- a/solution.py
+++ b/solution.py
@@ -76,10 +76,27 @@
     return fused_conv(carried, act, top, bottom, clip, w_mat)
 
 
+def both_taps(weights):
+    local = weights[0]
+    half = local.shape[1] // 2
+    section = lax.axis_index("section")
+    core = lax.axis_index("space") % 2
+    n_space = lax.axis_size("space")
+    mine = lax.dynamic_slice_in_dim(local, core * half, half, axis=1)
+    got = lax.ppermute(mine, "section", [(0, 1), (1, 0)])
+    other = lax.ppermute(got, "space", [(i, i ^ 1) for i in range(n_space)])
+    low = jnp.where(core == 0, got, other)
+    high = jnp.where(core == 0, other, got)
+    remote = jnp.concatenate([low, high], axis=1)
+    first = jnp.where(section == 0, local, remote)
+    second = jnp.where(section == 0, remote, local)
+    return first, second
+
+
 def body(video, weights):
-    all_taps = lax.all_gather(weights, "section", axis=0, tiled=True)
-    hidden = conv_block(video[0], tap_matrix(all_taps[0]))
-    finished = conv_block(hidden, tap_matrix(all_taps[1]))
+    first, second = both_taps(weights)
+    hidden = conv_block(video[0], tap_matrix(first))
+    finished = conv_block(hidden, tap_matrix(second))
     return finished[None]
 
 

time: 113 us -> 99.3 us (0.88)
  between operations: 13.6 us -> 0.19 us
  waiting for transfers between devices: 52.7 us -> 47.1 us
  starting transfers between devices: 19.3 us -> 23.5 us
    ppermute x2, waiting for transfers between devices: 41 us -> 24.8 us  [shift_tm(): return lax.ppermute(x, 'tm', [(i, i + 1) for i in range(n - 1)])]
    ppermute x0 -> x2, waiting for transfers between devices: none -> 9.47 us  [the longest x1 9.47 us: both_taps(): got = lax.ppermute(mine, 'section', [(0, 1), (1, 0)])]
    ppermute x0 -> x2, starting transfers between devices: none -> 3.14 us  [the longest x1 1.86 us: both_taps(): other = lax.ppermute(got, 'space', [(i, i ^ 1) for i in range(n_space)])]
    ppermute x2, waiting for transfers between devices: 1.87 us -> 3.98 us  [conv_block(): top = lax.ppermute(last_rows, 'space', [(i, i + 1) for i in range(n - 1)])]
    all_gather x1 -> x0, waiting for transfers between devices: 1.63 us -> none  [body(): all_taps = lax.all_gather(weights, 'section', axis=0, tiled=True)]
    slice x1 -> x0, local copies, waits for them, and re-layouts: 1.56 us -> none  [body(): finished = conv_block(hidden, tap_matrix(all_taps[1]))]
    another operation x2 -> x0, local copies, waits for them, and re-layouts: 1.53 us -> none  [tap_matrix(): taps.reshape(nine, 3, chans, chans).transpose(0, 2, 1, 3)]
    transpose x0 -> x2, local copies, waits for them, and re-layouts: none -> 1.53 us  [tap_matrix(): return taps.reshape(nine, 3, chans, chans).transpose(0, 2, 1, 3).reshape(...]
  transfers between devices with their start and end apart: 7 -> 8, of which waited for: 6 -> 7; matrix products, arithmetic and copies ran while one was open for 5% -> 5% of each run, Pallas kernels for 0% -> 0%
where the time goes in v2:
time: 99.3 us; the launch traced here: 98.9 us
  waiting for transfers between devices  47.1 us (47%)
  starting transfers between devices  23.5 us (24%)
  Pallas kernels  17.5 us (18%)
  local copies, waits for them, and re-layouts  6.49 us (7%)
  other arithmetic  4.18 us (4%)
    ppermute x2, waiting for transfers between devices, shift_tm(): return lax.ppermute(x, 'tm', [(i, i + 1) for i in range(n - 1)])  24.8 us
    pallas_call x2, Pallas kernels, fused_conv(): pl.pallas_call(conv_kernel, out_shape=jax.ShapeDtypeStruct(clip.shape, cl...  17.5 us
    ppermute x1, waiting for transfers between devices, both_taps(): got = lax.ppermute(mine, 'section', [(0, 1), (1, 0)])  9.47 us
    ppermute x2, starting transfers between devices, shift_tm(): return lax.ppermute(x, 'tm', [(i, i + 1) for i in range(n - 1)])  9.29 us
    ppermute x2, waiting for transfers between devices, conv_block(): lax.ppermute(first_rows, 'space', [(i + 1, i) for i in range(n - 1)])  8.91 us
    ppermute x2, starting transfers between devices, conv_block(): top = lax.ppermute(last_rows, 'space', [(i, i + 1) for i in range(n - 1)])  7.02 us
    ppermute x2, starting transfers between devices, conv_block(): lax.ppermute(first_rows, 'space', [(i + 1, i) for i in range(n - 1)])  4.02 us
    ppermute x2, waiting for transfers between devices, conv_block(): top = lax.ppermute(last_rows, 'space', [(i, i + 1) for i in range(n - 1)])  3.98 us
  transfers between devices with their start and end apart: 8, of which 7 were waited for; matrix products, arithmetic and copies ran while one was open for 5% of the time, Pallas kernels for 0%

profile of v2, /device:TPU:1, one launch (start us, length us, event | category | flops | bytes accessed | tf_op | source)
XLA Modules:
  0.0 98.9 jit_solution(9709275083664186341)
XLA Ops:
  0.0 0.0 copy-start.2
  0.0 1.9 %fusion.3.act_ref = bf16[2,4,512,128]{3,2,1,0:T(8,128)(2,1)S(1)} fusion(bf16[1,2,4,512,128]{4,3,2,1,0:T(8,128)(2,1)} %param.2), kind=kLoop, calls=%fused_computation.7 | loop fusion | flops 3145728 | bytes 2097152 | tf_op jit(solution)/shard_map/convert_element_type | solution.py:15
  1.9 0.0 copy-start
  1.9 5.0 %collective-permute-start = (bf16[2,4,512,128]{3,2,1,0:T(8,128)(2,1)S(1)}, bf16[2,4,512,128]{3,2,1,0:T(8,128)(2,1)}, u32[]{:S(2)}, u32[]{:S(2)}) collective-permute-start(bf16[2,4,512,128]{3,2,1,0:T(8,128)(2,1)S(1)} %fusion.3.act_ref), channel_id=1, source_target_pairs={{0,4},{4,8},{8,12},{1,5},{5,9},{9,13},{2,6},{6,10},{10,14},{3,7},{... | collective-permute-start | bytes 3145736 | tf_op jit(solution)/shard_map/ppermute | solution.py:11
  6.9 0.0 copy-done.2
  6.9 1.3 %collective-permute-start.3 = (bf16[9,192,128]{2,1,0:T(8,128)(2,1)S(1)}, bf16[9,192,128]{2,1,0:T(8,128)(2,1)S(1)}, u32[]{:S(2)}, u32[]{:S(2)}) collective-permute-start(bf16[9,192,128]{2,1,0:T(8,128)(2,1)S(1)} %dynamic-slice_bitcast_fusion), channel_id=1, source_target_pairs={{0,16},{16,0},{1,17},{17,1},{2,18},{18,2},{3,19},{19,3},{4,20},{20... | collective-permute-start | bytes 1327112 | tf_op jit(solution)/shard_map/ppermute | solution.py:86
  8.2 9.5 %collective-permute-done.3 = bf16[9,192,128]{2,1,0:T(8,128)(2,1)S(1)} collective-permute-done((bf16[9,192,128]{2,1,0:T(8,128)(2,1)S(1)}, bf16[9,192,128]{2,1,0:T(8,128)(2,1)S(1)}, u32[]{:S(2)}, u32[]{:S(2)}) %collective-permute-start.3) | collective-permute-done | bytes 442400 | tf_op jit(solution)/shard_map/ppermute | solution.py:86
  17.7 1.9 %collective-permute-start.4 = (bf16[9,192,128]{2,1,0:T(8,128)(2,1)S(1)}, bf16[9,192,128]{2,1,0:T(8,128)(2,1)S(1)}, u32[]{:S(2)}, u32[]{:S(2)}) collective-permute-start(bf16[9,192,128]{2,1,0:T(8,128)(2,1)S(1)} %collective-permute-done.3), channel_id=1, source_target_pairs={{0,1},{1,0},{2,3},{3,2},{4,5},{5,4},{6,7},{7,6},{8,9},{9,8},{10,11... | collective-permute-start | bytes 1327112 | tf_op jit(solution)/shard_map/ppermute | solution.py:87
  19.6 8.1 %collective-permute-done.carried_ref = bf16[2,4,512,128]{3,2,1,0:T(8,128)(2,1)} collective-permute-done((bf16[2,4,512,128]{3,2,1,0:T(8,128)(2,1)S(1)}, bf16[2,4,512,128]{3,2,1,0:T(8,128)(2,1)}, u32[]{:S(2)}, u32[]{:S(2)}) %collective-permute-start) | collective-permute-done | bytes 1048608 | tf_op jit(solution)/shard_map/ppermute | solution.py:11
  27.7 1.1 %fusion.10 = (bf16[2,1,512,128]{3,2,1,0:T(8,128)(2,1)S(1)}, bf16[2,1,512,128]{3,2,1,0:T(8,128)(2,1)S(1)}) fusion(bf16[2,4,512,128]{3,2,1,0:T(8,128)(2,1)} %collective-permute-done.carried_ref), kind=kLoop, calls=%fused_computation.26 | loop fusion | bytes 1048576 | tf_op jit(solution)/shard_map/slice | solution.py:73
  28.8 0.0 copy-done
  28.9 4.6 %collective-permute-start.1 = (bf16[4,1,512,128]{3,2,1,0:T(8,128)(2,1)S(1)}, bf16[4,1,512,128]{3,2,1,0:T(8,128)(2,1)S(1)}, u32[]{:S(2)}, u32[]{:S(2)}) collective-permute-start(bf16[4,1,512,128]{3,2,1,0:T(8,128)(2,1)S(1)} %pad_maximum_fusion.1), channel_id=1, source_target_pairs={{0,1},{1,2},{2,3},{4,5},{5,6},{6,7},{8,9},{9,10},{10,11},{12,13},{... | collective-permute-start | bytes 1572872 | tf_op jit(solution)/shard_map/ppermute | solution.py:74
  33.5 1.9 %collective-permute-start.2 = (bf16[4,1,512,128]{3,2,1,0:T(8,128)(2,1)S(1)}, bf16[4,1,512,128]{3,2,1,0:T(8,128)(2,1)S(1)}, u32[]{:S(2)}, u32[]{:S(2)}) collective-permute-start(bf16[4,1,512,128]{3,2,1,0:T(8,128)(2,1)S(1)} %pad_maximum_fusion.2), channel_id=1, source_target_pairs={{1,0},{2,1},{3,2},{5,4},{6,5},{7,6},{9,8},{10,9},{11,10},{13,12},{... | collective-permute-start | bytes 1572872 | tf_op jit(solution)/shard_map/ppermute | solution.py:75
  35.4 0.0 collective-permute-done.4
  35.4 0.1 broadcast_select_fusion.1
  35.5 0.1 pad_maximum_fusion
  35.6 0.2 select_bitcast_fusion
  35.8 0.8 copy.5
  36.6 1.1 %copy.12 = bf16[144,8,3,128]{3,1,2,0:T(8,128)(2,1)} copy(bf16[144,8,3,128]{3,2,1,0:T(4,128)(2,1)S(1)} %bitcast.21) | data formatting | bytes 1769472
  37.6 1.9 %collective-permute-done.1.top_ref = bf16[4,1,512,128]{3,2,1,0:T(8,128)(2,1)S(1)} collective-permute-done((bf16[4,1,512,128]{3,2,1,0:T(8,128)(2,1)S(1)}, bf16[4,1,512,128]{3,2,1,0:T(8,128)(2,1)S(1)}, u32[]{:S(2)}, u32[]{:S(2)}) %collective-permute-start.1) | collective-permute-done | bytes 524320 | tf_op jit(solution)/shard_map/ppermute | solution.py:74
  39.5 0.0 copy-start.4
  39.5 4.5 %collective-permute-done.2.bottom_ref = bf16[4,1,512,128]{3,2,1,0:T(8,128)(2,1)S(1)} collective-permute-done((bf16[4,1,512,128]{3,2,1,0:T(8,128)(2,1)S(1)}, bf16[4,1,512,128]{3,2,1,0:T(8,128)(2,1)S(1)}, u32[]{:S(2)}, u32[]{:S(2)}) %collective-permute-start.2) | collective-permute-done | bytes 524320 | tf_op jit(solution)/shard_map/ppermute | solution.py:75
  44.0 0.0 copy-start.5
  44.0 0.8 copy-done.5
  44.8 0.0 copy-done.4
  44.8 8.7 %shard_map.28.clip_ref = bf16[2,4,512,128]{3,2,1,0:T(8,128)(2,1)} custom-call(bf16[2,4,512,128]{3,2,1,0:T(8,128)(2,1)} %collective-permute-done.carried_ref, bf16[2,4,512,128]{3,2,1,0:T(8,128)(2,1)} %copy-done, bf16[4,1,512,128]{3,2,1,0:T(8,128)(2,1)} %copy-done.4, bf16[4,1,512,128]{3,2,1,0:T(8,128)(2,1)} %copy-done.5, bf16[2,4,512,128]{3,2,1,0:T(8,128)(2,1)} %bitcast.25, ...), custom_call_target="tpu_custom_call" | custom-call | flops 3623878656 | bytes 6127616 | tf_op jit(solution)/shard_map/pallas_call | solution.py:59
  53.5 1.8 %fusion.7.act_ref = bf16[2,4,512,128]{3,2,1,0:T(8,128)(2,1)S(1)} fusion(bf16[2,4,512,128]{3,2,1,0:T(8,128)(2,1)} %shard_map.28.clip_ref), kind=kLoop, calls=%fused_computation.11 | loop fusion | flops 3145728 | bytes 2097152 | tf_op jit(solution)/shard_map/convert_element_type | solution.py:15
  55.3 0.0 copy-start.1
  55.3 4.3 %collective-permute-start.5 = (bf16[2,4,512,128]{3,2,1,0:T(8,128)(2,1)S(1)}, bf16[2,4,512,128]{3,2,1,0:T(8,128)(2,1)S(1)}, u32[]{:S(2)}, u32[]{:S(2)}) collective-permute-start(bf16[2,4,512,128]{3,2,1,0:T(8,128)(2,1)S(1)} %fusion.7.act_ref), channel_id=1, source_target_pairs={{0,4},{4,8},{8,12},{1,5},{5,9},{9,13},{2,6},{6,10},{10,14},{3,7},{... | collective-permute-start | bytes 3145736 | tf_op jit(solution)/shard_map/ppermute | solution.py:11
  59.7 16.6 %collective-permute-done.5.carried_ref = bf16[2,4,512,128]{3,2,1,0:T(8,128)(2,1)S(1)} collective-permute-done((bf16[2,4,512,128]{3,2,1,0:T(8,128)(2,1)S(1)}, bf16[2,4,512,128]{3,2,1,0:T(8,128)(2,1)S(1)}, u32[]{:S(2)}, u32[]{:S(2)}) %collective-permute-start.5) | collective-permute-done | bytes 1048608 | tf_op jit(solution)/shard_map/ppermute | solution.py:11
  76.3 0.0 copy-start.3
  76.4 0.0 copy-done.1
  76.4 2.4 %collective-permute-start.6 = (bf16[4,1,512,128]{3,2,1,0:T(8,128)(2,1)S(1)}, bf16[4,1,512,128]{3,2,1,0:T(8,128)(2,1)S(1)}, u32[]{:S(2)}, u32[]{:S(2)}) collective-permute-start(bf16[4,1,512,128]{3,2,1,0:T(8,128)(2,1)S(1)} %pad_maximum_fusion.3), channel_id=1, source_target_pairs={{0,1},{1,2},{2,3},{4,5},{5,6},{6,7},{8,9},{9,10},{10,11},{12,13},{... | collective-permute-start | bytes 1572872 | tf_op jit(solution)/shard_map/ppermute | solution.py:74
  78.9 0.0 copy-done.3
  78.9 2.1 %collective-permute-start.7 = (bf16[4,1,512,128]{3,2,1,0:T(8,128)(2,1)S(1)}, bf16[4,1,512,128]{3,2,1,0:T(8,128)(2,1)S(1)}, u32[]{:S(2)}, u32[]{:S(2)}) collective-permute-start(bf16[4,1,512,128]{3,2,1,0:T(8,128)(2,1)S(1)} %pad_maximum_fusion.4), channel_id=1, source_target_pairs={{1,0},{2,1},{3,2},{5,4},{6,5},{7,6},{9,8},{10,9},{11,10},{13,12},{... | collective-permute-start | bytes 1572872 | tf_op jit(solution)/shard_map/ppermute | solution.py:75
  81.0 0.8 copy.6
  81.8 1.1 %copy.11 = bf16[144,8,3,128]{3,1,2,0:T(8,128)(2,1)} copy(bf16[144,8,3,128]{3,2,1,0:T(4,128)(2,1)S(1)} %bitcast.22) | data formatting | bytes 1769472
  82.9 2.1 %collective-permute-done.6.top_ref = bf16[4,1,512,128]{3,2,1,0:T(8,128)(2,1)S(1)} collective-permute-done((bf16[4,1,512,128]{3,2,1,0:T(8,128)(2,1)S(1)}, bf16[4,1,512,128]{3,2,1,0:T(8,128)(2,1)S(1)}, u32[]{:S(2)}, u32[]{:S(2)}) %collective-permute-start.6) | collective-permute-done | bytes 524320 | tf_op jit(solution)/shard_map/ppermute | solution.py:74
  85.0 0.0 copy-start.6
  85.0 4.5 %collective-permute-done.7.bottom_ref = bf16[4,1,512,128]{3,2,1,0:T(8,128)(2,1)S(1)} collective-permute-done((bf16[4,1,512,128]{3,2,1,0:T(8,128)(2,1)S(1)}, bf16[4,1,512,128]{3,2,1,0:T(8,128)(2,1)S(1)}, u32[]{:S(2)}, u32[]{:S(2)}) %collective-permute-start.7) | collective-permute-done | bytes 524320 | tf_op jit(solution)/shard_map/ppermute | solution.py:75
  89.4 0.0 copy-start.7
  89.4 0.0 copy-done.6
  89.4 0.8 copy-done.7
  90.2 8.7 %shard_map.29 = bf16[2,4,512,128]{3,2,1,0:T(8,128)(2,1)} custom-call(bf16[2,4,512,128]{3,2,1,0:T(8,128)(2,1)} %copy-done.3, bf16[2,4,512,128]{3,2,1,0:T(8,128)(2,1)} %copy-done.1, bf16[4,1,512,128]{3,2,1,0:T(8,128)(2,1)} %copy-done.6, bf16[4,1,512,128]{3,2,1,0:T(8,128)(2,1)} %copy-done.7, bf16[2,4,512,128]{3,2,1,0:T(8,128)(2,1)} %shard_map.28.clip_ref, ...), custom_call_target="tpu_custom_call" | custom-call | flops 3623878656 | bytes 6127616 | tf_op jit(solution)/shard_map/pallas_call | solution.py:59
  (8 shorter events, 0.3 us)
Async XLA Ops:
  0.0 6.9 %copy-start.2 = (bf16[1,9,384,128]{3,2,1,0:T(8,128)(2,1)S(1)}, bf16[1,9,384,128]{3,2,1,0:T(8,128)(2,1)}, u32[]{:S(2)}) copy-start(bf16[1,9,384,128]{3,2,1,0:T(8,128)(2,1)} %param.3) | copy-start | bytes 2654212
  1.9 26.9 %copy-start = (bf16[2,4,512,128]{3,2,1,0:T(8,128)(2,1)}, bf16[2,4,512,128]{3,2,1,0:T(8,128)(2,1)S(1)}, u32[]{:S(2)}) copy-start(bf16[2,4,512,128]{3,2,1,0:T(8,128)(2,1)S(1)} %fusion.3.act_ref) | copy-start | bytes 3145732
  1.9 25.8 %collective-permute-start = (bf16[2,4,512,128]{3,2,1,0:T(8,128)(2,1)S(1)}, bf16[2,4,512,128]{3,2,1,0:T(8,128)(2,1)}, u32[]{:S(2)}, u32[]{:S(2)}) collective-permute-start(bf16[2,4,512,128]{3,2,1,0:T(8,128)(2,1)S(1)} %fusion.3.act_ref), channel_id=1, source_target_pairs={{0,4},{4,8},{8,12},{1,5},{5,9},{9,13},{2,6},{6,10},{10,14},{3,7},{... | collective-permute-start | bytes 3145736 | tf_op jit(solution)/shard_map/ppermute | solution.py:11
  6.9 10.8 %collective-permute-start.3 = (bf16[9,192,128]{2,1,0:T(8,128)(2,1)S(1)}, bf16[9,192,128]{2,1,0:T(8,128)(2,1)S(1)}, u32[]{:S(2)}, u32[]{:S(2)}) collective-permute-start(bf16[9,192,128]{2,1,0:T(8,128)(2,1)S(1)} %dynamic-slice_bitcast_fusion), channel_id=1, source_target_pairs={{0,16},{16,0},{1,17},{17,1},{2,18},{18,2},{3,19},{19,3},{4,20},{20... | collective-permute-start | bytes 1327112 | tf_op jit(solution)/shard_map/ppermute | solution.py:86
  17.7 17.7 %collective-permute-start.4 = (bf16[9,192,128]{2,1,0:T(8,128)(2,1)S(1)}, bf16[9,192,128]{2,1,0:T(8,128)(2,1)S(1)}, u32[]{:S(2)}, u32[]{:S(2)}) collective-permute-start(bf16[9,192,128]{2,1,0:T(8,128)(2,1)S(1)} %collective-permute-done.3), channel_id=1, source_target_pairs={{0,1},{1,0},{2,3},{3,2},{4,5},{5,4},{6,7},{7,6},{8,9},{9,8},{10,11... | collective-permute-start | bytes 1327112 | tf_op jit(solution)/shard_map/ppermute | solution.py:87
  28.9 10.7 %collective-permute-start.1 = (bf16[4,1,512,128]{3,2,1,0:T(8,128)(2,1)S(1)}, bf16[4,1,512,128]{3,2,1,0:T(8,128)(2,1)S(1)}, u32[]{:S(2)}, u32[]{:S(2)}) collective-permute-start(bf16[4,1,512,128]{3,2,1,0:T(8,128)(2,1)S(1)} %pad_maximum_fusion.1), channel_id=1, source_target_pairs={{0,1},{1,2},{2,3},{4,5},{5,6},{6,7},{8,9},{9,10},{10,11},{12,13},{... | collective-permute-start | bytes 1572872 | tf_op jit(solution)/shard_map/ppermute | solution.py:74
  33.5 10.5 %collective-permute-start.2 = (bf16[4,1,512,128]{3,2,1,0:T(8,128)(2,1)S(1)}, bf16[4,1,512,128]{3,2,1,0:T(8,128)(2,1)S(1)}, u32[]{:S(2)}, u32[]{:S(2)}) collective-permute-start(bf16[4,1,512,128]{3,2,1,0:T(8,128)(2,1)S(1)} %pad_maximum_fusion.2), channel_id=1, source_target_pairs={{1,0},{2,1},{3,2},{5,4},{6,5},{7,6},{9,8},{10,9},{11,10},{13,12},{... | collective-permute-start | bytes 1572872 | tf_op jit(solution)/shard_map/ppermute | solution.py:75
  39.5 5.3 %copy-start.4 = (bf16[4,1,512,128]{3,2,1,0:T(8,128)(2,1)}, bf16[4,1,512,128]{3,2,1,0:T(8,128)(2,1)S(1)}, u32[]{:S(2)}) copy-start(bf16[4,1,512,128]{3,2,1,0:T(8,128)(2,1)S(1)} %collective-permute-done.1.top_ref) | copy-start | bytes 1572868
  44.0 0.8 copy-start.5
  55.3 21.1 %copy-start.1 = (bf16[2,4,512,128]{3,2,1,0:T(8,128)(2,1)}, bf16[2,4,512,128]{3,2,1,0:T(8,128)(2,1)S(1)}, u32[]{:S(2)}) copy-start(bf16[2,4,512,128]{3,2,1,0:T(8,128)(2,1)S(1)} %fusion.7.act_ref) | copy-start | bytes 3145732
  55.3 21.0 %collective-permute-start.5 = (bf16[2,4,512,128]{3,2,1,0:T(8,128)(2,1)S(1)}, bf16[2,4,512,128]{3,2,1,0:T(8,128)(2,1)S(1)}, u32[]{:S(2)}, u32[]{:S(2)}) collective-permute-start(bf16[2,4,512,128]{3,2,1,0:T(8,128)(2,1)S(1)} %fusion.7.act_ref), channel_id=1, source_target_pairs={{0,4},{4,8},{8,12},{1,5},{5,9},{9,13},{2,6},{6,10},{10,14},{3,7},{... | collective-permute-start | bytes 3145736 | tf_op jit(solution)/shard_map/ppermute | solution.py:11
  76.3 2.6 %copy-start.3 = (bf16[2,4,512,128]{3,2,1,0:T(8,128)(2,1)}, bf16[2,4,512,128]{3,2,1,0:T(8,128)(2,1)S(1)}, u32[]{:S(2)}) copy-start(bf16[2,4,512,128]{3,2,1,0:T(8,128)(2,1)S(1)} %collective-permute-done.5.carried_ref) | copy-start | bytes 3145732
  76.4 8.6 %collective-permute-start.6 = (bf16[4,1,512,128]{3,2,1,0:T(8,128)(2,1)S(1)}, bf16[4,1,512,128]{3,2,1,0:T(8,128)(2,1)S(1)}, u32[]{:S(2)}, u32[]{:S(2)}) collective-permute-start(bf16[4,1,512,128]{3,2,1,0:T(8,128)(2,1)S(1)} %pad_maximum_fusion.3), channel_id=1, source_target_pairs={{0,1},{1,2},{2,3},{4,5},{5,6},{6,7},{8,9},{9,10},{10,11},{12,13},{... | collective-permute-start | bytes 1572872 | tf_op jit(solution)/shard_map/ppermute | solution.py:74
  78.9 10.5 %collective-permute-start.7 = (bf16[4,1,512,128]{3,2,1,0:T(8,128)(2,1)S(1)}, bf16[4,1,512,128]{3,2,1,0:T(8,128)(2,1)S(1)}, u32[]{:S(2)}, u32[]{:S(2)}) collective-permute-start(bf16[4,1,512,128]{3,2,1,0:T(8,128)(2,1)S(1)} %pad_maximum_fusion.4), channel_id=1, source_target_pairs={{1,0},{2,1},{3,2},{5,4},{6,5},{7,6},{9,8},{10,9},{11,10},{13,12},{... | collective-permute-start | bytes 1572872 | tf_op jit(solution)/shard_map/ppermute | solution.py:75
  85.0 4.5 %copy-start.6 = (bf16[4,1,512,128]{3,2,1,0:T(8,128)(2,1)}, bf16[4,1,512,128]{3,2,1,0:T(8,128)(2,1)S(1)}, u32[]{:S(2)}) copy-start(bf16[4,1,512,128]{3,2,1,0:T(8,128)(2,1)S(1)} %collective-permute-done.6.top_ref) | copy-start | bytes 1572868
  89.4 0.8 copy-start.7

commit v3 on v2

--- a/solution.py
+++ b/solution.py
@@ -63,17 +63,18 @@
     )(carried, act, top, bottom, clip, w_mat)
 
 
-def conv_block(clip, w_mat):
+def conv_block(clip, w_mat, ahead=()):
     frames = clip.shape[0]
     assert frames == 2
     act = silu(clip)
     carried = shift_tm(act)
+    carried, w_mat, ahead = lax.optimization_barrier((carried, w_mat, ahead))
     n = lax.axis_size("space")
     last_rows = jnp.concatenate([carried[:, -1:], act[:, -1:]], axis=0)
     first_rows = jnp.concatenate([carried[:, :1], act[:, :1]], axis=0)
     top = lax.ppermute(last_rows, "space", [(i, i + 1) for i in range(n - 1)])
     bottom = lax.ppermute(first_rows, "space", [(i + 1, i) for i in range(n - 1)])
-    return fused_conv(carried, act, top, bottom, clip, w_mat)
+    return fused_conv(carried, act, top, bottom, clip, w_mat), ahead
 
 
 def both_taps(weights):
@@ -95,8 +96,8 @@
 
 def body(video, weights):
     first, second = both_taps(weights)
-    hidden = conv_block(video[0], tap_matrix(first))
-    finished = conv_block(hidden, tap_matrix(second))
+    hidden, second_mat = conv_block(video[0], tap_matrix(first), tap_matrix(second))
+    finished, _ = conv_block(hidden, second_mat)
     return finished[None]
 
 

time: 99.3 us -> 110 us (1.11)
  waiting for transfers between devices: 47.1 us -> 58 us
    ppermute x2, waiting for transfers between devices: 24.8 us -> 36.1 us  [shift_tm(): return lax.ppermute(x, 'tm', [(i, i + 1) for i in range(n - 1)])]
    ppermute x2, starting transfers between devices: 9.29 us -> 7.69 us  [shift_tm(): return lax.ppermute(x, 'tm', [(i, i + 1) for i in range(n - 1)])]
    reshape x0 -> x1, local copies, waits for them, and re-layouts: none -> 1.56 us  [tap_matrix(): return taps.reshape(nine, 3, chans, chans).transpose(0, 2, 1, 3).reshape(...]
    ppermute x2, waiting for transfers between devices: 3.98 us -> 2.49 us  [conv_block(): top = lax.ppermute(last_rows, 'space', [(i, i + 1) for i in range(n - 1)])]
where the time goes in v3:
time: 110 us; the launch traced here: 109 us
  waiting for transfers between devices  58 us (53%)
  starting transfers between devices  22.5 us (20%)
  Pallas kernels  17.5 us (16%)
  local copies, waits for them, and re-layouts  6.96 us (6%)
  other arithmetic  3.99 us (4%)
    ppermute x2, waiting for transfers between devices, shift_tm(): return lax.ppermute(x, 'tm', [(i, i + 1) for i in range(n - 1)])  36.1 us
    pallas_call x2, Pallas kernels, fused_conv(): pl.pallas_call(conv_kernel, out_shape=jax.ShapeDtypeStruct(clip.shape, cl...  17.5 us
    ppermute x1, waiting for transfers between devices, both_taps(): got = lax.ppermute(mine, 'section', [(0, 1), (1, 0)])  9.89 us
    ppermute x2, waiting for transfers between devices, conv_block(): lax.ppermute(first_rows, 'space', [(i + 1, i) for i in range(n - 1)])  9.53 us
    ppermute x2, starting transfers between devices, shift_tm(): return lax.ppermute(x, 'tm', [(i, i + 1) for i in range(n - 1)])  7.69 us
    ppermute x2, starting transfers between devices, conv_block(): top = lax.ppermute(last_rows, 'space', [(i, i + 1) for i in range(n - 1)])  6.87 us
    ppermute x2, starting transfers between devices, conv_block(): lax.ppermute(first_rows, 'space', [(i + 1, i) for i in range(n - 1)])  4.61 us
    convert_element_type x2, other arithmetic, silu(): return jax.nn.silu(x.astype(jnp.float32)).astype(jnp.bfloat16)  3.55 us
  transfers between devices with their start and end apart: 8, of which 7 were waited for; matrix products, arithmetic and copies ran while one was open for 5% of the time, Pallas kernels for 0%

profile of v3, /device:TPU:1, one launch (start us, length us, event | category | flops | bytes accessed | tf_op | source)
XLA Modules:
  0.0 109.1 jit_solution(5331838035773207376)
XLA Ops:
  0.0 1.0 dynamic-slice_bitcast_fusion
  1.0 2.1 %collective-permute-start.1 = (bf16[9,192,128]{2,1,0:T(8,128)(2,1)S(1)}, bf16[9,192,128]{2,1,0:T(8,128)(2,1)S(1)}, u32[]{:S(2)}, u32[]{:S(2)}) collective-permute-start(bf16[9,192,128]{2,1,0:T(8,128)(2,1)S(1)} %dynamic-slice_bitcast_fusion), channel_id=1, source_target_pairs={{0,16},{16,0},{1,17},{17,1},{2,18},{18,2},{3,19},{19,3},{4,20},{20... | collective-permute-start | bytes 1327112 | tf_op jit(solution)/shard_map/ppermute | solution.py:87
  3.2 9.9 %collective-permute-done.1 = bf16[9,192,128]{2,1,0:T(8,128)(2,1)S(1)} collective-permute-done((bf16[9,192,128]{2,1,0:T(8,128)(2,1)S(1)}, bf16[9,192,128]{2,1,0:T(8,128)(2,1)S(1)}, u32[]{:S(2)}, u32[]{:S(2)}) %collective-permute-start.1) | collective-permute-done | bytes 442400 | tf_op jit(solution)/shard_map/ppermute | solution.py:87
  13.0 1.2 %collective-permute-start.2 = (bf16[9,192,128]{2,1,0:T(8,128)(2,1)S(1)}, bf16[9,192,128]{2,1,0:T(8,128)(2,1)S(1)}, u32[]{:S(2)}, u32[]{:S(2)}) collective-permute-start(bf16[9,192,128]{2,1,0:T(8,128)(2,1)S(1)} %collective-permute-done.1), channel_id=1, source_target_pairs={{0,1},{1,0},{2,3},{3,2},{4,5},{5,4},{6,7},{7,6},{8,9},{9,8},{10,11... | collective-permute-start | bytes 1327112 | tf_op jit(solution)/shard_map/ppermute | solution.py:88
  14.3 1.8 %fusion.3.act_ref = bf16[2,4,512,128]{3,2,1,0:T(8,128)(2,1)S(1)} fusion(bf16[1,2,4,512,128]{4,3,2,1,0:T(8,128)(2,1)} %param.2), kind=kLoop, calls=%fused_computation.7 | loop fusion | flops 3145728 | bytes 2097152 | tf_op jit(solution)/shard_map/convert_element_type | solution.py:15
  16.1 0.0 copy-start
  16.1 3.5 %collective-permute-start = (bf16[2,4,512,128]{3,2,1,0:T(8,128)(2,1)S(1)}, bf16[2,4,512,128]{3,2,1,0:T(8,128)(2,1)S(1)}, u32[]{:S(2)}, u32[]{:S(2)}) collective-permute-start(bf16[2,4,512,128]{3,2,1,0:T(8,128)(2,1)S(1)} %fusion.3.act_ref), channel_id=1, source_target_pairs={{0,4},{4,8},{8,12},{1,5},{5,9},{9,13},{2,6},{6,10},{10,14},{3,7},{... | collective-permute-start | bytes 3145736 | tf_op jit(solution)/shard_map/ppermute | solution.py:11
  19.6 0.0 collective-permute-done.2
  19.7 0.1 broadcast_select_fusion.1
  19.7 0.0 copy-done
  19.7 0.0 copy-start.2
  19.7 0.1 pad_maximum_fusion
  19.8 1.1 copy-done.2
  20.9 0.1 select_bitcast_fusion
  21.0 0.8 copy.6
  21.8 0.8 copy.5
  22.6 1.6 %copy_bitcast_fusion = (bf16[1152,384]{1,0:T(8,128)(2,1)}, bf16[1152,384]{1,0:T(8,128)(2,1)}) fusion(bf16[144,8,3,128]{3,2,1,0:T(4,128)(2,1)S(1)} %bitcast.19, bf16[144,8,3,128]{3,2,1,0:T(4,128)(2,1)S(1)} %bitcast.20), kind=kLoop, calls=%fused_computation.12 | loop fusion | bytes 3538944 | tf_op jit(solution)/shard_map/reshape | solution.py:51
  24.1 18.0 %collective-permute-done.carried_ref = bf16[2,4,512,128]{3,2,1,0:T(8,128)(2,1)S(1)} collective-permute-done((bf16[2,4,512,128]{3,2,1,0:T(8,128)(2,1)S(1)}, bf16[2,4,512,128]{3,2,1,0:T(8,128)(2,1)S(1)}, u32[]{:S(2)}, u32[]{:S(2)}) %collective-permute-start) | collective-permute-done | bytes 1048608 | tf_op jit(solution)/shard_map/ppermute | solution.py:11
  42.1 0.0 copy-start.3
  42.2 2.7 %collective-permute-start.4 = (bf16[4,1,512,128]{3,2,1,0:T(8,128)(2,1)S(1)}, bf16[4,1,512,128]{3,2,1,0:T(8,128)(2,1)S(1)}, u32[]{:S(2)}, u32[]{:S(2)}) collective-permute-start(bf16[4,1,512,128]{3,2,1,0:T(8,128)(2,1)S(1)} %pad_maximum_fusion.2), channel_id=1, source_target_pairs={{1,0},{2,1},{3,2},{5,4},{6,5},{7,6},{9,8},{10,9},{11,10},{13,12},{... | collective-permute-start | bytes 1572872 | tf_op jit(solution)/shard_map/ppermute | solution.py:76
  44.9 0.0 copy-done.3
  45.0 3.0 %collective-permute-start.3 = (bf16[4,1,512,128]{3,2,1,0:T(8,128)(2,1)S(1)}, bf16[4,1,512,128]{3,2,1,0:T(8,128)(2,1)S(1)}, u32[]{:S(2)}, u32[]{:S(2)}) collective-permute-start(bf16[4,1,512,128]{3,2,1,0:T(8,128)(2,1)S(1)} %pad_maximum_fusion.1), channel_id=1, source_target_pairs={{0,1},{1,2},{2,3},{4,5},{5,6},{6,7},{8,9},{9,10},{10,11},{12,13},{... | collective-permute-start | bytes 1572872 | tf_op jit(solution)/shard_map/ppermute | solution.py:75
  48.0 4.9 %collective-permute-done.4.bottom_ref = bf16[4,1,512,128]{3,2,1,0:T(8,128)(2,1)S(1)} collective-permute-done((bf16[4,1,512,128]{3,2,1,0:T(8,128)(2,1)S(1)}, bf16[4,1,512,128]{3,2,1,0:T(8,128)(2,1)S(1)}, u32[]{:S(2)}, u32[]{:S(2)}) %collective-permute-start.4) | collective-permute-done | bytes 524320 | tf_op jit(solution)/shard_map/ppermute | solution.py:76
  52.9 0.0 copy-start.6
  52.9 1.2 %collective-permute-done.3.top_ref = bf16[4,1,512,128]{3,2,1,0:T(8,128)(2,1)S(1)} collective-permute-done((bf16[4,1,512,128]{3,2,1,0:T(8,128)(2,1)S(1)}, bf16[4,1,512,128]{3,2,1,0:T(8,128)(2,1)S(1)}, u32[]{:S(2)}, u32[]{:S(2)}) %collective-permute-start.3) | collective-permute-done | bytes 524320 | tf_op jit(solution)/shard_map/ppermute | solution.py:75
  54.1 0.0 copy-start.8
  54.1 0.0 copy-done.6
  54.1 0.8 copy-done.8
  54.9 8.7 %shard_map.28.clip_ref = bf16[2,4,512,128]{3,2,1,0:T(8,128)(2,1)} custom-call(bf16[2,4,512,128]{3,2,1,0:T(8,128)(2,1)} %copy-done.3, bf16[2,4,512,128]{3,2,1,0:T(8,128)(2,1)} %copy-done, bf16[4,1,512,128]{3,2,1,0:T(8,128)(2,1)} %copy-done.8, bf16[4,1,512,128]{3,2,1,0:T(8,128)(2,1)} %copy-done.6, bf16[2,4,512,128]{3,2,1,0:T(8,128)(2,1)} %bitcast.23, ...), custom_call_target="tpu_custom_call" | custom-call | flops 3623878656 | bytes 6127616 | tf_op jit(solution)/shard_map/pallas_call | solution.py:59
  63.7 1.8 %fusion.7.act_ref = bf16[2,4,512,128]{3,2,1,0:T(8,128)(2,1)S(1)} fusion(bf16[2,4,512,128]{3,2,1,0:T(8,128)(2,1)} %shard_map.28.clip_ref), kind=kLoop, calls=%fused_computation.11 | loop fusion | flops 3145728 | bytes 2097152 | tf_op jit(solution)/shard_map/convert_element_type | solution.py:15
  65.4 0.0 copy-start.1
  65.4 4.2 %collective-permute-start.5 = (bf16[2,4,512,128]{3,2,1,0:T(8,128)(2,1)S(1)}, bf16[2,4,512,128]{3,2,1,0:T(8,128)(2,1)S(1)}, u32[]{:S(2)}, u32[]{:S(2)}) collective-permute-start(bf16[2,4,512,128]{3,2,1,0:T(8,128)(2,1)S(1)} %fusion.7.act_ref), channel_id=1, source_target_pairs={{0,4},{4,8},{8,12},{1,5},{5,9},{9,13},{2,6},{6,10},{10,14},{3,7},{... | collective-permute-start | bytes 3145736 | tf_op jit(solution)/shard_map/ppermute | solution.py:11
  69.7 18.1 %collective-permute-done.5.carried_ref = bf16[2,4,512,128]{3,2,1,0:T(8,128)(2,1)S(1)} collective-permute-done((bf16[2,4,512,128]{3,2,1,0:T(8,128)(2,1)S(1)}, bf16[2,4,512,128]{3,2,1,0:T(8,128)(2,1)S(1)}, u32[]{:S(2)}, u32[]{:S(2)}) %collective-permute-start.5) | collective-permute-done | bytes 1048608 | tf_op jit(solution)/shard_map/ppermute | solution.py:11
  87.8 0.0 copy-start.4
  87.9 0.0 copy-done.1
  87.9 1.9 %collective-permute-start.7 = (bf16[4,1,512,128]{3,2,1,0:T(8,128)(2,1)S(1)}, bf16[4,1,512,128]{3,2,1,0:T(8,128)(2,1)S(1)}, u32[]{:S(2)}, u32[]{:S(2)}) collective-permute-start(bf16[4,1,512,128]{3,2,1,0:T(8,128)(2,1)S(1)} %pad_maximum_fusion.4), channel_id=1, source_target_pairs={{1,0},{2,1},{3,2},{5,4},{6,5},{7,6},{9,8},{10,9},{11,10},{13,12},{... | collective-permute-start | bytes 1572872 | tf_op jit(solution)/shard_map/ppermute | solution.py:76
  89.9 0.0 copy-done.4
  89.9 3.8 %collective-permute-start.6 = (bf16[4,1,512,128]{3,2,1,0:T(8,128)(2,1)S(1)}, bf16[4,1,512,128]{3,2,1,0:T(8,128)(2,1)S(1)}, u32[]{:S(2)}, u32[]{:S(2)}) collective-permute-start(bf16[4,1,512,128]{3,2,1,0:T(8,128)(2,1)S(1)} %pad_maximum_fusion.3), channel_id=1, source_target_pairs={{0,1},{1,2},{2,3},{4,5},{5,6},{6,7},{8,9},{9,10},{10,11},{12,13},{... | collective-permute-start | bytes 1572872 | tf_op jit(solution)/shard_map/ppermute | solution.py:75
  93.7 4.7 %collective-permute-done.7.bottom_ref = bf16[4,1,512,128]{3,2,1,0:T(8,128)(2,1)S(1)} collective-permute-done((bf16[4,1,512,128]{3,2,1,0:T(8,128)(2,1)S(1)}, bf16[4,1,512,128]{3,2,1,0:T(8,128)(2,1)S(1)}, u32[]{:S(2)}, u32[]{:S(2)}) %collective-permute-start.7) | collective-permute-done | bytes 524320 | tf_op jit(solution)/shard_map/ppermute | solution.py:76
  98.4 0.0 copy-start.5
  98.4 1.2 %collective-permute-done.6.top_ref = bf16[4,1,512,128]{3,2,1,0:T(8,128)(2,1)S(1)} collective-permute-done((bf16[4,1,512,128]{3,2,1,0:T(8,128)(2,1)S(1)}, bf16[4,1,512,128]{3,2,1,0:T(8,128)(2,1)S(1)}, u32[]{:S(2)}, u32[]{:S(2)}) %collective-permute-start.6) | collective-permute-done | bytes 524320 | tf_op jit(solution)/shard_map/ppermute | solution.py:75
  99.6 0.0 copy-done.5
  99.6 0.0 copy-start.7
  99.6 0.8 copy-done.7
  100.4 8.7 %shard_map.29 = bf16[2,4,512,128]{3,2,1,0:T(8,128)(2,1)} custom-call(bf16[2,4,512,128]{3,2,1,0:T(8,128)(2,1)} %copy-done.4, bf16[2,4,512,128]{3,2,1,0:T(8,128)(2,1)} %copy-done.1, bf16[4,1,512,128]{3,2,1,0:T(8,128)(2,1)} %copy-done.7, bf16[4,1,512,128]{3,2,1,0:T(8,128)(2,1)} %copy-done.5, bf16[2,4,512,128]{3,2,1,0:T(8,128)(2,1)} %shard_map.28.clip_ref, ...), custom_call_target="tpu_custom_call" | custom-call | flops 3623878656 | bytes 6127616 | tf_op jit(solution)/shard_map/pallas_call | solution.py:59
  (8 shorter events, 0.3 us)
Async XLA Ops:
  1.0 12.0 %collective-permute-start.1 = (bf16[9,192,128]{2,1,0:T(8,128)(2,1)S(1)}, bf16[9,192,128]{2,1,0:T(8,128)(2,1)S(1)}, u32[]{:S(2)}, u32[]{:S(2)}) collective-permute-start(bf16[9,192,128]{2,1,0:T(8,128)(2,1)S(1)} %dynamic-slice_bitcast_fusion), channel_id=1, source_target_pairs={{0,16},{16,0},{1,17},{17,1},{2,18},{18,2},{3,19},{19,3},{4,20},{20... | collective-permute-start | bytes 1327112 | tf_op jit(solution)/shard_map/ppermute | solution.py:87
  13.0 6.6 %collective-permute-start.2 = (bf16[9,192,128]{2,1,0:T(8,128)(2,1)S(1)}, bf16[9,192,128]{2,1,0:T(8,128)(2,1)S(1)}, u32[]{:S(2)}, u32[]{:S(2)}) collective-permute-start(bf16[9,192,128]{2,1,0:T(8,128)(2,1)S(1)} %collective-permute-done.1), channel_id=1, source_target_pairs={{0,1},{1,0},{2,3},{3,2},{4,5},{5,4},{6,7},{7,6},{8,9},{9,8},{10,11... | collective-permute-start | bytes 1327112 | tf_op jit(solution)/shard_map/ppermute | solution.py:88
  16.1 3.7 %copy-start = (bf16[2,4,512,128]{3,2,1,0:T(8,128)(2,1)}, bf16[2,4,512,128]{3,2,1,0:T(8,128)(2,1)S(1)}, u32[]{:S(2)}) copy-start(bf16[2,4,512,128]{3,2,1,0:T(8,128)(2,1)S(1)} %fusion.3.act_ref) | copy-start | bytes 3145732
  16.1 26.0 %collective-permute-start = (bf16[2,4,512,128]{3,2,1,0:T(8,128)(2,1)S(1)}, bf16[2,4,512,128]{3,2,1,0:T(8,128)(2,1)S(1)}, u32[]{:S(2)}, u32[]{:S(2)}) collective-permute-start(bf16[2,4,512,128]{3,2,1,0:T(8,128)(2,1)S(1)} %fusion.3.act_ref), channel_id=1, source_target_pairs={{0,4},{4,8},{8,12},{1,5},{5,9},{9,13},{2,6},{6,10},{10,14},{3,7},{... | collective-permute-start | bytes 3145736 | tf_op jit(solution)/shard_map/ppermute | solution.py:11
  19.7 1.2 %copy-start.2 = (bf16[1,9,384,128]{3,2,1,0:T(8,128)(2,1)S(1)}, bf16[1,9,384,128]{3,2,1,0:T(8,128)(2,1)}, u32[]{:S(2)}) copy-start(bf16[1,9,384,128]{3,2,1,0:T(8,128)(2,1)} %param.3) | copy-start | bytes 2654212
  42.1 2.9 %copy-start.3 = (bf16[2,4,512,128]{3,2,1,0:T(8,128)(2,1)}, bf16[2,4,512,128]{3,2,1,0:T(8,128)(2,1)S(1)}, u32[]{:S(2)}) copy-start(bf16[2,4,512,128]{3,2,1,0:T(8,128)(2,1)S(1)} %collective-permute-done.carried_ref) | copy-start | bytes 3145732
  42.2 10.7 %collective-permute-start.4 = (bf16[4,1,512,128]{3,2,1,0:T(8,128)(2,1)S(1)}, bf16[4,1,512,128]{3,2,1,0:T(8,128)(2,1)S(1)}, u32[]{:S(2)}, u32[]{:S(2)}) collective-permute-start(bf16[4,1,512,128]{3,2,1,0:T(8,128)(2,1)S(1)} %pad_maximum_fusion.2), channel_id=1, source_target_pairs={{1,0},{2,1},{3,2},{5,4},{6,5},{7,6},{9,8},{10,9},{11,10},{13,12},{... | collective-permute-start | bytes 1572872 | tf_op jit(solution)/shard_map/ppermute | solution.py:76
  45.0 9.2 %collective-permute-start.3 = (bf16[4,1,512,128]{3,2,1,0:T(8,128)(2,1)S(1)}, bf16[4,1,512,128]{3,2,1,0:T(8,128)(2,1)S(1)}, u32[]{:S(2)}, u32[]{:S(2)}) collective-permute-start(bf16[4,1,512,128]{3,2,1,0:T(8,128)(2,1)S(1)} %pad_maximum_fusion.1), channel_id=1, source_target_pairs={{0,1},{1,2},{2,3},{4,5},{5,6},{6,7},{8,9},{9,10},{10,11},{12,13},{... | collective-permute-start | bytes 1572872 | tf_op jit(solution)/shard_map/ppermute | solution.py:75
  52.9 1.3 %copy-start.6 = (bf16[4,1,512,128]{3,2,1,0:T(8,128)(2,1)}, bf16[4,1,512,128]{3,2,1,0:T(8,128)(2,1)S(1)}, u32[]{:S(2)}) copy-start(bf16[4,1,512,128]{3,2,1,0:T(8,128)(2,1)S(1)} %collective-permute-done.4.bottom_ref) | copy-start | bytes 1572868
  54.1 0.8 copy-start.8
  65.4 22.4 %copy-start.1 = (bf16[2,4,512,128]{3,2,1,0:T(8,128)(2,1)}, bf16[2,4,512,128]{3,2,1,0:T(8,128)(2,1)S(1)}, u32[]{:S(2)}) copy-start(bf16[2,4,512,128]{3,2,1,0:T(8,128)(2,1)S(1)} %fusion.7.act_ref) | copy-start | bytes 3145732
  65.4 22.3 %collective-permute-start.5 = (bf16[2,4,512,128]{3,2,1,0:T(8,128)(2,1)S(1)}, bf16[2,4,512,128]{3,2,1,0:T(8,128)(2,1)S(1)}, u32[]{:S(2)}, u32[]{:S(2)}) collective-permute-start(bf16[2,4,512,128]{3,2,1,0:T(8,128)(2,1)S(1)} %fusion.7.act_ref), channel_id=1, source_target_pairs={{0,4},{4,8},{8,12},{1,5},{5,9},{9,13},{2,6},{6,10},{10,14},{3,7},{... | collective-permute-start | bytes 3145736 | tf_op jit(solution)/shard_map/ppermute | solution.py:11
  87.8 2.1 %copy-start.4 = (bf16[2,4,512,128]{3,2,1,0:T(8,128)(2,1)}, bf16[2,4,512,128]{3,2,1,0:T(8,128)(2,1)S(1)}, u32[]{:S(2)}) copy-start(bf16[2,4,512,128]{3,2,1,0:T(8,128)(2,1)S(1)} %collective-permute-done.5.carried_ref) | copy-start | bytes 3145732
  87.9 10.5 %collective-permute-start.7 = (bf16[4,1,512,128]{3,2,1,0:T(8,128)(2,1)S(1)}, bf16[4,1,512,128]{3,2,1,0:T(8,128)(2,1)S(1)}, u32[]{:S(2)}, u32[]{:S(2)}) collective-permute-start(bf16[4,1,512,128]{3,2,1,0:T(8,128)(2,1)S(1)} %pad_maximum_fusion.4), channel_id=1, source_target_pairs={{1,0},{2,1},{3,2},{5,4},{6,5},{7,6},{9,8},{10,9},{11,10},{13,12},{... | collective-permute-start | bytes 1572872 | tf_op jit(solution)/shard_map/ppermute | solution.py:76
  89.9 9.8 %collective-permute-start.6 = (bf16[4,1,512,128]{3,2,1,0:T(8,128)(2,1)S(1)}, bf16[4,1,512,128]{3,2,1,0:T(8,128)(2,1)S(1)}, u32[]{:S(2)}, u32[]{:S(2)}) collective-permute-start(bf16[4,1,512,128]{3,2,1,0:T(8,128)(2,1)S(1)} %pad_maximum_fusion.3), channel_id=1, source_target_pairs={{0,1},{1,2},{2,3},{4,5},{5,6},{6,7},{8,9},{9,10},{10,11},{12,13},{... | collective-permute-start | bytes 1572872 | tf_op jit(solution)/shard_map/ppermute | solution.py:75
  98.4 1.3 %copy-start.5 = (bf16[4,1,512,128]{3,2,1,0:T(8,128)(2,1)}, bf16[4,1,512,128]{3,2,1,0:T(8,128)(2,1)S(1)}, u32[]{:S(2)}) copy-start(bf16[4,1,512,128]{3,2,1,0:T(8,128)(2,1)S(1)} %collective-permute-done.7.bottom_ref) | copy-start | bytes 1572868
  99.6 0.8 copy-start.7

commit v4 on v2

--- a/solution.py
+++ b/solution.py
@@ -63,11 +63,13 @@
     )(carried, act, top, bottom, clip, w_mat)
 
 
-def conv_block(clip, w_mat):
+def conv_block(clip, w_mat, tie_taps):
     frames = clip.shape[0]
     assert frames == 2
     act = silu(clip)
     carried = shift_tm(act)
+    if tie_taps:
+        carried, w_mat = lax.optimization_barrier((carried, w_mat))
     n = lax.axis_size("space")
     last_rows = jnp.concatenate([carried[:, -1:], act[:, -1:]], axis=0)
     first_rows = jnp.concatenate([carried[:, :1], act[:, :1]], axis=0)
@@ -95,8 +97,8 @@
 
 def body(video, weights):
     first, second = both_taps(weights)
-    hidden = conv_block(video[0], tap_matrix(first))
-    finished = conv_block(hidden, tap_matrix(second))
+    hidden = conv_block(video[0], tap_matrix(first), False)
+    finished = conv_block(hidden, tap_matrix(second), True)
     return finished[None]
 
 

time: 99.3 us -> 99.3 us (level)
    ppermute x2, waiting for transfers between devices: 3.98 us -> 5.83 us  [conv_block(): top = lax.ppermute(last_rows, 'space', [(i, i + 1) for i in range(n - 1)])]
    ppermute x2, waiting for transfers between devices: 24.8 us -> 22.9 us  [shift_tm(): return lax.ppermute(x, 'tm', [(i, i + 1) for i in range(n - 1)])]
where the time goes in v4:
time: 99.3 us; the launch traced here: 98.9 us
  waiting for transfers between devices  47.1 us (47%)
  starting transfers between devices  23.5 us (24%)
  Pallas kernels  17.5 us (18%)
  local copies, waits for them, and re-layouts  6.49 us (7%)
  other arithmetic  4.18 us (4%)
    ppermute x2, waiting for transfers between devices, shift_tm(): return lax.ppermute(x, 'tm', [(i, i + 1) for i in range(n - 1)])  22.9 us
    pallas_call x2, Pallas kernels, fused_conv(): pl.pallas_call(conv_kernel, out_shape=jax.ShapeDtypeStruct(clip.shape, cl...  17.5 us
    ppermute x1, waiting for transfers between devices, both_taps(): got = lax.ppermute(mine, 'section', [(0, 1), (1, 0)])  9.47 us
    ppermute x2, starting transfers between devices, shift_tm(): return lax.ppermute(x, 'tm', [(i, i + 1) for i in range(n - 1)])  9.29 us
    ppermute x2, waiting for transfers between devices, conv_block(): lax.ppermute(first_rows, 'space', [(i + 1, i) for i in range(n - 1)])  8.91 us
    ppermute x2, starting transfers between devices, conv_block(): top = lax.ppermute(last_rows, 'space', [(i, i + 1) for i in range(n - 1)])  7.02 us
    ppermute x2, waiting for transfers between devices, conv_block(): top = lax.ppermute(last_rows, 'space', [(i, i + 1) for i in range(n - 1)])  5.83 us
    ppermute x2, starting transfers between devices, conv_block(): lax.ppermute(first_rows, 'space', [(i + 1, i) for i in range(n - 1)])  4.02 us
  transfers between devices with their start and end apart: 8, of which 7 were waited for; matrix products, arithmetic and copies ran while one was open for 5% of the time, Pallas kernels for 0%

profile of v4, /device:TPU:1, one launch (start us, length us, event | category | flops | bytes accessed | tf_op | source)
XLA Modules:
  0.0 98.9 jit_solution(17698736923603051588)
XLA Ops:
  0.0 0.0 copy-start.2
  0.0 1.9 %fusion.3.act_ref = bf16[2,4,512,128]{3,2,1,0:T(8,128)(2,1)S(1)} fusion(bf16[1,2,4,512,128]{4,3,2,1,0:T(8,128)(2,1)} %param.2), kind=kLoop, calls=%fused_computation.7 | loop fusion | flops 3145728 | bytes 2097152 | tf_op jit(solution)/shard_map/convert_element_type | solution.py:15
  1.9 0.0 copy-start
  1.9 5.0 %collective-permute-start = (bf16[2,4,512,128]{3,2,1,0:T(8,128)(2,1)S(1)}, bf16[2,4,512,128]{3,2,1,0:T(8,128)(2,1)}, u32[]{:S(2)}, u32[]{:S(2)}) collective-permute-start(bf16[2,4,512,128]{3,2,1,0:T(8,128)(2,1)S(1)} %fusion.3.act_ref), channel_id=1, source_target_pairs={{0,4},{4,8},{8,12},{1,5},{5,9},{9,13},{2,6},{6,10},{10,14},{3,7},{... | collective-permute-start | bytes 3145736 | tf_op jit(solution)/shard_map/ppermute | solution.py:11
  6.9 0.0 copy-done.2
  6.9 1.3 %collective-permute-start.3 = (bf16[9,192,128]{2,1,0:T(8,128)(2,1)S(1)}, bf16[9,192,128]{2,1,0:T(8,128)(2,1)S(1)}, u32[]{:S(2)}, u32[]{:S(2)}) collective-permute-start(bf16[9,192,128]{2,1,0:T(8,128)(2,1)S(1)} %dynamic-slice_bitcast_fusion), channel_id=1, source_target_pairs={{0,16},{16,0},{1,17},{17,1},{2,18},{18,2},{3,19},{19,3},{4,20},{20... | collective-permute-start | bytes 1327112 | tf_op jit(solution)/shard_map/ppermute | solution.py:88
  8.2 9.5 %collective-permute-done.3 = bf16[9,192,128]{2,1,0:T(8,128)(2,1)S(1)} collective-permute-done((bf16[9,192,128]{2,1,0:T(8,128)(2,1)S(1)}, bf16[9,192,128]{2,1,0:T(8,128)(2,1)S(1)}, u32[]{:S(2)}, u32[]{:S(2)}) %collective-permute-start.3) | collective-permute-done | bytes 442400 | tf_op jit(solution)/shard_map/ppermute | solution.py:88
  17.7 1.9 %collective-permute-start.4 = (bf16[9,192,128]{2,1,0:T(8,128)(2,1)S(1)}, bf16[9,192,128]{2,1,0:T(8,128)(2,1)S(1)}, u32[]{:S(2)}, u32[]{:S(2)}) collective-permute-start(bf16[9,192,128]{2,1,0:T(8,128)(2,1)S(1)} %collective-permute-done.3), channel_id=1, source_target_pairs={{0,1},{1,0},{2,3},{3,2},{4,5},{5,4},{6,7},{7,6},{8,9},{9,8},{10,11... | collective-permute-start | bytes 1327112 | tf_op jit(solution)/shard_map/ppermute | solution.py:89
  19.6 8.1 %collective-permute-done.carried_ref = bf16[2,4,512,128]{3,2,1,0:T(8,128)(2,1)} collective-permute-done((bf16[2,4,512,128]{3,2,1,0:T(8,128)(2,1)S(1)}, bf16[2,4,512,128]{3,2,1,0:T(8,128)(2,1)}, u32[]{:S(2)}, u32[]{:S(2)}) %collective-permute-start) | collective-permute-done | bytes 1048608 | tf_op jit(solution)/shard_map/ppermute | solution.py:11
  27.7 1.1 %fusion.10 = (bf16[2,1,512,128]{3,2,1,0:T(8,128)(2,1)S(1)}, bf16[2,1,512,128]{3,2,1,0:T(8,128)(2,1)S(1)}) fusion(bf16[2,4,512,128]{3,2,1,0:T(8,128)(2,1)} %collective-permute-done.carried_ref), kind=kLoop, calls=%fused_computation.26 | loop fusion | bytes 1048576 | tf_op jit(solution)/shard_map/slice | solution.py:75
  28.8 0.0 copy-done
  28.9 4.6 %collective-permute-start.1 = (bf16[4,1,512,128]{3,2,1,0:T(8,128)(2,1)S(1)}, bf16[4,1,512,128]{3,2,1,0:T(8,128)(2,1)S(1)}, u32[]{:S(2)}, u32[]{:S(2)}) collective-permute-start(bf16[4,1,512,128]{3,2,1,0:T(8,128)(2,1)S(1)} %pad_maximum_fusion.1), channel_id=1, source_target_pairs={{0,1},{1,2},{2,3},{4,5},{5,6},{6,7},{8,9},{9,10},{10,11},{12,13},{... | collective-permute-start | bytes 1572872 | tf_op jit(solution)/shard_map/ppermute | solution.py:76
  33.5 1.9 %collective-permute-start.2 = (bf16[4,1,512,128]{3,2,1,0:T(8,128)(2,1)S(1)}, bf16[4,1,512,128]{3,2,1,0:T(8,128)(2,1)S(1)}, u32[]{:S(2)}, u32[]{:S(2)}) collective-permute-start(bf16[4,1,512,128]{3,2,1,0:T(8,128)(2,1)S(1)} %pad_maximum_fusion.2), channel_id=1, source_target_pairs={{1,0},{2,1},{3,2},{5,4},{6,5},{7,6},{9,8},{10,9},{11,10},{13,12},{... | collective-permute-start | bytes 1572872 | tf_op jit(solution)/shard_map/ppermute | solution.py:77
  35.4 0.0 collective-permute-done.4
  35.4 0.1 broadcast_select_fusion.1
  35.5 0.1 pad_maximum_fusion
  35.6 0.2 select_bitcast_fusion
  35.8 0.8 copy.5
  36.6 1.1 %copy.12 = bf16[144,8,3,128]{3,1,2,0:T(8,128)(2,1)} copy(bf16[144,8,3,128]{3,2,1,0:T(4,128)(2,1)S(1)} %bitcast.21) | data formatting | bytes 1769472
  37.6 1.9 %collective-permute-done.1.top_ref = bf16[4,1,512,128]{3,2,1,0:T(8,128)(2,1)S(1)} collective-permute-done((bf16[4,1,512,128]{3,2,1,0:T(8,128)(2,1)S(1)}, bf16[4,1,512,128]{3,2,1,0:T(8,128)(2,1)S(1)}, u32[]{:S(2)}, u32[]{:S(2)}) %collective-permute-start.1) | collective-permute-done | bytes 524320 | tf_op jit(solution)/shard_map/ppermute | solution.py:76
  39.5 0.0 copy-start.4
  39.5 4.5 %collective-permute-done.2.bottom_ref = bf16[4,1,512,128]{3,2,1,0:T(8,128)(2,1)S(1)} collective-permute-done((bf16[4,1,512,128]{3,2,1,0:T(8,128)(2,1)S(1)}, bf16[4,1,512,128]{3,2,1,0:T(8,128)(2,1)S(1)}, u32[]{:S(2)}, u32[]{:S(2)}) %collective-permute-start.2) | collective-permute-done | bytes 524320 | tf_op jit(solution)/shard_map/ppermute | solution.py:77
  44.0 0.0 copy-start.5
  44.0 0.8 copy-done.5
  44.8 0.0 copy-done.4
  44.8 8.7 %shard_map.28.clip_ref = bf16[2,4,512,128]{3,2,1,0:T(8,128)(2,1)} custom-call(bf16[2,4,512,128]{3,2,1,0:T(8,128)(2,1)} %collective-permute-done.carried_ref, bf16[2,4,512,128]{3,2,1,0:T(8,128)(2,1)} %copy-done, bf16[4,1,512,128]{3,2,1,0:T(8,128)(2,1)} %copy-done.4, bf16[4,1,512,128]{3,2,1,0:T(8,128)(2,1)} %copy-done.5, bf16[2,4,512,128]{3,2,1,0:T(8,128)(2,1)} %bitcast.25, ...), custom_call_target="tpu_custom_call" | custom-call | flops 3623878656 | bytes 6127616 | tf_op jit(solution)/shard_map/pallas_call | solution.py:59
  53.5 1.8 %fusion.7.act_ref = bf16[2,4,512,128]{3,2,1,0:T(8,128)(2,1)S(1)} fusion(bf16[2,4,512,128]{3,2,1,0:T(8,128)(2,1)} %shard_map.28.clip_ref), kind=kLoop, calls=%fused_computation.11 | loop fusion | flops 3145728 | bytes 2097152 | tf_op jit(solution)/shard_map/convert_element_type | solution.py:15
  55.3 0.0 copy-start.1
  55.3 4.3 %collective-permute-start.5 = (bf16[2,4,512,128]{3,2,1,0:T(8,128)(2,1)S(1)}, bf16[2,4,512,128]{3,2,1,0:T(8,128)(2,1)S(1)}, u32[]{:S(2)}, u32[]{:S(2)}) collective-permute-start(bf16[2,4,512,128]{3,2,1,0:T(8,128)(2,1)S(1)} %fusion.7.act_ref), channel_id=1, source_target_pairs={{0,4},{4,8},{8,12},{1,5},{5,9},{9,13},{2,6},{6,10},{10,14},{3,7},{... | collective-permute-start | bytes 3145736 | tf_op jit(solution)/shard_map/ppermute | solution.py:11
  59.6 0.8 copy.6
  60.4 1.1 %copy.11 = bf16[144,8,3,128]{3,1,2,0:T(8,128)(2,1)} copy(bf16[144,8,3,128]{3,2,1,0:T(4,128)(2,1)S(1)} %bitcast.22) | data formatting | bytes 1769472
  61.5 0.0 copy-done.1
  61.5 14.8 %collective-permute-done.5.carried_ref = bf16[2,4,512,128]{3,2,1,0:T(8,128)(2,1)S(1)} collective-permute-done((bf16[2,4,512,128]{3,2,1,0:T(8,128)(2,1)S(1)}, bf16[2,4,512,128]{3,2,1,0:T(8,128)(2,1)S(1)}, u32[]{:S(2)}, u32[]{:S(2)}) %collective-permute-start.5) | collective-permute-done | bytes 1048608 | tf_op jit(solution)/shard_map/ppermute | solution.py:11
  76.3 0.0 copy-start.3
  76.4 2.4 %collective-permute-start.6 = (bf16[4,1,512,128]{3,2,1,0:T(8,128)(2,1)S(1)}, bf16[4,1,512,128]{3,2,1,0:T(8,128)(2,1)S(1)}, u32[]{:S(2)}, u32[]{:S(2)}) collective-permute-start(bf16[4,1,512,128]{3,2,1,0:T(8,128)(2,1)S(1)} %pad_maximum_fusion.3), channel_id=1, source_target_pairs={{0,1},{1,2},{2,3},{4,5},{5,6},{6,7},{8,9},{9,10},{10,11},{12,13},{... | collective-permute-start | bytes 1572872 | tf_op jit(solution)/shard_map/ppermute | solution.py:76
  78.9 0.0 copy-done.3
  78.9 2.1 %collective-permute-start.7 = (bf16[4,1,512,128]{3,2,1,0:T(8,128)(2,1)S(1)}, bf16[4,1,512,128]{3,2,1,0:T(8,128)(2,1)S(1)}, u32[]{:S(2)}, u32[]{:S(2)}) collective-permute-start(bf16[4,1,512,128]{3,2,1,0:T(8,128)(2,1)S(1)} %pad_maximum_fusion.4), channel_id=1, source_target_pairs={{1,0},{2,1},{3,2},{5,4},{6,5},{7,6},{9,8},{10,9},{11,10},{13,12},{... | collective-permute-start | bytes 1572872 | tf_op jit(solution)/shard_map/ppermute | solution.py:77
  81.0 3.9 %collective-permute-done.6.top_ref = bf16[4,1,512,128]{3,2,1,0:T(8,128)(2,1)S(1)} collective-permute-done((bf16[4,1,512,128]{3,2,1,0:T(8,128)(2,1)S(1)}, bf16[4,1,512,128]{3,2,1,0:T(8,128)(2,1)S(1)}, u32[]{:S(2)}, u32[]{:S(2)}) %collective-permute-start.6) | collective-permute-done | bytes 524320 | tf_op jit(solution)/shard_map/ppermute | solution.py:76
  84.9 0.0 copy-start.6
  84.9 4.5 %collective-permute-done.7.bottom_ref = bf16[4,1,512,128]{3,2,1,0:T(8,128)(2,1)S(1)} collective-permute-done((bf16[4,1,512,128]{3,2,1,0:T(8,128)(2,1)S(1)}, bf16[4,1,512,128]{3,2,1,0:T(8,128)(2,1)S(1)}, u32[]{:S(2)}, u32[]{:S(2)}) %collective-permute-start.7) | collective-permute-done | bytes 524320 | tf_op jit(solution)/shard_map/ppermute | solution.py:77
  89.4 0.0 copy-done.6
  89.4 0.0 copy-start.7
  89.4 0.8 copy-done.7
  90.2 8.7 %shard_map.29 = bf16[2,4,512,128]{3,2,1,0:T(8,128)(2,1)} custom-call(bf16[2,4,512,128]{3,2,1,0:T(8,128)(2,1)} %copy-done.3, bf16[2,4,512,128]{3,2,1,0:T(8,128)(2,1)} %copy-done.1, bf16[4,1,512,128]{3,2,1,0:T(8,128)(2,1)} %copy-done.6, bf16[4,1,512,128]{3,2,1,0:T(8,128)(2,1)} %copy-done.7, bf16[2,4,512,128]{3,2,1,0:T(8,128)(2,1)} %shard_map.28.clip_ref, ...), custom_call_target="tpu_custom_call" | custom-call | flops 3623878656 | bytes 6127616 | tf_op jit(solution)/shard_map/pallas_call | solution.py:59
  (8 shorter events, 0.3 us)
Async XLA Ops:
  0.0 6.9 %copy-start.2 = (bf16[1,9,384,128]{3,2,1,0:T(8,128)(2,1)S(1)}, bf16[1,9,384,128]{3,2,1,0:T(8,128)(2,1)}, u32[]{:S(2)}) copy-start(bf16[1,9,384,128]{3,2,1,0:T(8,128)(2,1)} %param.3) | copy-start | bytes 2654212
  1.9 26.9 %copy-start = (bf16[2,4,512,128]{3,2,1,0:T(8,128)(2,1)}, bf16[2,4,512,128]{3,2,1,0:T(8,128)(2,1)S(1)}, u32[]{:S(2)}) copy-start(bf16[2,4,512,128]{3,2,1,0:T(8,128)(2,1)S(1)} %fusion.3.act_ref) | copy-start | bytes 3145732
  1.9 25.8 %collective-permute-start = (bf16[2,4,512,128]{3,2,1,0:T(8,128)(2,1)S(1)}, bf16[2,4,512,128]{3,2,1,0:T(8,128)(2,1)}, u32[]{:S(2)}, u32[]{:S(2)}) collective-permute-start(bf16[2,4,512,128]{3,2,1,0:T(8,128)(2,1)S(1)} %fusion.3.act_ref), channel_id=1, source_target_pairs={{0,4},{4,8},{8,12},{1,5},{5,9},{9,13},{2,6},{6,10},{10,14},{3,7},{... | collective-permute-start | bytes 3145736 | tf_op jit(solution)/shard_map/ppermute | solution.py:11
  6.9 10.8 %collective-permute-start.3 = (bf16[9,192,128]{2,1,0:T(8,128)(2,1)S(1)}, bf16[9,192,128]{2,1,0:T(8,128)(2,1)S(1)}, u32[]{:S(2)}, u32[]{:S(2)}) collective-permute-start(bf16[9,192,128]{2,1,0:T(8,128)(2,1)S(1)} %dynamic-slice_bitcast_fusion), channel_id=1, source_target_pairs={{0,16},{16,0},{1,17},{17,1},{2,18},{18,2},{3,19},{19,3},{4,20},{20... | collective-permute-start | bytes 1327112 | tf_op jit(solution)/shard_map/ppermute | solution.py:88
  17.7 17.7 %collective-permute-start.4 = (bf16[9,192,128]{2,1,0:T(8,128)(2,1)S(1)}, bf16[9,192,128]{2,1,0:T(8,128)(2,1)S(1)}, u32[]{:S(2)}, u32[]{:S(2)}) collective-permute-start(bf16[9,192,128]{2,1,0:T(8,128)(2,1)S(1)} %collective-permute-done.3), channel_id=1, source_target_pairs={{0,1},{1,0},{2,3},{3,2},{4,5},{5,4},{6,7},{7,6},{8,9},{9,8},{10,11... | collective-permute-start | bytes 1327112 | tf_op jit(solution)/shard_map/ppermute | solution.py:89
  28.9 10.7 %collective-permute-start.1 = (bf16[4,1,512,128]{3,2,1,0:T(8,128)(2,1)S(1)}, bf16[4,1,512,128]{3,2,1,0:T(8,128)(2,1)S(1)}, u32[]{:S(2)}, u32[]{:S(2)}) collective-permute-start(bf16[4,1,512,128]{3,2,1,0:T(8,128)(2,1)S(1)} %pad_maximum_fusion.1), channel_id=1, source_target_pairs={{0,1},{1,2},{2,3},{4,5},{5,6},{6,7},{8,9},{9,10},{10,11},{12,13},{... | collective-permute-start | bytes 1572872 | tf_op jit(solution)/shard_map/ppermute | solution.py:76
  33.5 10.5 %collective-permute-start.2 = (bf16[4,1,512,128]{3,2,1,0:T(8,128)(2,1)S(1)}, bf16[4,1,512,128]{3,2,1,0:T(8,128)(2,1)S(1)}, u32[]{:S(2)}, u32[]{:S(2)}) collective-permute-start(bf16[4,1,512,128]{3,2,1,0:T(8,128)(2,1)S(1)} %pad_maximum_fusion.2), channel_id=1, source_target_pairs={{1,0},{2,1},{3,2},{5,4},{6,5},{7,6},{9,8},{10,9},{11,10},{13,12},{... | collective-permute-start | bytes 1572872 | tf_op jit(solution)/shard_map/ppermute | solution.py:77
  39.5 5.3 %copy-start.4 = (bf16[4,1,512,128]{3,2,1,0:T(8,128)(2,1)}, bf16[4,1,512,128]{3,2,1,0:T(8,128)(2,1)S(1)}, u32[]{:S(2)}) copy-start(bf16[4,1,512,128]{3,2,1,0:T(8,128)(2,1)S(1)} %collective-permute-done.1.top_ref) | copy-start | bytes 1572868
  44.0 0.8 copy-start.5
  55.3 6.2 %copy-start.1 = (bf16[2,4,512,128]{3,2,1,0:T(8,128)(2,1)}, bf16[2,4,512,128]{3,2,1,0:T(8,128)(2,1)S(1)}, u32[]{:S(2)}) copy-start(bf16[2,4,512,128]{3,2,1,0:T(8,128)(2,1)S(1)} %fusion.7.act_ref) | copy-start | bytes 3145732
  55.3 21.0 %collective-permute-start.5 = (bf16[2,4,512,128]{3,2,1,0:T(8,128)(2,1)S(1)}, bf16[2,4,512,128]{3,2,1,0:T(8,128)(2,1)S(1)}, u32[]{:S(2)}, u32[]{:S(2)}) collective-permute-start(bf16[2,4,512,128]{3,2,1,0:T(8,128)(2,1)S(1)} %fusion.7.act_ref), channel_id=1, source_target_pairs={{0,4},{4,8},{8,12},{1,5},{5,9},{9,13},{2,6},{6,10},{10,14},{3,7},{... | collective-permute-start | bytes 3145736 | tf_op jit(solution)/shard_map/ppermute | solution.py:11
  76.3 2.6 %copy-start.3 = (bf16[2,4,512,128]{3,2,1,0:T(8,128)(2,1)}, bf16[2,4,512,128]{3,2,1,0:T(8,128)(2,1)S(1)}, u32[]{:S(2)}) copy-start(bf16[2,4,512,128]{3,2,1,0:T(8,128)(2,1)S(1)} %collective-permute-done.5.carried_ref) | copy-start | bytes 3145732
  76.4 8.6 %collective-permute-start.6 = (bf16[4,1,512,128]{3,2,1,0:T(8,128)(2,1)S(1)}, bf16[4,1,512,128]{3,2,1,0:T(8,128)(2,1)S(1)}, u32[]{:S(2)}, u32[]{:S(2)}) collective-permute-start(bf16[4,1,512,128]{3,2,1,0:T(8,128)(2,1)S(1)} %pad_maximum_fusion.3), channel_id=1, source_target_pairs={{0,1},{1,2},{2,3},{4,5},{5,6},{6,7},{8,9},{9,10},{10,11},{12,13},{... | collective-permute-start | bytes 1572872 | tf_op jit(solution)/shard_map/ppermute | solution.py:76
  78.9 10.5 %collective-permute-start.7 = (bf16[4,1,512,128]{3,2,1,0:T(8,128)(2,1)S(1)}, bf16[4,1,512,128]{3,2,1,0:T(8,128)(2,1)S(1)}, u32[]{:S(2)}, u32[]{:S(2)}) collective-permute-start(bf16[4,1,512,128]{3,2,1,0:T(8,128)(2,1)S(1)} %pad_maximum_fusion.4), channel_id=1, source_target_pairs={{1,0},{2,1},{3,2},{5,4},{6,5},{7,6},{9,8},{10,9},{11,10},{13,12},{... | collective-permute-start | bytes 1572872 | tf_op jit(solution)/shard_map/ppermute | solution.py:77
  84.9 4.5 %copy-start.6 = (bf16[4,1,512,128]{3,2,1,0:T(8,128)(2,1)}, bf16[4,1,512,128]{3,2,1,0:T(8,128)(2,1)S(1)}, u32[]{:S(2)}) copy-start(bf16[4,1,512,128]{3,2,1,0:T(8,128)(2,1)S(1)} %collective-permute-done.6.top_ref) | copy-start | bytes 1572868
  89.4 0.8 copy-start.7

commit v5 on v2

v5 whole, which is shorter than its diff:
```python
import functools

import jax
import jax.numpy as jnp
from jax import lax
from jax.experimental import pallas as pl
from jax.experimental.pallas import tpu as pltpu
from jax.sharding import PartitionSpec as P


def shift_tm(x):
    n = lax.axis_size("tm")
    return lax.ppermute(x, "tm", [(i, i + 1) for i in range(n - 1)])


def silu(x):
    return jax.nn.silu(x.astype(jnp.float32)).astype(jnp.bfloat16)


def frame_kernel(t, n_out, *refs):
    if t == 1:
        c1_ref, a0_ref, a1_ref, top_a, bot_a, base_ref, w_ref = refs[:7]
        sources = [(c1_ref, top_a, bot_a, 0), (a0_ref, top_a, bot_a, 1), (a1_ref, top_a, bot_a, 2)]
    else:
        c2_ref, c1_ref, a0_ref, top_a, bot_a, top_b, bot_b, base_ref, w_ref = refs[:9]
        sources = [(c2_ref, top_b, bot_b, 0), (c1_ref, top_a, bot_a, 0), (a0_ref, top_a, bot_a, 1)]
    outs = refs[len(refs) - n_out :]
    rows, width, chans = base_ref.shape

    def slab(a, j):
        ref, top, bottom, halo = sources[a]
        if j == 0:
            return top[halo, 0]
        if j == rows + 1:
            return bottom[halo, 0]
        return ref[j - 1]

    column = lax.broadcasted_iota(jnp.int32, (width, chans), 0)
    for h in range(rows):
        lhs = jnp.concatenate([slab(a, h + r) for a in range(3) for r in range(3)], axis=-1)
        z = jnp.dot(lhs, w_ref[...], preferred_element_type=jnp.float32)
        left = pltpu.roll(z[:, :chans], 1, 0)
        right = pltpu.roll(z[:, 2 * chans :], width - 1, 0)
        left = jnp.where(column == 0, 0.0, left)
        right = jnp.where(column == width - 1, 0.0, right)
        total = z[:, chans : 2 * chans] + left + right
        out = (base_ref[h].astype(jnp.float32) + total).astype(outs[0].dtype)
        outs[0][h] = out
        if len(outs) == 2:
            wide = out.astype(jnp.float32)
            outs[1][h] = (wide / (1.0 + jnp.exp(-wide))).astype(outs[1].dtype)


def tap_matrix(taps):
    nine, three_c, chans = taps.shape
    return (
        taps.reshape(nine, 3, chans, chans)
        .transpose(0, 2, 1, 3)
        .reshape(nine * chans, 3 * chans)
    )


def frame_conv(t, operands, base, w_mat, with_act):
    rows, width, chans = base.shape
    flops = 2 * rows * width * w_mat.shape[0] * w_mat.shape[1]
    nbytes = sum(x.size * x.dtype.itemsize for x in operands) + 3 * base.size * 2 + w_mat.size * 2
    shape = jax.ShapeDtypeStruct(base.shape, base.dtype)
    return pl.pallas_call(
        functools.partial(frame_kernel, t, 2 if with_act else 1),
        out_shape=(shape, shape) if with_act else (shape,),
        cost_estimate=pl.CostEstimate(flops=flops, bytes_accessed=nbytes, transcendentals=0),
    )(*operands, base, w_mat)


def conv_block(frames_in, acts, w_mat, with_act):
    x0, x1 = frames_in
    a0, a1 = acts
    n = lax.axis_size("space")
    down = [(i, i + 1) for i in range(n - 1)]
    up = [(i + 1, i) for i in range(n - 1)]
    c1 = shift_tm(a1)
    a0, c1 = lax.optimization_barrier((a0, c1))
    c2 = shift_tm(a0)
    top_a = lax.ppermute(jnp.stack([c1[-1:], a0[-1:], a1[-1:]]), "space", down)
    bot_a = lax.ppermute(jnp.stack([c1[:1], a0[:1], a1[:1]]), "space", up)
    outs1 = frame_conv(1, (c1, a0, a1, top_a, bot_a), x1, w_mat, with_act)
    top_b = lax.ppermute(c2[None, -1:], "space", down)
    bot_b = lax.ppermute(c2[None, :1], "space", up)
    outs0 = frame_conv(0, (c2, c1, a0, top_a, bot_a, top_b, bot_b), x0, w_mat, with_act)
    return outs0, outs1


def both_taps(weights):
    local = weights[0]
    half = local.shape[1] // 2
    section = lax.axis_index("section")
    core = lax.axis_index("space") % 2
    n_space = lax.axis_size("space")
    mine = lax.dynamic_slice_in_dim(local, core * half, half, axis=1)
    got = lax.ppermute(mine, "section", [(0, 1), (1, 0)])
    other = lax.ppermute(got, "space", [(i, i ^ 1) for i in range(n_space)])
    low = jnp.where(core == 0, got, other)
    high = jnp.where(core == 0, other, got)
    remote = jnp.concatenate([low, high], axis=1)
    first = jnp.where(section == 0, local, remote)
    second = jnp.where(section == 0, remote, local)
    return first, second


def body(video, weights):
    first, second = both_taps(weights)
    clip = video[0]
    assert clip.shape[0] == 2
    x0, x1 = clip[0], clip[1]
    a1 = silu(x1)
    a0 = silu(x0)
    (h0, s0), (h1, s1) = conv_block((x0, x1), (a0, a1), tap_matrix(first), True)
    (o0,), (o1,) = conv_block((h0, h1), (s0, s1), tap_matrix(second), False)
    return jnp.stack([o0, o1])[None]


def solution(mesh):
    return jax.shard_map(
        body,
        mesh=mesh,
        in_specs=(P("section", "tm", "space", None, None), P("section", None, None, None)),
        out_specs=P("section", "tm", "space", None, None),
        check_vma=False,
    )
```

time: 99.3 us -> 96.2 us (0.969)
  waiting for transfers between devices: 47.1 us -> 15.2 us
  starting transfers between devices: 23.5 us -> 40.4 us
  Pallas kernels: 17.5 us -> 23.1 us
  local copies, waits for them, and re-layouts: 6.49 us -> 11 us
  other arithmetic: 4.18 us -> 5.49 us
    ppermute x2 -> x4, waiting for transfers between devices: 24.8 us -> 1.85 us  [shift_tm(): return lax.ppermute(x, 'tm', [(i, i + 1) for i in range(n - 1)])]
    ppermute x4 -> x8, starting transfers between devices: 11 us -> 23.4 us  [the longest x2 8.24 us: conv_block(): top_a = lax.ppermute(jnp.stack([c1[-1:], a0[-1:], a1[-1:]]), 'space', down)]
    ppermute x4 -> x8, waiting for transfers between devices: 12.9 us -> 4.88 us  [the longest x2 3.95 us: conv_block(): bot_a = lax.ppermute(jnp.stack([c1[:1], a0[:1], a1[:1]]), 'space', up)]
    pallas_call x2 -> x4, Pallas kernels: 17.5 us -> 23.1 us  [frame_conv(): pl.pallas_call(functools.partial(frame_kernel, t, 2 if with_act else 1),...]
    ppermute x2 -> x4, starting transfers between devices: 9.29 us -> 13.8 us  [shift_tm(): return lax.ppermute(x, 'tm', [(i, i + 1) for i in range(n - 1)])]
    another operation x0 -> x5, local copies, waits for them, and re-layouts: none -> 3.21 us  [conv_block(): bot_a = lax.ppermute(jnp.stack([c1[:1], a0[:1], a1[:1]]), 'space', up)]
    broadcast_in_dim x0 -> x1, other arithmetic: none -> 2.11 us  [body(): return jnp.stack([o0, o1])[None]]
    convert_element_type x2 -> x1, other arithmetic: 3.63 us -> 1.83 us  [silu(): return jax.nn.silu(x.astype(jnp.float32)).astype(jnp.bfloat16)]
  transfers between devices with their start and end apart: 8 -> 14, of which waited for: 7 -> 4; matrix products, arithmetic and copies ran while one was open for 5% -> 9% of each run, Pallas kernels for 0% -> 18%
where the time goes in v5:
time: 96.2 us; the launch traced here: 95.5 us
  starting transfers between devices  40.4 us (42%)
  Pallas kernels  23.1 us (24%)
  waiting for transfers between devices  15.2 us (16%)
  local copies, waits for them, and re-layouts  11 us (11%)
  other arithmetic  5.49 us (6%)
    pallas_call x4, Pallas kernels, frame_conv(): pl.pallas_call(functools.partial(frame_kernel, t, 2 if with_act else 1),...  23.1 us
    ppermute x4, starting transfers between devices, shift_tm(): return lax.ppermute(x, 'tm', [(i, i + 1) for i in range(n - 1)])  13.8 us
    ppermute x1, waiting for transfers between devices, both_taps(): got = lax.ppermute(mine, 'section', [(0, 1), (1, 0)])  8.49 us
    ppermute x2, starting transfers between devices, conv_block(): top_a = lax.ppermute(jnp.stack([c1[-1:], a0[-1:], a1[-1:]]), 'space', down)  8.24 us
    ppermute x2, starting transfers between devices, conv_block(): top_b = lax.ppermute(c2[None, -1:], 'space', down)  7.46 us
    unnamed x34, local copies, waits for them, and re-layouts  5.11 us
    ppermute x2, waiting for transfers between devices, conv_block(): bot_a = lax.ppermute(jnp.stack([c1[:1], a0[:1], a1[:1]]), 'space', up)  3.95 us
    ppermute x2, starting transfers between devices, conv_block(): bot_a = lax.ppermute(jnp.stack([c1[:1], a0[:1], a1[:1]]), 'space', up)  3.84 us
  transfers between devices with their start and end apart: 14, of which 4 were waited for; matrix products, arithmetic and copies ran while one was open for 9% of the time, Pallas kernels for 18%

profile of v5, /device:TPU:1, one launch (start us, length us, event | category | flops | bytes accessed | tf_op | source)
XLA Modules:
  0.0 95.5 jit_solution(15917980084448171286)
XLA Ops:
  0.0 1.8 %fusion.7 = (bf16[4,512,128]{2,1,0:T(8,128)(2,1)S(1)}, bf16[4,512,128]{2,1,0:T(8,128)(2,1)S(1)}) fusion(bf16[1,2,4,512,128]{4,3,2,1,0:T(8,128)(2,1)} %param.2), kind=kLoop, calls=%fused_computation.11 | loop fusion | flops 3145728 | bytes 2097152 | tf_op jit(solution)/shard_map/convert_element_type | solution.py:17
  1.8 0.0 copy-start.2
  1.8 0.0 copy-start.3
  1.9 0.0 copy-start
  1.9 5.0 %collective-permute-start = (bf16[4,512,128]{2,1,0:T(8,128)(2,1)S(1)}, bf16[4,512,128]{2,1,0:T(8,128)(2,1)}, u32[]{:S(2)}, u32[]{:S(2)}) collective-permute-start(bf16[4,512,128]{2,1,0:T(8,128)(2,1)S(1)} %get-tuple-element.25.refs_2_), channel_id=1, source_target_pairs={{0,4},{4,8},{8,12},{1,5},{5,9},{9,13},{2,6},{6,10},{10,14},{3,7},{... | collective-permute-start | bytes 1572872 | tf_op jit(solution)/shard_map/ppermute | solution.py:13
  6.8 0.0 copy-done.1
  6.9 1.3 %collective-permute-start.6 = (bf16[9,192,128]{2,1,0:T(8,128)(2,1)S(1)}, bf16[9,192,128]{2,1,0:T(8,128)(2,1)}, u32[]{:S(2)}, u32[]{:S(2)}) collective-permute-start(bf16[9,192,128]{2,1,0:T(8,128)(2,1)S(1)} %dynamic-slice_bitcast_fusion), channel_id=1, source_target_pairs={{0,16},{16,0},{1,17},{17,1},{2,18},{18,2},{3,19},{19,3},{4,20},{20... | collective-permute-start | bytes 1327112 | tf_op jit(solution)/shard_map/ppermute | solution.py:100
  8.2 0.0 copy-done
  8.2 1.1 %slice_bitcast_fusion = (bf16[4,512,128]{2,1,0:T(8,128)(2,1)}, bf16[4,512,128]{2,1,0:T(8,128)(2,1)}) fusion(bf16[1,2,4,512,128]{4,3,2,1,0:T(8,128)(2,1)S(1)} %copy-done), kind=kLoop, calls=%fused_computation.18 | loop fusion | bytes 2097152 | tf_op jit(solution)/shard_map/squeeze | solution.py:114
  9.3 0.0 copy-done.2
  9.3 8.5 %collective-permute-done.6 = bf16[9,192,128]{2,1,0:T(8,128)(2,1)} collective-permute-done((bf16[9,192,128]{2,1,0:T(8,128)(2,1)S(1)}, bf16[9,192,128]{2,1,0:T(8,128)(2,1)}, u32[]{:S(2)}, u32[]{:S(2)}) %collective-permute-start.6) | collective-permute-done | bytes 442400 | tf_op jit(solution)/shard_map/ppermute | solution.py:100
  17.8 1.9 %collective-permute-start.7 = (bf16[9,192,128]{2,1,0:T(8,128)(2,1)}, bf16[9,192,128]{2,1,0:T(8,128)(2,1)S(1)}, u32[]{:S(2)}, u32[]{:S(2)}) collective-permute-start(bf16[9,192,128]{2,1,0:T(8,128)(2,1)} %collective-permute-done.6), channel_id=1, source_target_pairs={{0,1},{1,0},{2,3},{3,2},{4,5},{5,4},{6,7},{7,6},{8,9},{9,8},{10,11... | collective-permute-start | bytes 1327112 | tf_op jit(solution)/shard_map/ppermute | solution.py:101
  19.6 0.0 collective-permute-done.refs_1_.refs_0_
  19.6 2.5 %collective-permute-start.1 = (bf16[4,512,128]{2,1,0:T(8,128)(2,1)S(1)}, bf16[4,512,128]{2,1,0:T(8,128)(2,1)S(1)}, u32[]{:S(2)}, u32[]{:S(2)}) collective-permute-start(bf16[4,512,128]{2,1,0:T(8,128)(2,1)S(1)} %get-tuple-element.13.refs_2_.refs_1_), channel_id=1, source_target_pairs={{0,4},{4,8},{8,12},{1,5},{5,9},{9,13},{2,6},{6,10},{10,14},{3,7},{... | collective-permute-start | bytes 1572872 | tf_op jit(solution)/shard_map/ppermute | solution.py:13
  22.1 0.0 copy-done.3
  22.1 1.0 %slice_bitcast_fusion.14 = (bf16[1,1,512,128]{3,2,1,0:T(8,128)(2,1)S(1)}, bf16[1,1,512,128]{3,2,1,0:T(8,128)(2,1)S(1)}, bf16[1,1,512,128]{3,2,1,0:T(8,128)(2,1)S(1)}, bf16[1,1,512,128]{3,2,1,0:T(8,128)(2,1)S(1)}) fusion(bf16[4,512,128]{2,1,0:T(8,128)(2,1)S(1)} %get-tuple-element.13.refs_2_.refs_1_, bf16[4,512,128]{2,1,0:T(8,128)(2,1)} %collective-permute-done.refs_1_.refs_0_), kind=kLoop, calls=%fused_computation.39 | loop fusion | bytes 1048576 | tf_op jit(solution)/shard_map/stack | solution.py:85
  23.2 3.6 %collective-permute-start.2 = (bf16[3,1,512,128]{3,2,1,0:T(8,128)(2,1)S(1)}, bf16[3,1,512,128]{3,2,1,0:T(8,128)(2,1)S(1)}, u32[]{:S(2)}, u32[]{:S(2)}) collective-permute-start(bf16[3,1,512,128]{3,2,1,0:T(8,128)(2,1)S(1)} %pad_maximum_fusion.1), channel_id=1, source_target_pairs={{0,1},{1,2},{2,3},{4,5},{5,6},{6,7},{8,9},{9,10},{10,11},{12,13},{... | collective-permute-start | bytes 1179656 | tf_op jit(solution)/shard_map/ppermute | solution.py:84
  26.8 1.9 %collective-permute-start.3 = (bf16[3,1,512,128]{3,2,1,0:T(8,128)(2,1)S(1)}, bf16[3,1,512,128]{3,2,1,0:T(8,128)(2,1)S(1)}, u32[]{:S(2)}, u32[]{:S(2)}) collective-permute-start(bf16[3,1,512,128]{3,2,1,0:T(8,128)(2,1)S(1)} %pad_maximum_fusion.2), channel_id=1, source_target_pairs={{1,0},{2,1},{3,2},{5,4},{6,5},{7,6},{9,8},{10,9},{11,10},{13,12},{... | collective-permute-start | bytes 1179656 | tf_op jit(solution)/shard_map/ppermute | solution.py:85
  28.8 0.0 collective-permute-done.7
  28.8 1.1 %broadcast_select_fusion.1 = (bf16[9,192,128]{2,1,0:T(8,128)(2,1)S(1)}, bf16[9,192,128]{2,1,0:T(8,128)(2,1)S(1)}) fusion(bf16[9,192,128]{2,1,0:T(8,128)(2,1)} %collective-permute-done.6, bf16[9,192,128]{2,1,0:T(8,128)(2,1)S(1)} %collective-permute-done.7, pred[]{:T(512)S(6)} %eq.11), kind=kLoop, calls=%fused_computation.22 | loop fusion | flops 442368 | bytes 1769473 | tf_op jit(solution)/shard_map/jit(_where)/select_n | solution.py:102
  29.9 0.1 pad_maximum_fusion
  29.9 0.2 select_bitcast_fusion
  30.2 0.8 copy.5
  30.9 1.1 %copy.12 = bf16[144,8,3,128]{3,1,2,0:T(8,128)(2,1)} copy(bf16[144,8,3,128]{3,2,1,0:T(4,128)(2,1)S(1)} %bitcast.62) | data formatting | bytes 1769472
  32.0 0.0 collective-permute-done.2.refs_3_
  32.0 3.9 %collective-permute-done.3.refs_4_ = bf16[3,1,512,128]{3,2,1,0:T(8,128)(2,1)S(1)} collective-permute-done((bf16[3,1,512,128]{3,2,1,0:T(8,128)(2,1)S(1)}, bf16[3,1,512,128]{3,2,1,0:T(8,128)(2,1)S(1)}, u32[]{:S(2)}, u32[]{:S(2)}) %collective-permute-start.3) | collective-permute-done | bytes 393248 | tf_op jit(solution)/shard_map/ppermute | solution.py:85
  35.9 0.0 copy-done.8
  35.9 0.8 copy-done.9
  36.7 5.9 %shard_map.29 = (bf16[4,512,128]{2,1,0:T(8,128)(2,1)}, bf16[4,512,128]{2,1,0:T(8,128)(2,1)}) custom-call(bf16[4,512,128]{2,1,0:T(8,128)(2,1)} %collective-permute-done.refs_1_.refs_0_, bf16[4,512,128]{2,1,0:T(8,128)(2,1)} %copy-done.3, bf16[4,512,128]{2,1,0:T(8,128)(2,1)} %copy-done.2, bf16[3,1,512,128]{3,2,1,0:T(8,128)(2,1)} %copy-done.8, ...), custom_call_target="tpu_custom_call" | custom-call | flops 1811939328 | bytes 4816896 | tf_op jit(solution)/shard_map/pallas_call | solution.py:68
  42.6 3.2 %collective-permute-start.8 = (bf16[4,512,128]{2,1,0:T(8,128)(2,1)}, bf16[4,512,128]{2,1,0:T(8,128)(2,1)S(1)}, u32[]{:S(2)}, u32[]{:S(2)}) collective-permute-start(bf16[4,512,128]{2,1,0:T(8,128)(2,1)} %get-tuple-element.16.refs_2_), channel_id=1, source_target_pairs={{0,4},{4,8},{8,12},{1,5},{5,9},{9,13},{2,6},{6,10},{10,14},{3,7},{... | collective-permute-start | bytes 1572872 | tf_op jit(solution)/shard_map/ppermute | solution.py:13
  45.8 0.0 collective-permute-done.1.refs_0_
  45.8 0.0 copy-start.6
  45.8 1.9 %collective-permute-start.5 = (bf16[1,1,512,128]{3,2,1,0:T(8,128)(2,1)S(1)}, bf16[1,1,512,128]{3,2,1,0:T(8,128)(2,1)S(1)}, u32[]{:S(2)}, u32[]{:S(2)}) collective-permute-start(bf16[1,1,512,128]{3,2,1,0:T(8,128)(2,1)S(1)} %get-tuple-element.37), channel_id=1, source_target_pairs={{1,0},{2,1},{3,2},{5,4},{6,5},{7,6},{9,8},{10,9},{11,10},{13,12},{... | collective-permute-start | bytes 393224 | tf_op jit(solution)/shard_map/ppermute | solution.py:88
  47.8 3.6 %collective-permute-start.4 = (bf16[1,1,512,128]{3,2,1,0:T(8,128)(2,1)S(1)}, bf16[1,1,512,128]{3,2,1,0:T(8,128)(2,1)S(1)}, u32[]{:S(2)}, u32[]{:S(2)}) collective-permute-start(bf16[1,1,512,128]{3,2,1,0:T(8,128)(2,1)S(1)} %get-tuple-element.38), channel_id=1, source_target_pairs={{0,1},{1,2},{2,3},{4,5},{5,6},{6,7},{8,9},{9,10},{10,11},{12,13},{... | collective-permute-start | bytes 393224 | tf_op jit(solution)/shard_map/ppermute | solution.py:87
  51.4 1.0 %slice_bitcast_fusion.8 = (bf16[1,1,512,128]{3,2,1,0:T(8,128)(2,1)S(1)}, bf16[1,1,512,128]{3,2,1,0:T(8,128)(2,1)S(1)}) fusion(bf16[4,512,128]{2,1,0:T(8,128)(2,1)} %get-tuple-element.16.refs_2_), kind=kLoop, calls=%fused_computation.33 | loop fusion | bytes 524288 | tf_op jit(solution)/shard_map/stack | solution.py:85
  52.4 0.0 collective-permute-done.5.refs_6_
  52.4 0.0 copy-start.14
  52.4 0.9 collective-permute-done.4.refs_5_
  53.3 0.0 copy-done.14
  53.3 0.7 copy-done.15
  54.0 5.9 %shard_map.28 = (bf16[4,512,128]{2,1,0:T(8,128)(2,1)}, bf16[4,512,128]{2,1,0:T(8,128)(2,1)}) custom-call(bf16[4,512,128]{2,1,0:T(8,128)(2,1)} %copy-done.6, bf16[4,512,128]{2,1,0:T(8,128)(2,1)} %collective-permute-done.refs_1_.refs_0_, bf16[4,512,128]{2,1,0:T(8,128)(2,1)} %copy-done.3, bf16[3,1,512,128]{3,2,1,0:T(8,128)(2,1)} %copy-done.8, ...), custom_call_target="tpu_custom_call" | custom-call | flops 1811939328 | bytes 5079040 | tf_op jit(solution)/shard_map/pallas_call | solution.py:68
  59.9 0.0 collective-permute-done.8.refs_1_.refs_0_
  59.9 1.2 %slice_bitcast_fusion.9 = (bf16[1,1,512,128]{3,2,1,0:T(8,128)(2,1)S(1)}, bf16[1,1,512,128]{3,2,1,0:T(8,128)(2,1)S(1)}) fusion(bf16[4,512,128]{2,1,0:T(8,128)(2,1)} %get-tuple-element.17.refs_2_.refs_1_), kind=kLoop, calls=%fused_computation.34 | loop fusion | bytes 524288 | tf_op jit(solution)/shard_map/stack | solution.py:85
  61.1 3.2 %collective-permute-start.9 = (bf16[4,512,128]{2,1,0:T(8,128)(2,1)}, bf16[4,512,128]{2,1,0:T(8,128)(2,1)S(1)}, u32[]{:S(2)}, u32[]{:S(2)}) collective-permute-start(bf16[4,512,128]{2,1,0:T(8,128)(2,1)} %get-tuple-element.17.refs_2_.refs_1_), channel_id=1, source_target_pairs={{0,4},{4,8},{8,12},{1,5},{5,9},{9,13},{2,6},{6,10},{10,14},{3,7},{... | collective-permute-start | bytes 1572872 | tf_op jit(solution)/shard_map/ppermute | solution.py:13
  64.4 4.6 %collective-permute-start.10 = (bf16[3,1,512,128]{3,2,1,0:T(8,128)(2,1)S(1)}, bf16[3,1,512,128]{3,2,1,0:T(8,128)(2,1)S(1)}, u32[]{:S(2)}, u32[]{:S(2)}) collective-permute-start(bf16[3,1,512,128]{3,2,1,0:T(8,128)(2,1)S(1)} %pad_maximum_fusion.3), channel_id=1, source_target_pairs={{0,1},{1,2},{2,3},{4,5},{5,6},{6,7},{8,9},{9,10},{10,11},{12,13},{... | collective-permute-start | bytes 1179656 | tf_op jit(solution)/shard_map/ppermute | solution.py:84
  69.1 1.9 %collective-permute-start.11 = (bf16[3,1,512,128]{3,2,1,0:T(8,128)(2,1)S(1)}, bf16[3,1,512,128]{3,2,1,0:T(8,128)(2,1)S(1)}, u32[]{:S(2)}, u32[]{:S(2)}) collective-permute-start(bf16[3,1,512,128]{3,2,1,0:T(8,128)(2,1)S(1)} %pad_maximum_fusion.4), channel_id=1, source_target_pairs={{1,0},{2,1},{3,2},{5,4},{6,5},{7,6},{9,8},{10,9},{11,10},{13,12},{... | collective-permute-start | bytes 1179656 | tf_op jit(solution)/shard_map/ppermute | solution.py:85
  71.1 0.8 copy.6
  71.8 1.1 %copy.11 = bf16[144,8,3,128]{3,1,2,0:T(8,128)(2,1)} copy(bf16[144,8,3,128]{3,2,1,0:T(4,128)(2,1)S(1)} %bitcast.63) | data formatting | bytes 1769472
  72.9 1.8 %collective-permute-done.9.refs_0_ = bf16[4,512,128]{2,1,0:T(8,128)(2,1)S(1)} collective-permute-done((bf16[4,512,128]{2,1,0:T(8,128)(2,1)}, bf16[4,512,128]{2,1,0:T(8,128)(2,1)S(1)}, u32[]{:S(2)}, u32[]{:S(2)}) %collective-permute-start.9) | collective-permute-done | bytes 524320 | tf_op jit(solution)/shard_map/ppermute | solution.py:13
  74.7 1.9 %collective-permute-start.13 = (bf16[1,1,512,128]{3,2,1,0:T(8,128)(2,1)S(1)}, bf16[1,1,512,128]{3,2,1,0:T(8,128)(2,1)S(1)}, u32[]{:S(2)}, u32[]{:S(2)}) collective-permute-start(bf16[1,1,512,128]{3,2,1,0:T(8,128)(2,1)S(1)} %get-tuple-element.29), channel_id=1, source_target_pairs={{1,0},{2,1},{3,2},{5,4},{6,5},{7,6},{9,8},{10,9},{11,10},{13,12},{... | collective-permute-start | bytes 393224 | tf_op jit(solution)/shard_map/ppermute | solution.py:88
  76.7 3.8 %collective-permute-start.12 = (bf16[1,1,512,128]{3,2,1,0:T(8,128)(2,1)S(1)}, bf16[1,1,512,128]{3,2,1,0:T(8,128)(2,1)S(1)}, u32[]{:S(2)}, u32[]{:S(2)}) collective-permute-start(bf16[1,1,512,128]{3,2,1,0:T(8,128)(2,1)S(1)} %get-tuple-element.30), channel_id=1, source_target_pairs={{0,1},{1,2},{2,3},{4,5},{5,6},{6,7},{8,9},{9,10},{10,11},{12,13},{... | collective-permute-start | bytes 393224 | tf_op jit(solution)/shard_map/ppermute | solution.py:87
  80.5 0.0 collective-permute-done.10.refs_3_
  80.5 0.0 collective-permute-done.11.refs_4_
  80.5 0.7 copy-done.10
  81.3 0.1 copy-done.11
  81.4 5.6 %shard_map.31 = bf16[4,512,128]{2,1,0:T(8,128)(2,1)} custom-call(bf16[4,512,128]{2,1,0:T(8,128)(2,1)} %copy-done.5, bf16[4,512,128]{2,1,0:T(8,128)(2,1)} %get-tuple-element.17.refs_2_.refs_1_, bf16[4,512,128]{2,1,0:T(8,128)(2,1)} %get-tuple-element.16.refs_2_, bf16[3,1,512,128]{3,2,1,0:T(8,128)(2,1)} %copy-done.10, bf16[3,1,512,128]{3,2,1,0:T(8,128)(2,1)} %copy-done.11, ...), custom_call_target="tpu_custom_call" | custom-call | flops 1811939328 | bytes 4816896 | tf_op jit(solution)/shard_map/pallas_call | solution.py:68
  87.0 0.0 copy-done.7
  87.0 0.0 collective-permute-done.13.refs_6_
  87.0 0.0 collective-permute-done.12.refs_5_
  87.0 0.0 copy-start.13
  87.0 0.6 copy-done.12
  87.7 0.0 copy-done.13
  87.7 5.7 %shard_map.30 = bf16[4,512,128]{2,1,0:T(8,128)(2,1)} custom-call(bf16[4,512,128]{2,1,0:T(8,128)(2,1)} %copy-done.7, bf16[4,512,128]{2,1,0:T(8,128)(2,1)} %copy-done.5, bf16[4,512,128]{2,1,0:T(8,128)(2,1)} %get-tuple-element.17.refs_2_.refs_1_, bf16[3,1,512,128]{3,2,1,0:T(8,128)(2,1)} %copy-done.10, bf16[3,1,512,128]{3,2,1,0:T(8,128)(2,1)} %copy-done.11, ...), custom_call_target="tpu_custom_call" | custom-call | flops 1811939328 | bytes 5079040 | tf_op jit(solution)/shard_map/pallas_call | solution.py:68
  93.4 2.1 %maximum_bitcast_fusion = bf16[1,2,4,512,128]{4,3,2,1,0:T(8,128)(2,1)} fusion(bf16[1,4,512,128]{3,2,1,0:T(8,128)(2,1)S(1)} %bitcast.70, bf16[1,4,512,128]{3,2,1,0:T(8,128)(2,1)} %bitcast.71), kind=kLoop, calls=%fused_computation.12 | loop fusion | flops 524288 | bytes 2097152 | tf_op jit(solution)/shard_map/broadcast_in_dim | solution.py:119
  (22 shorter events, 0.3 us)
Async XLA Ops:
  0.0 6.8 %copy-start.1 = (bf16[1,9,384,128]{3,2,1,0:T(8,128)(2,1)S(1)}, bf16[1,9,384,128]{3,2,1,0:T(8,128)(2,1)}, u32[]{:S(2)}) copy-start(bf16[1,9,384,128]{3,2,1,0:T(8,128)(2,1)} %param.3) | copy-start | bytes 2654212
  1.8 7.4 %copy-start.2 = (bf16[4,512,128]{2,1,0:T(8,128)(2,1)}, bf16[4,512,128]{2,1,0:T(8,128)(2,1)S(1)}, u32[]{:S(2)}) copy-start(bf16[4,512,128]{2,1,0:T(8,128)(2,1)S(1)} %get-tuple-element.25.refs_2_) | copy-start | bytes 1572868
  1.8 20.3 %copy-start.3 = (bf16[4,512,128]{2,1,0:T(8,128)(2,1)}, bf16[4,512,128]{2,1,0:T(8,128)(2,1)S(1)}, u32[]{:S(2)}) copy-start(bf16[4,512,128]{2,1,0:T(8,128)(2,1)S(1)} %get-tuple-element.13.refs_2_.refs_1_) | copy-start | bytes 1572868
  1.9 6.3 %copy-start = (bf16[1,2,4,512,128]{4,3,2,1,0:T(8,128)(2,1)S(1)}, bf16[1,2,4,512,128]{4,3,2,1,0:T(8,128)(2,1)}, u32[]{:S(2)}) copy-start(bf16[1,2,4,512,128]{4,3,2,1,0:T(8,128)(2,1)} %param.2) | copy-start | bytes 3145732
  1.9 17.8 %collective-permute-start = (bf16[4,512,128]{2,1,0:T(8,128)(2,1)S(1)}, bf16[4,512,128]{2,1,0:T(8,128)(2,1)}, u32[]{:S(2)}, u32[]{:S(2)}) collective-permute-start(bf16[4,512,128]{2,1,0:T(8,128)(2,1)S(1)} %get-tuple-element.25.refs_2_), channel_id=1, source_target_pairs={{0,4},{4,8},{8,12},{1,5},{5,9},{9,13},{2,6},{6,10},{10,14},{3,7},{... | collective-permute-start | bytes 1572872 | tf_op jit(solution)/shard_map/ppermute | solution.py:13
  6.9 10.9 %collective-permute-start.6 = (bf16[9,192,128]{2,1,0:T(8,128)(2,1)S(1)}, bf16[9,192,128]{2,1,0:T(8,128)(2,1)}, u32[]{:S(2)}, u32[]{:S(2)}) collective-permute-start(bf16[9,192,128]{2,1,0:T(8,128)(2,1)S(1)} %dynamic-slice_bitcast_fusion), channel_id=1, source_target_pairs={{0,16},{16,0},{1,17},{17,1},{2,18},{18,2},{3,19},{19,3},{4,20},{20... | collective-permute-start | bytes 1327112 | tf_op jit(solution)/shard_map/ppermute | solution.py:100
  17.8 11.0 %collective-permute-start.7 = (bf16[9,192,128]{2,1,0:T(8,128)(2,1)}, bf16[9,192,128]{2,1,0:T(8,128)(2,1)S(1)}, u32[]{:S(2)}, u32[]{:S(2)}) collective-permute-start(bf16[9,192,128]{2,1,0:T(8,128)(2,1)} %collective-permute-done.6), channel_id=1, source_target_pairs={{0,1},{1,0},{2,3},{3,2},{4,5},{5,4},{6,7},{7,6},{8,9},{9,8},{10,11... | collective-permute-start | bytes 1327112 | tf_op jit(solution)/shard_map/ppermute | solution.py:101
  19.6 26.1 %collective-permute-start.1 = (bf16[4,512,128]{2,1,0:T(8,128)(2,1)S(1)}, bf16[4,512,128]{2,1,0:T(8,128)(2,1)S(1)}, u32[]{:S(2)}, u32[]{:S(2)}) collective-permute-start(bf16[4,512,128]{2,1,0:T(8,128)(2,1)S(1)} %get-tuple-element.13.refs_2_.refs_1_), channel_id=1, source_target_pairs={{0,4},{4,8},{8,12},{1,5},{5,9},{9,13},{2,6},{6,10},{10,14},{3,7},{... | collective-permute-start | bytes 1572872 | tf_op jit(solution)/shard_map/ppermute | solution.py:13
  23.2 8.8 %collective-permute-start.2 = (bf16[3,1,512,128]{3,2,1,0:T(8,128)(2,1)S(1)}, bf16[3,1,512,128]{3,2,1,0:T(8,128)(2,1)S(1)}, u32[]{:S(2)}, u32[]{:S(2)}) collective-permute-start(bf16[3,1,512,128]{3,2,1,0:T(8,128)(2,1)S(1)} %pad_maximum_fusion.1), channel_id=1, source_target_pairs={{0,1},{1,2},{2,3},{4,5},{5,6},{6,7},{8,9},{9,10},{10,11},{12,13},{... | collective-permute-start | bytes 1179656 | tf_op jit(solution)/shard_map/ppermute | solution.py:84
  26.8 9.1 %collective-permute-start.3 = (bf16[3,1,512,128]{3,2,1,0:T(8,128)(2,1)S(1)}, bf16[3,1,512,128]{3,2,1,0:T(8,128)(2,1)S(1)}, u32[]{:S(2)}, u32[]{:S(2)}) collective-permute-start(bf16[3,1,512,128]{3,2,1,0:T(8,128)(2,1)S(1)} %pad_maximum_fusion.2), channel_id=1, source_target_pairs={{1,0},{2,1},{3,2},{5,4},{6,5},{7,6},{9,8},{10,9},{11,10},{13,12},{... | collective-permute-start | bytes 1179656 | tf_op jit(solution)/shard_map/ppermute | solution.py:85
  32.0 4.0 %copy-start.8 = (bf16[3,1,512,128]{3,2,1,0:T(8,128)(2,1)}, bf16[3,1,512,128]{3,2,1,0:T(8,128)(2,1)S(1)}, u32[]{:S(2)}) copy-start(bf16[3,1,512,128]{3,2,1,0:T(8,128)(2,1)S(1)} %collective-permute-done.2.refs_3_) | copy-start | bytes 1179652
  35.9 0.8 copy-start.9
  42.6 17.4 %collective-permute-start.8 = (bf16[4,512,128]{2,1,0:T(8,128)(2,1)}, bf16[4,512,128]{2,1,0:T(8,128)(2,1)S(1)}, u32[]{:S(2)}, u32[]{:S(2)}) collective-permute-start(bf16[4,512,128]{2,1,0:T(8,128)(2,1)} %get-tuple-element.16.refs_2_), channel_id=1, source_target_pairs={{0,4},{4,8},{8,12},{1,5},{5,9},{9,13},{2,6},{6,10},{10,14},{3,7},{... | collective-permute-start | bytes 1572872 | tf_op jit(solution)/shard_map/ppermute | solution.py:13
  45.8 7.5 %copy-start.6 = (bf16[4,512,128]{2,1,0:T(8,128)(2,1)}, bf16[4,512,128]{2,1,0:T(8,128)(2,1)S(1)}, u32[]{:S(2)}) copy-start(bf16[4,512,128]{2,1,0:T(8,128)(2,1)S(1)} %collective-permute-done.1.refs_0_) | copy-start | bytes 1572868
  45.8 6.6 %collective-permute-start.5 = (bf16[1,1,512,128]{3,2,1,0:T(8,128)(2,1)S(1)}, bf16[1,1,512,128]{3,2,1,0:T(8,128)(2,1)S(1)}, u32[]{:S(2)}, u32[]{:S(2)}) collective-permute-start(bf16[1,1,512,128]{3,2,1,0:T(8,128)(2,1)S(1)} %get-tuple-element.37), channel_id=1, source_target_pairs={{1,0},{2,1},{3,2},{5,4},{6,5},{7,6},{9,8},{10,9},{11,10},{13,12},{... | collective-permute-start | bytes 393224 | tf_op jit(solution)/shard_map/ppermute | solution.py:88
  47.8 5.6 %collective-permute-start.4 = (bf16[1,1,512,128]{3,2,1,0:T(8,128)(2,1)S(1)}, bf16[1,1,512,128]{3,2,1,0:T(8,128)(2,1)S(1)}, u32[]{:S(2)}, u32[]{:S(2)}) collective-permute-start(bf16[1,1,512,128]{3,2,1,0:T(8,128)(2,1)S(1)} %get-tuple-element.38), channel_id=1, source_target_pairs={{0,1},{1,2},{2,3},{4,5},{5,6},{6,7},{8,9},{9,10},{10,11},{12,13},{... | collective-permute-start | bytes 393224 | tf_op jit(solution)/shard_map/ppermute | solution.py:87
  52.4 0.9 copy-start.14
  53.3 0.7 copy-start.15
  59.9 9.2 %copy-start.5 = (bf16[4,512,128]{2,1,0:T(8,128)(2,1)}, bf16[4,512,128]{2,1,0:T(8,128)(2,1)S(1)}, u32[]{:S(2)}) copy-start(bf16[4,512,128]{2,1,0:T(8,128)(2,1)S(1)} %collective-permute-done.8.refs_1_.refs_0_) | copy-start | bytes 1572868
  61.1 13.6 %collective-permute-start.9 = (bf16[4,512,128]{2,1,0:T(8,128)(2,1)}, bf16[4,512,128]{2,1,0:T(8,128)(2,1)S(1)}, u32[]{:S(2)}, u32[]{:S(2)}) collective-permute-start(bf16[4,512,128]{2,1,0:T(8,128)(2,1)} %get-tuple-element.17.refs_2_.refs_1_), channel_id=1, source_target_pairs={{0,4},{4,8},{8,12},{1,5},{5,9},{9,13},{2,6},{6,10},{10,14},{3,7},{... | collective-permute-start | bytes 1572872 | tf_op jit(solution)/shard_map/ppermute | solution.py:13
  64.4 16.1 %collective-permute-start.10 = (bf16[3,1,512,128]{3,2,1,0:T(8,128)(2,1)S(1)}, bf16[3,1,512,128]{3,2,1,0:T(8,128)(2,1)S(1)}, u32[]{:S(2)}, u32[]{:S(2)}) collective-permute-start(bf16[3,1,512,128]{3,2,1,0:T(8,128)(2,1)S(1)} %pad_maximum_fusion.3), channel_id=1, source_target_pairs={{0,1},{1,2},{2,3},{4,5},{5,6},{6,7},{8,9},{9,10},{10,11},{12,13},{... | collective-permute-start | bytes 1179656 | tf_op jit(solution)/shard_map/ppermute | solution.py:84
  69.1 11.4 %collective-permute-start.11 = (bf16[3,1,512,128]{3,2,1,0:T(8,128)(2,1)S(1)}, bf16[3,1,512,128]{3,2,1,0:T(8,128)(2,1)S(1)}, u32[]{:S(2)}, u32[]{:S(2)}) collective-permute-start(bf16[3,1,512,128]{3,2,1,0:T(8,128)(2,1)S(1)} %pad_maximum_fusion.4), channel_id=1, source_target_pairs={{1,0},{2,1},{3,2},{5,4},{6,5},{7,6},{9,8},{10,9},{11,10},{13,12},{... | collective-permute-start | bytes 1179656 | tf_op jit(solution)/shard_map/ppermute | solution.py:85
  74.7 12.3 %copy-start.7 = (bf16[4,512,128]{2,1,0:T(8,128)(2,1)}, bf16[4,512,128]{2,1,0:T(8,128)(2,1)S(1)}, u32[]{:S(2)}) copy-start(bf16[4,512,128]{2,1,0:T(8,128)(2,1)S(1)} %collective-permute-done.9.refs_0_) | copy-start | bytes 1572868
  74.7 12.2 %collective-permute-start.13 = (bf16[1,1,512,128]{3,2,1,0:T(8,128)(2,1)S(1)}, bf16[1,1,512,128]{3,2,1,0:T(8,128)(2,1)S(1)}, u32[]{:S(2)}, u32[]{:S(2)}) collective-permute-start(bf16[1,1,512,128]{3,2,1,0:T(8,128)(2,1)S(1)} %get-tuple-element.29), channel_id=1, source_target_pairs={{1,0},{2,1},{3,2},{5,4},{6,5},{7,6},{9,8},{10,9},{11,10},{13,12},{... | collective-permute-start | bytes 393224 | tf_op jit(solution)/shard_map/ppermute | solution.py:88
  76.7 10.3 %collective-permute-start.12 = (bf16[1,1,512,128]{3,2,1,0:T(8,128)(2,1)S(1)}, bf16[1,1,512,128]{3,2,1,0:T(8,128)(2,1)S(1)}, u32[]{:S(2)}, u32[]{:S(2)}) collective-permute-start(bf16[1,1,512,128]{3,2,1,0:T(8,128)(2,1)S(1)} %get-tuple-element.30), channel_id=1, source_target_pairs={{0,1},{1,2},{2,3},{4,5},{5,6},{6,7},{8,9},{9,10},{10,11},{12,13},{... | collective-permute-start | bytes 393224 | tf_op jit(solution)/shard_map/ppermute | solution.py:87
  80.5 0.8 copy-start.10
  80.5 0.9 copy-start.11
  87.0 0.7 copy-start.12
  87.0 0.7 copy-start.13
  87.7 5.7 %copy-start.4 = (bf16[4,512,128]{2,1,0:T(8,128)(2,1)S(1)}, bf16[4,512,128]{2,1,0:T(8,128)(2,1)}, u32[]{:S(2)}) copy-start(bf16[4,512,128]{2,1,0:T(8,128)(2,1)} %shard_map.31) | copy-start | bytes 1572868

commit v6 on v5

--- a/solution.py
+++ b/solution.py
@@ -17,13 +17,19 @@
     return jax.nn.silu(x.astype(jnp.float32)).astype(jnp.bfloat16)
 
 
-def frame_kernel(t, n_out, *refs):
+def frame_kernel(t, n_out, merge, *refs):
     if t == 1:
-        c1_ref, a0_ref, a1_ref, top_a, bot_a, base_ref, w_ref = refs[:7]
+        c1_ref, a0_ref, a1_ref, top_a, bot_a = refs[:5]
         sources = [(c1_ref, top_a, bot_a, 0), (a0_ref, top_a, bot_a, 1), (a1_ref, top_a, bot_a, 2)]
+        at = 5
     else:
-        c2_ref, c1_ref, a0_ref, top_a, bot_a, top_b, bot_b, base_ref, w_ref = refs[:9]
+        c2_ref, c1_ref, a0_ref, top_a, bot_a, top_b, bot_b = refs[:7]
         sources = [(c2_ref, top_b, bot_b, 0), (c1_ref, top_a, bot_a, 0), (a0_ref, top_a, bot_a, 1)]
+        at = 7
+    if merge:
+        other_ref = refs[at]
+        at += 1
+    base_ref, w_ref = refs[at], refs[at + 1]
     outs = refs[len(refs) - n_out :]
     rows, width, chans = base_ref.shape
 
@@ -45,10 +51,15 @@
         right = jnp.where(column == width - 1, 0.0, right)
         total = z[:, chans : 2 * chans] + left + right
         out = (base_ref[h].astype(jnp.float32) + total).astype(outs[0].dtype)
-        outs[0][h] = out
+        if merge:
+            outs[0][t, h] = out
+        else:
+            outs[0][h] = out
         if len(outs) == 2:
             wide = out.astype(jnp.float32)
             outs[1][h] = (wide / (1.0 + jnp.exp(-wide))).astype(outs[1].dtype)
+    if merge:
+        outs[0][1 - t] = other_ref[...]
 
 
 def tap_matrix(taps):
@@ -60,19 +71,23 @@
     )
 
 
-def frame_conv(t, operands, base, w_mat, with_act):
+def frame_conv(t, operands, base, w_mat, with_act, merge=None):
     rows, width, chans = base.shape
+    if merge is not None:
+        operands = operands + (merge,)
     flops = 2 * rows * width * w_mat.shape[0] * w_mat.shape[1]
     nbytes = sum(x.size * x.dtype.itemsize for x in operands) + 3 * base.size * 2 + w_mat.size * 2
     shape = jax.ShapeDtypeStruct(base.shape, base.dtype)
+    if merge is not None:
+        shape = jax.ShapeDtypeStruct((2,) + base.shape, base.dtype)
     return pl.pallas_call(
-        functools.partial(frame_kernel, t, 2 if with_act else 1),
+        functools.partial(frame_kernel, t, 2 if with_act else 1, merge is not None),
         out_shape=(shape, shape) if with_act else (shape,),
         cost_estimate=pl.CostEstimate(flops=flops, bytes_accessed=nbytes, transcendentals=0),
     )(*operands, base, w_mat)
 
 
-def conv_block(frames_in, acts, w_mat, with_act):
+def conv_block(frames_in, acts, w_mat, with_act, merge):
     x0, x1 = frames_in
     a0, a1 = acts
     n = lax.axis_size("space")
@@ -86,22 +101,23 @@
     outs1 = frame_conv(1, (c1, a0, a1, top_a, bot_a), x1, w_mat, with_act)
     top_b = lax.ppermute(c2[None, -1:], "space", down)
     bot_b = lax.ppermute(c2[None, :1], "space", up)
-    outs0 = frame_conv(0, (c2, c1, a0, top_a, bot_a, top_b, bot_b), x0, w_mat, with_act)
+    last = outs1[0] if merge else None
+    outs0 = frame_conv(0, (c2, c1, a0, top_a, bot_a, top_b, bot_b), x0, w_mat, with_act, last)
     return outs0, outs1
 
 
 def both_taps(weights):
-    local = weights[0]
-    half = local.shape[1] // 2
+    local = tap_matrix(weights[0])
+    half = local.shape[0] // 2
     section = lax.axis_index("section")
     core = lax.axis_index("space") % 2
     n_space = lax.axis_size("space")
-    mine = lax.dynamic_slice_in_dim(local, core * half, half, axis=1)
+    mine = lax.dynamic_slice_in_dim(local, core * half, half, axis=0)
     got = lax.ppermute(mine, "section", [(0, 1), (1, 0)])
     other = lax.ppermute(got, "space", [(i, i ^ 1) for i in range(n_space)])
     low = jnp.where(core == 0, got, other)
     high = jnp.where(core == 0, other, got)
-    remote = jnp.concatenate([low, high], axis=1)
+    remote = jnp.concatenate([low, high], axis=0)
     first = jnp.where(section == 0, local, remote)
     second = jnp.where(section == 0, remote, local)
     return first, second
@@ -114,9 +130,9 @@
     x0, x1 = clip[0], clip[1]
     a1 = silu(x1)
     a0 = silu(x0)
-    (h0, s0), (h1, s1) = conv_block((x0, x1), (a0, a1), tap_matrix(first), True)
-    (o0,), (o1,) = conv_block((h0, h1), (s0, s1), tap_matrix(second), False)
-    return jnp.stack([o0, o1])[None]
+    (h0, s0), (h1, s1) = conv_block((x0, x1), (a0, a1), first, True, False)
+    (whole,), _ = conv_block((h0, h1), (s0, s1), second, False, True)
+    return whole[None]
 
 
 def solution(mesh):

time: 96.2 us -> 94.1 us (0.978)
  starting transfers between devices: 40.4 us -> 38.3 us
  local copies, waits for them, and re-layouts: 11 us -> 9.25 us
  waiting for transfers between devices: 15.2 us -> 16.6 us
    ppermute x2, waiting for transfers between devices: 0.01 us -> 3.35 us  [conv_block(): bot_b = lax.ppermute(c2[None, :1], 'space', up)]
    ppermute x2, waiting for transfers between devices: 3.95 us -> 0.82 us  [conv_block(): bot_a = lax.ppermute(jnp.stack([c1[:1], a0[:1], a1[:1]]), 'space', up)]
    broadcast_in_dim x1 -> x0, other arithmetic: 2.11 us -> none  [body(): return jnp.stack([o0, o1])[None]]
    unnamed x34 -> x29, local copies, waits for them, and re-layouts: 5.11 us -> 3.12 us
    ppermute x4, waiting for transfers between devices: 1.85 us -> 3.72 us  [shift_tm(): return lax.ppermute(x, 'tm', [(i, i + 1) for i in range(n - 1)])]
    select_n x0 -> x1, other arithmetic: none -> 1.53 us  [both_taps(): second = jnp.where(section == 0, remote, local)]
    transpose x2 -> x0, local copies, waits for them, and re-layouts: 1.53 us -> none  [tap_matrix(): return taps.reshape(nine, 3, chans, chans).transpose(0, 2, 1, 3).reshape(...]
    ppermute x2, starting transfers between devices: 8.24 us -> 7 us  [conv_block(): top_a = lax.ppermute(jnp.stack([c1[-1:], a0[-1:], a1[-1:]]), 'space', down)]
  transfers between devices with their start and end apart: 14 -> 14, of which waited for: 4 -> 5; matrix products, arithmetic and copies ran while one was open for 9% -> 8% of each run, Pallas kernels for 18% -> 19%
where the time goes in v6:
time: 94.1 us; the launch traced here: 93.5 us
  starting transfers between devices  38.3 us (41%)
  Pallas kernels  23.4 us (25%)
  waiting for transfers between devices  16.6 us (18%)
  local copies, waits for them, and re-layouts  9.25 us (10%)
  other arithmetic  5.63 us (6%)
    pallas_call x4, Pallas kernels, frame_conv(): pl.pallas_call(functools.partial(frame_kernel, t, 2 if with_act else 1, m...  23.4 us
    ppermute x4, starting transfers between devices, shift_tm(): return lax.ppermute(x, 'tm', [(i, i + 1) for i in range(n - 1)])  12.9 us
    ppermute x1, waiting for transfers between devices, both_taps(): got = lax.ppermute(mine, 'section', [(0, 1), (1, 0)])  7.5 us
    ppermute x2, starting transfers between devices, conv_block(): top_a = lax.ppermute(jnp.stack([c1[-1:], a0[-1:], a1[-1:]]), 'space', down)  7 us
    ppermute x2, starting transfers between devices, conv_block(): top_b = lax.ppermute(c2[None, -1:], 'space', down)  6.59 us
    ppermute x2, starting transfers between devices, conv_block(): bot_b = lax.ppermute(c2[None, :1], 'space', up)  4.51 us
    another operation x5, local copies, waits for them, and re-layouts, conv_block(): bot_a = lax.ppermute(jnp.stack([c1[:1], a0[:1], a1[:1]]), 'space', up)  4.17 us
    ppermute x2, starting transfers between devices, conv_block(): bot_a = lax.ppermute(jnp.stack([c1[:1], a0[:1], a1[:1]]), 'space', up)  4.13 us
  transfers between devices with their start and end apart: 14, of which 5 were waited for; matrix products, arithmetic and copies ran while one was open for 8% of the time, Pallas kernels for 19%

profile of v6, /device:TPU:1, one launch (start us, length us, event | category | flops | bytes accessed | tf_op | source)
XLA Modules:
  0.0 93.5 jit_solution(12471470063510958104)
XLA Ops:
  0.0 2.8 %fusion.7 = (bf16[4,512,128]{2,1,0:T(8,128)(2,1)}, bf16[4,512,128]{2,1,0:T(8,128)(2,1)}) fusion(bf16[1,2,4,512,128]{4,3,2,1,0:T(8,128)(2,1)} %param.2), kind=kLoop, calls=%fused_computation.11 | loop fusion | flops 3145728 | bytes 2097152 | tf_op jit(solution)/shard_map/convert_element_type | solution.py:17
  2.8 4.8 %collective-permute-start = (bf16[4,512,128]{2,1,0:T(8,128)(2,1)}, bf16[4,512,128]{2,1,0:T(8,128)(2,1)}, u32[]{:S(2)}, u32[]{:S(2)}) collective-permute-start(bf16[4,512,128]{2,1,0:T(8,128)(2,1)} %get-tuple-element.25.refs_2_), channel_id=1, source_target_pairs={{0,4},{4,8},{8,12},{1,5},{5,9},{9,13},{2,6},{6,10},{10,14},{3,7},{... | collective-permute-start | bytes 1572872 | tf_op jit(solution)/shard_map/ppermute | solution.py:13
  7.6 0.0 copy-done.2
  7.6 0.8 copy.4
  8.4 0.1 copy.9
  8.6 0.0 copy-start
  8.6 0.1 constant_dynamic-slice_fusion
  8.6 1.3 %collective-permute-start.6 = (bf16[576,384]{1,0:T(8,128)(2,1)S(1)}, bf16[576,384]{1,0:T(8,128)(2,1)}, u32[]{:S(2)}, u32[]{:S(2)}) collective-permute-start(bf16[576,384]{1,0:T(8,128)(2,1)S(1)} %constant_dynamic-slice_fusion), channel_id=1, source_target_pairs={{0,16},{16,0},{1,17},{17,1},{2,18},{18,2},{3,19},{19,3},{4,20},{20... | collective-permute-start | bytes 1327112 | tf_op jit(solution)/shard_map/ppermute | solution.py:116
  9.9 1.0 %slice_bitcast_fusion.6 = (bf16[1,1,512,128]{3,2,1,0:T(8,128)(2,1)S(1)}, bf16[1,1,512,128]{3,2,1,0:T(8,128)(2,1)S(1)}) fusion(bf16[4,512,128]{2,1,0:T(8,128)(2,1)} %get-tuple-element.25.refs_2_), kind=kLoop, calls=%fused_computation.28 | loop fusion | bytes 524288 | tf_op jit(solution)/shard_map/stack | solution.py:100
  10.9 0.0 copy-done
  10.9 0.0 copy-start.1
  10.9 1.1 %slice_bitcast_fusion = (bf16[4,512,128]{2,1,0:T(8,128)(2,1)}, bf16[4,512,128]{2,1,0:T(8,128)(2,1)}) fusion(bf16[1,2,4,512,128]{4,3,2,1,0:T(8,128)(2,1)S(1)} %copy-done), kind=kLoop, calls=%fused_computation.16 | loop fusion | bytes 2097152 | tf_op jit(solution)/shard_map/squeeze | solution.py:130
  12.0 7.5 %collective-permute-done.6 = bf16[576,384]{1,0:T(8,128)(2,1)} collective-permute-done((bf16[576,384]{1,0:T(8,128)(2,1)S(1)}, bf16[576,384]{1,0:T(8,128)(2,1)}, u32[]{:S(2)}, u32[]{:S(2)}) %collective-permute-start.6) | collective-permute-done | bytes 442400 | tf_op jit(solution)/shard_map/ppermute | solution.py:116
  19.5 1.9 %collective-permute-start.7 = (bf16[576,384]{1,0:T(8,128)(2,1)}, bf16[576,384]{1,0:T(8,128)(2,1)S(1)}, u32[]{:S(2)}, u32[]{:S(2)}) collective-permute-start(bf16[576,384]{1,0:T(8,128)(2,1)} %collective-permute-done.6), channel_id=1, source_target_pairs={{0,1},{1,0},{2,3},{3,2},{4,5},{5,4},{6,7},{7,6},{8,9},{9,8},{10,11... | collective-permute-start | bytes 1327112 | tf_op jit(solution)/shard_map/ppermute | solution.py:117
  21.4 0.0 collective-permute-done.refs_1_.refs_0_
  21.4 0.0 copy-done.1
  21.4 2.5 %collective-permute-start.1 = (bf16[4,512,128]{2,1,0:T(8,128)(2,1)S(1)}, bf16[4,512,128]{2,1,0:T(8,128)(2,1)S(1)}, u32[]{:S(2)}, u32[]{:S(2)}) collective-permute-start(bf16[4,512,128]{2,1,0:T(8,128)(2,1)S(1)} %copy-done.1), channel_id=1, source_target_pairs={{0,4},{4,8},{8,12},{1,5},{5,9},{9,13},{2,6},{6,10},{10,14},{3,7},{... | collective-permute-start | bytes 1572872 | tf_op jit(solution)/shard_map/ppermute | solution.py:13
  23.9 1.0 %slice_bitcast_fusion.14 = (bf16[1,1,512,128]{3,2,1,0:T(8,128)(2,1)S(1)}, bf16[1,1,512,128]{3,2,1,0:T(8,128)(2,1)S(1)}, bf16[1,1,512,128]{3,2,1,0:T(8,128)(2,1)S(1)}, bf16[1,1,512,128]{3,2,1,0:T(8,128)(2,1)S(1)}) fusion(bf16[4,512,128]{2,1,0:T(8,128)(2,1)S(1)} %copy-done.1, bf16[4,512,128]{2,1,0:T(8,128)(2,1)} %collective-permute-done.refs_1_.refs_0_), kind=kLoop, calls=%fused_computation.36 | loop fusion | bytes 1048576 | tf_op jit(solution)/shard_map/stack | solution.py:100
  24.9 2.2 %collective-permute-start.3 = (bf16[3,1,512,128]{3,2,1,0:T(8,128)(2,1)S(1)}, bf16[3,1,512,128]{3,2,1,0:T(8,128)(2,1)S(1)}, u32[]{:S(2)}, u32[]{:S(2)}) collective-permute-start(bf16[3,1,512,128]{3,2,1,0:T(8,128)(2,1)S(1)} %pad_maximum_fusion.2), channel_id=1, source_target_pairs={{1,0},{2,1},{3,2},{5,4},{6,5},{7,6},{9,8},{10,9},{11,10},{13,12},{... | collective-permute-start | bytes 1179656 | tf_op jit(solution)/shard_map/ppermute | solution.py:100
  27.2 3.4 %collective-permute-start.2 = (bf16[3,1,512,128]{3,2,1,0:T(8,128)(2,1)S(1)}, bf16[3,1,512,128]{3,2,1,0:T(8,128)(2,1)S(1)}, u32[]{:S(2)}, u32[]{:S(2)}) collective-permute-start(bf16[3,1,512,128]{3,2,1,0:T(8,128)(2,1)S(1)} %pad_maximum_fusion.1), channel_id=1, source_target_pairs={{0,1},{1,2},{2,3},{4,5},{5,6},{6,7},{8,9},{9,10},{10,11},{12,13},{... | collective-permute-start | bytes 1179656 | tf_op jit(solution)/shard_map/ppermute | solution.py:99
  30.6 0.0 collective-permute-done.7
  30.6 1.1 %broadcast_select_fusion.3 = (bf16[576,384]{1,0:T(8,128)(2,1)S(1)}, bf16[576,384]{1,0:T(8,128)(2,1)S(1)}) fusion(bf16[576,384]{1,0:T(8,128)(2,1)} %collective-permute-done.6, bf16[576,384]{1,0:T(8,128)(2,1)S(1)} %collective-permute-done.7, pred[]{:T(512)S(6)} %eq.11), kind=kLoop, calls=%fused_computation.19 | loop fusion | flops 442368 | bytes 1769473 | tf_op jit(solution)/shard_map/jit(_where)/select_n | solution.py:118
  31.7 1.5 %broadcast_select_fusion = (bf16[1152,384]{1,0:T(8,128)(2,1)}, bf16[1152,384]{1,0:T(8,128)(2,1)}) fusion(pred[]{:T(512)S(6)} %eq.10, bf16[576,384]{1,0:T(8,128)(2,1)S(1)} %get-tuple-element.28, bf16[576,384]{1,0:T(8,128)(2,1)S(1)} %get-tuple-element.27, bf16[144,8,3,128]{3,2,1,0:T(4,128)(2,1)S(1)} %bitcast.51), kind=kLoop, calls=%fused_computation.14 | loop fusion | flops 2654208 | bytes 3538945 | tf_op jit(solution)/shard_map/jit(_where)/select_n | solution.py:122
  33.2 0.8 collective-permute-done.3.refs_4_
  34.0 1.2 %collective-permute-done.2.refs_3_ = bf16[3,1,512,128]{3,2,1,0:T(8,128)(2,1)S(1)} collective-permute-done((bf16[3,1,512,128]{3,2,1,0:T(8,128)(2,1)S(1)}, bf16[3,1,512,128]{3,2,1,0:T(8,128)(2,1)S(1)}, u32[]{:S(2)}, u32[]{:S(2)}) %collective-permute-start.2) | collective-permute-done | bytes 393248 | tf_op jit(solution)/shard_map/ppermute | solution.py:99
  35.3 0.0 copy-done.6
  35.3 0.7 copy-done.7
  36.0 5.8 %shard_map.29 = (bf16[4,512,128]{2,1,0:T(8,128)(2,1)}, bf16[4,512,128]{2,1,0:T(8,128)(2,1)}) custom-call(bf16[4,512,128]{2,1,0:T(8,128)(2,1)} %collective-permute-done.refs_1_.refs_0_, bf16[4,512,128]{2,1,0:T(8,128)(2,1)} %get-tuple-element.13.refs_2_.refs_1_, bf16[4,512,128]{2,1,0:T(8,128)(2,1)} %get-tuple-element.25.refs_2_, ...), custom_call_target="tpu_custom_call" | custom-call | flops 1811939328 | bytes 4816896 | tf_op jit(solution)/shard_map/pallas_call | solution.py:83
  41.9 3.2 %collective-permute-start.8 = (bf16[4,512,128]{2,1,0:T(8,128)(2,1)}, bf16[4,512,128]{2,1,0:T(8,128)(2,1)S(1)}, u32[]{:S(2)}, u32[]{:S(2)}) collective-permute-start(bf16[4,512,128]{2,1,0:T(8,128)(2,1)} %get-tuple-element.16.refs_2_), channel_id=1, source_target_pairs={{0,4},{4,8},{8,12},{1,5},{5,9},{9,13},{2,6},{6,10},{10,14},{3,7},{... | collective-permute-start | bytes 1572872 | tf_op jit(solution)/shard_map/ppermute | solution.py:13
  45.1 0.0 collective-permute-done.1.refs_0_
  45.1 0.0 copy-start.4
  45.1 4.7 %collective-permute-start.4 = (bf16[1,1,512,128]{3,2,1,0:T(8,128)(2,1)S(1)}, bf16[1,1,512,128]{3,2,1,0:T(8,128)(2,1)S(1)}, u32[]{:S(2)}, u32[]{:S(2)}) collective-permute-start(bf16[1,1,512,128]{3,2,1,0:T(8,128)(2,1)S(1)} %get-tuple-element.38), channel_id=1, source_target_pairs={{0,1},{1,2},{2,3},{4,5},{5,6},{6,7},{8,9},{9,10},{10,11},{12,13},{... | collective-permute-start | bytes 393224 | tf_op jit(solution)/shard_map/ppermute | solution.py:102
  49.8 1.9 %collective-permute-start.5 = (bf16[1,1,512,128]{3,2,1,0:T(8,128)(2,1)S(1)}, bf16[1,1,512,128]{3,2,1,0:T(8,128)(2,1)S(1)}, u32[]{:S(2)}, u32[]{:S(2)}) collective-permute-start(bf16[1,1,512,128]{3,2,1,0:T(8,128)(2,1)S(1)} %get-tuple-element.37), channel_id=1, source_target_pairs={{1,0},{2,1},{3,2},{5,4},{6,5},{7,6},{9,8},{10,9},{11,10},{13,12},{... | collective-permute-start | bytes 393224 | tf_op jit(solution)/shard_map/ppermute | solution.py:103
  51.7 1.0 %slice_bitcast_fusion.8 = (bf16[1,1,512,128]{3,2,1,0:T(8,128)(2,1)S(1)}, bf16[1,1,512,128]{3,2,1,0:T(8,128)(2,1)S(1)}) fusion(bf16[4,512,128]{2,1,0:T(8,128)(2,1)} %get-tuple-element.16.refs_2_), kind=kLoop, calls=%fused_computation.30 | loop fusion | bytes 524288 | tf_op jit(solution)/shard_map/stack | solution.py:100
  52.7 0.0 collective-permute-done.4.refs_5_
  52.7 0.0 copy-start.12
  52.7 3.3 %collective-permute-done.5.refs_6_ = bf16[1,1,512,128]{3,2,1,0:T(8,128)(2,1)S(1)} collective-permute-done((bf16[1,1,512,128]{3,2,1,0:T(8,128)(2,1)S(1)}, bf16[1,1,512,128]{3,2,1,0:T(8,128)(2,1)S(1)}, u32[]{:S(2)}, u32[]{:S(2)}) %collective-permute-start.5) | collective-permute-done | bytes 131104 | tf_op jit(solution)/shard_map/ppermute | solution.py:103
  56.1 0.0 copy-done.4
  56.1 0.0 copy-done.12
  56.1 0.6 copy-done.13
  56.7 5.9 %shard_map.28 = (bf16[4,512,128]{2,1,0:T(8,128)(2,1)}, bf16[4,512,128]{2,1,0:T(8,128)(2,1)}) custom-call(bf16[4,512,128]{2,1,0:T(8,128)(2,1)} %copy-done.4, bf16[4,512,128]{2,1,0:T(8,128)(2,1)} %collective-permute-done.refs_1_.refs_0_, bf16[4,512,128]{2,1,0:T(8,128)(2,1)} %get-tuple-element.13.refs_2_.refs_1_, bf16[3,1,512,128]{3,2,1,0:T(8,128)(2,1)} %copy-done.7, ...), custom_call_target="tpu_custom_call" | custom-call | flops 1811939328 | bytes 5079040 | tf_op jit(solution)/shard_map/pallas_call | solution.py:83
  62.7 0.0 collective-permute-done.8.refs_0_.refs_1_
  62.7 1.2 %slice_bitcast_fusion.9 = (bf16[1,1,512,128]{3,2,1,0:T(8,128)(2,1)S(1)}, bf16[1,1,512,128]{3,2,1,0:T(8,128)(2,1)S(1)}) fusion(bf16[4,512,128]{2,1,0:T(8,128)(2,1)} %get-tuple-element.17.refs_1_.refs_2_), kind=kLoop, calls=%fused_computation.31 | loop fusion | bytes 524288 | tf_op jit(solution)/shard_map/stack | solution.py:100
  63.8 2.4 %collective-permute-start.9 = (bf16[4,512,128]{2,1,0:T(8,128)(2,1)}, bf16[4,512,128]{2,1,0:T(8,128)(2,1)S(1)}, u32[]{:S(2)}, u32[]{:S(2)}) collective-permute-start(bf16[4,512,128]{2,1,0:T(8,128)(2,1)} %get-tuple-element.17.refs_1_.refs_2_), channel_id=1, source_target_pairs={{0,4},{4,8},{8,12},{1,5},{5,9},{9,13},{2,6},{6,10},{10,14},{3,7},{... | collective-permute-start | bytes 1572872 | tf_op jit(solution)/shard_map/ppermute | solution.py:13
  66.4 1.9 %collective-permute-start.11 = (bf16[3,1,512,128]{3,2,1,0:T(8,128)(2,1)S(1)}, bf16[3,1,512,128]{3,2,1,0:T(8,128)(2,1)S(1)}, u32[]{:S(2)}, u32[]{:S(2)}) collective-permute-start(bf16[3,1,512,128]{3,2,1,0:T(8,128)(2,1)S(1)} %pad_maximum_fusion.4), channel_id=1, source_target_pairs={{1,0},{2,1},{3,2},{5,4},{6,5},{7,6},{9,8},{10,9},{11,10},{13,12},{... | collective-permute-start | bytes 1179656 | tf_op jit(solution)/shard_map/ppermute | solution.py:100
  68.3 0.0 copy-done.3
  68.4 3.6 %collective-permute-start.10 = (bf16[3,1,512,128]{3,2,1,0:T(8,128)(2,1)S(1)}, bf16[3,1,512,128]{3,2,1,0:T(8,128)(2,1)S(1)}, u32[]{:S(2)}, u32[]{:S(2)}) collective-permute-start(bf16[3,1,512,128]{3,2,1,0:T(8,128)(2,1)S(1)} %pad_maximum_fusion.3), channel_id=1, source_target_pairs={{0,1},{1,2},{2,3},{4,5},{5,6},{6,7},{8,9},{9,10},{10,11},{12,13},{... | collective-permute-start | bytes 1179656 | tf_op jit(solution)/shard_map/ppermute | solution.py:99
  72.0 3.7 %collective-permute-done.9.refs_0_ = bf16[4,512,128]{2,1,0:T(8,128)(2,1)S(1)} collective-permute-done((bf16[4,512,128]{2,1,0:T(8,128)(2,1)}, bf16[4,512,128]{2,1,0:T(8,128)(2,1)S(1)}, u32[]{:S(2)}, u32[]{:S(2)}) %collective-permute-start.9) | collective-permute-done | bytes 524320 | tf_op jit(solution)/shard_map/ppermute | solution.py:13
  75.7 1.9 %collective-permute-start.12 = (bf16[1,1,512,128]{3,2,1,0:T(8,128)(2,1)S(1)}, bf16[1,1,512,128]{3,2,1,0:T(8,128)(2,1)S(1)}, u32[]{:S(2)}, u32[]{:S(2)}) collective-permute-start(bf16[1,1,512,128]{3,2,1,0:T(8,128)(2,1)S(1)} %get-tuple-element.30), channel_id=1, source_target_pairs={{0,1},{1,2},{2,3},{4,5},{5,6},{6,7},{8,9},{9,10},{10,11},{12,13},{... | collective-permute-start | bytes 393224 | tf_op jit(solution)/shard_map/ppermute | solution.py:102
  77.7 2.6 %collective-permute-start.13 = (bf16[1,1,512,128]{3,2,1,0:T(8,128)(2,1)S(1)}, bf16[1,1,512,128]{3,2,1,0:T(8,128)(2,1)S(1)}, u32[]{:S(2)}, u32[]{:S(2)}) collective-permute-start(bf16[1,1,512,128]{3,2,1,0:T(8,128)(2,1)S(1)} %get-tuple-element.29), channel_id=1, source_target_pairs={{1,0},{2,1},{3,2},{5,4},{6,5},{7,6},{9,8},{10,9},{11,10},{13,12},{... | collective-permute-start | bytes 393224 | tf_op jit(solution)/shard_map/ppermute | solution.py:103
  80.3 0.0 collective-permute-done.11.refs_4_
  80.3 0.0 copy-start.8
  80.3 0.0 collective-permute-done.10.refs_3_
  80.3 0.0 copy-start.9
  80.3 0.7 copy-done.8
  81.0 0.1 copy-done.9
  81.2 5.6 %shard_map.30.refs_7_ = bf16[4,512,128]{2,1,0:T(8,128)(2,1)} custom-call(bf16[4,512,128]{2,1,0:T(8,128)(2,1)} %copy-done.3, bf16[4,512,128]{2,1,0:T(8,128)(2,1)} %get-tuple-element.17.refs_1_.refs_2_, bf16[4,512,128]{2,1,0:T(8,128)(2,1)} %get-tuple-element.16.refs_2_, bf16[3,1,512,128]{3,2,1,0:T(8,128)(2,1)} %copy-done.9, ...), custom_call_target="tpu_custom_call" | custom-call | flops 1811939328 | bytes 4816896 | tf_op jit(solution)/shard_map/pallas_call | solution.py:83
  86.8 0.0 copy-done.5
  86.8 0.0 collective-permute-done.12.refs_5_
  86.8 0.0 collective-permute-done.13.refs_6_
  86.8 0.0 copy-start.11
  86.8 0.6 copy-done.10
  87.4 0.1 copy-done.11
  87.5 6.0 %shard_map.31 = bf16[2,4,512,128]{3,2,1,0:T(8,128)(2,1)} custom-call(bf16[4,512,128]{2,1,0:T(8,128)(2,1)} %copy-done.5, bf16[4,512,128]{2,1,0:T(8,128)(2,1)} %copy-done.3, bf16[4,512,128]{2,1,0:T(8,128)(2,1)} %get-tuple-element.17.refs_1_.refs_2_, bf16[3,1,512,128]{3,2,1,0:T(8,128)(2,1)} %copy-done.9, bf16[3,1,512,128]{3,2,1,0:T(8,128)(2,1)} %copy-done.8, ...), custom_call_target="tpu_custom_call" | custom-call | flops 1811939328 | bytes 5603328 | tf_op jit(solution)/shard_map/pallas_call | solution.py:83
  (14 shorter events, 0.3 us)
Async XLA Ops:
  0.0 7.6 %copy-start.2 = (bf16[1,9,384,128]{3,2,1,0:T(8,128)(2,1)S(1)}, bf16[1,9,384,128]{3,2,1,0:T(8,128)(2,1)}, u32[]{:S(2)}) copy-start(bf16[1,9,384,128]{3,2,1,0:T(8,128)(2,1)} %param.3) | copy-start | bytes 2654212
  2.8 18.6 %collective-permute-start = (bf16[4,512,128]{2,1,0:T(8,128)(2,1)}, bf16[4,512,128]{2,1,0:T(8,128)(2,1)}, u32[]{:S(2)}, u32[]{:S(2)}) collective-permute-start(bf16[4,512,128]{2,1,0:T(8,128)(2,1)} %get-tuple-element.25.refs_2_), channel_id=1, source_target_pairs={{0,4},{4,8},{8,12},{1,5},{5,9},{9,13},{2,6},{6,10},{10,14},{3,7},{... | collective-permute-start | bytes 1572872 | tf_op jit(solution)/shard_map/ppermute | solution.py:13
  8.6 2.3 %copy-start = (bf16[1,2,4,512,128]{4,3,2,1,0:T(8,128)(2,1)S(1)}, bf16[1,2,4,512,128]{4,3,2,1,0:T(8,128)(2,1)}, u32[]{:S(2)}) copy-start(bf16[1,2,4,512,128]{4,3,2,1,0:T(8,128)(2,1)} %param.2) | copy-start | bytes 3145732
  8.6 10.9 %collective-permute-start.6 = (bf16[576,384]{1,0:T(8,128)(2,1)S(1)}, bf16[576,384]{1,0:T(8,128)(2,1)}, u32[]{:S(2)}, u32[]{:S(2)}) collective-permute-start(bf16[576,384]{1,0:T(8,128)(2,1)S(1)} %constant_dynamic-slice_fusion), channel_id=1, source_target_pairs={{0,16},{16,0},{1,17},{17,1},{2,18},{18,2},{3,19},{19,3},{4,20},{20... | collective-permute-start | bytes 1327112 | tf_op jit(solution)/shard_map/ppermute | solution.py:116
  10.9 10.5 %copy-start.1 = (bf16[4,512,128]{2,1,0:T(8,128)(2,1)S(1)}, bf16[4,512,128]{2,1,0:T(8,128)(2,1)}, u32[]{:S(2)}) copy-start(bf16[4,512,128]{2,1,0:T(8,128)(2,1)} %get-tuple-element.13.refs_2_.refs_1_) | copy-start | bytes 1572868
  19.5 11.0 %collective-permute-start.7 = (bf16[576,384]{1,0:T(8,128)(2,1)}, bf16[576,384]{1,0:T(8,128)(2,1)S(1)}, u32[]{:S(2)}, u32[]{:S(2)}) collective-permute-start(bf16[576,384]{1,0:T(8,128)(2,1)} %collective-permute-done.6), channel_id=1, source_target_pairs={{0,1},{1,0},{2,3},{3,2},{4,5},{5,4},{6,7},{7,6},{8,9},{9,8},{10,11... | collective-permute-start | bytes 1327112 | tf_op jit(solution)/shard_map/ppermute | solution.py:117
  21.4 23.7 %collective-permute-start.1 = (bf16[4,512,128]{2,1,0:T(8,128)(2,1)S(1)}, bf16[4,512,128]{2,1,0:T(8,128)(2,1)S(1)}, u32[]{:S(2)}, u32[]{:S(2)}) collective-permute-start(bf16[4,512,128]{2,1,0:T(8,128)(2,1)S(1)} %copy-done.1), channel_id=1, source_target_pairs={{0,4},{4,8},{8,12},{1,5},{5,9},{9,13},{2,6},{6,10},{10,14},{3,7},{... | collective-permute-start | bytes 1572872 | tf_op jit(solution)/shard_map/ppermute | solution.py:13
  24.9 9.1 %collective-permute-start.3 = (bf16[3,1,512,128]{3,2,1,0:T(8,128)(2,1)S(1)}, bf16[3,1,512,128]{3,2,1,0:T(8,128)(2,1)S(1)}, u32[]{:S(2)}, u32[]{:S(2)}) collective-permute-start(bf16[3,1,512,128]{3,2,1,0:T(8,128)(2,1)S(1)} %pad_maximum_fusion.2), channel_id=1, source_target_pairs={{1,0},{2,1},{3,2},{5,4},{6,5},{7,6},{9,8},{10,9},{11,10},{13,12},{... | collective-permute-start | bytes 1179656 | tf_op jit(solution)/shard_map/ppermute | solution.py:100
  27.2 8.1 %collective-permute-start.2 = (bf16[3,1,512,128]{3,2,1,0:T(8,128)(2,1)S(1)}, bf16[3,1,512,128]{3,2,1,0:T(8,128)(2,1)S(1)}, u32[]{:S(2)}, u32[]{:S(2)}) collective-permute-start(bf16[3,1,512,128]{3,2,1,0:T(8,128)(2,1)S(1)} %pad_maximum_fusion.1), channel_id=1, source_target_pairs={{0,1},{1,2},{2,3},{4,5},{5,6},{6,7},{8,9},{9,10},{10,11},{12,13},{... | collective-permute-start | bytes 1179656 | tf_op jit(solution)/shard_map/ppermute | solution.py:99
  34.0 1.2 %copy-start.6 = (bf16[3,1,512,128]{3,2,1,0:T(8,128)(2,1)}, bf16[3,1,512,128]{3,2,1,0:T(8,128)(2,1)S(1)}, u32[]{:S(2)}) copy-start(bf16[3,1,512,128]{3,2,1,0:T(8,128)(2,1)S(1)} %collective-permute-done.3.refs_4_) | copy-start | bytes 1179652
  35.3 0.7 copy-start.7
  41.9 20.8 %collective-permute-start.8 = (bf16[4,512,128]{2,1,0:T(8,128)(2,1)}, bf16[4,512,128]{2,1,0:T(8,128)(2,1)S(1)}, u32[]{:S(2)}, u32[]{:S(2)}) collective-permute-start(bf16[4,512,128]{2,1,0:T(8,128)(2,1)} %get-tuple-element.16.refs_2_), channel_id=1, source_target_pairs={{0,4},{4,8},{8,12},{1,5},{5,9},{9,13},{2,6},{6,10},{10,14},{3,7},{... | collective-permute-start | bytes 1572872 | tf_op jit(solution)/shard_map/ppermute | solution.py:13
  45.1 11.0 %copy-start.4 = (bf16[4,512,128]{2,1,0:T(8,128)(2,1)}, bf16[4,512,128]{2,1,0:T(8,128)(2,1)S(1)}, u32[]{:S(2)}) copy-start(bf16[4,512,128]{2,1,0:T(8,128)(2,1)S(1)} %collective-permute-done.1.refs_0_) | copy-start | bytes 1572868
  45.1 7.6 %collective-permute-start.4 = (bf16[1,1,512,128]{3,2,1,0:T(8,128)(2,1)S(1)}, bf16[1,1,512,128]{3,2,1,0:T(8,128)(2,1)S(1)}, u32[]{:S(2)}, u32[]{:S(2)}) collective-permute-start(bf16[1,1,512,128]{3,2,1,0:T(8,128)(2,1)S(1)} %get-tuple-element.38), channel_id=1, source_target_pairs={{0,1},{1,2},{2,3},{4,5},{5,6},{6,7},{8,9},{9,10},{10,11},{12,13},{... | collective-permute-start | bytes 393224 | tf_op jit(solution)/shard_map/ppermute | solution.py:102
  49.8 6.3 %collective-permute-start.5 = (bf16[1,1,512,128]{3,2,1,0:T(8,128)(2,1)S(1)}, bf16[1,1,512,128]{3,2,1,0:T(8,128)(2,1)S(1)}, u32[]{:S(2)}, u32[]{:S(2)}) collective-permute-start(bf16[1,1,512,128]{3,2,1,0:T(8,128)(2,1)S(1)} %get-tuple-element.37), channel_id=1, source_target_pairs={{1,0},{2,1},{3,2},{5,4},{6,5},{7,6},{9,8},{10,9},{11,10},{13,12},{... | collective-permute-start | bytes 393224 | tf_op jit(solution)/shard_map/ppermute | solution.py:103
  52.7 3.4 %copy-start.12 = (bf16[1,1,512,128]{3,2,1,0:T(8,128)(2,1)}, bf16[1,1,512,128]{3,2,1,0:T(8,128)(2,1)S(1)}, u32[]{:S(2)}) copy-start(bf16[1,1,512,128]{3,2,1,0:T(8,128)(2,1)S(1)} %collective-permute-done.4.refs_5_) | copy-start | bytes 393220
  56.1 0.7 copy-start.13
  62.7 5.7 %copy-start.3 = (bf16[4,512,128]{2,1,0:T(8,128)(2,1)}, bf16[4,512,128]{2,1,0:T(8,128)(2,1)S(1)}, u32[]{:S(2)}) copy-start(bf16[4,512,128]{2,1,0:T(8,128)(2,1)S(1)} %collective-permute-done.8.refs_0_.refs_1_) | copy-start | bytes 1572868
  63.8 11.9 %collective-permute-start.9 = (bf16[4,512,128]{2,1,0:T(8,128)(2,1)}, bf16[4,512,128]{2,1,0:T(8,128)(2,1)S(1)}, u32[]{:S(2)}, u32[]{:S(2)}) collective-permute-start(bf16[4,512,128]{2,1,0:T(8,128)(2,1)} %get-tuple-element.17.refs_1_.refs_2_), channel_id=1, source_target_pairs={{0,4},{4,8},{8,12},{1,5},{5,9},{9,13},{2,6},{6,10},{10,14},{3,7},{... | collective-permute-start | bytes 1572872 | tf_op jit(solution)/shard_map/ppermute | solution.py:13
  66.4 13.9 %collective-permute-start.11 = (bf16[3,1,512,128]{3,2,1,0:T(8,128)(2,1)S(1)}, bf16[3,1,512,128]{3,2,1,0:T(8,128)(2,1)S(1)}, u32[]{:S(2)}, u32[]{:S(2)}) collective-permute-start(bf16[3,1,512,128]{3,2,1,0:T(8,128)(2,1)S(1)} %pad_maximum_fusion.4), channel_id=1, source_target_pairs={{1,0},{2,1},{3,2},{5,4},{6,5},{7,6},{9,8},{10,9},{11,10},{13,12},{... | collective-permute-start | bytes 1179656 | tf_op jit(solution)/shard_map/ppermute | solution.py:100
  68.4 11.9 %collective-permute-start.10 = (bf16[3,1,512,128]{3,2,1,0:T(8,128)(2,1)S(1)}, bf16[3,1,512,128]{3,2,1,0:T(8,128)(2,1)S(1)}, u32[]{:S(2)}, u32[]{:S(2)}) collective-permute-start(bf16[3,1,512,128]{3,2,1,0:T(8,128)(2,1)S(1)} %pad_maximum_fusion.3), channel_id=1, source_target_pairs={{0,1},{1,2},{2,3},{4,5},{5,6},{6,7},{8,9},{9,10},{10,11},{12,13},{... | collective-permute-start | bytes 1179656 | tf_op jit(solution)/shard_map/ppermute | solution.py:99
  75.7 11.1 %copy-start.5 = (bf16[4,512,128]{2,1,0:T(8,128)(2,1)}, bf16[4,512,128]{2,1,0:T(8,128)(2,1)S(1)}, u32[]{:S(2)}) copy-start(bf16[4,512,128]{2,1,0:T(8,128)(2,1)S(1)} %collective-permute-done.9.refs_0_) | copy-start | bytes 1572868
  75.7 11.0 %collective-permute-start.12 = (bf16[1,1,512,128]{3,2,1,0:T(8,128)(2,1)S(1)}, bf16[1,1,512,128]{3,2,1,0:T(8,128)(2,1)S(1)}, u32[]{:S(2)}, u32[]{:S(2)}) collective-permute-start(bf16[1,1,512,128]{3,2,1,0:T(8,128)(2,1)S(1)} %get-tuple-element.30), channel_id=1, source_target_pairs={{0,1},{1,2},{2,3},{4,5},{5,6},{6,7},{8,9},{9,10},{10,11},{12,13},{... | collective-permute-start | bytes 393224 | tf_op jit(solution)/shard_map/ppermute | solution.py:102
  77.7 9.1 %collective-permute-start.13 = (bf16[1,1,512,128]{3,2,1,0:T(8,128)(2,1)S(1)}, bf16[1,1,512,128]{3,2,1,0:T(8,128)(2,1)S(1)}, u32[]{:S(2)}, u32[]{:S(2)}) collective-permute-start(bf16[1,1,512,128]{3,2,1,0:T(8,128)(2,1)S(1)} %get-tuple-element.29), channel_id=1, source_target_pairs={{1,0},{2,1},{3,2},{5,4},{6,5},{7,6},{9,8},{10,9},{11,10},{13,12},{... | collective-permute-start | bytes 393224 | tf_op jit(solution)/shard_map/ppermute | solution.py:103
  80.3 0.8 copy-start.8
  80.3 0.9 copy-start.9
  86.8 0.7 copy-start.10
  86.8 0.7 copy-start.11

commit v7 on v6

--- a/solution.py
+++ b/solution.py
@@ -94,6 +94,9 @@
     down = [(i, i + 1) for i in range(n - 1)]
     up = [(i + 1, i) for i in range(n - 1)]
     c1 = shift_tm(a1)
+    if merge:
+        c1, w_mat = lax.optimization_barrier((c1, w_mat))
+        w_mat = pick_second(*w_mat)
     a0, c1 = lax.optimization_barrier((a0, c1))
     c2 = shift_tm(a0)
     top_a = lax.ppermute(jnp.stack([c1[-1:], a0[-1:], a1[-1:]]), "space", down)
@@ -119,8 +122,11 @@
     high = jnp.where(core == 0, other, got)
     remote = jnp.concatenate([low, high], axis=0)
     first = jnp.where(section == 0, local, remote)
-    second = jnp.where(section == 0, remote, local)
-    return first, second
+    return first, (local, remote)
+
+
+def pick_second(local, remote):
+    return jnp.where(lax.axis_index("section") == 0, remote, local)
 
 
 def body(video, weights):

time: 94.1 us -> 95.9 us (1.019)
  local copies, waits for them, and re-layouts: 9.25 us -> 11 us
    concatenate x0 -> x1, other arithmetic: none -> 1.32 us  [both_taps(): remote = jnp.concatenate([low, high], axis=0)]
    ppermute x4, waiting for transfers between devices: 3.72 us -> 2.68 us  [shift_tm(): return lax.ppermute(x, 'tm', [(i, i + 1) for i in range(n - 1)])]
    broadcast_in_dim x2, local copies, waits for them, and re-layouts: 0.04 us -> 1.01 us  [conv_block(): bot_b = lax.ppermute(c2[None, :1], 'space', up)]
    unnamed x29 -> x25, local copies, waits for them, and re-layouts: 3.12 us -> 3.76 us
  transfers between devices with their start and end apart: 14 -> 14, of which waited for: 5 -> 5; matrix products, arithmetic and copies ran while one was open for 8% -> 10% of each run, Pallas kernels for 19% -> 18%
where the time goes in v7:
time: 95.9 us; the launch traced here: 95.2 us
  starting transfers between devices  38.3 us (40%)
  Pallas kernels  23.4 us (24%)
  waiting for transfers between devices  15.8 us (16%)
  local copies, waits for them, and re-layouts  11 us (11%)
  other arithmetic  6.47 us (7%)
    pallas_call x4, Pallas kernels, frame_conv(): pl.pallas_call(functools.partial(frame_kernel, t, 2 if with_act else 1, m...  23.4 us
    ppermute x4, starting transfers between devices, shift_tm(): return lax.ppermute(x, 'tm', [(i, i + 1) for i in range(n - 1)])  12.9 us
    ppermute x1, waiting for transfers between devices, both_taps(): got = lax.ppermute(mine, 'section', [(0, 1), (1, 0)])  7.51 us
    ppermute x2, starting transfers between devices, conv_block(): top_a = lax.ppermute(jnp.stack([c1[-1:], a0[-1:], a1[-1:]]), 'space', down)  7.01 us
    ppermute x2, starting transfers between devices, conv_block(): top_b = lax.ppermute(c2[None, -1:], 'space', down)  6.59 us
    ppermute x2, starting transfers between devices, conv_block(): bot_b = lax.ppermute(c2[None, :1], 'space', up)  4.51 us
    another operation x5, local copies, waits for them, and re-layouts, conv_block(): bot_a = lax.ppermute(jnp.stack([c1[:1], a0[:1], a1[:1]]), 'space', up)  4.3 us
    ppermute x2, starting transfers between devices, conv_block(): bot_a = lax.ppermute(jnp.stack([c1[:1], a0[:1], a1[:1]]), 'space', up)  4.11 us
  transfers between devices with their start and end apart: 14, of which 5 were waited for; matrix products, arithmetic and copies ran while one was open for 10% of the time, Pallas kernels for 18%

profile of v7, /device:TPU:1, one launch (start us, length us, event | category | flops | bytes accessed | tf_op | source)
XLA Modules:
  0.0 95.2 jit_solution(5990487168977451904)
XLA Ops:
  0.0 0.0 copy-start.1
  0.0 2.8 %fusion.7 = (bf16[4,512,128]{2,1,0:T(8,128)(2,1)}, bf16[4,512,128]{2,1,0:T(8,128)(2,1)}) fusion(bf16[1,2,4,512,128]{4,3,2,1,0:T(8,128)(2,1)} %param.2), kind=kLoop, calls=%fused_computation.11 | loop fusion | flops 3145728 | bytes 2097152 | tf_op jit(solution)/shard_map/convert_element_type | solution.py:17
  2.8 4.8 %collective-permute-start = (bf16[4,512,128]{2,1,0:T(8,128)(2,1)}, bf16[4,512,128]{2,1,0:T(8,128)(2,1)}, u32[]{:S(2)}, u32[]{:S(2)}) collective-permute-start(bf16[4,512,128]{2,1,0:T(8,128)(2,1)} %get-tuple-element.29.refs_2_), channel_id=1, source_target_pairs={{0,4},{4,8},{8,12},{1,5},{5,9},{9,13},{2,6},{6,10},{10,14},{3,7},{... | collective-permute-start | bytes 1572872 | tf_op jit(solution)/shard_map/ppermute | solution.py:13
  7.7 0.0 copy-done.1
  7.7 0.8 copy.4
  8.4 0.1 copy.9
  8.6 0.0 copy-start
  8.6 0.1 constant_dynamic-slice_fusion
  8.7 1.3 %collective-permute-start.6 = (bf16[576,384]{1,0:T(8,128)(2,1)S(1)}, bf16[576,384]{1,0:T(8,128)(2,1)}, u32[]{:S(2)}, u32[]{:S(2)}) collective-permute-start(bf16[576,384]{1,0:T(8,128)(2,1)S(1)} %constant_dynamic-slice_fusion), channel_id=1, source_target_pairs={{0,16},{16,0},{1,17},{17,1},{2,18},{18,2},{3,19},{19,3},{4,20},{20... | collective-permute-start | bytes 1327112 | tf_op jit(solution)/shard_map/ppermute | solution.py:119
  9.9 1.0 %slice_bitcast_fusion.6 = (bf16[1,1,512,128]{3,2,1,0:T(8,128)(2,1)S(1)}, bf16[1,1,512,128]{3,2,1,0:T(8,128)(2,1)S(1)}) fusion(bf16[4,512,128]{2,1,0:T(8,128)(2,1)} %get-tuple-element.29.refs_2_), kind=kLoop, calls=%fused_computation.28 | loop fusion | bytes 524288 | tf_op jit(solution)/shard_map/stack | solution.py:103
  10.9 0.0 copy-done
  10.9 1.1 %slice_bitcast_fusion = (bf16[4,512,128]{2,1,0:T(8,128)(2,1)}, bf16[4,512,128]{2,1,0:T(8,128)(2,1)}) fusion(bf16[1,2,4,512,128]{4,3,2,1,0:T(8,128)(2,1)S(1)} %copy-done), kind=kLoop, calls=%fused_computation.16 | loop fusion | bytes 2097152 | tf_op jit(solution)/shard_map/squeeze | solution.py:136
  12.0 7.5 %collective-permute-done.6 = bf16[576,384]{1,0:T(8,128)(2,1)} collective-permute-done((bf16[576,384]{1,0:T(8,128)(2,1)S(1)}, bf16[576,384]{1,0:T(8,128)(2,1)}, u32[]{:S(2)}, u32[]{:S(2)}) %collective-permute-start.6) | collective-permute-done | bytes 442400 | tf_op jit(solution)/shard_map/ppermute | solution.py:119
  19.6 1.9 %collective-permute-start.7 = (bf16[576,384]{1,0:T(8,128)(2,1)}, bf16[576,384]{1,0:T(8,128)(2,1)S(1)}, u32[]{:S(2)}, u32[]{:S(2)}) collective-permute-start(bf16[576,384]{1,0:T(8,128)(2,1)} %collective-permute-done.6), channel_id=1, source_target_pairs={{0,1},{1,0},{2,3},{3,2},{4,5},{5,4},{6,7},{7,6},{8,9},{9,8},{10,11... | collective-permute-start | bytes 1327112 | tf_op jit(solution)/shard_map/ppermute | solution.py:120
  21.4 0.0 collective-permute-done.refs_1_.refs_0_
  21.4 3.2 %collective-permute-start.1 = (bf16[4,512,128]{2,1,0:T(8,128)(2,1)}, bf16[4,512,128]{2,1,0:T(8,128)(2,1)}, u32[]{:S(2)}, u32[]{:S(2)}) collective-permute-start(bf16[4,512,128]{2,1,0:T(8,128)(2,1)} %get-tuple-element.16.refs_2_.refs_1_), channel_id=1, source_target_pairs={{0,4},{4,8},{8,12},{1,5},{5,9},{9,13},{2,6},{6,10},{10,14},{3,7},{... | collective-permute-start | bytes 1572872 | tf_op jit(solution)/shard_map/ppermute | solution.py:13
  24.6 1.1 %slice_bitcast_fusion.14 = (bf16[1,1,512,128]{3,2,1,0:T(8,128)(2,1)S(1)}, bf16[1,1,512,128]{3,2,1,0:T(8,128)(2,1)S(1)}, bf16[1,1,512,128]{3,2,1,0:T(8,128)(2,1)S(1)}, bf16[1,1,512,128]{3,2,1,0:T(8,128)(2,1)S(1)}) fusion(bf16[4,512,128]{2,1,0:T(8,128)(2,1)} %get-tuple-element.16.refs_2_.refs_1_, bf16[4,512,128]{2,1,0:T(8,128)(2,1)} %collective-permute-done.refs_1_.refs_0_), kind=kLoop, calls=%fused_computation.36 | loop fusion | bytes 1048576 | tf_op jit(solution)/shard_map/stack | solution.py:103
  25.8 2.2 %collective-permute-start.3 = (bf16[3,1,512,128]{3,2,1,0:T(8,128)(2,1)S(1)}, bf16[3,1,512,128]{3,2,1,0:T(8,128)(2,1)S(1)}, u32[]{:S(2)}, u32[]{:S(2)}) collective-permute-start(bf16[3,1,512,128]{3,2,1,0:T(8,128)(2,1)S(1)} %pad_maximum_fusion.2), channel_id=1, source_target_pairs={{1,0},{2,1},{3,2},{5,4},{6,5},{7,6},{9,8},{10,9},{11,10},{13,12},{... | collective-permute-start | bytes 1179656 | tf_op jit(solution)/shard_map/ppermute | solution.py:103
  28.1 3.4 %collective-permute-start.2 = (bf16[3,1,512,128]{3,2,1,0:T(8,128)(2,1)S(1)}, bf16[3,1,512,128]{3,2,1,0:T(8,128)(2,1)S(1)}, u32[]{:S(2)}, u32[]{:S(2)}) collective-permute-start(bf16[3,1,512,128]{3,2,1,0:T(8,128)(2,1)S(1)} %pad_maximum_fusion.1), channel_id=1, source_target_pairs={{0,1},{1,2},{2,3},{4,5},{5,6},{6,7},{8,9},{9,10},{10,11},{12,13},{... | collective-permute-start | bytes 1179656 | tf_op jit(solution)/shard_map/ppermute | solution.py:102
  31.4 0.0 collective-permute-done.7
  31.5 1.1 %broadcast_select_fusion.3 = (bf16[576,384]{1,0:T(8,128)(2,1)S(1)}, bf16[576,384]{1,0:T(8,128)(2,1)S(1)}) fusion(bf16[576,384]{1,0:T(8,128)(2,1)} %collective-permute-done.6, bf16[576,384]{1,0:T(8,128)(2,1)S(1)} %collective-permute-done.7, pred[]{:T(512)S(6)} %eq.11), kind=kLoop, calls=%fused_computation.19 | loop fusion | flops 442368 | bytes 1769473 | tf_op jit(solution)/shard_map/jit(_where)/select_n | solution.py:121
  32.6 1.3 %pad_maximum_fusion = (bf16[1152,384]{1,0:T(8,128)(2,1)S(1)}, bf16[1152,384]{1,0:T(8,128)(2,1)}) fusion(bf16[576,384]{1,0:T(8,128)(2,1)S(1)} %get-tuple-element.34, bf16[576,384]{1,0:T(8,128)(2,1)S(1)} %get-tuple-element.33, pred[]{:T(512)S(6)} %eq.10, bf16[144,8,3,128]{3,2,1,0:T(4,128)(2,1)S(1)} %bitcast.51), kind=kLoop, calls=%fused_computation.13 | loop fusion | flops 2211840 | bytes 3538945 | tf_op jit(solution)/shard_map/concatenate | solution.py:123
  33.9 1.0 %collective-permute-done.3.refs_4_ = bf16[3,1,512,128]{3,2,1,0:T(8,128)(2,1)S(1)} collective-permute-done((bf16[3,1,512,128]{3,2,1,0:T(8,128)(2,1)S(1)}, bf16[3,1,512,128]{3,2,1,0:T(8,128)(2,1)S(1)}, u32[]{:S(2)}, u32[]{:S(2)}) %collective-permute-start.3) | collective-permute-done | bytes 393248 | tf_op jit(solution)/shard_map/ppermute | solution.py:103
  34.9 0.0 copy-start.4
  34.9 1.2 %collective-permute-done.2.refs_3_ = bf16[3,1,512,128]{3,2,1,0:T(8,128)(2,1)S(1)} collective-permute-done((bf16[3,1,512,128]{3,2,1,0:T(8,128)(2,1)S(1)}, bf16[3,1,512,128]{3,2,1,0:T(8,128)(2,1)S(1)}, u32[]{:S(2)}, u32[]{:S(2)}) %collective-permute-start.2) | collective-permute-done | bytes 393248 | tf_op jit(solution)/shard_map/ppermute | solution.py:102
  36.1 0.0 copy-start.5
  36.1 0.8 copy-done.5
  36.9 0.0 copy-done.4
  36.9 5.8 %shard_map.29 = (bf16[4,512,128]{2,1,0:T(8,128)(2,1)}, bf16[4,512,128]{2,1,0:T(8,128)(2,1)}) custom-call(bf16[4,512,128]{2,1,0:T(8,128)(2,1)} %collective-permute-done.refs_1_.refs_0_, bf16[4,512,128]{2,1,0:T(8,128)(2,1)} %get-tuple-element.16.refs_2_.refs_1_, bf16[4,512,128]{2,1,0:T(8,128)(2,1)} %get-tuple-element.29.refs_2_, ...), custom_call_target="tpu_custom_call" | custom-call | flops 1811939328 | bytes 4816896 | tf_op jit(solution)/shard_map/pallas_call | solution.py:83
  42.7 2.4 %collective-permute-start.8 = (bf16[4,512,128]{2,1,0:T(8,128)(2,1)}, bf16[4,512,128]{2,1,0:T(8,128)(2,1)S(1)}, u32[]{:S(2)}, u32[]{:S(2)}) collective-permute-start(bf16[4,512,128]{2,1,0:T(8,128)(2,1)} %get-tuple-element.19.refs_2_), channel_id=1, source_target_pairs={{0,4},{4,8},{8,12},{1,5},{5,9},{9,13},{2,6},{6,10},{10,14},{3,7},{... | collective-permute-start | bytes 1572872 | tf_op jit(solution)/shard_map/ppermute | solution.py:13
  45.2 0.0 collective-permute-done.1.refs_0_
  45.2 1.0 %slice_bitcast_fusion.4 = (bf16[1,1,512,128]{3,2,1,0:T(8,128)(2,1)S(1)}, bf16[1,1,512,128]{3,2,1,0:T(8,128)(2,1)S(1)}) fusion(bf16[4,512,128]{2,1,0:T(8,128)(2,1)} %collective-permute-done.1.refs_0_), kind=kLoop, calls=%fused_computation.26 | loop fusion | bytes 524288 | tf_op jit(solution)/shard_map/broadcast_in_dim | solution.py:106
  46.2 4.7 %collective-permute-start.4 = (bf16[1,1,512,128]{3,2,1,0:T(8,128)(2,1)S(1)}, bf16[1,1,512,128]{3,2,1,0:T(8,128)(2,1)S(1)}, u32[]{:S(2)}, u32[]{:S(2)}) collective-permute-start(bf16[1,1,512,128]{3,2,1,0:T(8,128)(2,1)S(1)} %get-tuple-element.44), channel_id=1, source_target_pairs={{0,1},{1,2},{2,3},{4,5},{5,6},{6,7},{8,9},{9,10},{10,11},{12,13},{... | collective-permute-start | bytes 393224 | tf_op jit(solution)/shard_map/ppermute | solution.py:105
  50.9 1.9 %collective-permute-start.5 = (bf16[1,1,512,128]{3,2,1,0:T(8,128)(2,1)S(1)}, bf16[1,1,512,128]{3,2,1,0:T(8,128)(2,1)S(1)}, u32[]{:S(2)}, u32[]{:S(2)}) collective-permute-start(bf16[1,1,512,128]{3,2,1,0:T(8,128)(2,1)S(1)} %get-tuple-element.43), channel_id=1, source_target_pairs={{1,0},{2,1},{3,2},{5,4},{6,5},{7,6},{9,8},{10,9},{11,10},{13,12},{... | collective-permute-start | bytes 393224 | tf_op jit(solution)/shard_map/ppermute | solution.py:106
  52.8 1.0 %slice_bitcast_fusion.8 = (bf16[1,1,512,128]{3,2,1,0:T(8,128)(2,1)S(1)}, bf16[1,1,512,128]{3,2,1,0:T(8,128)(2,1)S(1)}) fusion(bf16[4,512,128]{2,1,0:T(8,128)(2,1)} %get-tuple-element.19.refs_2_), kind=kLoop, calls=%fused_computation.30 | loop fusion | bytes 524288 | tf_op jit(solution)/shard_map/stack | solution.py:103
  53.8 0.0 collective-permute-done.4.refs_5_
  53.8 0.0 copy-start.10
  53.8 3.3 %collective-permute-done.5.refs_6_ = bf16[1,1,512,128]{3,2,1,0:T(8,128)(2,1)S(1)} collective-permute-done((bf16[1,1,512,128]{3,2,1,0:T(8,128)(2,1)S(1)}, bf16[1,1,512,128]{3,2,1,0:T(8,128)(2,1)S(1)}, u32[]{:S(2)}, u32[]{:S(2)}) %collective-permute-start.5) | collective-permute-done | bytes 131104 | tf_op jit(solution)/shard_map/ppermute | solution.py:106
  57.2 0.0 copy-done.10
  57.2 0.6 copy-done.11
  57.8 5.9 %shard_map.28 = (bf16[4,512,128]{2,1,0:T(8,128)(2,1)}, bf16[4,512,128]{2,1,0:T(8,128)(2,1)}) custom-call(bf16[4,512,128]{2,1,0:T(8,128)(2,1)} %collective-permute-done.1.refs_0_, bf16[4,512,128]{2,1,0:T(8,128)(2,1)} %collective-permute-done.refs_1_.refs_0_, bf16[4,512,128]{2,1,0:T(8,128)(2,1)} %get-tuple-element.16.refs_2_.refs_1_, ...), custom_call_target="tpu_custom_call" | custom-call | flops 1811939328 | bytes 5079040 | tf_op jit(solution)/shard_map/pallas_call | solution.py:83
  63.8 0.0 collective-permute-done.8.refs_0_.refs_1_
  63.8 1.2 %slice_bitcast_fusion.9 = (bf16[1,1,512,128]{3,2,1,0:T(8,128)(2,1)S(1)}, bf16[1,1,512,128]{3,2,1,0:T(8,128)(2,1)S(1)}) fusion(bf16[4,512,128]{2,1,0:T(8,128)(2,1)} %get-tuple-element.21.refs_1_.refs_2_), kind=kLoop, calls=%fused_computation.31 | loop fusion | bytes 524288 | tf_op jit(solution)/shard_map/stack | solution.py:103
  64.9 2.4 %collective-permute-start.9 = (bf16[4,512,128]{2,1,0:T(8,128)(2,1)}, bf16[4,512,128]{2,1,0:T(8,128)(2,1)S(1)}, u32[]{:S(2)}, u32[]{:S(2)}) collective-permute-start(bf16[4,512,128]{2,1,0:T(8,128)(2,1)} %get-tuple-element.21.refs_1_.refs_2_), channel_id=1, source_target_pairs={{0,4},{4,8},{8,12},{1,5},{5,9},{9,13},{2,6},{6,10},{10,14},{3,7},{... | collective-permute-start | bytes 1572872 | tf_op jit(solution)/shard_map/ppermute | solution.py:13
  67.5 1.9 %collective-permute-start.11 = (bf16[3,1,512,128]{3,2,1,0:T(8,128)(2,1)S(1)}, bf16[3,1,512,128]{3,2,1,0:T(8,128)(2,1)S(1)}, u32[]{:S(2)}, u32[]{:S(2)}) collective-permute-start(bf16[3,1,512,128]{3,2,1,0:T(8,128)(2,1)S(1)} %pad_maximum_fusion.4), channel_id=1, source_target_pairs={{1,0},{2,1},{3,2},{5,4},{6,5},{7,6},{9,8},{10,9},{11,10},{13,12},{... | collective-permute-start | bytes 1179656 | tf_op jit(solution)/shard_map/ppermute | solution.py:103
  69.4 0.0 copy-done.2
  69.5 3.6 %collective-permute-start.10 = (bf16[3,1,512,128]{3,2,1,0:T(8,128)(2,1)S(1)}, bf16[3,1,512,128]{3,2,1,0:T(8,128)(2,1)S(1)}, u32[]{:S(2)}, u32[]{:S(2)}) collective-permute-start(bf16[3,1,512,128]{3,2,1,0:T(8,128)(2,1)S(1)} %pad_maximum_fusion.3), channel_id=1, source_target_pairs={{0,1},{1,2},{2,3},{4,5},{5,6},{6,7},{8,9},{9,10},{10,11},{12,13},{... | collective-permute-start | bytes 1179656 | tf_op jit(solution)/shard_map/ppermute | solution.py:102
  73.1 1.0 %broadcast_select_fusion.refs_6_.refs_9_ = bf16[1152,384]{1,0:T(8,128)(2,1)} fusion(bf16[1152,384]{1,0:T(8,128)(2,1)S(1)} %get-tuple-element.24, bf16[1152,384]{1,0:T(8,128)(2,1)S(1)} %bitcast.53, pred[]{:T(512)S(6)} %eq.10), kind=kLoop, calls=%fused_computation.14 | loop fusion | flops 442368 | bytes 2654209 | tf_op jit(solution)/shard_map/jit(_where)/select_n | solution.py:129
  74.1 2.7 %collective-permute-done.9.refs_0_ = bf16[4,512,128]{2,1,0:T(8,128)(2,1)S(1)} collective-permute-done((bf16[4,512,128]{2,1,0:T(8,128)(2,1)}, bf16[4,512,128]{2,1,0:T(8,128)(2,1)S(1)}, u32[]{:S(2)}, u32[]{:S(2)}) %collective-permute-start.9) | collective-permute-done | bytes 524320 | tf_op jit(solution)/shard_map/ppermute | solution.py:13
  76.8 1.9 %collective-permute-start.12 = (bf16[1,1,512,128]{3,2,1,0:T(8,128)(2,1)S(1)}, bf16[1,1,512,128]{3,2,1,0:T(8,128)(2,1)S(1)}, u32[]{:S(2)}, u32[]{:S(2)}) collective-permute-start(bf16[1,1,512,128]{3,2,1,0:T(8,128)(2,1)S(1)} %get-tuple-element.36), channel_id=1, source_target_pairs={{0,1},{1,2},{2,3},{4,5},{5,6},{6,7},{8,9},{9,10},{10,11},{12,13},{... | collective-permute-start | bytes 393224 | tf_op jit(solution)/shard_map/ppermute | solution.py:105
  78.8 2.6 %collective-permute-start.13 = (bf16[1,1,512,128]{3,2,1,0:T(8,128)(2,1)S(1)}, bf16[1,1,512,128]{3,2,1,0:T(8,128)(2,1)S(1)}, u32[]{:S(2)}, u32[]{:S(2)}) collective-permute-start(bf16[1,1,512,128]{3,2,1,0:T(8,128)(2,1)S(1)} %get-tuple-element.35), channel_id=1, source_target_pairs={{1,0},{2,1},{3,2},{5,4},{6,5},{7,6},{9,8},{10,9},{11,10},{13,12},{... | collective-permute-start | bytes 393224 | tf_op jit(solution)/shard_map/ppermute | solution.py:106
  81.4 0.0 collective-permute-done.11.refs_4_
  81.4 0.0 copy-start.6
  81.4 0.0 collective-permute-done.10.refs_3_
  81.4 0.0 copy-done.3
  81.4 0.7 copy-done.6
  82.2 0.8 copy-done.7
  82.9 5.6 %shard_map.30.refs_7_ = bf16[4,512,128]{2,1,0:T(8,128)(2,1)} custom-call(bf16[4,512,128]{2,1,0:T(8,128)(2,1)} %copy-done.2, bf16[4,512,128]{2,1,0:T(8,128)(2,1)} %get-tuple-element.21.refs_1_.refs_2_, bf16[4,512,128]{2,1,0:T(8,128)(2,1)} %get-tuple-element.19.refs_2_, bf16[3,1,512,128]{3,2,1,0:T(8,128)(2,1)} %copy-done.7, ...), custom_call_target="tpu_custom_call" | custom-call | flops 1811939328 | bytes 4816896 | tf_op jit(solution)/shard_map/pallas_call | solution.py:83
  88.5 0.0 collective-permute-done.12.refs_5_
  88.5 0.0 collective-permute-done.13.refs_6_
  88.5 0.0 copy-start.9
  88.5 0.6 copy-done.8
  89.2 0.1 copy-done.9
  89.2 6.0 %shard_map.31 = bf16[2,4,512,128]{3,2,1,0:T(8,128)(2,1)} custom-call(bf16[4,512,128]{2,1,0:T(8,128)(2,1)} %copy-done.3, bf16[4,512,128]{2,1,0:T(8,128)(2,1)} %copy-done.2, bf16[4,512,128]{2,1,0:T(8,128)(2,1)} %get-tuple-element.21.refs_1_.refs_2_, bf16[3,1,512,128]{3,2,1,0:T(8,128)(2,1)} %copy-done.7, bf16[3,1,512,128]{3,2,1,0:T(8,128)(2,1)} %copy-done.6, ...), custom_call_target="tpu_custom_call" | custom-call | flops 1811939328 | bytes 5603328 | tf_op jit(solution)/shard_map/pallas_call | solution.py:83
  (11 shorter events, 0.2 us)
Async XLA Ops:
  0.0 7.7 %copy-start.1 = (bf16[1,9,384,128]{3,2,1,0:T(8,128)(2,1)S(1)}, bf16[1,9,384,128]{3,2,1,0:T(8,128)(2,1)}, u32[]{:S(2)}) copy-start(bf16[1,9,384,128]{3,2,1,0:T(8,128)(2,1)} %param.3) | copy-start | bytes 2654212
  2.8 18.6 %collective-permute-start = (bf16[4,512,128]{2,1,0:T(8,128)(2,1)}, bf16[4,512,128]{2,1,0:T(8,128)(2,1)}, u32[]{:S(2)}, u32[]{:S(2)}) collective-permute-start(bf16[4,512,128]{2,1,0:T(8,128)(2,1)} %get-tuple-element.29.refs_2_), channel_id=1, source_target_pairs={{0,4},{4,8},{8,12},{1,5},{5,9},{9,13},{2,6},{6,10},{10,14},{3,7},{... | collective-permute-start | bytes 1572872 | tf_op jit(solution)/shard_map/ppermute | solution.py:13
  8.6 2.3 %copy-start = (bf16[1,2,4,512,128]{4,3,2,1,0:T(8,128)(2,1)S(1)}, bf16[1,2,4,512,128]{4,3,2,1,0:T(8,128)(2,1)}, u32[]{:S(2)}) copy-start(bf16[1,2,4,512,128]{4,3,2,1,0:T(8,128)(2,1)} %param.2) | copy-start | bytes 3145732
  8.7 10.9 %collective-permute-start.6 = (bf16[576,384]{1,0:T(8,128)(2,1)S(1)}, bf16[576,384]{1,0:T(8,128)(2,1)}, u32[]{:S(2)}, u32[]{:S(2)}) collective-permute-start(bf16[576,384]{1,0:T(8,128)(2,1)S(1)} %constant_dynamic-slice_fusion), channel_id=1, source_target_pairs={{0,16},{16,0},{1,17},{17,1},{2,18},{18,2},{3,19},{19,3},{4,20},{20... | collective-permute-start | bytes 1327112 | tf_op jit(solution)/shard_map/ppermute | solution.py:119
  19.6 11.9 %collective-permute-start.7 = (bf16[576,384]{1,0:T(8,128)(2,1)}, bf16[576,384]{1,0:T(8,128)(2,1)S(1)}, u32[]{:S(2)}, u32[]{:S(2)}) collective-permute-start(bf16[576,384]{1,0:T(8,128)(2,1)} %collective-permute-done.6), channel_id=1, source_target_pairs={{0,1},{1,0},{2,3},{3,2},{4,5},{5,4},{6,7},{7,6},{8,9},{9,8},{10,11... | collective-permute-start | bytes 1327112 | tf_op jit(solution)/shard_map/ppermute | solution.py:120
  21.4 23.8 %collective-permute-start.1 = (bf16[4,512,128]{2,1,0:T(8,128)(2,1)}, bf16[4,512,128]{2,1,0:T(8,128)(2,1)}, u32[]{:S(2)}, u32[]{:S(2)}) collective-permute-start(bf16[4,512,128]{2,1,0:T(8,128)(2,1)} %get-tuple-element.16.refs_2_.refs_1_), channel_id=1, source_target_pairs={{0,4},{4,8},{8,12},{1,5},{5,9},{9,13},{2,6},{6,10},{10,14},{3,7},{... | collective-permute-start | bytes 1572872 | tf_op jit(solution)/shard_map/ppermute | solution.py:13
  25.8 9.1 %collective-permute-start.3 = (bf16[3,1,512,128]{3,2,1,0:T(8,128)(2,1)S(1)}, bf16[3,1,512,128]{3,2,1,0:T(8,128)(2,1)S(1)}, u32[]{:S(2)}, u32[]{:S(2)}) collective-permute-start(bf16[3,1,512,128]{3,2,1,0:T(8,128)(2,1)S(1)} %pad_maximum_fusion.2), channel_id=1, source_target_pairs={{1,0},{2,1},{3,2},{5,4},{6,5},{7,6},{9,8},{10,9},{11,10},{13,12},{... | collective-permute-start | bytes 1179656 | tf_op jit(solution)/shard_map/ppermute | solution.py:103
  28.1 8.1 %collective-permute-start.2 = (bf16[3,1,512,128]{3,2,1,0:T(8,128)(2,1)S(1)}, bf16[3,1,512,128]{3,2,1,0:T(8,128)(2,1)S(1)}, u32[]{:S(2)}, u32[]{:S(2)}) collective-permute-start(bf16[3,1,512,128]{3,2,1,0:T(8,128)(2,1)S(1)} %pad_maximum_fusion.1), channel_id=1, source_target_pairs={{0,1},{1,2},{2,3},{4,5},{5,6},{6,7},{8,9},{9,10},{10,11},{12,13},{... | collective-permute-start | bytes 1179656 | tf_op jit(solution)/shard_map/ppermute | solution.py:102
  34.9 2.0 %copy-start.4 = (bf16[3,1,512,128]{3,2,1,0:T(8,128)(2,1)}, bf16[3,1,512,128]{3,2,1,0:T(8,128)(2,1)S(1)}, u32[]{:S(2)}) copy-start(bf16[3,1,512,128]{3,2,1,0:T(8,128)(2,1)S(1)} %collective-permute-done.3.refs_4_) | copy-start | bytes 1179652
  36.1 0.8 copy-start.5
  42.7 21.0 %collective-permute-start.8 = (bf16[4,512,128]{2,1,0:T(8,128)(2,1)}, bf16[4,512,128]{2,1,0:T(8,128)(2,1)S(1)}, u32[]{:S(2)}, u32[]{:S(2)}) collective-permute-start(bf16[4,512,128]{2,1,0:T(8,128)(2,1)} %get-tuple-element.19.refs_2_), channel_id=1, source_target_pairs={{0,4},{4,8},{8,12},{1,5},{5,9},{9,13},{2,6},{6,10},{10,14},{3,7},{... | collective-permute-start | bytes 1572872 | tf_op jit(solution)/shard_map/ppermute | solution.py:13
  46.2 7.6 %collective-permute-start.4 = (bf16[1,1,512,128]{3,2,1,0:T(8,128)(2,1)S(1)}, bf16[1,1,512,128]{3,2,1,0:T(8,128)(2,1)S(1)}, u32[]{:S(2)}, u32[]{:S(2)}) collective-permute-start(bf16[1,1,512,128]{3,2,1,0:T(8,128)(2,1)S(1)} %get-tuple-element.44), channel_id=1, source_target_pairs={{0,1},{1,2},{2,3},{4,5},{5,6},{6,7},{8,9},{9,10},{10,11},{12,13},{... | collective-permute-start | bytes 393224 | tf_op jit(solution)/shard_map/ppermute | solution.py:105
  50.9 6.3 %collective-permute-start.5 = (bf16[1,1,512,128]{3,2,1,0:T(8,128)(2,1)S(1)}, bf16[1,1,512,128]{3,2,1,0:T(8,128)(2,1)S(1)}, u32[]{:S(2)}, u32[]{:S(2)}) collective-permute-start(bf16[1,1,512,128]{3,2,1,0:T(8,128)(2,1)S(1)} %get-tuple-element.43), channel_id=1, source_target_pairs={{1,0},{2,1},{3,2},{5,4},{6,5},{7,6},{9,8},{10,9},{11,10},{13,12},{... | collective-permute-start | bytes 393224 | tf_op jit(solution)/shard_map/ppermute | solution.py:106
  53.8 3.4 %copy-start.10 = (bf16[1,1,512,128]{3,2,1,0:T(8,128)(2,1)}, bf16[1,1,512,128]{3,2,1,0:T(8,128)(2,1)S(1)}, u32[]{:S(2)}) copy-start(bf16[1,1,512,128]{3,2,1,0:T(8,128)(2,1)S(1)} %collective-permute-done.4.refs_5_) | copy-start | bytes 393220
  57.2 0.7 copy-start.11
  63.8 5.7 %copy-start.2 = (bf16[4,512,128]{2,1,0:T(8,128)(2,1)}, bf16[4,512,128]{2,1,0:T(8,128)(2,1)S(1)}, u32[]{:S(2)}) copy-start(bf16[4,512,128]{2,1,0:T(8,128)(2,1)S(1)} %collective-permute-done.8.refs_0_.refs_1_) | copy-start | bytes 1572868
  64.9 11.9 %collective-permute-start.9 = (bf16[4,512,128]{2,1,0:T(8,128)(2,1)}, bf16[4,512,128]{2,1,0:T(8,128)(2,1)S(1)}, u32[]{:S(2)}, u32[]{:S(2)}) collective-permute-start(bf16[4,512,128]{2,1,0:T(8,128)(2,1)} %get-tuple-element.21.refs_1_.refs_2_), channel_id=1, source_target_pairs={{0,4},{4,8},{8,12},{1,5},{5,9},{9,13},{2,6},{6,10},{10,14},{3,7},{... | collective-permute-start | bytes 1572872 | tf_op jit(solution)/shard_map/ppermute | solution.py:13
  67.5 13.9 %collective-permute-start.11 = (bf16[3,1,512,128]{3,2,1,0:T(8,128)(2,1)S(1)}, bf16[3,1,512,128]{3,2,1,0:T(8,128)(2,1)S(1)}, u32[]{:S(2)}, u32[]{:S(2)}) collective-permute-start(bf16[3,1,512,128]{3,2,1,0:T(8,128)(2,1)S(1)} %pad_maximum_fusion.4), channel_id=1, source_target_pairs={{1,0},{2,1},{3,2},{5,4},{6,5},{7,6},{9,8},{10,9},{11,10},{13,12},{... | collective-permute-start | bytes 1179656 | tf_op jit(solution)/shard_map/ppermute | solution.py:103
  69.5 11.9 %collective-permute-start.10 = (bf16[3,1,512,128]{3,2,1,0:T(8,128)(2,1)S(1)}, bf16[3,1,512,128]{3,2,1,0:T(8,128)(2,1)S(1)}, u32[]{:S(2)}, u32[]{:S(2)}) collective-permute-start(bf16[3,1,512,128]{3,2,1,0:T(8,128)(2,1)S(1)} %pad_maximum_fusion.3), channel_id=1, source_target_pairs={{0,1},{1,2},{2,3},{4,5},{5,6},{6,7},{8,9},{9,10},{10,11},{12,13},{... | collective-permute-start | bytes 1179656 | tf_op jit(solution)/shard_map/ppermute | solution.py:102
  76.8 4.6 %copy-start.3 = (bf16[4,512,128]{2,1,0:T(8,128)(2,1)}, bf16[4,512,128]{2,1,0:T(8,128)(2,1)S(1)}, u32[]{:S(2)}) copy-start(bf16[4,512,128]{2,1,0:T(8,128)(2,1)S(1)} %collective-permute-done.9.refs_0_) | copy-start | bytes 1572868
  76.8 11.7 %collective-permute-start.12 = (bf16[1,1,512,128]{3,2,1,0:T(8,128)(2,1)S(1)}, bf16[1,1,512,128]{3,2,1,0:T(8,128)(2,1)S(1)}, u32[]{:S(2)}, u32[]{:S(2)}) collective-permute-start(bf16[1,1,512,128]{3,2,1,0:T(8,128)(2,1)S(1)} %get-tuple-element.36), channel_id=1, source_target_pairs={{0,1},{1,2},{2,3},{4,5},{5,6},{6,7},{8,9},{9,10},{10,11},{12,13},{... | collective-permute-start | bytes 393224 | tf_op jit(solution)/shard_map/ppermute | solution.py:105
  78.8 9.8 %collective-permute-start.13 = (bf16[1,1,512,128]{3,2,1,0:T(8,128)(2,1)S(1)}, bf16[1,1,512,128]{3,2,1,0:T(8,128)(2,1)S(1)}, u32[]{:S(2)}, u32[]{:S(2)}) collective-permute-start(bf16[1,1,512,128]{3,2,1,0:T(8,128)(2,1)S(1)} %get-tuple-element.35), channel_id=1, source_target_pairs={{1,0},{2,1},{3,2},{5,4},{6,5},{7,6},{9,8},{10,9},{11,10},{13,12},{... | collective-permute-start | bytes 393224 | tf_op jit(solution)/shard_map/ppermute | solution.py:106
  81.4 0.8 copy-start.6
  82.2 0.8 copy-start.7
  88.5 0.6 copy-start.8
  88.5 0.7 copy-start.9

commit v8 on v6

--- a/solution.py
+++ b/solution.py
@@ -99,6 +99,7 @@
     top_a = lax.ppermute(jnp.stack([c1[-1:], a0[-1:], a1[-1:]]), "space", down)
     bot_a = lax.ppermute(jnp.stack([c1[:1], a0[:1], a1[:1]]), "space", up)
     outs1 = frame_conv(1, (c1, a0, a1, top_a, bot_a), x1, w_mat, with_act)
+    c2, outs1 = lax.optimization_barrier((c2, outs1))
     top_b = lax.ppermute(c2[None, -1:], "space", down)
     bot_b = lax.ppermute(c2[None, :1], "space", up)
     last = outs1[0] if merge else None

time: 94.1 us -> 98.6 us (1.048)
  waiting for transfers between devices: 16.6 us -> 21.5 us
    ppermute x2, waiting for transfers between devices: 3.35 us -> 7.32 us  [conv_block(): bot_b = lax.ppermute(c2[None, :1], 'space', up)]
    ppermute x4, waiting for transfers between devices: 3.72 us -> 2.35 us  [shift_tm(): return lax.ppermute(x, 'tm', [(i, i + 1) for i in range(n - 1)])]
    ppermute x2, waiting for transfers between devices: 1.24 us -> 2.48 us  [conv_block(): top_a = lax.ppermute(jnp.stack([c1[-1:], a0[-1:], a1[-1:]]), 'space', down)]
    ppermute x2, waiting for transfers between devices: 0.82 us -> 1.83 us  [conv_block(): bot_a = lax.ppermute(jnp.stack([c1[:1], a0[:1], a1[:1]]), 'space', up)]
    unnamed x29 -> x31, local copies, waits for them, and re-layouts: 3.12 us -> 2.98 us
  transfers between devices with their start and end apart: 14 -> 14, of which waited for: 5 -> 8; matrix products, arithmetic and copies ran while one was open for 8% -> 8% of each run, Pallas kernels for 19% -> 18%
where the time goes in v8:
time: 98.6 us; the launch traced here: 98 us
  starting transfers between devices  38.1 us (39%)
  Pallas kernels  23.4 us (24%)
  waiting for transfers between devices  21.5 us (22%)
  local copies, waits for them, and re-layouts  9.07 us (9%)
  other arithmetic  5.64 us (6%)
    pallas_call x4, Pallas kernels, frame_conv(): pl.pallas_call(functools.partial(frame_kernel, t, 2 if with_act else 1, m...  23.4 us
    ppermute x4, starting transfers between devices, shift_tm(): return lax.ppermute(x, 'tm', [(i, i + 1) for i in range(n - 1)])  12.9 us
    ppermute x1, waiting for transfers between devices, both_taps(): got = lax.ppermute(mine, 'section', [(0, 1), (1, 0)])  7.54 us
    ppermute x2, waiting for transfers between devices, conv_block(): bot_b = lax.ppermute(c2[None, :1], 'space', up)  7.32 us
    ppermute x2, starting transfers between devices, conv_block(): top_a = lax.ppermute(jnp.stack([c1[-1:], a0[-1:], a1[-1:]]), 'space', down)  7 us
    ppermute x2, starting transfers between devices, conv_block(): top_b = lax.ppermute(c2[None, -1:], 'space', down)  6.71 us
    ppermute x2, starting transfers between devices, conv_block(): bot_b = lax.ppermute(c2[None, :1], 'space', up)  4.2 us
    another operation x5, local copies, waits for them, and re-layouts, conv_block(): bot_a = lax.ppermute(jnp.stack([c1[:1], a0[:1], a1[:1]]), 'space', up)  4.17 us
  transfers between devices with their start and end apart: 14, of which 8 were waited for; matrix products, arithmetic and copies ran while one was open for 8% of the time, Pallas kernels for 18%

profile of v8, /device:TPU:1, one launch (start us, length us, event | category | flops | bytes accessed | tf_op | source)
XLA Modules:
  0.0 98.0 jit_solution(13972045521461294635)
XLA Ops:
  0.0 0.0 copy-start.2
  0.0 2.8 %fusion.7 = (bf16[4,512,128]{2,1,0:T(8,128)(2,1)}, bf16[4,512,128]{2,1,0:T(8,128)(2,1)}) fusion(bf16[1,2,4,512,128]{4,3,2,1,0:T(8,128)(2,1)} %param.2), kind=kLoop, calls=%fused_computation.11 | loop fusion | flops 3145728 | bytes 2097152 | tf_op jit(solution)/shard_map/convert_element_type | solution.py:17
  2.8 4.8 %collective-permute-start = (bf16[4,512,128]{2,1,0:T(8,128)(2,1)}, bf16[4,512,128]{2,1,0:T(8,128)(2,1)}, u32[]{:S(2)}, u32[]{:S(2)}) collective-permute-start(bf16[4,512,128]{2,1,0:T(8,128)(2,1)} %get-tuple-element.35.refs_2_), channel_id=1, source_target_pairs={{0,4},{4,8},{8,12},{1,5},{5,9},{9,13},{2,6},{6,10},{10,14},{3,7},{... | collective-permute-start | bytes 1572872 | tf_op jit(solution)/shard_map/ppermute | solution.py:13
  7.6 0.0 copy-done.2
  7.6 0.8 copy.4
  8.4 0.1 copy.9
  8.6 0.0 copy-start
  8.6 0.1 constant_dynamic-slice_fusion
  8.6 1.3 %collective-permute-start.4 = (bf16[576,384]{1,0:T(8,128)(2,1)S(1)}, bf16[576,384]{1,0:T(8,128)(2,1)}, u32[]{:S(2)}, u32[]{:S(2)}) collective-permute-start(bf16[576,384]{1,0:T(8,128)(2,1)S(1)} %constant_dynamic-slice_fusion), channel_id=1, source_target_pairs={{0,16},{16,0},{1,17},{17,1},{2,18},{18,2},{3,19},{19,3},{4,20},{20... | collective-permute-start | bytes 1327112 | tf_op jit(solution)/shard_map/ppermute | solution.py:117
  9.9 1.0 %slice_bitcast_fusion.2 = (bf16[1,1,512,128]{3,2,1,0:T(8,128)(2,1)S(1)}, bf16[1,1,512,128]{3,2,1,0:T(8,128)(2,1)S(1)}) fusion(bf16[4,512,128]{2,1,0:T(8,128)(2,1)} %get-tuple-element.35.refs_2_), kind=kLoop, calls=%fused_computation.24 | loop fusion | bytes 524288 | tf_op jit(solution)/shard_map/stack | solution.py:100
  10.9 0.0 copy-done
  10.9 0.0 copy-start.1
  10.9 1.1 %slice_bitcast_fusion.1 = (bf16[4,512,128]{2,1,0:T(8,128)(2,1)}, bf16[4,512,128]{2,1,0:T(8,128)(2,1)}) fusion(bf16[1,2,4,512,128]{4,3,2,1,0:T(8,128)(2,1)S(1)} %copy-done), kind=kLoop, calls=%fused_computation.17 | loop fusion | bytes 2097152 | tf_op jit(solution)/shard_map/squeeze | solution.py:131
  12.0 7.5 %collective-permute-done.4 = bf16[576,384]{1,0:T(8,128)(2,1)} collective-permute-done((bf16[576,384]{1,0:T(8,128)(2,1)S(1)}, bf16[576,384]{1,0:T(8,128)(2,1)}, u32[]{:S(2)}, u32[]{:S(2)}) %collective-permute-start.4) | collective-permute-done | bytes 442400 | tf_op jit(solution)/shard_map/ppermute | solution.py:117
  19.5 1.9 %collective-permute-start.5 = (bf16[576,384]{1,0:T(8,128)(2,1)}, bf16[576,384]{1,0:T(8,128)(2,1)S(1)}, u32[]{:S(2)}, u32[]{:S(2)}) collective-permute-start(bf16[576,384]{1,0:T(8,128)(2,1)} %collective-permute-done.4), channel_id=1, source_target_pairs={{0,1},{1,0},{2,3},{3,2},{4,5},{5,4},{6,7},{7,6},{8,9},{9,8},{10,11... | collective-permute-start | bytes 1327112 | tf_op jit(solution)/shard_map/ppermute | solution.py:118
  21.4 0.0 collective-permute-done.refs_0_.refs_1_
  21.4 0.0 copy-done.1
  21.4 2.5 %collective-permute-start.1 = (bf16[4,512,128]{2,1,0:T(8,128)(2,1)S(1)}, bf16[4,512,128]{2,1,0:T(8,128)(2,1)S(1)}, u32[]{:S(2)}, u32[]{:S(2)}) collective-permute-start(bf16[4,512,128]{2,1,0:T(8,128)(2,1)S(1)} %copy-done.1), channel_id=1, source_target_pairs={{0,4},{4,8},{8,12},{1,5},{5,9},{9,13},{2,6},{6,10},{10,14},{3,7},{... | collective-permute-start | bytes 1572872 | tf_op jit(solution)/shard_map/ppermute | solution.py:13
  23.9 1.0 %slice_bitcast_fusion.14 = (bf16[1,1,512,128]{3,2,1,0:T(8,128)(2,1)S(1)}, bf16[1,1,512,128]{3,2,1,0:T(8,128)(2,1)S(1)}, bf16[1,1,512,128]{3,2,1,0:T(8,128)(2,1)S(1)}, bf16[1,1,512,128]{3,2,1,0:T(8,128)(2,1)S(1)}) fusion(bf16[4,512,128]{2,1,0:T(8,128)(2,1)S(1)} %copy-done.1, bf16[4,512,128]{2,1,0:T(8,128)(2,1)} %collective-permute-done.refs_0_.refs_1_), kind=kLoop, calls=%fused_computation.36 | loop fusion | bytes 1048576 | tf_op jit(solution)/shard_map/stack | solution.py:100
  24.9 2.2 %collective-permute-start.3 = (bf16[3,1,512,128]{3,2,1,0:T(8,128)(2,1)S(1)}, bf16[3,1,512,128]{3,2,1,0:T(8,128)(2,1)S(1)}, u32[]{:S(2)}, u32[]{:S(2)}) collective-permute-start(bf16[3,1,512,128]{3,2,1,0:T(8,128)(2,1)S(1)} %pad_maximum_fusion.2), channel_id=1, source_target_pairs={{1,0},{2,1},{3,2},{5,4},{6,5},{7,6},{9,8},{10,9},{11,10},{13,12},{... | collective-permute-start | bytes 1179656 | tf_op jit(solution)/shard_map/ppermute | solution.py:100
  27.2 3.4 %collective-permute-start.2 = (bf16[3,1,512,128]{3,2,1,0:T(8,128)(2,1)S(1)}, bf16[3,1,512,128]{3,2,1,0:T(8,128)(2,1)S(1)}, u32[]{:S(2)}, u32[]{:S(2)}) collective-permute-start(bf16[3,1,512,128]{3,2,1,0:T(8,128)(2,1)S(1)} %pad_maximum_fusion.1), channel_id=1, source_target_pairs={{0,1},{1,2},{2,3},{4,5},{5,6},{6,7},{8,9},{9,10},{10,11},{12,13},{... | collective-permute-start | bytes 1179656 | tf_op jit(solution)/shard_map/ppermute | solution.py:99
  30.6 0.0 collective-permute-done.5
  30.6 1.1 %broadcast_select_fusion.3 = (bf16[576,384]{1,0:T(8,128)(2,1)S(1)}, bf16[576,384]{1,0:T(8,128)(2,1)S(1)}) fusion(bf16[576,384]{1,0:T(8,128)(2,1)} %collective-permute-done.4, bf16[576,384]{1,0:T(8,128)(2,1)S(1)} %collective-permute-done.5, pred[]{:T(512)S(6)} %eq.11), kind=kLoop, calls=%fused_computation.19 | loop fusion | flops 442368 | bytes 1769473 | tf_op jit(solution)/shard_map/jit(_where)/select_n | solution.py:119
  31.7 1.5 %broadcast_select_fusion = (bf16[1152,384]{1,0:T(8,128)(2,1)}, bf16[1152,384]{1,0:T(8,128)(2,1)}) fusion(pred[]{:T(512)S(6)} %eq.10, bf16[576,384]{1,0:T(8,128)(2,1)S(1)} %get-tuple-element.38, bf16[576,384]{1,0:T(8,128)(2,1)S(1)} %get-tuple-element.37, bf16[144,8,3,128]{3,2,1,0:T(4,128)(2,1)S(1)} %bitcast.51), kind=kLoop, calls=%fused_computation.14 | loop fusion | flops 2654208 | bytes 3538945 | tf_op jit(solution)/shard_map/jit(_where)/select_n | solution.py:123
  33.2 0.8 collective-permute-done.3.refs_4_
  34.0 1.2 %collective-permute-done.2.refs_3_ = bf16[3,1,512,128]{3,2,1,0:T(8,128)(2,1)S(1)} collective-permute-done((bf16[3,1,512,128]{3,2,1,0:T(8,128)(2,1)S(1)}, bf16[3,1,512,128]{3,2,1,0:T(8,128)(2,1)S(1)}, u32[]{:S(2)}, u32[]{:S(2)}) %collective-permute-start.2) | collective-permute-done | bytes 393248 | tf_op jit(solution)/shard_map/ppermute | solution.py:99
  35.3 0.0 copy-done.7
  35.3 0.7 copy-done.8
  36.0 5.8 %shard_map.28 = (bf16[4,512,128]{2,1,0:T(8,128)(2,1)}, bf16[4,512,128]{2,1,0:T(8,128)(2,1)}) custom-call(bf16[4,512,128]{2,1,0:T(8,128)(2,1)} %collective-permute-done.refs_0_.refs_1_, bf16[4,512,128]{2,1,0:T(8,128)(2,1)} %get-tuple-element.18.refs_1_.refs_2_, bf16[4,512,128]{2,1,0:T(8,128)(2,1)} %get-tuple-element.35.refs_2_, ...), custom_call_target="tpu_custom_call" | custom-call | flops 1811939328 | bytes 4816896 | tf_op jit(solution)/shard_map/pallas_call | solution.py:83
  41.9 0.0 collective-permute-done.1.refs_0_
  41.9 3.2 %collective-permute-start.8 = (bf16[4,512,128]{2,1,0:T(8,128)(2,1)}, bf16[4,512,128]{2,1,0:T(8,128)(2,1)S(1)}, u32[]{:S(2)}, u32[]{:S(2)}) collective-permute-start(bf16[4,512,128]{2,1,0:T(8,128)(2,1)} %get-tuple-element.24.refs_2_), channel_id=1, source_target_pairs={{0,4},{4,8},{8,12},{1,5},{5,9},{9,13},{2,6},{6,10},{10,14},{3,7},{... | collective-permute-start | bytes 1572872 | tf_op jit(solution)/shard_map/ppermute | solution.py:13
  45.1 4.7 %collective-permute-start.6 = (bf16[1,1,512,128]{3,2,1,0:T(8,128)(2,1)S(1)}, bf16[1,1,512,128]{3,2,1,0:T(8,128)(2,1)S(1)}, u32[]{:S(2)}, u32[]{:S(2)}) collective-permute-start(bf16[1,1,512,128]{3,2,1,0:T(8,128)(2,1)S(1)} %get-tuple-element.48), channel_id=1, source_target_pairs={{0,1},{1,2},{2,3},{4,5},{5,6},{6,7},{8,9},{9,10},{10,11},{12,13},{... | collective-permute-start | bytes 393224 | tf_op jit(solution)/shard_map/ppermute | solution.py:103
  49.8 1.9 %collective-permute-start.7 = (bf16[1,1,512,128]{3,2,1,0:T(8,128)(2,1)S(1)}, bf16[1,1,512,128]{3,2,1,0:T(8,128)(2,1)S(1)}, u32[]{:S(2)}, u32[]{:S(2)}) collective-permute-start(bf16[1,1,512,128]{3,2,1,0:T(8,128)(2,1)S(1)} %get-tuple-element.47), channel_id=1, source_target_pairs={{1,0},{2,1},{3,2},{5,4},{6,5},{7,6},{9,8},{10,9},{11,10},{13,12},{... | collective-permute-start | bytes 393224 | tf_op jit(solution)/shard_map/ppermute | solution.py:104
  51.7 1.0 %slice_bitcast_fusion.6 = (bf16[1,1,512,128]{3,2,1,0:T(8,128)(2,1)S(1)}, bf16[1,1,512,128]{3,2,1,0:T(8,128)(2,1)S(1)}) fusion(bf16[4,512,128]{2,1,0:T(8,128)(2,1)} %get-tuple-element.24.refs_2_), kind=kLoop, calls=%fused_computation.28 | loop fusion | bytes 524288 | tf_op jit(solution)/shard_map/stack | solution.py:100
  52.7 0.0 collective-permute-done.6.refs_5_
  52.7 0.0 copy-start.11
  52.7 3.3 %collective-permute-done.7.refs_6_ = bf16[1,1,512,128]{3,2,1,0:T(8,128)(2,1)S(1)} collective-permute-done((bf16[1,1,512,128]{3,2,1,0:T(8,128)(2,1)S(1)}, bf16[1,1,512,128]{3,2,1,0:T(8,128)(2,1)S(1)}, u32[]{:S(2)}, u32[]{:S(2)}) %collective-permute-start.7) | collective-permute-done | bytes 131104 | tf_op jit(solution)/shard_map/ppermute | solution.py:104
  56.1 0.0 copy-done.4
  56.1 0.0 copy-done.11
  56.1 0.6 copy-done.12
  56.7 6.0 %shard_map.29 = (bf16[4,512,128]{2,1,0:T(8,128)(2,1)}, bf16[4,512,128]{2,1,0:T(8,128)(2,1)}) custom-call(bf16[4,512,128]{2,1,0:T(8,128)(2,1)} %copy-done.4, bf16[4,512,128]{2,1,0:T(8,128)(2,1)} %collective-permute-done.refs_0_.refs_1_, bf16[4,512,128]{2,1,0:T(8,128)(2,1)} %get-tuple-element.18.refs_1_.refs_2_, bf16[3,1,512,128]{3,2,1,0:T(8,128)(2,1)} %copy-done.8, ...), custom_call_target="tpu_custom_call" | custom-call | flops 1811939328 | bytes 5079040 | tf_op jit(solution)/shard_map/pallas_call | solution.py:83
  62.7 0.0 collective-permute-done.8.refs_0_.refs_1_
  62.7 0.0 copy-start.5
  62.7 1.2 %slice_bitcast_fusion.7 = (bf16[1,1,512,128]{3,2,1,0:T(8,128)(2,1)S(1)}, bf16[1,1,512,128]{3,2,1,0:T(8,128)(2,1)S(1)}) fusion(bf16[4,512,128]{2,1,0:T(8,128)(2,1)} %get-tuple-element.25.refs_1_.refs_2_), kind=kLoop, calls=%fused_computation.29 | loop fusion | bytes 524288 | tf_op jit(solution)/shard_map/stack | solution.py:100
  63.9 1.9 %collective-permute-start.11 = (bf16[3,1,512,128]{3,2,1,0:T(8,128)(2,1)S(1)}, bf16[3,1,512,128]{3,2,1,0:T(8,128)(2,1)S(1)}, u32[]{:S(2)}, u32[]{:S(2)}) collective-permute-start(bf16[3,1,512,128]{3,2,1,0:T(8,128)(2,1)S(1)} %pad_maximum_fusion.4), channel_id=1, source_target_pairs={{1,0},{2,1},{3,2},{5,4},{6,5},{7,6},{9,8},{10,9},{11,10},{13,12},{... | collective-permute-start | bytes 1179656 | tf_op jit(solution)/shard_map/ppermute | solution.py:100
  65.9 0.0 copy-done.3
  65.9 3.6 %collective-permute-start.10 = (bf16[3,1,512,128]{3,2,1,0:T(8,128)(2,1)S(1)}, bf16[3,1,512,128]{3,2,1,0:T(8,128)(2,1)S(1)}, u32[]{:S(2)}, u32[]{:S(2)}) collective-permute-start(bf16[3,1,512,128]{3,2,1,0:T(8,128)(2,1)S(1)} %pad_maximum_fusion.3), channel_id=1, source_target_pairs={{0,1},{1,2},{2,3},{4,5},{5,6},{6,7},{8,9},{9,10},{10,11},{12,13},{... | collective-permute-start | bytes 1179656 | tf_op jit(solution)/shard_map/ppermute | solution.py:99
  69.6 0.0 copy-done.5
  69.6 2.4 %collective-permute-start.9 = (bf16[4,512,128]{2,1,0:T(8,128)(2,1)S(1)}, bf16[4,512,128]{2,1,0:T(8,128)(2,1)S(1)}, u32[]{:S(2)}, u32[]{:S(2)}) collective-permute-start(bf16[4,512,128]{2,1,0:T(8,128)(2,1)S(1)} %copy-done.5), channel_id=1, source_target_pairs={{0,4},{4,8},{8,12},{1,5},{5,9},{9,13},{2,6},{6,10},{10,14},{3,7},{... | collective-permute-start | bytes 1572872 | tf_op jit(solution)/shard_map/ppermute | solution.py:13
  72.0 1.0 %collective-permute-done.11.refs_4_ = bf16[3,1,512,128]{3,2,1,0:T(8,128)(2,1)S(1)} collective-permute-done((bf16[3,1,512,128]{3,2,1,0:T(8,128)(2,1)S(1)}, bf16[3,1,512,128]{3,2,1,0:T(8,128)(2,1)S(1)}, u32[]{:S(2)}, u32[]{:S(2)}) %collective-permute-start.11) | collective-permute-done | bytes 393248 | tf_op jit(solution)/shard_map/ppermute | solution.py:100
  73.0 1.2 %collective-permute-done.10.refs_3_ = bf16[3,1,512,128]{3,2,1,0:T(8,128)(2,1)S(1)} collective-permute-done((bf16[3,1,512,128]{3,2,1,0:T(8,128)(2,1)S(1)}, bf16[3,1,512,128]{3,2,1,0:T(8,128)(2,1)S(1)}, u32[]{:S(2)}, u32[]{:S(2)}) %collective-permute-start.10) | collective-permute-done | bytes 393248 | tf_op jit(solution)/shard_map/ppermute | solution.py:99
  74.3 0.0 copy-done.9
  74.3 0.8 copy-done.10
  75.0 5.6 %shard_map.30.refs_7_ = bf16[4,512,128]{2,1,0:T(8,128)(2,1)} custom-call(bf16[4,512,128]{2,1,0:T(8,128)(2,1)} %copy-done.3, bf16[4,512,128]{2,1,0:T(8,128)(2,1)} %get-tuple-element.25.refs_1_.refs_2_, bf16[4,512,128]{2,1,0:T(8,128)(2,1)} %get-tuple-element.24.refs_2_, bf16[3,1,512,128]{3,2,1,0:T(8,128)(2,1)} %copy-done.10, ...), custom_call_target="tpu_custom_call" | custom-call | flops 1811939328 | bytes 4816896 | tf_op jit(solution)/shard_map/pallas_call | solution.py:83
  80.6 2.3 %collective-permute-done.9.refs_0_ = bf16[4,512,128]{2,1,0:T(8,128)(2,1)S(1)} collective-permute-done((bf16[4,512,128]{2,1,0:T(8,128)(2,1)S(1)}, bf16[4,512,128]{2,1,0:T(8,128)(2,1)S(1)}, u32[]{:S(2)}, u32[]{:S(2)}) %collective-permute-start.9) | collective-permute-done | bytes 524320 | tf_op jit(solution)/shard_map/ppermute | solution.py:13
  83.0 2.0 %collective-permute-start.12 = (bf16[1,1,512,128]{3,2,1,0:T(8,128)(2,1)S(1)}, bf16[1,1,512,128]{3,2,1,0:T(8,128)(2,1)S(1)}, u32[]{:S(2)}, u32[]{:S(2)}) collective-permute-start(bf16[1,1,512,128]{3,2,1,0:T(8,128)(2,1)S(1)} %get-tuple-element.40), channel_id=1, source_target_pairs={{0,1},{1,2},{2,3},{4,5},{5,6},{6,7},{8,9},{9,10},{10,11},{12,13},{... | collective-permute-start | bytes 393224 | tf_op jit(solution)/shard_map/ppermute | solution.py:103
  85.1 2.3 %collective-permute-start.13 = (bf16[1,1,512,128]{3,2,1,0:T(8,128)(2,1)S(1)}, bf16[1,1,512,128]{3,2,1,0:T(8,128)(2,1)S(1)}, u32[]{:S(2)}, u32[]{:S(2)}) collective-permute-start(bf16[1,1,512,128]{3,2,1,0:T(8,128)(2,1)S(1)} %get-tuple-element.39), channel_id=1, source_target_pairs={{1,0},{2,1},{3,2},{5,4},{6,5},{7,6},{9,8},{10,9},{11,10},{13,12},{... | collective-permute-start | bytes 393224 | tf_op jit(solution)/shard_map/ppermute | solution.py:104
  87.3 0.0 collective-permute-done.12.refs_5_
  87.4 0.0 copy-start.13
  87.4 4.0 %collective-permute-done.13.refs_6_ = bf16[1,1,512,128]{3,2,1,0:T(8,128)(2,1)S(1)} collective-permute-done((bf16[1,1,512,128]{3,2,1,0:T(8,128)(2,1)S(1)}, bf16[1,1,512,128]{3,2,1,0:T(8,128)(2,1)S(1)}, u32[]{:S(2)}, u32[]{:S(2)}) %collective-permute-start.13) | collective-permute-done | bytes 131104 | tf_op jit(solution)/shard_map/ppermute | solution.py:104
  91.3 0.0 copy-done.6
  91.3 0.0 copy-done.13
  91.3 0.6 copy-done.14
  92.0 6.0 %shard_map.31 = bf16[2,4,512,128]{3,2,1,0:T(8,128)(2,1)} custom-call(bf16[4,512,128]{2,1,0:T(8,128)(2,1)} %copy-done.6, bf16[4,512,128]{2,1,0:T(8,128)(2,1)} %copy-done.3, bf16[4,512,128]{2,1,0:T(8,128)(2,1)} %get-tuple-element.25.refs_1_.refs_2_, bf16[3,1,512,128]{3,2,1,0:T(8,128)(2,1)} %copy-done.10, bf16[3,1,512,128]{3,2,1,0:T(8,128)(2,1)} %copy-done.9, ...), custom_call_target="tpu_custom_call" | custom-call | flops 1811939328 | bytes 5603328 | tf_op jit(solution)/shard_map/pallas_call | solution.py:83
  (16 shorter events, 0.3 us)
Async XLA Ops:
  0.0 7.6 %copy-start.2 = (bf16[1,9,384,128]{3,2,1,0:T(8,128)(2,1)S(1)}, bf16[1,9,384,128]{3,2,1,0:T(8,128)(2,1)}, u32[]{:S(2)}) copy-start(bf16[1,9,384,128]{3,2,1,0:T(8,128)(2,1)} %param.3) | copy-start | bytes 2654212
  2.8 18.6 %collective-permute-start = (bf16[4,512,128]{2,1,0:T(8,128)(2,1)}, bf16[4,512,128]{2,1,0:T(8,128)(2,1)}, u32[]{:S(2)}, u32[]{:S(2)}) collective-permute-start(bf16[4,512,128]{2,1,0:T(8,128)(2,1)} %get-tuple-element.35.refs_2_), channel_id=1, source_target_pairs={{0,4},{4,8},{8,12},{1,5},{5,9},{9,13},{2,6},{6,10},{10,14},{3,7},{... | collective-permute-start | bytes 1572872 | tf_op jit(solution)/shard_map/ppermute | solution.py:13
  8.6 2.3 %copy-start = (bf16[1,2,4,512,128]{4,3,2,1,0:T(8,128)(2,1)S(1)}, bf16[1,2,4,512,128]{4,3,2,1,0:T(8,128)(2,1)}, u32[]{:S(2)}) copy-start(bf16[1,2,4,512,128]{4,3,2,1,0:T(8,128)(2,1)} %param.2) | copy-start | bytes 3145732
  8.6 10.9 %collective-permute-start.4 = (bf16[576,384]{1,0:T(8,128)(2,1)S(1)}, bf16[576,384]{1,0:T(8,128)(2,1)}, u32[]{:S(2)}, u32[]{:S(2)}) collective-permute-start(bf16[576,384]{1,0:T(8,128)(2,1)S(1)} %constant_dynamic-slice_fusion), channel_id=1, source_target_pairs={{0,16},{16,0},{1,17},{17,1},{2,18},{18,2},{3,19},{19,3},{4,20},{20... | collective-permute-start | bytes 1327112 | tf_op jit(solution)/shard_map/ppermute | solution.py:117
  10.9 10.5 %copy-start.1 = (bf16[4,512,128]{2,1,0:T(8,128)(2,1)S(1)}, bf16[4,512,128]{2,1,0:T(8,128)(2,1)}, u32[]{:S(2)}) copy-start(bf16[4,512,128]{2,1,0:T(8,128)(2,1)} %get-tuple-element.18.refs_1_.refs_2_) | copy-start | bytes 1572868
  19.5 11.0 %collective-permute-start.5 = (bf16[576,384]{1,0:T(8,128)(2,1)}, bf16[576,384]{1,0:T(8,128)(2,1)S(1)}, u32[]{:S(2)}, u32[]{:S(2)}) collective-permute-start(bf16[576,384]{1,0:T(8,128)(2,1)} %collective-permute-done.4), channel_id=1, source_target_pairs={{0,1},{1,0},{2,3},{3,2},{4,5},{5,4},{6,7},{7,6},{8,9},{9,8},{10,11... | collective-permute-start | bytes 1327112 | tf_op jit(solution)/shard_map/ppermute | solution.py:118
  21.4 20.5 %collective-permute-start.1 = (bf16[4,512,128]{2,1,0:T(8,128)(2,1)S(1)}, bf16[4,512,128]{2,1,0:T(8,128)(2,1)S(1)}, u32[]{:S(2)}, u32[]{:S(2)}) collective-permute-start(bf16[4,512,128]{2,1,0:T(8,128)(2,1)S(1)} %copy-done.1), channel_id=1, source_target_pairs={{0,4},{4,8},{8,12},{1,5},{5,9},{9,13},{2,6},{6,10},{10,14},{3,7},{... | collective-permute-start | bytes 1572872 | tf_op jit(solution)/shard_map/ppermute | solution.py:13
  24.9 9.1 %collective-permute-start.3 = (bf16[3,1,512,128]{3,2,1,0:T(8,128)(2,1)S(1)}, bf16[3,1,512,128]{3,2,1,0:T(8,128)(2,1)S(1)}, u32[]{:S(2)}, u32[]{:S(2)}) collective-permute-start(bf16[3,1,512,128]{3,2,1,0:T(8,128)(2,1)S(1)} %pad_maximum_fusion.2), channel_id=1, source_target_pairs={{1,0},{2,1},{3,2},{5,4},{6,5},{7,6},{9,8},{10,9},{11,10},{13,12},{... | collective-permute-start | bytes 1179656 | tf_op jit(solution)/shard_map/ppermute | solution.py:100
  27.2 8.1 %collective-permute-start.2 = (bf16[3,1,512,128]{3,2,1,0:T(8,128)(2,1)S(1)}, bf16[3,1,512,128]{3,2,1,0:T(8,128)(2,1)S(1)}, u32[]{:S(2)}, u32[]{:S(2)}) collective-permute-start(bf16[3,1,512,128]{3,2,1,0:T(8,128)(2,1)S(1)} %pad_maximum_fusion.1), channel_id=1, source_target_pairs={{0,1},{1,2},{2,3},{4,5},{5,6},{6,7},{8,9},{9,10},{10,11},{12,13},{... | collective-permute-start | bytes 1179656 | tf_op jit(solution)/shard_map/ppermute | solution.py:99
  34.0 1.2 %copy-start.7 = (bf16[3,1,512,128]{3,2,1,0:T(8,128)(2,1)}, bf16[3,1,512,128]{3,2,1,0:T(8,128)(2,1)S(1)}, u32[]{:S(2)}) copy-start(bf16[3,1,512,128]{3,2,1,0:T(8,128)(2,1)S(1)} %collective-permute-done.3.refs_4_) | copy-start | bytes 1179652
  35.3 0.7 copy-start.8
  41.9 14.2 %copy-start.4 = (bf16[4,512,128]{2,1,0:T(8,128)(2,1)}, bf16[4,512,128]{2,1,0:T(8,128)(2,1)S(1)}, u32[]{:S(2)}) copy-start(bf16[4,512,128]{2,1,0:T(8,128)(2,1)S(1)} %collective-permute-done.1.refs_0_) | copy-start | bytes 1572868
  41.9 20.8 %collective-permute-start.8 = (bf16[4,512,128]{2,1,0:T(8,128)(2,1)}, bf16[4,512,128]{2,1,0:T(8,128)(2,1)S(1)}, u32[]{:S(2)}, u32[]{:S(2)}) collective-permute-start(bf16[4,512,128]{2,1,0:T(8,128)(2,1)} %get-tuple-element.24.refs_2_), channel_id=1, source_target_pairs={{0,4},{4,8},{8,12},{1,5},{5,9},{9,13},{2,6},{6,10},{10,14},{3,7},{... | collective-permute-start | bytes 1572872 | tf_op jit(solution)/shard_map/ppermute | solution.py:13
  45.1 7.6 %collective-permute-start.6 = (bf16[1,1,512,128]{3,2,1,0:T(8,128)(2,1)S(1)}, bf16[1,1,512,128]{3,2,1,0:T(8,128)(2,1)S(1)}, u32[]{:S(2)}, u32[]{:S(2)}) collective-permute-start(bf16[1,1,512,128]{3,2,1,0:T(8,128)(2,1)S(1)} %get-tuple-element.48), channel_id=1, source_target_pairs={{0,1},{1,2},{2,3},{4,5},{5,6},{6,7},{8,9},{9,10},{10,11},{12,13},{... | collective-permute-start | bytes 393224 | tf_op jit(solution)/shard_map/ppermute | solution.py:103
  49.8 6.3 %collective-permute-start.7 = (bf16[1,1,512,128]{3,2,1,0:T(8,128)(2,1)S(1)}, bf16[1,1,512,128]{3,2,1,0:T(8,128)(2,1)S(1)}, u32[]{:S(2)}, u32[]{:S(2)}) collective-permute-start(bf16[1,1,512,128]{3,2,1,0:T(8,128)(2,1)S(1)} %get-tuple-element.47), channel_id=1, source_target_pairs={{1,0},{2,1},{3,2},{5,4},{6,5},{7,6},{9,8},{10,9},{11,10},{13,12},{... | collective-permute-start | bytes 393224 | tf_op jit(solution)/shard_map/ppermute | solution.py:104
  52.7 3.4 %copy-start.11 = (bf16[1,1,512,128]{3,2,1,0:T(8,128)(2,1)}, bf16[1,1,512,128]{3,2,1,0:T(8,128)(2,1)S(1)}, u32[]{:S(2)}) copy-start(bf16[1,1,512,128]{3,2,1,0:T(8,128)(2,1)S(1)} %collective-permute-done.6.refs_5_) | copy-start | bytes 393220
  56.1 0.7 copy-start.12
  62.7 3.3 %copy-start.3 = (bf16[4,512,128]{2,1,0:T(8,128)(2,1)}, bf16[4,512,128]{2,1,0:T(8,128)(2,1)S(1)}, u32[]{:S(2)}) copy-start(bf16[4,512,128]{2,1,0:T(8,128)(2,1)S(1)} %collective-permute-done.8.refs_0_.refs_1_) | copy-start | bytes 1572868
  62.7 6.9 %copy-start.5 = (bf16[4,512,128]{2,1,0:T(8,128)(2,1)S(1)}, bf16[4,512,128]{2,1,0:T(8,128)(2,1)}, u32[]{:S(2)}) copy-start(bf16[4,512,128]{2,1,0:T(8,128)(2,1)} %get-tuple-element.25.refs_1_.refs_2_) | copy-start | bytes 1572868
  63.9 9.1 %collective-permute-start.11 = (bf16[3,1,512,128]{3,2,1,0:T(8,128)(2,1)S(1)}, bf16[3,1,512,128]{3,2,1,0:T(8,128)(2,1)S(1)}, u32[]{:S(2)}, u32[]{:S(2)}) collective-permute-start(bf16[3,1,512,128]{3,2,1,0:T(8,128)(2,1)S(1)} %pad_maximum_fusion.4), channel_id=1, source_target_pairs={{1,0},{2,1},{3,2},{5,4},{6,5},{7,6},{9,8},{10,9},{11,10},{13,12},{... | collective-permute-start | bytes 1179656 | tf_op jit(solution)/shard_map/ppermute | solution.py:100
  65.9 8.3 %collective-permute-start.10 = (bf16[3,1,512,128]{3,2,1,0:T(8,128)(2,1)S(1)}, bf16[3,1,512,128]{3,2,1,0:T(8,128)(2,1)S(1)}, u32[]{:S(2)}, u32[]{:S(2)}) collective-permute-start(bf16[3,1,512,128]{3,2,1,0:T(8,128)(2,1)S(1)} %pad_maximum_fusion.3), channel_id=1, source_target_pairs={{0,1},{1,2},{2,3},{4,5},{5,6},{6,7},{8,9},{9,10},{10,11},{12,13},{... | collective-permute-start | bytes 1179656 | tf_op jit(solution)/shard_map/ppermute | solution.py:99
  69.6 13.4 %collective-permute-start.9 = (bf16[4,512,128]{2,1,0:T(8,128)(2,1)S(1)}, bf16[4,512,128]{2,1,0:T(8,128)(2,1)S(1)}, u32[]{:S(2)}, u32[]{:S(2)}) collective-permute-start(bf16[4,512,128]{2,1,0:T(8,128)(2,1)S(1)} %copy-done.5), channel_id=1, source_target_pairs={{0,4},{4,8},{8,12},{1,5},{5,9},{9,13},{2,6},{6,10},{10,14},{3,7},{... | collective-permute-start | bytes 1572872 | tf_op jit(solution)/shard_map/ppermute | solution.py:13
  73.0 1.3 %copy-start.9 = (bf16[3,1,512,128]{3,2,1,0:T(8,128)(2,1)}, bf16[3,1,512,128]{3,2,1,0:T(8,128)(2,1)S(1)}, u32[]{:S(2)}) copy-start(bf16[3,1,512,128]{3,2,1,0:T(8,128)(2,1)S(1)} %collective-permute-done.11.refs_4_) | copy-start | bytes 1179652
  74.3 0.8 copy-start.10
  83.0 8.4 %copy-start.6 = (bf16[4,512,128]{2,1,0:T(8,128)(2,1)}, bf16[4,512,128]{2,1,0:T(8,128)(2,1)S(1)}, u32[]{:S(2)}) copy-start(bf16[4,512,128]{2,1,0:T(8,128)(2,1)S(1)} %collective-permute-done.9.refs_0_) | copy-start | bytes 1572868
  83.0 4.3 %collective-permute-start.12 = (bf16[1,1,512,128]{3,2,1,0:T(8,128)(2,1)S(1)}, bf16[1,1,512,128]{3,2,1,0:T(8,128)(2,1)S(1)}, u32[]{:S(2)}, u32[]{:S(2)}) collective-permute-start(bf16[1,1,512,128]{3,2,1,0:T(8,128)(2,1)S(1)} %get-tuple-element.40), channel_id=1, source_target_pairs={{0,1},{1,2},{2,3},{4,5},{5,6},{6,7},{8,9},{9,10},{10,11},{12,13},{... | collective-permute-start | bytes 393224 | tf_op jit(solution)/shard_map/ppermute | solution.py:103
  85.1 6.3 %collective-permute-start.13 = (bf16[1,1,512,128]{3,2,1,0:T(8,128)(2,1)S(1)}, bf16[1,1,512,128]{3,2,1,0:T(8,128)(2,1)S(1)}, u32[]{:S(2)}, u32[]{:S(2)}) collective-permute-start(bf16[1,1,512,128]{3,2,1,0:T(8,128)(2,1)S(1)} %get-tuple-element.39), channel_id=1, source_target_pairs={{1,0},{2,1},{3,2},{5,4},{6,5},{7,6},{9,8},{10,9},{11,10},{13,12},{... | collective-permute-start | bytes 393224 | tf_op jit(solution)/shard_map/ppermute | solution.py:104
  87.4 4.0 %copy-start.13 = (bf16[1,1,512,128]{3,2,1,0:T(8,128)(2,1)}, bf16[1,1,512,128]{3,2,1,0:T(8,128)(2,1)S(1)}, u32[]{:S(2)}) copy-start(bf16[1,1,512,128]{3,2,1,0:T(8,128)(2,1)S(1)} %collective-permute-done.12.refs_5_) | copy-start | bytes 393220
  91.3 0.6 copy-start.14

commit v9 on v6

--- a/solution.py
+++ b/solution.py
@@ -87,7 +87,7 @@
     )(*operands, base, w_mat)
 
 
-def conv_block(frames_in, acts, w_mat, with_act, merge):
+def conv_block(frames_in, acts, w_mat, with_act, merge, taps=None):
     x0, x1 = frames_in
     a0, a1 = acts
     n = lax.axis_size("space")
@@ -96,6 +96,10 @@
     c1 = shift_tm(a1)
     a0, c1 = lax.optimization_barrier((a0, c1))
     c2 = shift_tm(a0)
+    later = None
+    if taps is not None:
+        c2, got = lax.optimization_barrier((c2, taps[1]))
+        w_mat, later = both_taps(taps[0], got)
     top_a = lax.ppermute(jnp.stack([c1[-1:], a0[-1:], a1[-1:]]), "space", down)
     bot_a = lax.ppermute(jnp.stack([c1[:1], a0[:1], a1[:1]]), "space", up)
     outs1 = frame_conv(1, (c1, a0, a1, top_a, bot_a), x1, w_mat, with_act)
@@ -103,17 +107,21 @@
     bot_b = lax.ppermute(c2[None, :1], "space", up)
     last = outs1[0] if merge else None
     outs0 = frame_conv(0, (c2, c1, a0, top_a, bot_a, top_b, bot_b), x0, w_mat, with_act, last)
-    return outs0, outs1
+    return outs0, outs1, later
 
 
-def both_taps(weights):
+def send_taps(weights):
     local = tap_matrix(weights[0])
     half = local.shape[0] // 2
+    core = lax.axis_index("space") % 2
+    mine = lax.dynamic_slice_in_dim(local, core * half, half, axis=0)
+    return local, lax.ppermute(mine, "section", [(0, 1), (1, 0)])
+
+
+def both_taps(local, got):
     section = lax.axis_index("section")
     core = lax.axis_index("space") % 2
     n_space = lax.axis_size("space")
-    mine = lax.dynamic_slice_in_dim(local, core * half, half, axis=0)
-    got = lax.ppermute(mine, "section", [(0, 1), (1, 0)])
     other = lax.ppermute(got, "space", [(i, i ^ 1) for i in range(n_space)])
     low = jnp.where(core == 0, got, other)
     high = jnp.where(core == 0, other, got)
@@ -124,14 +132,14 @@
 
 
 def body(video, weights):
-    first, second = both_taps(weights)
+    taps = send_taps(weights)
     clip = video[0]
     assert clip.shape[0] == 2
     x0, x1 = clip[0], clip[1]
     a1 = silu(x1)
     a0 = silu(x0)
-    (h0, s0), (h1, s1) = conv_block((x0, x1), (a0, a1), first, True, False)
-    (whole,), _ = conv_block((h0, h1), (s0, s1), second, False, True)
+    (h0, s0), (h1, s1), second = conv_block((x0, x1), (a0, a1), None, True, False, taps)
+    (whole,), _, _ = conv_block((h0, h1), (s0, s1), second, False, True)
     return whole[None]
 
 

time: 94.1 us -> 106 us (1.13)
  waiting for transfers between devices: 16.6 us -> 24.5 us
  starting transfers between devices: 38.3 us -> 41.7 us
    ppermute x4, waiting for transfers between devices: 3.72 us -> 24.4 us  [shift_tm(): return lax.ppermute(x, 'tm', [(i, i + 1) for i in range(n - 1)])]
    ppermute x1, waiting for transfers between devices: 7.5 us -> 0.01 us  [send_taps(): return (local, lax.ppermute(mine, 'section', [(0, 1), (1, 0)]))]
    ppermute x4, starting transfers between devices: 12.9 us -> 17.9 us  [shift_tm(): return lax.ppermute(x, 'tm', [(i, i + 1) for i in range(n - 1)])]
    ppermute x2, waiting for transfers between devices: 3.35 us -> 0.01 us  [conv_block(): bot_b = lax.ppermute(c2[None, :1], 'space', up)]
    ppermute x2, starting transfers between devices: 6.59 us -> 3.84 us  [conv_block(): top_b = lax.ppermute(c2[None, -1:], 'space', down)]
    ppermute x2, waiting for transfers between devices: 1.24 us -> 0.01 us  [conv_block(): top_a = lax.ppermute(jnp.stack([c1[-1:], a0[-1:], a1[-1:]]), 'space', down)]
  transfers between devices with their start and end apart: 14 -> 14, of which waited for: 5 -> 4; matrix products, arithmetic and copies ran while one was open for 8% -> 8% of each run, Pallas kernels for 19% -> 17%
where the time goes in v9:
time: 106 us; the launch traced here: 105 us
  starting transfers between devices  41.7 us (39%)
  waiting for transfers between devices  24.5 us (23%)
  Pallas kernels  23.5 us (22%)
  local copies, waits for them, and re-layouts  9.37 us (9%)
  other arithmetic  5.63 us (5%)
    ppermute x4, waiting for transfers between devices, shift_tm(): return lax.ppermute(x, 'tm', [(i, i + 1) for i in range(n - 1)])  24.4 us
    pallas_call x4, Pallas kernels, frame_conv(): pl.pallas_call(functools.partial(frame_kernel, t, 2 if with_act else 1, m...  23.5 us
    ppermute x4, starting transfers between devices, shift_tm(): return lax.ppermute(x, 'tm', [(i, i + 1) for i in range(n - 1)])  17.9 us
    ppermute x2, starting transfers between devices, conv_block(): top_a = lax.ppermute(jnp.stack([c1[-1:], a0[-1:], a1[-1:]]), 'space', down)  6.62 us
    ppermute x2, starting transfers between devices, conv_block(): bot_b = lax.ppermute(c2[None, :1], 'space', up)  5.1 us
    ppermute x2, starting transfers between devices, conv_block(): bot_a = lax.ppermute(jnp.stack([c1[:1], a0[:1], a1[:1]]), 'space', up)  4.5 us
    ppermute x2, starting transfers between devices, conv_block(): top_b = lax.ppermute(c2[None, -1:], 'space', down)  3.84 us
    unnamed x29, local copies, waits for them, and re-layouts  3.28 us
  transfers between devices with their start and end apart: 14, of which 4 were waited for; matrix products, arithmetic and copies ran while one was open for 8% of the time, Pallas kernels for 17%

profile of v9, /device:TPU:1, one launch (start us, length us, event | category | flops | bytes accessed | tf_op | source)
XLA Modules:
  0.0 104.9 jit_solution(3683785747118745370)
XLA Ops:
  0.0 2.8 %fusion.7 = (bf16[4,512,128]{2,1,0:T(8,128)(2,1)}, bf16[4,512,128]{2,1,0:T(8,128)(2,1)}) fusion(bf16[1,2,4,512,128]{4,3,2,1,0:T(8,128)(2,1)} %param.2), kind=kLoop, calls=%fused_computation.11 | loop fusion | flops 3145728 | bytes 2097152 | tf_op jit(solution)/shard_map/convert_element_type | solution.py:17
  2.8 4.8 %collective-permute-start = (bf16[4,512,128]{2,1,0:T(8,128)(2,1)}, bf16[4,512,128]{2,1,0:T(8,128)(2,1)}, u32[]{:S(2)}, u32[]{:S(2)}) collective-permute-start(bf16[4,512,128]{2,1,0:T(8,128)(2,1)} %get-tuple-element.29.refs_2_), channel_id=1, source_target_pairs={{0,4},{4,8},{8,12},{1,5},{5,9},{9,13},{2,6},{6,10},{10,14},{3,7},{... | collective-permute-start | bytes 1572872 | tf_op jit(solution)/shard_map/ppermute | solution.py:13
  7.6 0.0 copy-done.2
  7.6 0.8 copy.4
  8.4 0.0 copy-start
  8.4 0.1 copy.9
  8.6 0.1 constant_dynamic-slice_fusion
  8.6 1.3 %collective-permute-start.2 = (bf16[576,384]{1,0:T(8,128)(2,1)S(1)}, bf16[576,384]{1,0:T(8,128)(2,1)}, u32[]{:S(2)}, u32[]{:S(2)}) collective-permute-start(bf16[576,384]{1,0:T(8,128)(2,1)S(1)} %constant_dynamic-slice_fusion), channel_id=1, source_target_pairs={{0,16},{16,0},{1,17},{17,1},{2,18},{18,2},{3,19},{19,3},{4,20},{20... | collective-permute-start | bytes 1327112 | tf_op jit(solution)/shard_map/ppermute | solution.py:118
  9.9 7.8 %collective-permute-done.refs_1_.refs_0_ = bf16[4,512,128]{2,1,0:T(8,128)(2,1)} collective-permute-done((bf16[4,512,128]{2,1,0:T(8,128)(2,1)}, bf16[4,512,128]{2,1,0:T(8,128)(2,1)}, u32[]{:S(2)}, u32[]{:S(2)}) %collective-permute-start) | collective-permute-done | bytes 524320 | tf_op jit(solution)/shard_map/ppermute | solution.py:13
  17.7 5.1 %collective-permute-start.1 = (bf16[4,512,128]{2,1,0:T(8,128)(2,1)}, bf16[4,512,128]{2,1,0:T(8,128)(2,1)}, u32[]{:S(2)}, u32[]{:S(2)}) collective-permute-start(bf16[4,512,128]{2,1,0:T(8,128)(2,1)} %get-tuple-element.15.refs_2_.refs_1_), channel_id=1, source_target_pairs={{0,4},{4,8},{8,12},{1,5},{5,9},{9,13},{2,6},{6,10},{10,14},{3,7},{... | collective-permute-start | bytes 1572872 | tf_op jit(solution)/shard_map/ppermute | solution.py:13
  22.8 0.0 copy-done
  22.8 1.1 %slice_bitcast_fusion = (bf16[4,512,128]{2,1,0:T(8,128)(2,1)}, bf16[4,512,128]{2,1,0:T(8,128)(2,1)}) fusion(bf16[1,2,4,512,128]{4,3,2,1,0:T(8,128)(2,1)S(1)} %copy-done), kind=kLoop, calls=%fused_computation.16 | loop fusion | bytes 2097152 | tf_op jit(solution)/shard_map/squeeze | solution.py:138
  23.9 1.0 slice_bitcast_fusion.4
  24.8 0.0 copy-done.1
  24.9 1.0 slice_bitcast_fusion.14
  25.9 0.0 collective-permute-done.2
  25.9 6.1 %collective-permute-done.1.refs_0_ = bf16[4,512,128]{2,1,0:T(8,128)(2,1)} collective-permute-done((bf16[4,512,128]{2,1,0:T(8,128)(2,1)}, bf16[4,512,128]{2,1,0:T(8,128)(2,1)}, u32[]{:S(2)}, u32[]{:S(2)}) %collective-permute-start.1) | collective-permute-done | bytes 524320 | tf_op jit(solution)/shard_map/ppermute | solution.py:13
  31.9 2.5 %collective-permute-start.7 = (bf16[576,384]{1,0:T(8,128)(2,1)}, bf16[576,384]{1,0:T(8,128)(2,1)S(1)}, u32[]{:S(2)}, u32[]{:S(2)}) collective-permute-start(bf16[576,384]{1,0:T(8,128)(2,1)} %collective-permute-done.2), channel_id=1, source_target_pairs={{0,1},{1,0},{2,3},{3,2},{4,5},{5,4},{6,7},{7,6},{8,9},{9,8},{10,11... | collective-permute-start | bytes 1327112 | tf_op jit(solution)/shard_map/ppermute | solution.py:125
  34.4 1.9 %collective-permute-start.4 = (bf16[3,1,512,128]{3,2,1,0:T(8,128)(2,1)S(1)}, bf16[3,1,512,128]{3,2,1,0:T(8,128)(2,1)S(1)}, u32[]{:S(2)}, u32[]{:S(2)}) collective-permute-start(bf16[3,1,512,128]{3,2,1,0:T(8,128)(2,1)S(1)} %pad_maximum_fusion.2), channel_id=1, source_target_pairs={{1,0},{2,1},{3,2},{5,4},{6,5},{7,6},{9,8},{10,9},{11,10},{13,12},{... | collective-permute-start | bytes 1179656 | tf_op jit(solution)/shard_map/ppermute | solution.py:104
  36.4 3.6 %collective-permute-start.3 = (bf16[3,1,512,128]{3,2,1,0:T(8,128)(2,1)S(1)}, bf16[3,1,512,128]{3,2,1,0:T(8,128)(2,1)S(1)}, u32[]{:S(2)}, u32[]{:S(2)}) collective-permute-start(bf16[3,1,512,128]{3,2,1,0:T(8,128)(2,1)S(1)} %pad_maximum_fusion.1), channel_id=1, source_target_pairs={{0,1},{1,2},{2,3},{4,5},{5,6},{6,7},{8,9},{9,10},{10,11},{12,13},{... | collective-permute-start | bytes 1179656 | tf_op jit(solution)/shard_map/ppermute | solution.py:103
  40.1 1.0 slice_bitcast_fusion.12
  41.1 1.9 %collective-permute-start.5 = (bf16[1,1,512,128]{3,2,1,0:T(8,128)(2,1)S(1)}, bf16[1,1,512,128]{3,2,1,0:T(8,128)(2,1)S(1)}, u32[]{:S(2)}, u32[]{:S(2)}) collective-permute-start(bf16[1,1,512,128]{3,2,1,0:T(8,128)(2,1)S(1)} %get-tuple-element.42), channel_id=1, source_target_pairs={{0,1},{1,2},{2,3},{4,5},{5,6},{6,7},{8,9},{9,10},{10,11},{12,13},{... | collective-permute-start | bytes 393224 | tf_op jit(solution)/shard_map/ppermute | solution.py:106
  43.0 2.4 %collective-permute-start.6 = (bf16[1,1,512,128]{3,2,1,0:T(8,128)(2,1)S(1)}, bf16[1,1,512,128]{3,2,1,0:T(8,128)(2,1)S(1)}, u32[]{:S(2)}, u32[]{:S(2)}) collective-permute-start(bf16[1,1,512,128]{3,2,1,0:T(8,128)(2,1)S(1)} %get-tuple-element.41), channel_id=1, source_target_pairs={{1,0},{2,1},{3,2},{5,4},{6,5},{7,6},{9,8},{10,9},{11,10},{13,12},{... | collective-permute-start | bytes 393224 | tf_op jit(solution)/shard_map/ppermute | solution.py:107
  45.4 0.0 collective-permute-done.7
  45.4 1.1 %broadcast_select_fusion.3 = (bf16[576,384]{1,0:T(8,128)(2,1)S(1)}, bf16[576,384]{1,0:T(8,128)(2,1)S(1)}) fusion(bf16[576,384]{1,0:T(8,128)(2,1)} %collective-permute-done.2, bf16[576,384]{1,0:T(8,128)(2,1)S(1)} %collective-permute-done.7, pred[]{:T(512)S(6)} %eq.12), kind=kLoop, calls=%fused_computation.19 | loop fusion | flops 442368 | bytes 1769473 | tf_op jit(solution)/shard_map/jit(_where)/select_n | solution.py:126
  46.5 1.5 %broadcast_select_fusion = (bf16[1152,384]{1,0:T(8,128)(2,1)}, bf16[1152,384]{1,0:T(8,128)(2,1)}) fusion(pred[]{:T(512)S(6)} %eq.11, bf16[576,384]{1,0:T(8,128)(2,1)S(1)} %get-tuple-element.32, bf16[576,384]{1,0:T(8,128)(2,1)S(1)} %get-tuple-element.31, bf16[144,8,3,128]{3,2,1,0:T(4,128)(2,1)S(1)} %bitcast.51), kind=kLoop, calls=%fused_computation.14 | loop fusion | flops 2654208 | bytes 3538945 | tf_op jit(solution)/shard_map/jit(_where)/select_n | solution.py:130
  48.1 0.0 collective-permute-done.4.refs_4_
  48.1 0.0 collective-permute-done.3.refs_3_
  48.1 0.0 copy-start.7
  48.1 0.7 copy-done.6
  48.8 0.2 copy-done.7
  49.0 5.8 %shard_map.29 = (bf16[4,512,128]{2,1,0:T(8,128)(2,1)}, bf16[4,512,128]{2,1,0:T(8,128)(2,1)}) custom-call(bf16[4,512,128]{2,1,0:T(8,128)(2,1)} %collective-permute-done.refs_1_.refs_0_, bf16[4,512,128]{2,1,0:T(8,128)(2,1)} %get-tuple-element.15.refs_2_.refs_1_, bf16[4,512,128]{2,1,0:T(8,128)(2,1)} %get-tuple-element.29.refs_2_, ...), custom_call_target="tpu_custom_call" | custom-call | flops 1811939328 | bytes 4816896 | tf_op jit(solution)/shard_map/pallas_call | solution.py:83
  54.8 4.1 %collective-permute-start.8 = (bf16[4,512,128]{2,1,0:T(8,128)(2,1)}, bf16[4,512,128]{2,1,0:T(8,128)(2,1)S(1)}, u32[]{:S(2)}, u32[]{:S(2)}) collective-permute-start(bf16[4,512,128]{2,1,0:T(8,128)(2,1)} %get-tuple-element.20.refs_2_), channel_id=1, source_target_pairs={{0,4},{4,8},{8,12},{1,5},{5,9},{9,13},{2,6},{6,10},{10,14},{3,7},{... | collective-permute-start | bytes 1572872 | tf_op jit(solution)/shard_map/ppermute | solution.py:13
  59.0 0.0 collective-permute-done.5.refs_5_
  59.0 0.0 copy-start.10
  59.0 0.0 collective-permute-done.6.refs_6_
  59.0 0.0 copy-start.11
  59.0 0.6 copy-done.10
  59.6 0.1 copy-done.11
  59.7 6.0 %shard_map.28 = (bf16[4,512,128]{2,1,0:T(8,128)(2,1)}, bf16[4,512,128]{2,1,0:T(8,128)(2,1)}) custom-call(bf16[4,512,128]{2,1,0:T(8,128)(2,1)} %collective-permute-done.1.refs_0_, bf16[4,512,128]{2,1,0:T(8,128)(2,1)} %collective-permute-done.refs_1_.refs_0_, bf16[4,512,128]{2,1,0:T(8,128)(2,1)} %get-tuple-element.15.refs_2_.refs_1_, ...), custom_call_target="tpu_custom_call" | custom-call | flops 1811939328 | bytes 5079040 | tf_op jit(solution)/shard_map/pallas_call | solution.py:83
  65.7 0.0 copy-done.4
  65.7 5.1 %collective-permute-done.8.refs_0_.refs_1_ = bf16[4,512,128]{2,1,0:T(8,128)(2,1)S(1)} collective-permute-done((bf16[4,512,128]{2,1,0:T(8,128)(2,1)}, bf16[4,512,128]{2,1,0:T(8,128)(2,1)S(1)}, u32[]{:S(2)}, u32[]{:S(2)}) %collective-permute-start.8) | collective-permute-done | bytes 524320 | tf_op jit(solution)/shard_map/ppermute | solution.py:13
  70.8 1.2 %slice_bitcast_fusion.7 = (bf16[1,1,512,128]{3,2,1,0:T(8,128)(2,1)S(1)}, bf16[1,1,512,128]{3,2,1,0:T(8,128)(2,1)S(1)}) fusion(bf16[4,512,128]{2,1,0:T(8,128)(2,1)} %get-tuple-element.21.refs_1_.refs_2_), kind=kLoop, calls=%fused_computation.29 | loop fusion | bytes 524288 | tf_op jit(solution)/shard_map/stack | solution.py:104
  72.0 3.9 %collective-permute-start.9 = (bf16[4,512,128]{2,1,0:T(8,128)(2,1)}, bf16[4,512,128]{2,1,0:T(8,128)(2,1)S(1)}, u32[]{:S(2)}, u32[]{:S(2)}) collective-permute-start(bf16[4,512,128]{2,1,0:T(8,128)(2,1)} %get-tuple-element.21.refs_1_.refs_2_), channel_id=1, source_target_pairs={{0,4},{4,8},{8,12},{1,5},{5,9},{9,13},{2,6},{6,10},{10,14},{3,7},{... | collective-permute-start | bytes 1572872 | tf_op jit(solution)/shard_map/ppermute | solution.py:13
  76.0 2.6 %collective-permute-start.11 = (bf16[3,1,512,128]{3,2,1,0:T(8,128)(2,1)S(1)}, bf16[3,1,512,128]{3,2,1,0:T(8,128)(2,1)S(1)}, u32[]{:S(2)}, u32[]{:S(2)}) collective-permute-start(bf16[3,1,512,128]{3,2,1,0:T(8,128)(2,1)S(1)} %pad_maximum_fusion.4), channel_id=1, source_target_pairs={{1,0},{2,1},{3,2},{5,4},{6,5},{7,6},{9,8},{10,9},{11,10},{13,12},{... | collective-permute-start | bytes 1179656 | tf_op jit(solution)/shard_map/ppermute | solution.py:104
  78.6 0.0 copy-done.3
  78.6 3.0 %collective-permute-start.10 = (bf16[3,1,512,128]{3,2,1,0:T(8,128)(2,1)S(1)}, bf16[3,1,512,128]{3,2,1,0:T(8,128)(2,1)S(1)}, u32[]{:S(2)}, u32[]{:S(2)}) collective-permute-start(bf16[3,1,512,128]{3,2,1,0:T(8,128)(2,1)S(1)} %pad_maximum_fusion.3), channel_id=1, source_target_pairs={{0,1},{1,2},{2,3},{4,5},{5,6},{6,7},{8,9},{9,10},{10,11},{12,13},{... | collective-permute-start | bytes 1179656 | tf_op jit(solution)/shard_map/ppermute | solution.py:103
  81.6 5.4 %collective-permute-done.9.refs_0_ = bf16[4,512,128]{2,1,0:T(8,128)(2,1)S(1)} collective-permute-done((bf16[4,512,128]{2,1,0:T(8,128)(2,1)}, bf16[4,512,128]{2,1,0:T(8,128)(2,1)S(1)}, u32[]{:S(2)}, u32[]{:S(2)}) %collective-permute-start.9) | collective-permute-done | bytes 524320 | tf_op jit(solution)/shard_map/ppermute | solution.py:13
  87.1 1.9 %collective-permute-start.12 = (bf16[1,1,512,128]{3,2,1,0:T(8,128)(2,1)S(1)}, bf16[1,1,512,128]{3,2,1,0:T(8,128)(2,1)S(1)}, u32[]{:S(2)}, u32[]{:S(2)}) collective-permute-start(bf16[1,1,512,128]{3,2,1,0:T(8,128)(2,1)S(1)} %get-tuple-element.34), channel_id=1, source_target_pairs={{0,1},{1,2},{2,3},{4,5},{5,6},{6,7},{8,9},{9,10},{10,11},{12,13},{... | collective-permute-start | bytes 393224 | tf_op jit(solution)/shard_map/ppermute | solution.py:106
  89.0 2.7 %collective-permute-start.13 = (bf16[1,1,512,128]{3,2,1,0:T(8,128)(2,1)S(1)}, bf16[1,1,512,128]{3,2,1,0:T(8,128)(2,1)S(1)}, u32[]{:S(2)}, u32[]{:S(2)}) collective-permute-start(bf16[1,1,512,128]{3,2,1,0:T(8,128)(2,1)S(1)} %get-tuple-element.33), channel_id=1, source_target_pairs={{1,0},{2,1},{3,2},{5,4},{6,5},{7,6},{9,8},{10,9},{11,10},{13,12},{... | collective-permute-start | bytes 393224 | tf_op jit(solution)/shard_map/ppermute | solution.py:107
  91.7 0.0 collective-permute-done.11.refs_4_
  91.7 0.0 copy-start.8
  91.7 0.0 collective-permute-done.10.refs_3_
  91.7 0.0 copy-start.9
  91.7 0.7 copy-done.8
  92.5 0.1 copy-done.9
  92.6 5.6 %shard_map.30.refs_7_ = bf16[4,512,128]{2,1,0:T(8,128)(2,1)} custom-call(bf16[4,512,128]{2,1,0:T(8,128)(2,1)} %copy-done.3, bf16[4,512,128]{2,1,0:T(8,128)(2,1)} %get-tuple-element.21.refs_1_.refs_2_, bf16[4,512,128]{2,1,0:T(8,128)(2,1)} %get-tuple-element.20.refs_2_, bf16[3,1,512,128]{3,2,1,0:T(8,128)(2,1)} %copy-done.9, ...), custom_call_target="tpu_custom_call" | custom-call | flops 1811939328 | bytes 4816896 | tf_op jit(solution)/shard_map/pallas_call | solution.py:83
  98.2 0.0 copy-done.5
  98.2 0.0 collective-permute-done.12.refs_5_
  98.2 0.0 collective-permute-done.13.refs_6_
  98.2 0.0 copy-start.13
  98.2 0.6 copy-done.12
  98.9 0.1 copy-done.13
  98.9 6.0 %shard_map.31 = bf16[2,4,512,128]{3,2,1,0:T(8,128)(2,1)} custom-call(bf16[4,512,128]{2,1,0:T(8,128)(2,1)} %copy-done.5, bf16[4,512,128]{2,1,0:T(8,128)(2,1)} %copy-done.3, bf16[4,512,128]{2,1,0:T(8,128)(2,1)} %get-tuple-element.21.refs_1_.refs_2_, bf16[3,1,512,128]{3,2,1,0:T(8,128)(2,1)} %copy-done.9, bf16[3,1,512,128]{3,2,1,0:T(8,128)(2,1)} %copy-done.8, ...), custom_call_target="tpu_custom_call" | custom-call | flops 1811939328 | bytes 5603328 | tf_op jit(solution)/shard_map/pallas_call | solution.py:83
  (14 shorter events, 0.3 us)
Async XLA Ops:
  0.0 7.6 %copy-start.2 = (bf16[1,9,384,128]{3,2,1,0:T(8,128)(2,1)S(1)}, bf16[1,9,384,128]{3,2,1,0:T(8,128)(2,1)}, u32[]{:S(2)}) copy-start(bf16[1,9,384,128]{3,2,1,0:T(8,128)(2,1)} %param.3) | copy-start | bytes 2654212
  2.8 14.9 %collective-permute-start = (bf16[4,512,128]{2,1,0:T(8,128)(2,1)}, bf16[4,512,128]{2,1,0:T(8,128)(2,1)}, u32[]{:S(2)}, u32[]{:S(2)}) collective-permute-start(bf16[4,512,128]{2,1,0:T(8,128)(2,1)} %get-tuple-element.29.refs_2_), channel_id=1, source_target_pairs={{0,4},{4,8},{8,12},{1,5},{5,9},{9,13},{2,6},{6,10},{10,14},{3,7},{... | collective-permute-start | bytes 1572872 | tf_op jit(solution)/shard_map/ppermute | solution.py:13
  8.4 14.4 %copy-start = (bf16[1,2,4,512,128]{4,3,2,1,0:T(8,128)(2,1)S(1)}, bf16[1,2,4,512,128]{4,3,2,1,0:T(8,128)(2,1)}, u32[]{:S(2)}) copy-start(bf16[1,2,4,512,128]{4,3,2,1,0:T(8,128)(2,1)} %param.2) | copy-start | bytes 3145732
  8.6 17.2 %collective-permute-start.2 = (bf16[576,384]{1,0:T(8,128)(2,1)S(1)}, bf16[576,384]{1,0:T(8,128)(2,1)}, u32[]{:S(2)}, u32[]{:S(2)}) collective-permute-start(bf16[576,384]{1,0:T(8,128)(2,1)S(1)} %constant_dynamic-slice_fusion), channel_id=1, source_target_pairs={{0,16},{16,0},{1,17},{17,1},{2,18},{18,2},{3,19},{19,3},{4,20},{20... | collective-permute-start | bytes 1327112 | tf_op jit(solution)/shard_map/ppermute | solution.py:118
  17.7 7.1 %copy-start.1 = (bf16[4,512,128]{2,1,0:T(8,128)(2,1)S(1)}, bf16[4,512,128]{2,1,0:T(8,128)(2,1)}, u32[]{:S(2)}) copy-start(bf16[4,512,128]{2,1,0:T(8,128)(2,1)} %get-tuple-element.15.refs_2_.refs_1_) | copy-start | bytes 1572868
  17.7 14.2 %collective-permute-start.1 = (bf16[4,512,128]{2,1,0:T(8,128)(2,1)}, bf16[4,512,128]{2,1,0:T(8,128)(2,1)}, u32[]{:S(2)}, u32[]{:S(2)}) collective-permute-start(bf16[4,512,128]{2,1,0:T(8,128)(2,1)} %get-tuple-element.15.refs_2_.refs_1_), channel_id=1, source_target_pairs={{0,4},{4,8},{8,12},{1,5},{5,9},{9,13},{2,6},{6,10},{10,14},{3,7},{... | collective-permute-start | bytes 1572872 | tf_op jit(solution)/shard_map/ppermute | solution.py:13
  31.9 13.5 %collective-permute-start.7 = (bf16[576,384]{1,0:T(8,128)(2,1)}, bf16[576,384]{1,0:T(8,128)(2,1)S(1)}, u32[]{:S(2)}, u32[]{:S(2)}) collective-permute-start(bf16[576,384]{1,0:T(8,128)(2,1)} %collective-permute-done.2), channel_id=1, source_target_pairs={{0,1},{1,0},{2,3},{3,2},{4,5},{5,4},{6,7},{7,6},{8,9},{9,8},{10,11... | collective-permute-start | bytes 1327112 | tf_op jit(solution)/shard_map/ppermute | solution.py:125
  34.4 13.6 %collective-permute-start.4 = (bf16[3,1,512,128]{3,2,1,0:T(8,128)(2,1)S(1)}, bf16[3,1,512,128]{3,2,1,0:T(8,128)(2,1)S(1)}, u32[]{:S(2)}, u32[]{:S(2)}) collective-permute-start(bf16[3,1,512,128]{3,2,1,0:T(8,128)(2,1)S(1)} %pad_maximum_fusion.2), channel_id=1, source_target_pairs={{1,0},{2,1},{3,2},{5,4},{6,5},{7,6},{9,8},{10,9},{11,10},{13,12},{... | collective-permute-start | bytes 1179656 | tf_op jit(solution)/shard_map/ppermute | solution.py:104
  36.4 11.6 %collective-permute-start.3 = (bf16[3,1,512,128]{3,2,1,0:T(8,128)(2,1)S(1)}, bf16[3,1,512,128]{3,2,1,0:T(8,128)(2,1)S(1)}, u32[]{:S(2)}, u32[]{:S(2)}) collective-permute-start(bf16[3,1,512,128]{3,2,1,0:T(8,128)(2,1)S(1)} %pad_maximum_fusion.1), channel_id=1, source_target_pairs={{0,1},{1,2},{2,3},{4,5},{5,6},{6,7},{8,9},{9,10},{10,11},{12,13},{... | collective-permute-start | bytes 1179656 | tf_op jit(solution)/shard_map/ppermute | solution.py:103
  41.1 17.9 %collective-permute-start.5 = (bf16[1,1,512,128]{3,2,1,0:T(8,128)(2,1)S(1)}, bf16[1,1,512,128]{3,2,1,0:T(8,128)(2,1)S(1)}, u32[]{:S(2)}, u32[]{:S(2)}) collective-permute-start(bf16[1,1,512,128]{3,2,1,0:T(8,128)(2,1)S(1)} %get-tuple-element.42), channel_id=1, source_target_pairs={{0,1},{1,2},{2,3},{4,5},{5,6},{6,7},{8,9},{9,10},{10,11},{12,13},{... | collective-permute-start | bytes 393224 | tf_op jit(solution)/shard_map/ppermute | solution.py:106
  43.0 16.0 %collective-permute-start.6 = (bf16[1,1,512,128]{3,2,1,0:T(8,128)(2,1)S(1)}, bf16[1,1,512,128]{3,2,1,0:T(8,128)(2,1)S(1)}, u32[]{:S(2)}, u32[]{:S(2)}) collective-permute-start(bf16[1,1,512,128]{3,2,1,0:T(8,128)(2,1)S(1)} %get-tuple-element.41), channel_id=1, source_target_pairs={{1,0},{2,1},{3,2},{5,4},{6,5},{7,6},{9,8},{10,9},{11,10},{13,12},{... | collective-permute-start | bytes 393224 | tf_op jit(solution)/shard_map/ppermute | solution.py:107
  48.1 0.8 copy-start.6
  48.1 0.9 copy-start.7
  54.8 16.0 %collective-permute-start.8 = (bf16[4,512,128]{2,1,0:T(8,128)(2,1)}, bf16[4,512,128]{2,1,0:T(8,128)(2,1)S(1)}, u32[]{:S(2)}, u32[]{:S(2)}) collective-permute-start(bf16[4,512,128]{2,1,0:T(8,128)(2,1)} %get-tuple-element.20.refs_2_), channel_id=1, source_target_pairs={{0,4},{4,8},{8,12},{1,5},{5,9},{9,13},{2,6},{6,10},{10,14},{3,7},{... | collective-permute-start | bytes 1572872 | tf_op jit(solution)/shard_map/ppermute | solution.py:13
  59.0 0.6 copy-start.10
  59.0 0.7 copy-start.11
  59.7 6.0 %copy-start.4 = (bf16[4,512,128]{2,1,0:T(8,128)(2,1)S(1)}, bf16[4,512,128]{2,1,0:T(8,128)(2,1)}, u32[]{:S(2)}) copy-start(bf16[4,512,128]{2,1,0:T(8,128)(2,1)} %get-tuple-element.20.refs_2_) | copy-start | bytes 1572868
  70.8 7.8 %copy-start.3 = (bf16[4,512,128]{2,1,0:T(8,128)(2,1)}, bf16[4,512,128]{2,1,0:T(8,128)(2,1)S(1)}, u32[]{:S(2)}) copy-start(bf16[4,512,128]{2,1,0:T(8,128)(2,1)S(1)} %collective-permute-done.8.refs_0_.refs_1_) | copy-start | bytes 1572868
  72.0 15.1 %collective-permute-start.9 = (bf16[4,512,128]{2,1,0:T(8,128)(2,1)}, bf16[4,512,128]{2,1,0:T(8,128)(2,1)S(1)}, u32[]{:S(2)}, u32[]{:S(2)}) collective-permute-start(bf16[4,512,128]{2,1,0:T(8,128)(2,1)} %get-tuple-element.21.refs_1_.refs_2_), channel_id=1, source_target_pairs={{0,4},{4,8},{8,12},{1,5},{5,9},{9,13},{2,6},{6,10},{10,14},{3,7},{... | collective-permute-start | bytes 1572872 | tf_op jit(solution)/shard_map/ppermute | solution.py:13
  76.0 15.7 %collective-permute-start.11 = (bf16[3,1,512,128]{3,2,1,0:T(8,128)(2,1)S(1)}, bf16[3,1,512,128]{3,2,1,0:T(8,128)(2,1)S(1)}, u32[]{:S(2)}, u32[]{:S(2)}) collective-permute-start(bf16[3,1,512,128]{3,2,1,0:T(8,128)(2,1)S(1)} %pad_maximum_fusion.4), channel_id=1, source_target_pairs={{1,0},{2,1},{3,2},{5,4},{6,5},{7,6},{9,8},{10,9},{11,10},{13,12},{... | collective-permute-start | bytes 1179656 | tf_op jit(solution)/shard_map/ppermute | solution.py:104
  78.6 13.1 %collective-permute-start.10 = (bf16[3,1,512,128]{3,2,1,0:T(8,128)(2,1)S(1)}, bf16[3,1,512,128]{3,2,1,0:T(8,128)(2,1)S(1)}, u32[]{:S(2)}, u32[]{:S(2)}) collective-permute-start(bf16[3,1,512,128]{3,2,1,0:T(8,128)(2,1)S(1)} %pad_maximum_fusion.3), channel_id=1, source_target_pairs={{0,1},{1,2},{2,3},{4,5},{5,6},{6,7},{8,9},{9,10},{10,11},{12,13},{... | collective-permute-start | bytes 1179656 | tf_op jit(solution)/shard_map/ppermute | solution.py:103
  87.0 11.2 %copy-start.5 = (bf16[4,512,128]{2,1,0:T(8,128)(2,1)}, bf16[4,512,128]{2,1,0:T(8,128)(2,1)S(1)}, u32[]{:S(2)}) copy-start(bf16[4,512,128]{2,1,0:T(8,128)(2,1)S(1)} %collective-permute-done.9.refs_0_) | copy-start | bytes 1572868
  87.1 11.1 %collective-permute-start.12 = (bf16[1,1,512,128]{3,2,1,0:T(8,128)(2,1)S(1)}, bf16[1,1,512,128]{3,2,1,0:T(8,128)(2,1)S(1)}, u32[]{:S(2)}, u32[]{:S(2)}) collective-permute-start(bf16[1,1,512,128]{3,2,1,0:T(8,128)(2,1)S(1)} %get-tuple-element.34), channel_id=1, source_target_pairs={{0,1},{1,2},{2,3},{4,5},{5,6},{6,7},{8,9},{9,10},{10,11},{12,13},{... | collective-permute-start | bytes 393224 | tf_op jit(solution)/shard_map/ppermute | solution.py:106
  89.0 9.2 %collective-permute-start.13 = (bf16[1,1,512,128]{3,2,1,0:T(8,128)(2,1)S(1)}, bf16[1,1,512,128]{3,2,1,0:T(8,128)(2,1)S(1)}, u32[]{:S(2)}, u32[]{:S(2)}) collective-permute-start(bf16[1,1,512,128]{3,2,1,0:T(8,128)(2,1)S(1)} %get-tuple-element.33), channel_id=1, source_target_pairs={{1,0},{2,1},{3,2},{5,4},{6,5},{7,6},{9,8},{10,9},{11,10},{13,12},{... | collective-permute-start | bytes 393224 | tf_op jit(solution)/shard_map/ppermute | solution.py:107
  91.7 0.8 copy-start.8
  91.7 0.9 copy-start.9
  98.2 0.7 copy-start.12
  98.2 0.7 copy-start.13

commit v10 on v5

--- a/solution.py
+++ b/solution.py
@@ -17,14 +17,7 @@
     return jax.nn.silu(x.astype(jnp.float32)).astype(jnp.bfloat16)
 
 
-def frame_kernel(t, n_out, *refs):
-    if t == 1:
-        c1_ref, a0_ref, a1_ref, top_a, bot_a, base_ref, w_ref = refs[:7]
-        sources = [(c1_ref, top_a, bot_a, 0), (a0_ref, top_a, bot_a, 1), (a1_ref, top_a, bot_a, 2)]
-    else:
-        c2_ref, c1_ref, a0_ref, top_a, bot_a, top_b, bot_b, base_ref, w_ref = refs[:9]
-        sources = [(c2_ref, top_b, bot_b, 0), (c1_ref, top_a, bot_a, 0), (a0_ref, top_a, bot_a, 1)]
-    outs = refs[len(refs) - n_out :]
+def conv_rows(sources, base_ref, w_ref, store):
     rows, width, chans = base_ref.shape
 
     def slab(a, j):
@@ -44,11 +37,42 @@
         left = jnp.where(column == 0, 0.0, left)
         right = jnp.where(column == width - 1, 0.0, right)
         total = z[:, chans : 2 * chans] + left + right
-        out = (base_ref[h].astype(jnp.float32) + total).astype(outs[0].dtype)
+        store(h, base_ref[h].astype(jnp.float32) + total)
+
+
+def frame_sources(t, c2_ref, c1_ref, a0_ref, a1_ref, top_a, bot_a, top_b, bot_b):
+    if t == 1:
+        return [(c1_ref, top_a, bot_a, 0), (a0_ref, top_a, bot_a, 1), (a1_ref, top_a, bot_a, 2)]
+    return [(c2_ref, top_b, bot_b, 0), (c1_ref, top_a, bot_a, 0), (a0_ref, top_a, bot_a, 1)]
+
+
+def frame_kernel(t, with_act, *refs):
+    if t == 1:
+        c1_ref, a0_ref, a1_ref, top_a, bot_a, base_ref, w_ref = refs[:7]
+        sources = frame_sources(1, None, c1_ref, a0_ref, a1_ref, top_a, bot_a, None, None)
+    else:
+        c2_ref, c1_ref, a0_ref, top_a, bot_a, top_b, bot_b, base_ref, w_ref = refs[:9]
+        sources = frame_sources(0, c2_ref, c1_ref, a0_ref, None, top_a, bot_a, top_b, bot_b)
+    outs = refs[len(refs) - (2 if with_act else 1) :]
+
+    def store(h, value):
+        out = value.astype(outs[0].dtype)
         outs[0][h] = out
-        if len(outs) == 2:
+        if with_act:
             wide = out.astype(jnp.float32)
             outs[1][h] = (wide / (1.0 + jnp.exp(-wide))).astype(outs[1].dtype)
+
+    conv_rows(sources, base_ref, w_ref, store)
+
+
+def pair_kernel(c2_ref, c1_ref, a0_ref, a1_ref, top_a, bot_a, top_b, bot_b, x0_ref, x1_ref, w_ref, out_ref):
+    for t, base_ref in ((1, x1_ref), (0, x0_ref)):
+        sources = frame_sources(t, c2_ref, c1_ref, a0_ref, a1_ref, top_a, bot_a, top_b, bot_b)
+
+        def store(h, value, t=t):
+            out_ref[t, h] = value.astype(out_ref.dtype)
+
+        conv_rows(sources, base_ref, w_ref, store)
 
 
 def tap_matrix(taps):
@@ -66,13 +90,24 @@
     nbytes = sum(x.size * x.dtype.itemsize for x in operands) + 3 * base.size * 2 + w_mat.size * 2
     shape = jax.ShapeDtypeStruct(base.shape, base.dtype)
     return pl.pallas_call(
-        functools.partial(frame_kernel, t, 2 if with_act else 1),
+        functools.partial(frame_kernel, t, with_act),
         out_shape=(shape, shape) if with_act else (shape,),
         cost_estimate=pl.CostEstimate(flops=flops, bytes_accessed=nbytes, transcendentals=0),
     )(*operands, base, w_mat)
 
 
-def conv_block(frames_in, acts, w_mat, with_act):
+def pair_conv(operands, x0, x1, w_mat):
+    rows, width, chans = x0.shape
+    flops = 4 * rows * width * w_mat.shape[0] * w_mat.shape[1]
+    nbytes = sum(x.size * x.dtype.itemsize for x in operands) + 4 * x0.size * 2 + w_mat.size * 2
+    return pl.pallas_call(
+        pair_kernel,
+        out_shape=jax.ShapeDtypeStruct((2,) + x0.shape, x0.dtype),
+        cost_estimate=pl.CostEstimate(flops=flops, bytes_accessed=nbytes, transcendentals=0),
+    )(*operands, x0, x1, w_mat)
+
+
+def conv_block(frames_in, acts, w_mat, with_act, merge):
     x0, x1 = frames_in
     a0, a1 = acts
     n = lax.axis_size("space")
@@ -83,6 +118,10 @@
     c2 = shift_tm(a0)
     top_a = lax.ppermute(jnp.stack([c1[-1:], a0[-1:], a1[-1:]]), "space", down)
     bot_a = lax.ppermute(jnp.stack([c1[:1], a0[:1], a1[:1]]), "space", up)
+    if merge:
+        top_b = lax.ppermute(c2[None, -1:], "space", down)
+        bot_b = lax.ppermute(c2[None, :1], "space", up)
+        return pair_conv((c2, c1, a0, a1, top_a, bot_a, top_b, bot_b), x0, x1, w_mat)
     outs1 = frame_conv(1, (c1, a0, a1, top_a, bot_a), x1, w_mat, with_act)
     top_b = lax.ppermute(c2[None, -1:], "space", down)
     bot_b = lax.ppermute(c2[None, :1], "space", up)
@@ -91,17 +130,17 @@
 
 
 def both_taps(weights):
-    local = weights[0]
-    half = local.shape[1] // 2
+    local = tap_matrix(weights[0])
+    half = local.shape[0] // 2
     section = lax.axis_index("section")
     core = lax.axis_index("space") % 2
     n_space = lax.axis_size("space")
-    mine = lax.dynamic_slice_in_dim(local, core * half, half, axis=1)
+    mine = lax.dynamic_slice_in_dim(local, core * half, half, axis=0)
     got = lax.ppermute(mine, "section", [(0, 1), (1, 0)])
     other = lax.ppermute(got, "space", [(i, i ^ 1) for i in range(n_space)])
     low = jnp.where(core == 0, got, other)
     high = jnp.where(core == 0, other, got)
-    remote = jnp.concatenate([low, high], axis=1)
+    remote = jnp.concatenate([low, high], axis=0)
     first = jnp.where(section == 0, local, remote)
     second = jnp.where(section == 0, remote, local)
     return first, second
@@ -114,9 +153,9 @@
     x0, x1 = clip[0], clip[1]
     a1 = silu(x1)
     a0 = silu(x0)
-    (h0, s0), (h1, s1) = conv_block((x0, x1), (a0, a1), tap_matrix(first), True)
-    (o0,), (o1,) = conv_block((h0, h1), (s0, s1), tap_matrix(second), False)
-    return jnp.stack([o0, o1])[None]
+    (h0, s0), (h1, s1) = conv_block((x0, x1), (a0, a1), first, True, False)
+    whole = conv_block((h0, h1), (s0, s1), second, False, True)
+    return whole[None]
 
 
 def solution(mesh):

time: 96.2 us -> 92.8 us (0.965)
  waiting for transfers between devices: 15.2 us -> 19.3 us
  local copies, waits for them, and re-layouts: 11 us -> 8.19 us
  Pallas kernels: 23.1 us -> 20.5 us
  starting transfers between devices: 40.4 us -> 38.3 us
    ppermute x2, waiting for transfers between devices: 0.01 us -> 6.97 us  [conv_block(): bot_b = lax.ppermute(c2[None, :1], 'space', up)]
    ppermute x2, waiting for transfers between devices: 3.95 us -> 0.82 us  [conv_block(): bot_a = lax.ppermute(jnp.stack([c1[:1], a0[:1], a1[:1]]), 'space', up)]
    unnamed x34 -> x29, local copies, waits for them, and re-layouts: 5.11 us -> 2.24 us
    pallas_call x4 -> x3, Pallas kernels: 23.1 us -> 20.5 us  [the longest x2 11.8 us: frame_conv(): pl.pallas_call(functools.partial(frame_kernel, t, with_act), out_shape=(s...]
    broadcast_in_dim x1 -> x0, other arithmetic: 2.11 us -> none  [body(): return jnp.stack([o0, o1])[None]]
    select_n x0 -> x1, other arithmetic: none -> 1.53 us  [both_taps(): second = jnp.where(section == 0, remote, local)]
    transpose x2 -> x0, local copies, waits for them, and re-layouts: 1.53 us -> none  [tap_matrix(): return taps.reshape(nine, 3, chans, chans).transpose(0, 2, 1, 3).reshape(...]
    ppermute x2, starting transfers between devices: 8.24 us -> 7 us  [conv_block(): top_a = lax.ppermute(jnp.stack([c1[-1:], a0[-1:], a1[-1:]]), 'space', down)]
  transfers between devices with their start and end apart: 14 -> 14, of which waited for: 4 -> 6; matrix products, arithmetic and copies ran while one was open for 9% -> 10% of each run, Pallas kernels for 18% -> 13%
where the time goes in v10:
time: 92.8 us; the launch traced here: 92.2 us
  starting transfers between devices  38.3 us (41%)
  Pallas kernels  20.5 us (22%)
  waiting for transfers between devices  19.3 us (21%)
  local copies, waits for them, and re-layouts  8.19 us (9%)
  other arithmetic  5.63 us (6%)
    ppermute x4, starting transfers between devices, shift_tm(): return lax.ppermute(x, 'tm', [(i, i + 1) for i in range(n - 1)])  12.9 us
    pallas_call x2, Pallas kernels, frame_conv(): pl.pallas_call(functools.partial(frame_kernel, t, with_act), out_shape=(s...  11.8 us
    pallas_call x1, Pallas kernels, pair_conv(): pl.pallas_call(pair_kernel, out_shape=jax.ShapeDtypeStruct((2,) + x0.shap...  8.73 us
    ppermute x1, waiting for transfers between devices, both_taps(): got = lax.ppermute(mine, 'section', [(0, 1), (1, 0)])  7.5 us
    ppermute x2, starting transfers between devices, conv_block(): top_a = lax.ppermute(jnp.stack([c1[-1:], a0[-1:], a1[-1:]]), 'space', down)  7 us
    ppermute x2, waiting for transfers between devices, conv_block(): bot_b = lax.ppermute(c2[None, :1], 'space', up)  6.97 us
    ppermute x2, starting transfers between devices, conv_block(): top_b = lax.ppermute(c2[None, -1:], 'space', down)  6.59 us
    ppermute x2, starting transfers between devices, conv_block(): bot_b = lax.ppermute(c2[None, :1], 'space', up)  4.51 us
  transfers between devices with their start and end apart: 14, of which 6 were waited for; matrix products, arithmetic and copies ran while one was open for 10% of the time, Pallas kernels for 13%

profile of v10, /device:TPU:1, one launch (start us, length us, event | category | flops | bytes accessed | tf_op | source)
XLA Modules:
  0.0 92.2 jit_solution(8151785925927266548)
XLA Ops:
  0.0 0.0 copy-start.2
  0.0 2.8 %fusion.7 = (bf16[4,512,128]{2,1,0:T(8,128)(2,1)}, bf16[4,512,128]{2,1,0:T(8,128)(2,1)}) fusion(bf16[1,2,4,512,128]{4,3,2,1,0:T(8,128)(2,1)} %param.2), kind=kLoop, calls=%fused_computation.11 | loop fusion | flops 3145728 | bytes 2097152 | tf_op jit(solution)/shard_map/convert_element_type | solution.py:17
  2.8 4.8 %collective-permute-start = (bf16[4,512,128]{2,1,0:T(8,128)(2,1)}, bf16[4,512,128]{2,1,0:T(8,128)(2,1)}, u32[]{:S(2)}, u32[]{:S(2)}) collective-permute-start(bf16[4,512,128]{2,1,0:T(8,128)(2,1)} %get-tuple-element.25.refs_2_), channel_id=1, source_target_pairs={{0,4},{4,8},{8,12},{1,5},{5,9},{9,13},{2,6},{6,10},{10,14},{3,7},{... | collective-permute-start | bytes 1572872 | tf_op jit(solution)/shard_map/ppermute | solution.py:13
  7.6 0.0 copy-done.2
  7.6 0.8 copy.4
  8.4 0.1 copy.9
  8.6 0.0 copy-start
  8.6 0.1 constant_dynamic-slice_fusion
  8.6 1.3 %collective-permute-start.6 = (bf16[576,384]{1,0:T(8,128)(2,1)S(1)}, bf16[576,384]{1,0:T(8,128)(2,1)}, u32[]{:S(2)}, u32[]{:S(2)}) collective-permute-start(bf16[576,384]{1,0:T(8,128)(2,1)S(1)} %constant_dynamic-slice_fusion), channel_id=1, source_target_pairs={{0,16},{16,0},{1,17},{17,1},{2,18},{18,2},{3,19},{19,3},{4,20},{20... | collective-permute-start | bytes 1327112 | tf_op jit(solution)/shard_map/ppermute | solution.py:139
  9.9 1.0 %slice_bitcast_fusion.6 = (bf16[1,1,512,128]{3,2,1,0:T(8,128)(2,1)S(1)}, bf16[1,1,512,128]{3,2,1,0:T(8,128)(2,1)S(1)}) fusion(bf16[4,512,128]{2,1,0:T(8,128)(2,1)} %get-tuple-element.25.refs_2_), kind=kLoop, calls=%fused_computation.28 | loop fusion | bytes 524288 | tf_op jit(solution)/shard_map/stack | solution.py:120
  10.9 0.0 copy-done
  10.9 0.0 copy-start.1
  10.9 1.1 %slice_bitcast_fusion = (bf16[4,512,128]{2,1,0:T(8,128)(2,1)}, bf16[4,512,128]{2,1,0:T(8,128)(2,1)}) fusion(bf16[1,2,4,512,128]{4,3,2,1,0:T(8,128)(2,1)S(1)} %copy-done), kind=kLoop, calls=%fused_computation.16 | loop fusion | bytes 2097152 | tf_op jit(solution)/shard_map/squeeze | solution.py:153
  12.0 7.5 %collective-permute-done.6 = bf16[576,384]{1,0:T(8,128)(2,1)} collective-permute-done((bf16[576,384]{1,0:T(8,128)(2,1)S(1)}, bf16[576,384]{1,0:T(8,128)(2,1)}, u32[]{:S(2)}, u32[]{:S(2)}) %collective-permute-start.6) | collective-permute-done | bytes 442400 | tf_op jit(solution)/shard_map/ppermute | solution.py:139
  19.5 1.9 %collective-permute-start.7 = (bf16[576,384]{1,0:T(8,128)(2,1)}, bf16[576,384]{1,0:T(8,128)(2,1)S(1)}, u32[]{:S(2)}, u32[]{:S(2)}) collective-permute-start(bf16[576,384]{1,0:T(8,128)(2,1)} %collective-permute-done.6), channel_id=1, source_target_pairs={{0,1},{1,0},{2,3},{3,2},{4,5},{5,4},{6,7},{7,6},{8,9},{9,8},{10,11... | collective-permute-start | bytes 1327112 | tf_op jit(solution)/shard_map/ppermute | solution.py:140
  21.4 0.0 collective-permute-done.refs_1_.refs_0_
  21.4 0.0 copy-done.1
  21.4 2.5 %collective-permute-start.1 = (bf16[4,512,128]{2,1,0:T(8,128)(2,1)S(1)}, bf16[4,512,128]{2,1,0:T(8,128)(2,1)S(1)}, u32[]{:S(2)}, u32[]{:S(2)}) collective-permute-start(bf16[4,512,128]{2,1,0:T(8,128)(2,1)S(1)} %copy-done.1), channel_id=1, source_target_pairs={{0,4},{4,8},{8,12},{1,5},{5,9},{9,13},{2,6},{6,10},{10,14},{3,7},{... | collective-permute-start | bytes 1572872 | tf_op jit(solution)/shard_map/ppermute | solution.py:13
  23.9 1.0 %slice_bitcast_fusion.14 = (bf16[1,1,512,128]{3,2,1,0:T(8,128)(2,1)S(1)}, bf16[1,1,512,128]{3,2,1,0:T(8,128)(2,1)S(1)}, bf16[1,1,512,128]{3,2,1,0:T(8,128)(2,1)S(1)}, bf16[1,1,512,128]{3,2,1,0:T(8,128)(2,1)S(1)}) fusion(bf16[4,512,128]{2,1,0:T(8,128)(2,1)S(1)} %copy-done.1, bf16[4,512,128]{2,1,0:T(8,128)(2,1)} %collective-permute-done.refs_1_.refs_0_), kind=kLoop, calls=%fused_computation.36 | loop fusion | bytes 1048576 | tf_op jit(solution)/shard_map/stack | solution.py:120
  24.9 2.2 %collective-permute-start.3 = (bf16[3,1,512,128]{3,2,1,0:T(8,128)(2,1)S(1)}, bf16[3,1,512,128]{3,2,1,0:T(8,128)(2,1)S(1)}, u32[]{:S(2)}, u32[]{:S(2)}) collective-permute-start(bf16[3,1,512,128]{3,2,1,0:T(8,128)(2,1)S(1)} %pad_maximum_fusion.2), channel_id=1, source_target_pairs={{1,0},{2,1},{3,2},{5,4},{6,5},{7,6},{9,8},{10,9},{11,10},{13,12},{... | collective-permute-start | bytes 1179656 | tf_op jit(solution)/shard_map/ppermute | solution.py:120
  27.2 3.4 %collective-permute-start.2 = (bf16[3,1,512,128]{3,2,1,0:T(8,128)(2,1)S(1)}, bf16[3,1,512,128]{3,2,1,0:T(8,128)(2,1)S(1)}, u32[]{:S(2)}, u32[]{:S(2)}) collective-permute-start(bf16[3,1,512,128]{3,2,1,0:T(8,128)(2,1)S(1)} %pad_maximum_fusion.1), channel_id=1, source_target_pairs={{0,1},{1,2},{2,3},{4,5},{5,6},{6,7},{8,9},{9,10},{10,11},{12,13},{... | collective-permute-start | bytes 1179656 | tf_op jit(solution)/shard_map/ppermute | solution.py:119
  30.6 0.0 collective-permute-done.7
  30.6 1.1 %broadcast_select_fusion.3 = (bf16[576,384]{1,0:T(8,128)(2,1)S(1)}, bf16[576,384]{1,0:T(8,128)(2,1)S(1)}) fusion(bf16[576,384]{1,0:T(8,128)(2,1)} %collective-permute-done.6, bf16[576,384]{1,0:T(8,128)(2,1)S(1)} %collective-permute-done.7, pred[]{:T(512)S(6)} %eq.11), kind=kLoop, calls=%fused_computation.19 | loop fusion | flops 442368 | bytes 1769473 | tf_op jit(solution)/shard_map/jit(_where)/select_n | solution.py:141
  31.7 1.5 %broadcast_select_fusion = (bf16[1152,384]{1,0:T(8,128)(2,1)}, bf16[1152,384]{1,0:T(8,128)(2,1)}) fusion(pred[]{:T(512)S(6)} %eq.10, bf16[576,384]{1,0:T(8,128)(2,1)S(1)} %get-tuple-element.28, bf16[576,384]{1,0:T(8,128)(2,1)S(1)} %get-tuple-element.27, bf16[144,8,3,128]{3,2,1,0:T(4,128)(2,1)S(1)} %bitcast.51), kind=kLoop, calls=%fused_computation.14 | loop fusion | flops 2654208 | bytes 3538945 | tf_op jit(solution)/shard_map/jit(_where)/select_n | solution.py:145
  33.2 0.8 collective-permute-done.3.refs_4_
  34.0 1.2 %collective-permute-done.2.refs_3_ = bf16[3,1,512,128]{3,2,1,0:T(8,128)(2,1)S(1)} collective-permute-done((bf16[3,1,512,128]{3,2,1,0:T(8,128)(2,1)S(1)}, bf16[3,1,512,128]{3,2,1,0:T(8,128)(2,1)S(1)}, u32[]{:S(2)}, u32[]{:S(2)}) %collective-permute-start.2) | collective-permute-done | bytes 393248 | tf_op jit(solution)/shard_map/ppermute | solution.py:119
  35.3 0.0 copy-done.6
  35.3 0.7 copy-done.7
  36.0 5.8 %shard_map.29 = (bf16[4,512,128]{2,1,0:T(8,128)(2,1)}, bf16[4,512,128]{2,1,0:T(8,128)(2,1)}) custom-call(bf16[4,512,128]{2,1,0:T(8,128)(2,1)} %collective-permute-done.refs_1_.refs_0_, bf16[4,512,128]{2,1,0:T(8,128)(2,1)} %get-tuple-element.13.refs_2_.refs_1_, bf16[4,512,128]{2,1,0:T(8,128)(2,1)} %get-tuple-element.25.refs_2_, ...), custom_call_target="tpu_custom_call" | custom-call | flops 1811939328 | bytes 4816896 | tf_op jit(solution)/shard_map/pallas_call | solution.py:92
  41.9 3.2 %collective-permute-start.8 = (bf16[4,512,128]{2,1,0:T(8,128)(2,1)}, bf16[4,512,128]{2,1,0:T(8,128)(2,1)S(1)}, u32[]{:S(2)}, u32[]{:S(2)}) collective-permute-start(bf16[4,512,128]{2,1,0:T(8,128)(2,1)} %get-tuple-element.16.a1_ref), channel_id=1, source_target_pairs={{0,4},{4,8},{8,12},{1,5},{5,9},{9,13},{2,6},{6,10},{10,14},{3,7},{... | collective-permute-start | bytes 1572872 | tf_op jit(solution)/shard_map/ppermute | solution.py:13
  45.1 0.0 collective-permute-done.1.refs_0_
  45.1 0.0 copy-start.4
  45.1 4.7 %collective-permute-start.4 = (bf16[1,1,512,128]{3,2,1,0:T(8,128)(2,1)S(1)}, bf16[1,1,512,128]{3,2,1,0:T(8,128)(2,1)S(1)}, u32[]{:S(2)}, u32[]{:S(2)}) collective-permute-start(bf16[1,1,512,128]{3,2,1,0:T(8,128)(2,1)S(1)} %get-tuple-element.38), channel_id=1, source_target_pairs={{0,1},{1,2},{2,3},{4,5},{5,6},{6,7},{8,9},{9,10},{10,11},{12,13},{... | collective-permute-start | bytes 393224 | tf_op jit(solution)/shard_map/ppermute | solution.py:126
  49.8 1.9 %collective-permute-start.5 = (bf16[1,1,512,128]{3,2,1,0:T(8,128)(2,1)S(1)}, bf16[1,1,512,128]{3,2,1,0:T(8,128)(2,1)S(1)}, u32[]{:S(2)}, u32[]{:S(2)}) collective-permute-start(bf16[1,1,512,128]{3,2,1,0:T(8,128)(2,1)S(1)} %get-tuple-element.37), channel_id=1, source_target_pairs={{1,0},{2,1},{3,2},{5,4},{6,5},{7,6},{9,8},{10,9},{11,10},{13,12},{... | collective-permute-start | bytes 393224 | tf_op jit(solution)/shard_map/ppermute | solution.py:127
  51.7 1.0 %slice_bitcast_fusion.8 = (bf16[1,1,512,128]{3,2,1,0:T(8,128)(2,1)S(1)}, bf16[1,1,512,128]{3,2,1,0:T(8,128)(2,1)S(1)}) fusion(bf16[4,512,128]{2,1,0:T(8,128)(2,1)} %get-tuple-element.16.a1_ref), kind=kLoop, calls=%fused_computation.30 | loop fusion | bytes 524288 | tf_op jit(solution)/shard_map/stack | solution.py:120
  52.7 0.0 collective-permute-done.4.refs_5_
  52.7 0.0 copy-start.12
  52.7 3.3 %collective-permute-done.5.refs_6_ = bf16[1,1,512,128]{3,2,1,0:T(8,128)(2,1)S(1)} collective-permute-done((bf16[1,1,512,128]{3,2,1,0:T(8,128)(2,1)S(1)}, bf16[1,1,512,128]{3,2,1,0:T(8,128)(2,1)S(1)}, u32[]{:S(2)}, u32[]{:S(2)}) %collective-permute-start.5) | collective-permute-done | bytes 131104 | tf_op jit(solution)/shard_map/ppermute | solution.py:127
  56.1 0.0 copy-done.4
  56.1 0.0 copy-done.12
  56.1 0.6 copy-done.13
  56.7 5.9 %shard_map.28 = (bf16[4,512,128]{2,1,0:T(8,128)(2,1)}, bf16[4,512,128]{2,1,0:T(8,128)(2,1)}) custom-call(bf16[4,512,128]{2,1,0:T(8,128)(2,1)} %copy-done.4, bf16[4,512,128]{2,1,0:T(8,128)(2,1)} %collective-permute-done.refs_1_.refs_0_, bf16[4,512,128]{2,1,0:T(8,128)(2,1)} %get-tuple-element.13.refs_2_.refs_1_, bf16[3,1,512,128]{3,2,1,0:T(8,128)(2,1)} %copy-done.7, ...), custom_call_target="tpu_custom_call" | custom-call | flops 1811939328 | bytes 5079040 | tf_op jit(solution)/shard_map/pallas_call | solution.py:92
  62.7 0.0 collective-permute-done.8.c1_ref
  62.7 2.4 %collective-permute-start.9 = (bf16[4,512,128]{2,1,0:T(8,128)(2,1)}, bf16[4,512,128]{2,1,0:T(8,128)(2,1)S(1)}, u32[]{:S(2)}, u32[]{:S(2)}) collective-permute-start(bf16[4,512,128]{2,1,0:T(8,128)(2,1)} %get-tuple-element.17.a0_ref), channel_id=1, source_target_pairs={{0,4},{4,8},{8,12},{1,5},{5,9},{9,13},{2,6},{6,10},{10,14},{3,7},{... | collective-permute-start | bytes 1572872 | tf_op jit(solution)/shard_map/ppermute | solution.py:13
  65.1 1.0 %slice_bitcast_fusion.9 = (bf16[1,1,512,128]{3,2,1,0:T(8,128)(2,1)S(1)}, bf16[1,1,512,128]{3,2,1,0:T(8,128)(2,1)S(1)}) fusion(bf16[4,512,128]{2,1,0:T(8,128)(2,1)} %get-tuple-element.17.a0_ref), kind=kLoop, calls=%fused_computation.31 | loop fusion | bytes 524288 | tf_op jit(solution)/shard_map/stack | solution.py:120
  66.2 1.9 %collective-permute-start.11 = (bf16[3,1,512,128]{3,2,1,0:T(8,128)(2,1)S(1)}, bf16[3,1,512,128]{3,2,1,0:T(8,128)(2,1)S(1)}, u32[]{:S(2)}, u32[]{:S(2)}) collective-permute-start(bf16[3,1,512,128]{3,2,1,0:T(8,128)(2,1)S(1)} %pad_maximum_fusion.4), channel_id=1, source_target_pairs={{1,0},{2,1},{3,2},{5,4},{6,5},{7,6},{9,8},{10,9},{11,10},{13,12},{... | collective-permute-start | bytes 1179656 | tf_op jit(solution)/shard_map/ppermute | solution.py:120
  68.2 0.0 copy-done.3
  68.2 3.6 %collective-permute-start.10 = (bf16[3,1,512,128]{3,2,1,0:T(8,128)(2,1)S(1)}, bf16[3,1,512,128]{3,2,1,0:T(8,128)(2,1)S(1)}, u32[]{:S(2)}, u32[]{:S(2)}) collective-permute-start(bf16[3,1,512,128]{3,2,1,0:T(8,128)(2,1)S(1)} %pad_maximum_fusion.3), channel_id=1, source_target_pairs={{0,1},{1,2},{2,3},{4,5},{5,6},{6,7},{8,9},{9,10},{10,11},{12,13},{... | collective-permute-start | bytes 1179656 | tf_op jit(solution)/shard_map/ppermute | solution.py:119
  71.8 2.7 %collective-permute-done.9.c2_ref = bf16[4,512,128]{2,1,0:T(8,128)(2,1)S(1)} collective-permute-done((bf16[4,512,128]{2,1,0:T(8,128)(2,1)}, bf16[4,512,128]{2,1,0:T(8,128)(2,1)S(1)}, u32[]{:S(2)}, u32[]{:S(2)}) %collective-permute-start.9) | collective-permute-done | bytes 524320 | tf_op jit(solution)/shard_map/ppermute | solution.py:13
  74.6 1.9 %collective-permute-start.12 = (bf16[1,1,512,128]{3,2,1,0:T(8,128)(2,1)S(1)}, bf16[1,1,512,128]{3,2,1,0:T(8,128)(2,1)S(1)}, u32[]{:S(2)}, u32[]{:S(2)}) collective-permute-start(bf16[1,1,512,128]{3,2,1,0:T(8,128)(2,1)S(1)} %get-tuple-element.30), channel_id=1, source_target_pairs={{0,1},{1,2},{2,3},{4,5},{5,6},{6,7},{8,9},{9,10},{10,11},{12,13},{... | collective-permute-start | bytes 393224 | tf_op jit(solution)/shard_map/ppermute | solution.py:122
  76.5 2.6 %collective-permute-start.13 = (bf16[1,1,512,128]{3,2,1,0:T(8,128)(2,1)S(1)}, bf16[1,1,512,128]{3,2,1,0:T(8,128)(2,1)S(1)}, u32[]{:S(2)}, u32[]{:S(2)}) collective-permute-start(bf16[1,1,512,128]{3,2,1,0:T(8,128)(2,1)S(1)} %get-tuple-element.29), channel_id=1, source_target_pairs={{1,0},{2,1},{3,2},{5,4},{6,5},{7,6},{9,8},{10,9},{11,10},{13,12},{... | collective-permute-start | bytes 393224 | tf_op jit(solution)/shard_map/ppermute | solution.py:123
  79.1 0.0 collective-permute-done.11.bot_a
  79.1 0.0 copy-start.8
  79.1 0.0 collective-permute-done.10.top_a
  79.1 0.0 copy-start.9
  79.1 0.0 collective-permute-done.12.top_b
  79.1 0.0 copy-start.10
  79.1 3.6 %collective-permute-done.13.bot_b = bf16[1,1,512,128]{3,2,1,0:T(8,128)(2,1)S(1)} collective-permute-done((bf16[1,1,512,128]{3,2,1,0:T(8,128)(2,1)S(1)}, bf16[1,1,512,128]{3,2,1,0:T(8,128)(2,1)S(1)}, u32[]{:S(2)}, u32[]{:S(2)}) %collective-permute-start.13) | collective-permute-done | bytes 131104 | tf_op jit(solution)/shard_map/ppermute | solution.py:123
  82.8 0.0 copy-done.5
  82.8 0.0 copy-done.8
  82.8 0.0 copy-done.9
  82.8 0.0 copy-done.10
  82.8 0.7 copy-done.11
  83.5 8.7 %shard_map.30 = bf16[2,4,512,128]{3,2,1,0:T(8,128)(2,1)} custom-call(bf16[4,512,128]{2,1,0:T(8,128)(2,1)} %copy-done.5, bf16[4,512,128]{2,1,0:T(8,128)(2,1)} %copy-done.3, bf16[4,512,128]{2,1,0:T(8,128)(2,1)} %get-tuple-element.17.a0_ref, bf16[4,512,128]{2,1,0:T(8,128)(2,1)} %get-tuple-element.16.a1_ref, bf16[3,1,512,128]{3,2,1,0:T(8,128)(2,1)} %copy-done.9, ...), custom_call_target="tpu_custom_call" | custom-call | flops 3623878656 | bytes 6127616 | tf_op jit(solution)/shard_map/pallas_call | solution.py:103
  (13 shorter events, 0.3 us)
Async XLA Ops:
  0.0 7.6 %copy-start.2 = (bf16[1,9,384,128]{3,2,1,0:T(8,128)(2,1)S(1)}, bf16[1,9,384,128]{3,2,1,0:T(8,128)(2,1)}, u32[]{:S(2)}) copy-start(bf16[1,9,384,128]{3,2,1,0:T(8,128)(2,1)} %param.3) | copy-start | bytes 2654212
  2.8 18.6 %collective-permute-start = (bf16[4,512,128]{2,1,0:T(8,128)(2,1)}, bf16[4,512,128]{2,1,0:T(8,128)(2,1)}, u32[]{:S(2)}, u32[]{:S(2)}) collective-permute-start(bf16[4,512,128]{2,1,0:T(8,128)(2,1)} %get-tuple-element.25.refs_2_), channel_id=1, source_target_pairs={{0,4},{4,8},{8,12},{1,5},{5,9},{9,13},{2,6},{6,10},{10,14},{3,7},{... | collective-permute-start | bytes 1572872 | tf_op jit(solution)/shard_map/ppermute | solution.py:13
  8.6 2.3 %copy-start = (bf16[1,2,4,512,128]{4,3,2,1,0:T(8,128)(2,1)S(1)}, bf16[1,2,4,512,128]{4,3,2,1,0:T(8,128)(2,1)}, u32[]{:S(2)}) copy-start(bf16[1,2,4,512,128]{4,3,2,1,0:T(8,128)(2,1)} %param.2) | copy-start | bytes 3145732
  8.6 10.9 %collective-permute-start.6 = (bf16[576,384]{1,0:T(8,128)(2,1)S(1)}, bf16[576,384]{1,0:T(8,128)(2,1)}, u32[]{:S(2)}, u32[]{:S(2)}) collective-permute-start(bf16[576,384]{1,0:T(8,128)(2,1)S(1)} %constant_dynamic-slice_fusion), channel_id=1, source_target_pairs={{0,16},{16,0},{1,17},{17,1},{2,18},{18,2},{3,19},{19,3},{4,20},{20... | collective-permute-start | bytes 1327112 | tf_op jit(solution)/shard_map/ppermute | solution.py:139
  10.9 10.5 %copy-start.1 = (bf16[4,512,128]{2,1,0:T(8,128)(2,1)S(1)}, bf16[4,512,128]{2,1,0:T(8,128)(2,1)}, u32[]{:S(2)}) copy-start(bf16[4,512,128]{2,1,0:T(8,128)(2,1)} %get-tuple-element.13.refs_2_.refs_1_) | copy-start | bytes 1572868
  19.5 11.0 %collective-permute-start.7 = (bf16[576,384]{1,0:T(8,128)(2,1)}, bf16[576,384]{1,0:T(8,128)(2,1)S(1)}, u32[]{:S(2)}, u32[]{:S(2)}) collective-permute-start(bf16[576,384]{1,0:T(8,128)(2,1)} %collective-permute-done.6), channel_id=1, source_target_pairs={{0,1},{1,0},{2,3},{3,2},{4,5},{5,4},{6,7},{7,6},{8,9},{9,8},{10,11... | collective-permute-start | bytes 1327112 | tf_op jit(solution)/shard_map/ppermute | solution.py:140
  21.4 23.7 %collective-permute-start.1 = (bf16[4,512,128]{2,1,0:T(8,128)(2,1)S(1)}, bf16[4,512,128]{2,1,0:T(8,128)(2,1)S(1)}, u32[]{:S(2)}, u32[]{:S(2)}) collective-permute-start(bf16[4,512,128]{2,1,0:T(8,128)(2,1)S(1)} %copy-done.1), channel_id=1, source_target_pairs={{0,4},{4,8},{8,12},{1,5},{5,9},{9,13},{2,6},{6,10},{10,14},{3,7},{... | collective-permute-start | bytes 1572872 | tf_op jit(solution)/shard_map/ppermute | solution.py:13
  24.9 9.1 %collective-permute-start.3 = (bf16[3,1,512,128]{3,2,1,0:T(8,128)(2,1)S(1)}, bf16[3,1,512,128]{3,2,1,0:T(8,128)(2,1)S(1)}, u32[]{:S(2)}, u32[]{:S(2)}) collective-permute-start(bf16[3,1,512,128]{3,2,1,0:T(8,128)(2,1)S(1)} %pad_maximum_fusion.2), channel_id=1, source_target_pairs={{1,0},{2,1},{3,2},{5,4},{6,5},{7,6},{9,8},{10,9},{11,10},{13,12},{... | collective-permute-start | bytes 1179656 | tf_op jit(solution)/shard_map/ppermute | solution.py:120
  27.2 8.1 %collective-permute-start.2 = (bf16[3,1,512,128]{3,2,1,0:T(8,128)(2,1)S(1)}, bf16[3,1,512,128]{3,2,1,0:T(8,128)(2,1)S(1)}, u32[]{:S(2)}, u32[]{:S(2)}) collective-permute-start(bf16[3,1,512,128]{3,2,1,0:T(8,128)(2,1)S(1)} %pad_maximum_fusion.1), channel_id=1, source_target_pairs={{0,1},{1,2},{2,3},{4,5},{5,6},{6,7},{8,9},{9,10},{10,11},{12,13},{... | collective-permute-start | bytes 1179656 | tf_op jit(solution)/shard_map/ppermute | solution.py:119
  34.0 1.2 %copy-start.6 = (bf16[3,1,512,128]{3,2,1,0:T(8,128)(2,1)}, bf16[3,1,512,128]{3,2,1,0:T(8,128)(2,1)S(1)}, u32[]{:S(2)}) copy-start(bf16[3,1,512,128]{3,2,1,0:T(8,128)(2,1)S(1)} %collective-permute-done.3.refs_4_) | copy-start | bytes 1179652
  35.3 0.7 copy-start.7
  41.9 20.8 %collective-permute-start.8 = (bf16[4,512,128]{2,1,0:T(8,128)(2,1)}, bf16[4,512,128]{2,1,0:T(8,128)(2,1)S(1)}, u32[]{:S(2)}, u32[]{:S(2)}) collective-permute-start(bf16[4,512,128]{2,1,0:T(8,128)(2,1)} %get-tuple-element.16.a1_ref), channel_id=1, source_target_pairs={{0,4},{4,8},{8,12},{1,5},{5,9},{9,13},{2,6},{6,10},{10,14},{3,7},{... | collective-permute-start | bytes 1572872 | tf_op jit(solution)/shard_map/ppermute | solution.py:13
  45.1 11.0 %copy-start.4 = (bf16[4,512,128]{2,1,0:T(8,128)(2,1)}, bf16[4,512,128]{2,1,0:T(8,128)(2,1)S(1)}, u32[]{:S(2)}) copy-start(bf16[4,512,128]{2,1,0:T(8,128)(2,1)S(1)} %collective-permute-done.1.refs_0_) | copy-start | bytes 1572868
  45.1 7.6 %collective-permute-start.4 = (bf16[1,1,512,128]{3,2,1,0:T(8,128)(2,1)S(1)}, bf16[1,1,512,128]{3,2,1,0:T(8,128)(2,1)S(1)}, u32[]{:S(2)}, u32[]{:S(2)}) collective-permute-start(bf16[1,1,512,128]{3,2,1,0:T(8,128)(2,1)S(1)} %get-tuple-element.38), channel_id=1, source_target_pairs={{0,1},{1,2},{2,3},{4,5},{5,6},{6,7},{8,9},{9,10},{10,11},{12,13},{... | collective-permute-start | bytes 393224 | tf_op jit(solution)/shard_map/ppermute | solution.py:126
  49.8 6.3 %collective-permute-start.5 = (bf16[1,1,512,128]{3,2,1,0:T(8,128)(2,1)S(1)}, bf16[1,1,512,128]{3,2,1,0:T(8,128)(2,1)S(1)}, u32[]{:S(2)}, u32[]{:S(2)}) collective-permute-start(bf16[1,1,512,128]{3,2,1,0:T(8,128)(2,1)S(1)} %get-tuple-element.37), channel_id=1, source_target_pairs={{1,0},{2,1},{3,2},{5,4},{6,5},{7,6},{9,8},{10,9},{11,10},{13,12},{... | collective-permute-start | bytes 393224 | tf_op jit(solution)/shard_map/ppermute | solution.py:127
  52.7 3.4 %copy-start.12 = (bf16[1,1,512,128]{3,2,1,0:T(8,128)(2,1)}, bf16[1,1,512,128]{3,2,1,0:T(8,128)(2,1)S(1)}, u32[]{:S(2)}) copy-start(bf16[1,1,512,128]{3,2,1,0:T(8,128)(2,1)S(1)} %collective-permute-done.4.refs_5_) | copy-start | bytes 393220
  56.1 0.7 copy-start.13
  62.7 5.5 %copy-start.3 = (bf16[4,512,128]{2,1,0:T(8,128)(2,1)}, bf16[4,512,128]{2,1,0:T(8,128)(2,1)S(1)}, u32[]{:S(2)}) copy-start(bf16[4,512,128]{2,1,0:T(8,128)(2,1)S(1)} %collective-permute-done.8.c1_ref) | copy-start | bytes 1572868
  62.7 11.9 %collective-permute-start.9 = (bf16[4,512,128]{2,1,0:T(8,128)(2,1)}, bf16[4,512,128]{2,1,0:T(8,128)(2,1)S(1)}, u32[]{:S(2)}, u32[]{:S(2)}) collective-permute-start(bf16[4,512,128]{2,1,0:T(8,128)(2,1)} %get-tuple-element.17.a0_ref), channel_id=1, source_target_pairs={{0,4},{4,8},{8,12},{1,5},{5,9},{9,13},{2,6},{6,10},{10,14},{3,7},{... | collective-permute-start | bytes 1572872 | tf_op jit(solution)/shard_map/ppermute | solution.py:13
  66.2 12.9 %collective-permute-start.11 = (bf16[3,1,512,128]{3,2,1,0:T(8,128)(2,1)S(1)}, bf16[3,1,512,128]{3,2,1,0:T(8,128)(2,1)S(1)}, u32[]{:S(2)}, u32[]{:S(2)}) collective-permute-start(bf16[3,1,512,128]{3,2,1,0:T(8,128)(2,1)S(1)} %pad_maximum_fusion.4), channel_id=1, source_target_pairs={{1,0},{2,1},{3,2},{5,4},{6,5},{7,6},{9,8},{10,9},{11,10},{13,12},{... | collective-permute-start | bytes 1179656 | tf_op jit(solution)/shard_map/ppermute | solution.py:120
  68.2 10.9 %collective-permute-start.10 = (bf16[3,1,512,128]{3,2,1,0:T(8,128)(2,1)S(1)}, bf16[3,1,512,128]{3,2,1,0:T(8,128)(2,1)S(1)}, u32[]{:S(2)}, u32[]{:S(2)}) collective-permute-start(bf16[3,1,512,128]{3,2,1,0:T(8,128)(2,1)S(1)} %pad_maximum_fusion.3), channel_id=1, source_target_pairs={{0,1},{1,2},{2,3},{4,5},{5,6},{6,7},{8,9},{9,10},{10,11},{12,13},{... | collective-permute-start | bytes 1179656 | tf_op jit(solution)/shard_map/ppermute | solution.py:119
  74.5 8.2 %copy-start.5 = (bf16[4,512,128]{2,1,0:T(8,128)(2,1)}, bf16[4,512,128]{2,1,0:T(8,128)(2,1)S(1)}, u32[]{:S(2)}) copy-start(bf16[4,512,128]{2,1,0:T(8,128)(2,1)S(1)} %collective-permute-done.9.c2_ref) | copy-start | bytes 1572868
  74.6 4.6 %collective-permute-start.12 = (bf16[1,1,512,128]{3,2,1,0:T(8,128)(2,1)S(1)}, bf16[1,1,512,128]{3,2,1,0:T(8,128)(2,1)S(1)}, u32[]{:S(2)}, u32[]{:S(2)}) collective-permute-start(bf16[1,1,512,128]{3,2,1,0:T(8,128)(2,1)S(1)} %get-tuple-element.30), channel_id=1, source_target_pairs={{0,1},{1,2},{2,3},{4,5},{5,6},{6,7},{8,9},{9,10},{10,11},{12,13},{... | collective-permute-start | bytes 393224 | tf_op jit(solution)/shard_map/ppermute | solution.py:122
  76.5 6.3 %collective-permute-start.13 = (bf16[1,1,512,128]{3,2,1,0:T(8,128)(2,1)S(1)}, bf16[1,1,512,128]{3,2,1,0:T(8,128)(2,1)S(1)}, u32[]{:S(2)}, u32[]{:S(2)}) collective-permute-start(bf16[1,1,512,128]{3,2,1,0:T(8,128)(2,1)S(1)} %get-tuple-element.29), channel_id=1, source_target_pairs={{1,0},{2,1},{3,2},{5,4},{6,5},{7,6},{9,8},{10,9},{11,10},{13,12},{... | collective-permute-start | bytes 393224 | tf_op jit(solution)/shard_map/ppermute | solution.py:123
  79.1 3.7 %copy-start.8 = (bf16[3,1,512,128]{3,2,1,0:T(8,128)(2,1)}, bf16[3,1,512,128]{3,2,1,0:T(8,128)(2,1)S(1)}, u32[]{:S(2)}) copy-start(bf16[3,1,512,128]{3,2,1,0:T(8,128)(2,1)S(1)} %collective-permute-done.11.bot_a) | copy-start | bytes 1179652
  79.1 3.7 %copy-start.9 = (bf16[3,1,512,128]{3,2,1,0:T(8,128)(2,1)}, bf16[3,1,512,128]{3,2,1,0:T(8,128)(2,1)S(1)}, u32[]{:S(2)}) copy-start(bf16[3,1,512,128]{3,2,1,0:T(8,128)(2,1)S(1)} %collective-permute-done.10.top_a) | copy-start | bytes 1179652
  79.1 3.7 %copy-start.10 = (bf16[1,1,512,128]{3,2,1,0:T(8,128)(2,1)}, bf16[1,1,512,128]{3,2,1,0:T(8,128)(2,1)S(1)}, u32[]{:S(2)}) copy-start(bf16[1,1,512,128]{3,2,1,0:T(8,128)(2,1)S(1)} %collective-permute-done.12.top_b) | copy-start | bytes 393220
  82.8 0.7 copy-start.11

commit v11 on v10

--- a/solution.py
+++ b/solution.py
@@ -65,9 +65,10 @@
     conv_rows(sources, base_ref, w_ref, store)
 
 
-def pair_kernel(c2_ref, c1_ref, a0_ref, a1_ref, top_a, bot_a, top_b, bot_b, x0_ref, x1_ref, w_ref, out_ref):
+def pair_kernel(c2_ref, c1_ref, a0_ref, a1_ref, top, bottom, x0_ref, x1_ref, w_ref, out_ref):
+    frames = [c2_ref, c1_ref, a0_ref, a1_ref]
     for t, base_ref in ((1, x1_ref), (0, x0_ref)):
-        sources = frame_sources(t, c2_ref, c1_ref, a0_ref, a1_ref, top_a, bot_a, top_b, bot_b)
+        sources = [(frames[t + a], top, bottom, t + a) for a in range(3)]
 
         def store(h, value, t=t):
             out_ref[t, h] = value.astype(out_ref.dtype)
@@ -116,12 +117,12 @@
     c1 = shift_tm(a1)
     a0, c1 = lax.optimization_barrier((a0, c1))
     c2 = shift_tm(a0)
+    if merge:
+        top = lax.ppermute(jnp.stack([c2[-1:], c1[-1:], a0[-1:], a1[-1:]]), "space", down)
+        bottom = lax.ppermute(jnp.stack([c2[:1], c1[:1], a0[:1], a1[:1]]), "space", up)
+        return pair_conv((c2, c1, a0, a1, top, bottom), x0, x1, w_mat)
     top_a = lax.ppermute(jnp.stack([c1[-1:], a0[-1:], a1[-1:]]), "space", down)
     bot_a = lax.ppermute(jnp.stack([c1[:1], a0[:1], a1[:1]]), "space", up)
-    if merge:
-        top_b = lax.ppermute(c2[None, -1:], "space", down)
-        bot_b = lax.ppermute(c2[None, :1], "space", up)
-        return pair_conv((c2, c1, a0, a1, top_a, bot_a, top_b, bot_b), x0, x1, w_mat)
     outs1 = frame_conv(1, (c1, a0, a1, top_a, bot_a), x1, w_mat, with_act)
     top_b = lax.ppermute(c2[None, -1:], "space", down)
     bot_b = lax.ppermute(c2[None, :1], "space", up)

time: 92.8 us -> 96.8 us (1.043)
  waiting for transfers between devices: 19.3 us -> 28.3 us
  starting transfers between devices: 38.3 us -> 33.9 us
    ppermute x0 -> x2, waiting for transfers between devices: none -> 5.92 us  [the longest x1 4.65 us: conv_block(): lax.ppermute(jnp.stack([c2[:1], c1[:1], a0[:1], a1[:1]]), 'space', up)]
    ppermute x0 -> x2, starting transfers between devices: none -> 5.74 us  [the longest x1 3.82 us: conv_block(): lax.ppermute(jnp.stack([c2[-1:], c1[-1:], a0[-1:], a1[-1:]]), 'space', down)]
    ppermute x4, waiting for transfers between devices: 2.73 us -> 8.39 us  [shift_tm(): return lax.ppermute(x, 'tm', [(i, i + 1) for i in range(n - 1)])]
    ppermute x2 -> x1, starting transfers between devices: 7 us -> 3.36 us  [conv_block(): top_a = lax.ppermute(jnp.stack([c1[-1:], a0[-1:], a1[-1:]]), 'space', down)]
    ppermute x2 -> x1, waiting for transfers between devices: 6.97 us -> 4.34 us  [conv_block(): bot_b = lax.ppermute(c2[None, :1], 'space', up)]
    ppermute x2 -> x1, starting transfers between devices: 4.51 us -> 1.92 us  [conv_block(): bot_b = lax.ppermute(c2[None, :1], 'space', up)]
    another operation x5 -> x2, local copies, waits for them, and re-layouts: 3.98 us -> 1.99 us  [conv_block(): bot_a = lax.ppermute(jnp.stack([c1[:1], a0[:1], a1[:1]]), 'space', up)]
    ppermute x2 -> x1, starting transfers between devices: 4.13 us -> 2.2 us  [conv_block(): bot_a = lax.ppermute(jnp.stack([c1[:1], a0[:1], a1[:1]]), 'space', up)]
  transfers between devices with their start and end apart: 14 -> 12, of which waited for: 6 -> 7; matrix products, arithmetic and copies ran while one was open for 10% -> 8% of each run, Pallas kernels for 13% -> 12%
where the time goes in v11:
time: 96.8 us; the launch traced here: 96 us
  starting transfers between devices  33.9 us (35%)
  waiting for transfers between devices  28.3 us (29%)
  Pallas kernels  20.5 us (21%)
  local copies, waits for them, and re-layouts  7.3 us (8%)
  other arithmetic  5.67 us (6%)
    ppermute x4, starting transfers between devices, shift_tm(): return lax.ppermute(x, 'tm', [(i, i + 1) for i in range(n - 1)])  12.9 us
    pallas_call x2, Pallas kernels, frame_conv(): pl.pallas_call(functools.partial(frame_kernel, t, with_act), out_shape=(s...  11.8 us
    pallas_call x1, Pallas kernels, pair_conv(): pl.pallas_call(pair_kernel, out_shape=jax.ShapeDtypeStruct((2,) + x0.shap...  8.73 us
    ppermute x4, waiting for transfers between devices, shift_tm(): return lax.ppermute(x, 'tm', [(i, i + 1) for i in range(n - 1)])  8.39 us
    ppermute x1, waiting for transfers between devices, both_taps(): got = lax.ppermute(mine, 'section', [(0, 1), (1, 0)])  7.57 us
    ppermute x1, starting transfers between devices, conv_block(): top_b = lax.ppermute(c2[None, -1:], 'space', down)  4.67 us
    ppermute x1, waiting for transfers between devices, conv_block(): lax.ppermute(jnp.stack([c2[:1], c1[:1], a0[:1], a1[:1]]), 'space', up)  4.65 us
    ppermute x1, waiting for transfers between devices, conv_block(): bot_b = lax.ppermute(c2[None, :1], 'space', up)  4.34 us
  transfers between devices with their start and end apart: 12, of which 7 were waited for; matrix products, arithmetic and copies ran while one was open for 8% of the time, Pallas kernels for 12%

profile of v11, /device:TPU:1, one launch (start us, length us, event | category | flops | bytes accessed | tf_op | source)
XLA Modules:
  0.0 96.0 jit_solution(15659613239620089497)
XLA Ops:
  0.0 0.0 copy-start.2
  0.0 2.8 %fusion.7 = (bf16[4,512,128]{2,1,0:T(8,128)(2,1)}, bf16[4,512,128]{2,1,0:T(8,128)(2,1)}) fusion(bf16[1,2,4,512,128]{4,3,2,1,0:T(8,128)(2,1)} %param.2), kind=kLoop, calls=%fused_computation.11 | loop fusion | flops 3145728 | bytes 2097152 | tf_op jit(solution)/shard_map/convert_element_type | solution.py:17
  2.8 4.8 %collective-permute-start = (bf16[4,512,128]{2,1,0:T(8,128)(2,1)}, bf16[4,512,128]{2,1,0:T(8,128)(2,1)}, u32[]{:S(2)}, u32[]{:S(2)}) collective-permute-start(bf16[4,512,128]{2,1,0:T(8,128)(2,1)} %get-tuple-element.25.refs_2_), channel_id=1, source_target_pairs={{0,4},{4,8},{8,12},{1,5},{5,9},{9,13},{2,6},{6,10},{10,14},{3,7},{... | collective-permute-start | bytes 1572872 | tf_op jit(solution)/shard_map/ppermute | solution.py:13
  7.6 0.0 copy-done.2
  7.6 0.8 copy.4
  8.4 0.1 copy.9
  8.5 0.0 copy-start
  8.6 0.1 constant_dynamic-slice_fusion
  8.6 1.3 %collective-permute-start.6 = (bf16[576,384]{1,0:T(8,128)(2,1)S(1)}, bf16[576,384]{1,0:T(8,128)(2,1)}, u32[]{:S(2)}, u32[]{:S(2)}) collective-permute-start(bf16[576,384]{1,0:T(8,128)(2,1)S(1)} %constant_dynamic-slice_fusion), channel_id=1, source_target_pairs={{0,16},{16,0},{1,17},{17,1},{2,18},{18,2},{3,19},{19,3},{4,20},{20... | collective-permute-start | bytes 1327112 | tf_op jit(solution)/shard_map/ppermute | solution.py:140
  9.9 1.0 %slice_bitcast_fusion.6 = (bf16[1,1,512,128]{3,2,1,0:T(8,128)(2,1)S(1)}, bf16[1,1,512,128]{3,2,1,0:T(8,128)(2,1)S(1)}) fusion(bf16[4,512,128]{2,1,0:T(8,128)(2,1)} %get-tuple-element.25.refs_2_), kind=kLoop, calls=%fused_computation.28 | loop fusion | bytes 524288 | tf_op jit(solution)/shard_map/stack | solution.py:125
  10.9 0.0 copy-done
  10.9 0.0 copy-start.1
  10.9 1.0 %slice_bitcast_fusion = (bf16[4,512,128]{2,1,0:T(8,128)(2,1)}, bf16[4,512,128]{2,1,0:T(8,128)(2,1)}) fusion(bf16[1,2,4,512,128]{4,3,2,1,0:T(8,128)(2,1)S(1)} %copy-done), kind=kLoop, calls=%fused_computation.18 | loop fusion | bytes 2097152 | tf_op jit(solution)/shard_map/squeeze | solution.py:154
  11.9 7.6 %collective-permute-done.6 = bf16[576,384]{1,0:T(8,128)(2,1)} collective-permute-done((bf16[576,384]{1,0:T(8,128)(2,1)S(1)}, bf16[576,384]{1,0:T(8,128)(2,1)}, u32[]{:S(2)}, u32[]{:S(2)}) %collective-permute-start.6) | collective-permute-done | bytes 442400 | tf_op jit(solution)/shard_map/ppermute | solution.py:140
  19.5 1.9 %collective-permute-start.7 = (bf16[576,384]{1,0:T(8,128)(2,1)}, bf16[576,384]{1,0:T(8,128)(2,1)S(1)}, u32[]{:S(2)}, u32[]{:S(2)}) collective-permute-start(bf16[576,384]{1,0:T(8,128)(2,1)} %collective-permute-done.6), channel_id=1, source_target_pairs={{0,1},{1,0},{2,3},{3,2},{4,5},{5,4},{6,7},{7,6},{8,9},{9,8},{10,11... | collective-permute-start | bytes 1327112 | tf_op jit(solution)/shard_map/ppermute | solution.py:141
  21.4 0.0 collective-permute-done.refs_1_.refs_0_
  21.4 0.0 copy-done.1
  21.4 2.5 %collective-permute-start.1 = (bf16[4,512,128]{2,1,0:T(8,128)(2,1)S(1)}, bf16[4,512,128]{2,1,0:T(8,128)(2,1)S(1)}, u32[]{:S(2)}, u32[]{:S(2)}) collective-permute-start(bf16[4,512,128]{2,1,0:T(8,128)(2,1)S(1)} %copy-done.1), channel_id=1, source_target_pairs={{0,4},{4,8},{8,12},{1,5},{5,9},{9,13},{2,6},{6,10},{10,14},{3,7},{... | collective-permute-start | bytes 1572872 | tf_op jit(solution)/shard_map/ppermute | solution.py:13
  23.9 1.0 %slice_bitcast_fusion.14 = (bf16[1,1,512,128]{3,2,1,0:T(8,128)(2,1)S(1)}, bf16[1,1,512,128]{3,2,1,0:T(8,128)(2,1)S(1)}, bf16[1,1,512,128]{3,2,1,0:T(8,128)(2,1)S(1)}, bf16[1,1,512,128]{3,2,1,0:T(8,128)(2,1)S(1)}) fusion(bf16[4,512,128]{2,1,0:T(8,128)(2,1)S(1)} %copy-done.1, bf16[4,512,128]{2,1,0:T(8,128)(2,1)} %collective-permute-done.refs_1_.refs_0_), kind=kLoop, calls=%fused_computation.36 | loop fusion | bytes 1048576 | tf_op jit(solution)/shard_map/stack | solution.py:125
  24.9 2.2 %collective-permute-start.3 = (bf16[3,1,512,128]{3,2,1,0:T(8,128)(2,1)S(1)}, bf16[3,1,512,128]{3,2,1,0:T(8,128)(2,1)S(1)}, u32[]{:S(2)}, u32[]{:S(2)}) collective-permute-start(bf16[3,1,512,128]{3,2,1,0:T(8,128)(2,1)S(1)} %pad_maximum_fusion.4), channel_id=1, source_target_pairs={{1,0},{2,1},{3,2},{5,4},{6,5},{7,6},{9,8},{10,9},{11,10},{13,12},{... | collective-permute-start | bytes 1179656 | tf_op jit(solution)/shard_map/ppermute | solution.py:125
  27.2 3.4 %collective-permute-start.2 = (bf16[3,1,512,128]{3,2,1,0:T(8,128)(2,1)S(1)}, bf16[3,1,512,128]{3,2,1,0:T(8,128)(2,1)S(1)}, u32[]{:S(2)}, u32[]{:S(2)}) collective-permute-start(bf16[3,1,512,128]{3,2,1,0:T(8,128)(2,1)S(1)} %pad_maximum_fusion.3), channel_id=1, source_target_pairs={{0,1},{1,2},{2,3},{4,5},{5,6},{6,7},{8,9},{9,10},{10,11},{12,13},{... | collective-permute-start | bytes 1179656 | tf_op jit(solution)/shard_map/ppermute | solution.py:124
  30.6 0.0 collective-permute-done.7
  30.6 1.1 %broadcast_select_fusion.3 = (bf16[576,384]{1,0:T(8,128)(2,1)S(1)}, bf16[576,384]{1,0:T(8,128)(2,1)S(1)}) fusion(bf16[576,384]{1,0:T(8,128)(2,1)} %collective-permute-done.6, bf16[576,384]{1,0:T(8,128)(2,1)S(1)} %collective-permute-done.7, pred[]{:T(512)S(6)} %eq.11), kind=kLoop, calls=%fused_computation.21 | loop fusion | flops 442368 | bytes 1769473 | tf_op jit(solution)/shard_map/jit(_where)/select_n | solution.py:142
  31.7 1.5 %broadcast_select_fusion = (bf16[1152,384]{1,0:T(8,128)(2,1)}, bf16[1152,384]{1,0:T(8,128)(2,1)}) fusion(pred[]{:T(512)S(6)} %eq.10, bf16[576,384]{1,0:T(8,128)(2,1)S(1)} %get-tuple-element.28, bf16[576,384]{1,0:T(8,128)(2,1)S(1)} %get-tuple-element.27, bf16[144,8,3,128]{3,2,1,0:T(4,128)(2,1)S(1)} %bitcast.51), kind=kLoop, calls=%fused_computation.14 | loop fusion | flops 2654208 | bytes 3538945 | tf_op jit(solution)/shard_map/jit(_where)/select_n | solution.py:146
  33.2 0.8 collective-permute-done.3.refs_4_
  34.0 0.0 copy-start.9
  34.0 1.2 %collective-permute-done.2.refs_3_ = bf16[3,1,512,128]{3,2,1,0:T(8,128)(2,1)S(1)} collective-permute-done((bf16[3,1,512,128]{3,2,1,0:T(8,128)(2,1)S(1)}, bf16[3,1,512,128]{3,2,1,0:T(8,128)(2,1)S(1)}, u32[]{:S(2)}, u32[]{:S(2)}) %collective-permute-start.2) | collective-permute-done | bytes 393248 | tf_op jit(solution)/shard_map/ppermute | solution.py:124
  35.3 0.0 copy-done.9
  35.3 0.0 copy-start.10
  35.3 0.8 copy-done.10
  36.0 5.8 %shard_map.29 = (bf16[4,512,128]{2,1,0:T(8,128)(2,1)}, bf16[4,512,128]{2,1,0:T(8,128)(2,1)}) custom-call(bf16[4,512,128]{2,1,0:T(8,128)(2,1)} %collective-permute-done.refs_1_.refs_0_, bf16[4,512,128]{2,1,0:T(8,128)(2,1)} %get-tuple-element.13.refs_2_.refs_1_, bf16[4,512,128]{2,1,0:T(8,128)(2,1)} %get-tuple-element.25.refs_2_, ...), custom_call_target="tpu_custom_call" | custom-call | flops 1811939328 | bytes 4816896 | tf_op jit(solution)/shard_map/pallas_call | solution.py:93
  41.8 3.2 %collective-permute-start.8 = (bf16[4,512,128]{2,1,0:T(8,128)(2,1)}, bf16[4,512,128]{2,1,0:T(8,128)(2,1)S(1)}, u32[]{:S(2)}, u32[]{:S(2)}) collective-permute-start(bf16[4,512,128]{2,1,0:T(8,128)(2,1)} %get-tuple-element.16.a1_ref), channel_id=1, source_target_pairs={{0,4},{4,8},{8,12},{1,5},{5,9},{9,13},{2,6},{6,10},{10,14},{3,7},{... | collective-permute-start | bytes 1572872 | tf_op jit(solution)/shard_map/ppermute | solution.py:13
  45.0 0.0 collective-permute-done.1.refs_0_
  45.1 0.0 copy-start.5
  45.1 4.7 %collective-permute-start.4 = (bf16[1,1,512,128]{3,2,1,0:T(8,128)(2,1)S(1)}, bf16[1,1,512,128]{3,2,1,0:T(8,128)(2,1)S(1)}, u32[]{:S(2)}, u32[]{:S(2)}) collective-permute-start(bf16[1,1,512,128]{3,2,1,0:T(8,128)(2,1)S(1)} %get-tuple-element.38), channel_id=1, source_target_pairs={{0,1},{1,2},{2,3},{4,5},{5,6},{6,7},{8,9},{9,10},{10,11},{12,13},{... | collective-permute-start | bytes 393224 | tf_op jit(solution)/shard_map/ppermute | solution.py:127
  49.8 1.9 %collective-permute-start.5 = (bf16[1,1,512,128]{3,2,1,0:T(8,128)(2,1)S(1)}, bf16[1,1,512,128]{3,2,1,0:T(8,128)(2,1)S(1)}, u32[]{:S(2)}, u32[]{:S(2)}) collective-permute-start(bf16[1,1,512,128]{3,2,1,0:T(8,128)(2,1)S(1)} %get-tuple-element.37), channel_id=1, source_target_pairs={{1,0},{2,1},{3,2},{5,4},{6,5},{7,6},{9,8},{10,9},{11,10},{13,12},{... | collective-permute-start | bytes 393224 | tf_op jit(solution)/shard_map/ppermute | solution.py:128
  51.7 0.0 collective-permute-done.4.refs_5_
  51.7 0.0 copy-start.11
  51.7 4.3 %collective-permute-done.5.refs_6_ = bf16[1,1,512,128]{3,2,1,0:T(8,128)(2,1)S(1)} collective-permute-done((bf16[1,1,512,128]{3,2,1,0:T(8,128)(2,1)S(1)}, bf16[1,1,512,128]{3,2,1,0:T(8,128)(2,1)S(1)}, u32[]{:S(2)}, u32[]{:S(2)}) %collective-permute-start.5) | collective-permute-done | bytes 131104 | tf_op jit(solution)/shard_map/ppermute | solution.py:128
  56.1 0.0 copy-start.12
  56.1 0.0 copy-done.5
  56.1 0.0 copy-done.11
  56.1 0.6 copy-done.12
  56.7 0.0 copy-start.3
  56.7 6.0 %shard_map.28 = (bf16[4,512,128]{2,1,0:T(8,128)(2,1)}, bf16[4,512,128]{2,1,0:T(8,128)(2,1)}) custom-call(bf16[4,512,128]{2,1,0:T(8,128)(2,1)} %copy-done.5, bf16[4,512,128]{2,1,0:T(8,128)(2,1)} %collective-permute-done.refs_1_.refs_0_, bf16[4,512,128]{2,1,0:T(8,128)(2,1)} %get-tuple-element.13.refs_2_.refs_1_, bf16[3,1,512,128]{3,2,1,0:T(8,128)(2,1)} %copy-done.10, ...), custom_call_target="tpu_custom_call" | custom-call | flops 1811939328 | bytes 5079040 | tf_op jit(solution)/shard_map/pallas_call | solution.py:93
  62.7 0.0 collective-permute-done.8.c1_ref
  62.7 0.0 copy-start.4
  62.7 2.4 %collective-permute-start.9 = (bf16[4,512,128]{2,1,0:T(8,128)(2,1)}, bf16[4,512,128]{2,1,0:T(8,128)(2,1)S(1)}, u32[]{:S(2)}, u32[]{:S(2)}) collective-permute-start(bf16[4,512,128]{2,1,0:T(8,128)(2,1)} %get-tuple-element.17.a0_ref), channel_id=1, source_target_pairs={{0,4},{4,8},{8,12},{1,5},{5,9},{9,13},{2,6},{6,10},{10,14},{3,7},{... | collective-permute-start | bytes 1572872 | tf_op jit(solution)/shard_map/ppermute | solution.py:13
  65.1 0.0 copy-done.3
  65.2 1.0 %slice_bitcast_fusion.9 = (bf16[1,1,512,128]{3,2,1,0:T(8,128)(2,1)S(1)}, bf16[1,1,512,128]{3,2,1,0:T(8,128)(2,1)S(1)}) fusion(bf16[4,512,128]{2,1,0:T(8,128)(2,1)} %get-tuple-element.17.a0_ref), kind=kLoop, calls=%fused_computation.31 | loop fusion | bytes 524288 | tf_op jit(solution)/shard_map/stack | solution.py:122
  66.2 8.4 %collective-permute-done.9.c2_ref = bf16[4,512,128]{2,1,0:T(8,128)(2,1)S(1)} collective-permute-done((bf16[4,512,128]{2,1,0:T(8,128)(2,1)}, bf16[4,512,128]{2,1,0:T(8,128)(2,1)S(1)}, u32[]{:S(2)}, u32[]{:S(2)}) %collective-permute-start.9) | collective-permute-done | bytes 524320 | tf_op jit(solution)/shard_map/ppermute | solution.py:13
  74.6 0.0 copy-start.6
  74.6 0.1 pad_maximum_fusion.2
  74.7 0.0 copy-done.4
  74.7 1.9 %collective-permute-start.11 = (bf16[4,1,512,128]{3,2,1,0:T(8,128)(2,1)S(1)}, bf16[4,1,512,128]{3,2,1,0:T(8,128)(2,1)S(1)}, u32[]{:S(2)}, u32[]{:S(2)}) collective-permute-start(bf16[4,1,512,128]{3,2,1,0:T(8,128)(2,1)S(1)} %pad_maximum_fusion.2), channel_id=1, source_target_pairs={{1,0},{2,1},{3,2},{5,4},{6,5},{7,6},{9,8},{10,9},{11,10},{13,12},{... | collective-permute-start | bytes 1572872 | tf_op jit(solution)/shard_map/ppermute | solution.py:122
  76.6 0.1 pad_maximum_fusion.1
  76.7 0.0 copy-done.6
  76.7 3.8 %collective-permute-start.10 = (bf16[4,1,512,128]{3,2,1,0:T(8,128)(2,1)S(1)}, bf16[4,1,512,128]{3,2,1,0:T(8,128)(2,1)S(1)}, u32[]{:S(2)}, u32[]{:S(2)}) collective-permute-start(bf16[4,1,512,128]{3,2,1,0:T(8,128)(2,1)S(1)} %pad_maximum_fusion.1), channel_id=1, source_target_pairs={{0,1},{1,2},{2,3},{4,5},{5,6},{6,7},{8,9},{9,10},{10,11},{12,13},{... | collective-permute-start | bytes 1572872 | tf_op jit(solution)/shard_map/ppermute | solution.py:121
  80.5 4.7 %collective-permute-done.11.bottom = bf16[4,1,512,128]{3,2,1,0:T(8,128)(2,1)S(1)} collective-permute-done((bf16[4,1,512,128]{3,2,1,0:T(8,128)(2,1)S(1)}, bf16[4,1,512,128]{3,2,1,0:T(8,128)(2,1)S(1)}, u32[]{:S(2)}, u32[]{:S(2)}) %collective-permute-start.11) | collective-permute-done | bytes 524320 | tf_op jit(solution)/shard_map/ppermute | solution.py:122
  85.2 0.0 copy-start.7
  85.2 1.3 %collective-permute-done.10.top = bf16[4,1,512,128]{3,2,1,0:T(8,128)(2,1)S(1)} collective-permute-done((bf16[4,1,512,128]{3,2,1,0:T(8,128)(2,1)S(1)}, bf16[4,1,512,128]{3,2,1,0:T(8,128)(2,1)S(1)}, u32[]{:S(2)}, u32[]{:S(2)}) %collective-permute-start.10) | collective-permute-done | bytes 524320 | tf_op jit(solution)/shard_map/ppermute | solution.py:121
  86.4 0.0 copy-done.7
  86.4 0.8 copy-done.8
  87.2 8.7 %shard_map.30 = bf16[2,4,512,128]{3,2,1,0:T(8,128)(2,1)} custom-call(bf16[4,512,128]{2,1,0:T(8,128)(2,1)} %copy-done.6, bf16[4,512,128]{2,1,0:T(8,128)(2,1)} %copy-done.4, bf16[4,512,128]{2,1,0:T(8,128)(2,1)} %get-tuple-element.17.a0_ref, bf16[4,512,128]{2,1,0:T(8,128)(2,1)} %get-tuple-element.16.a1_ref, bf16[4,1,512,128]{3,2,1,0:T(8,128)(2,1)} %copy-done.8, ...), custom_call_target="tpu_custom_call" | custom-call | flops 3623878656 | bytes 6127616 | tf_op jit(solution)/shard_map/pallas_call | solution.py:104
  (7 shorter events, 0.2 us)
Async XLA Ops:
  0.0 7.6 %copy-start.2 = (bf16[1,9,384,128]{3,2,1,0:T(8,128)(2,1)S(1)}, bf16[1,9,384,128]{3,2,1,0:T(8,128)(2,1)}, u32[]{:S(2)}) copy-start(bf16[1,9,384,128]{3,2,1,0:T(8,128)(2,1)} %param.3) | copy-start | bytes 2654212
  2.8 18.6 %collective-permute-start = (bf16[4,512,128]{2,1,0:T(8,128)(2,1)}, bf16[4,512,128]{2,1,0:T(8,128)(2,1)}, u32[]{:S(2)}, u32[]{:S(2)}) collective-permute-start(bf16[4,512,128]{2,1,0:T(8,128)(2,1)} %get-tuple-element.25.refs_2_), channel_id=1, source_target_pairs={{0,4},{4,8},{8,12},{1,5},{5,9},{9,13},{2,6},{6,10},{10,14},{3,7},{... | collective-permute-start | bytes 1572872 | tf_op jit(solution)/shard_map/ppermute | solution.py:13
  8.5 2.3 %copy-start = (bf16[1,2,4,512,128]{4,3,2,1,0:T(8,128)(2,1)S(1)}, bf16[1,2,4,512,128]{4,3,2,1,0:T(8,128)(2,1)}, u32[]{:S(2)}) copy-start(bf16[1,2,4,512,128]{4,3,2,1,0:T(8,128)(2,1)} %param.2) | copy-start | bytes 3145732
  8.6 10.9 %collective-permute-start.6 = (bf16[576,384]{1,0:T(8,128)(2,1)S(1)}, bf16[576,384]{1,0:T(8,128)(2,1)}, u32[]{:S(2)}, u32[]{:S(2)}) collective-permute-start(bf16[576,384]{1,0:T(8,128)(2,1)S(1)} %constant_dynamic-slice_fusion), channel_id=1, source_target_pairs={{0,16},{16,0},{1,17},{17,1},{2,18},{18,2},{3,19},{19,3},{4,20},{20... | collective-permute-start | bytes 1327112 | tf_op jit(solution)/shard_map/ppermute | solution.py:140
  10.9 10.5 %copy-start.1 = (bf16[4,512,128]{2,1,0:T(8,128)(2,1)S(1)}, bf16[4,512,128]{2,1,0:T(8,128)(2,1)}, u32[]{:S(2)}) copy-start(bf16[4,512,128]{2,1,0:T(8,128)(2,1)} %get-tuple-element.13.refs_2_.refs_1_) | copy-start | bytes 1572868
  19.5 11.0 %collective-permute-start.7 = (bf16[576,384]{1,0:T(8,128)(2,1)}, bf16[576,384]{1,0:T(8,128)(2,1)S(1)}, u32[]{:S(2)}, u32[]{:S(2)}) collective-permute-start(bf16[576,384]{1,0:T(8,128)(2,1)} %collective-permute-done.6), channel_id=1, source_target_pairs={{0,1},{1,0},{2,3},{3,2},{4,5},{5,4},{6,7},{7,6},{8,9},{9,8},{10,11... | collective-permute-start | bytes 1327112 | tf_op jit(solution)/shard_map/ppermute | solution.py:141
  21.4 23.7 %collective-permute-start.1 = (bf16[4,512,128]{2,1,0:T(8,128)(2,1)S(1)}, bf16[4,512,128]{2,1,0:T(8,128)(2,1)S(1)}, u32[]{:S(2)}, u32[]{:S(2)}) collective-permute-start(bf16[4,512,128]{2,1,0:T(8,128)(2,1)S(1)} %copy-done.1), channel_id=1, source_target_pairs={{0,4},{4,8},{8,12},{1,5},{5,9},{9,13},{2,6},{6,10},{10,14},{3,7},{... | collective-permute-start | bytes 1572872 | tf_op jit(solution)/shard_map/ppermute | solution.py:13
  24.9 9.1 %collective-permute-start.3 = (bf16[3,1,512,128]{3,2,1,0:T(8,128)(2,1)S(1)}, bf16[3,1,512,128]{3,2,1,0:T(8,128)(2,1)S(1)}, u32[]{:S(2)}, u32[]{:S(2)}) collective-permute-start(bf16[3,1,512,128]{3,2,1,0:T(8,128)(2,1)S(1)} %pad_maximum_fusion.4), channel_id=1, source_target_pairs={{1,0},{2,1},{3,2},{5,4},{6,5},{7,6},{9,8},{10,9},{11,10},{13,12},{... | collective-permute-start | bytes 1179656 | tf_op jit(solution)/shard_map/ppermute | solution.py:125
  27.2 8.1 %collective-permute-start.2 = (bf16[3,1,512,128]{3,2,1,0:T(8,128)(2,1)S(1)}, bf16[3,1,512,128]{3,2,1,0:T(8,128)(2,1)S(1)}, u32[]{:S(2)}, u32[]{:S(2)}) collective-permute-start(bf16[3,1,512,128]{3,2,1,0:T(8,128)(2,1)S(1)} %pad_maximum_fusion.3), channel_id=1, source_target_pairs={{0,1},{1,2},{2,3},{4,5},{5,6},{6,7},{8,9},{9,10},{10,11},{12,13},{... | collective-permute-start | bytes 1179656 | tf_op jit(solution)/shard_map/ppermute | solution.py:124
  34.0 1.2 %copy-start.9 = (bf16[3,1,512,128]{3,2,1,0:T(8,128)(2,1)}, bf16[3,1,512,128]{3,2,1,0:T(8,128)(2,1)S(1)}, u32[]{:S(2)}) copy-start(bf16[3,1,512,128]{3,2,1,0:T(8,128)(2,1)S(1)} %collective-permute-done.3.refs_4_) | copy-start | bytes 1179652
  35.3 0.8 copy-start.10
  41.8 20.8 %collective-permute-start.8 = (bf16[4,512,128]{2,1,0:T(8,128)(2,1)}, bf16[4,512,128]{2,1,0:T(8,128)(2,1)S(1)}, u32[]{:S(2)}, u32[]{:S(2)}) collective-permute-start(bf16[4,512,128]{2,1,0:T(8,128)(2,1)} %get-tuple-element.16.a1_ref), channel_id=1, source_target_pairs={{0,4},{4,8},{8,12},{1,5},{5,9},{9,13},{2,6},{6,10},{10,14},{3,7},{... | collective-permute-start | bytes 1572872 | tf_op jit(solution)/shard_map/ppermute | solution.py:13
  45.1 11.0 %copy-start.5 = (bf16[4,512,128]{2,1,0:T(8,128)(2,1)}, bf16[4,512,128]{2,1,0:T(8,128)(2,1)S(1)}, u32[]{:S(2)}) copy-start(bf16[4,512,128]{2,1,0:T(8,128)(2,1)S(1)} %collective-permute-done.1.refs_0_) | copy-start | bytes 1572868
  45.1 6.6 %collective-permute-start.4 = (bf16[1,1,512,128]{3,2,1,0:T(8,128)(2,1)S(1)}, bf16[1,1,512,128]{3,2,1,0:T(8,128)(2,1)S(1)}, u32[]{:S(2)}, u32[]{:S(2)}) collective-permute-start(bf16[1,1,512,128]{3,2,1,0:T(8,128)(2,1)S(1)} %get-tuple-element.38), channel_id=1, source_target_pairs={{0,1},{1,2},{2,3},{4,5},{5,6},{6,7},{8,9},{9,10},{10,11},{12,13},{... | collective-permute-start | bytes 393224 | tf_op jit(solution)/shard_map/ppermute | solution.py:127
  49.8 6.3 %collective-permute-start.5 = (bf16[1,1,512,128]{3,2,1,0:T(8,128)(2,1)S(1)}, bf16[1,1,512,128]{3,2,1,0:T(8,128)(2,1)S(1)}, u32[]{:S(2)}, u32[]{:S(2)}) collective-permute-start(bf16[1,1,512,128]{3,2,1,0:T(8,128)(2,1)S(1)} %get-tuple-element.37), channel_id=1, source_target_pairs={{1,0},{2,1},{3,2},{5,4},{6,5},{7,6},{9,8},{10,9},{11,10},{13,12},{... | collective-permute-start | bytes 393224 | tf_op jit(solution)/shard_map/ppermute | solution.py:128
  51.7 4.4 %copy-start.11 = (bf16[1,1,512,128]{3,2,1,0:T(8,128)(2,1)}, bf16[1,1,512,128]{3,2,1,0:T(8,128)(2,1)S(1)}, u32[]{:S(2)}) copy-start(bf16[1,1,512,128]{3,2,1,0:T(8,128)(2,1)S(1)} %collective-permute-done.4.refs_5_) | copy-start | bytes 393220
  56.1 0.7 copy-start.12
  56.7 8.4 %copy-start.3 = (bf16[4,512,128]{2,1,0:T(8,128)(2,1)S(1)}, bf16[4,512,128]{2,1,0:T(8,128)(2,1)}, u32[]{:S(2)}) copy-start(bf16[4,512,128]{2,1,0:T(8,128)(2,1)} %get-tuple-element.16.a1_ref) | copy-start | bytes 1572868
  62.7 12.0 %copy-start.4 = (bf16[4,512,128]{2,1,0:T(8,128)(2,1)}, bf16[4,512,128]{2,1,0:T(8,128)(2,1)S(1)}, u32[]{:S(2)}) copy-start(bf16[4,512,128]{2,1,0:T(8,128)(2,1)S(1)} %collective-permute-done.8.c1_ref) | copy-start | bytes 1572868
  62.7 11.9 %collective-permute-start.9 = (bf16[4,512,128]{2,1,0:T(8,128)(2,1)}, bf16[4,512,128]{2,1,0:T(8,128)(2,1)S(1)}, u32[]{:S(2)}, u32[]{:S(2)}) collective-permute-start(bf16[4,512,128]{2,1,0:T(8,128)(2,1)} %get-tuple-element.17.a0_ref), channel_id=1, source_target_pairs={{0,4},{4,8},{8,12},{1,5},{5,9},{9,13},{2,6},{6,10},{10,14},{3,7},{... | collective-permute-start | bytes 1572872 | tf_op jit(solution)/shard_map/ppermute | solution.py:13
  74.6 2.1 %copy-start.6 = (bf16[4,512,128]{2,1,0:T(8,128)(2,1)}, bf16[4,512,128]{2,1,0:T(8,128)(2,1)S(1)}, u32[]{:S(2)}) copy-start(bf16[4,512,128]{2,1,0:T(8,128)(2,1)S(1)} %collective-permute-done.9.c2_ref) | copy-start | bytes 1572868
  74.7 10.5 %collective-permute-start.11 = (bf16[4,1,512,128]{3,2,1,0:T(8,128)(2,1)S(1)}, bf16[4,1,512,128]{3,2,1,0:T(8,128)(2,1)S(1)}, u32[]{:S(2)}, u32[]{:S(2)}) collective-permute-start(bf16[4,1,512,128]{3,2,1,0:T(8,128)(2,1)S(1)} %pad_maximum_fusion.2), channel_id=1, source_target_pairs={{1,0},{2,1},{3,2},{5,4},{6,5},{7,6},{9,8},{10,9},{11,10},{13,12},{... | collective-permute-start | bytes 1572872 | tf_op jit(solution)/shard_map/ppermute | solution.py:122
  76.7 9.8 %collective-permute-start.10 = (bf16[4,1,512,128]{3,2,1,0:T(8,128)(2,1)S(1)}, bf16[4,1,512,128]{3,2,1,0:T(8,128)(2,1)S(1)}, u32[]{:S(2)}, u32[]{:S(2)}) collective-permute-start(bf16[4,1,512,128]{3,2,1,0:T(8,128)(2,1)S(1)} %pad_maximum_fusion.1), channel_id=1, source_target_pairs={{0,1},{1,2},{2,3},{4,5},{5,6},{6,7},{8,9},{9,10},{10,11},{12,13},{... | collective-permute-start | bytes 1572872 | tf_op jit(solution)/shard_map/ppermute | solution.py:121
  85.2 1.3 %copy-start.7 = (bf16[4,1,512,128]{3,2,1,0:T(8,128)(2,1)}, bf16[4,1,512,128]{3,2,1,0:T(8,128)(2,1)S(1)}, u32[]{:S(2)}) copy-start(bf16[4,1,512,128]{3,2,1,0:T(8,128)(2,1)S(1)} %collective-permute-done.11.bottom) | copy-start | bytes 1572868
  86.4 0.8 copy-start.8

commit v12 on v10

--- a/solution.py
+++ b/solution.py
@@ -113,7 +113,10 @@
     n = lax.axis_size("space")
     down = [(i, i + 1) for i in range(n - 1)]
     up = [(i + 1, i) for i in range(n - 1)]
-    c1 = shift_tm(a1)
+    if merge:
+        c1 = shift_tm(a1)
+    else:
+        c1 = silu(shift_tm(x1))
     a0, c1 = lax.optimization_barrier((a0, c1))
     c2 = shift_tm(a0)
     top_a = lax.ppermute(jnp.stack([c1[-1:], a0[-1:], a1[-1:]]), "space", down)

time: 92.8 us -> 96.6 us (1.041)
  starting transfers between devices: 38.3 us -> 41.6 us
    ppermute x4, waiting for transfers between devices: 2.73 us -> 6.12 us  [shift_tm(): return lax.ppermute(x, 'tm', [(i, i + 1) for i in range(n - 1)])]
    ppermute x1, waiting for transfers between devices: 7.5 us -> 4.55 us  [both_taps(): got = lax.ppermute(mine, 'section', [(0, 1), (1, 0)])]
    another operation x5, local copies, waits for them, and re-layouts: 3.98 us -> 2.05 us  [conv_block(): bot_a = lax.ppermute(jnp.stack([c1[:1], a0[:1], a1[:1]]), 'space', up)]
    ppermute x2, starting transfers between devices: 4.13 us -> 5.97 us  [conv_block(): bot_a = lax.ppermute(jnp.stack([c1[:1], a0[:1], a1[:1]]), 'space', up)]
    ppermute x4, starting transfers between devices: 12.9 us -> 14.5 us  [shift_tm(): return lax.ppermute(x, 'tm', [(i, i + 1) for i in range(n - 1)])]
    another operation x1, local copies, waits for them, and re-layouts: 0.76 us -> 1.93 us  [tap_matrix(): taps.reshape(nine, 3, chans, chans).transpose(0, 2, 1, 3)]
    broadcast_in_dim x2, local copies, waits for them, and re-layouts: 0.04 us -> 1.01 us  [conv_block(): bot_b = lax.ppermute(c2[None, :1], 'space', up)]
    convert_element_type x1 -> x2, other arithmetic: 2.81 us -> 1.87 us  [silu(): return jax.nn.silu(x.astype(jnp.float32)).astype(jnp.bfloat16)]
  transfers between devices with their start and end apart: 14 -> 14, of which waited for: 6 -> 7; matrix products, arithmetic and copies ran while one was open for 10% -> 9% of each run, Pallas kernels for 13% -> 12%
where the time goes in v12:
time: 96.6 us; the launch traced here: 95.9 us
  starting transfers between devices  41.6 us (43%)
  Pallas kernels  20.5 us (21%)
  waiting for transfers between devices  19.7 us (20%)
  local copies, waits for them, and re-layouts  9.1 us (9%)
  other arithmetic  4.7 us (5%)
    ppermute x4, starting transfers between devices, shift_tm(): return lax.ppermute(x, 'tm', [(i, i + 1) for i in range(n - 1)])  14.5 us
    pallas_call x2, Pallas kernels, frame_conv(): pl.pallas_call(functools.partial(frame_kernel, t, with_act), out_shape=(s...  11.8 us
    pallas_call x1, Pallas kernels, pair_conv(): pl.pallas_call(pair_kernel, out_shape=jax.ShapeDtypeStruct((2,) + x0.shap...  8.73 us
    ppermute x2, waiting for transfers between devices, conv_block(): bot_b = lax.ppermute(c2[None, :1], 'space', up)  6.97 us
    ppermute x2, starting transfers between devices, conv_block(): top_a = lax.ppermute(jnp.stack([c1[-1:], a0[-1:], a1[-1:]]), 'space', down)  6.69 us
    ppermute x2, starting transfers between devices, conv_block(): top_b = lax.ppermute(c2[None, -1:], 'space', down)  6.59 us
    ppermute x4, waiting for transfers between devices, shift_tm(): return lax.ppermute(x, 'tm', [(i, i + 1) for i in range(n - 1)])  6.12 us
    ppermute x2, starting transfers between devices, conv_block(): bot_a = lax.ppermute(jnp.stack([c1[:1], a0[:1], a1[:1]]), 'space', up)  5.97 us
  transfers between devices with their start and end apart: 14, of which 7 were waited for; matrix products, arithmetic and copies ran while one was open for 9% of the time, Pallas kernels for 12%

profile of v12, /device:TPU:1, one launch (start us, length us, event | category | flops | bytes accessed | tf_op | source)
XLA Modules:
  0.0 95.9 jit_solution(3212036975848322735)
XLA Ops:
  0.0 1.9 %copy.4 = bf16[9,3,128,128]{3,1,2,0:T(4,128)(2,1)S(1)} copy(bf16[9,3,128,128]{3,2,1,0:T(8,128)(2,1)} %bitcast.53) | data formatting | bytes 1769472 | tf_op jit(solution)/shard_map/reshape;squeeze | solution.py:81
  1.9 0.0 copy-start
  1.9 0.1 copy.9
  2.1 0.8 constant_dynamic-slice_fusion
  2.9 2.0 %collective-permute-start.6 = (bf16[576,384]{1,0:T(8,128)(2,1)}, bf16[576,384]{1,0:T(8,128)(2,1)}, u32[]{:S(2)}, u32[]{:S(2)}) collective-permute-start(bf16[576,384]{1,0:T(8,128)(2,1)} %constant_dynamic-slice_fusion), channel_id=1, source_target_pairs={{0,16},{16,0},{1,17},{17,1},{2,18},{18,2},{3,19},{19,3},{4,20},{20... | collective-permute-start | bytes 1327112 | tf_op jit(solution)/shard_map/ppermute | solution.py:142
  5.0 0.0 copy-done
  5.0 1.1 %slice_bitcast_fusion.1 = (bf16[4,512,128]{2,1,0:T(8,128)(2,1)}, bf16[4,512,128]{2,1,0:T(8,128)(2,1)}) fusion(bf16[1,2,4,512,128]{4,3,2,1,0:T(8,128)(2,1)S(1)} %copy-done), kind=kLoop, calls=%fused_computation.23 | loop fusion | bytes 2097152 | tf_op jit(solution)/shard_map/squeeze | solution.py:156
  6.0 4.0 %collective-permute-start = (bf16[4,512,128]{2,1,0:T(8,128)(2,1)}, bf16[4,512,128]{2,1,0:T(8,128)(2,1)}, u32[]{:S(2)}, u32[]{:S(2)}) collective-permute-start(bf16[4,512,128]{2,1,0:T(8,128)(2,1)} %get-tuple-element.24.refs_5_), channel_id=1, source_target_pairs={{0,4},{4,8},{8,12},{1,5},{5,9},{9,13},{2,6},{6,10},{10,14},{3,7},{... | collective-permute-start | bytes 1572872 | tf_op jit(solution)/shard_map/ppermute | solution.py:13
  10.0 0.6 fusion.11
  10.6 0.0 copy-start.2
  10.6 0.0 copy-start.3
  10.6 4.5 %collective-permute-done.6 = bf16[576,384]{1,0:T(8,128)(2,1)} collective-permute-done((bf16[576,384]{1,0:T(8,128)(2,1)}, bf16[576,384]{1,0:T(8,128)(2,1)}, u32[]{:S(2)}, u32[]{:S(2)}) %collective-permute-start.6) | collective-permute-done | bytes 442400 | tf_op jit(solution)/shard_map/ppermute | solution.py:142
  15.2 1.2 %collective-permute-start.7 = (bf16[576,384]{1,0:T(8,128)(2,1)}, bf16[576,384]{1,0:T(8,128)(2,1)S(1)}, u32[]{:S(2)}, u32[]{:S(2)}) collective-permute-start(bf16[576,384]{1,0:T(8,128)(2,1)} %collective-permute-done.6), channel_id=1, source_target_pairs={{0,1},{1,0},{2,3},{3,2},{4,5},{5,4},{6,7},{7,6},{8,9},{9,8},{10,11... | collective-permute-start | bytes 1327112 | tf_op jit(solution)/shard_map/ppermute | solution.py:143
  16.4 3.4 %collective-permute-done = bf16[4,512,128]{2,1,0:T(8,128)(2,1)} collective-permute-done((bf16[4,512,128]{2,1,0:T(8,128)(2,1)}, bf16[4,512,128]{2,1,0:T(8,128)(2,1)}, u32[]{:S(2)}, u32[]{:S(2)}) %collective-permute-start) | collective-permute-done | bytes 524320 | tf_op jit(solution)/shard_map/ppermute | solution.py:13
  19.8 1.3 %fusion.7.refs_1_.refs_0_ = bf16[4,512,128]{2,1,0:T(8,128)(2,1)S(1)} fusion(bf16[4,512,128]{2,1,0:T(8,128)(2,1)} %collective-permute-done), kind=kLoop, calls=%fused_computation.13 | loop fusion | flops 1572864 | bytes 1048576 | tf_op jit(solution)/shard_map/convert_element_type | solution.py:17
  21.1 0.0 copy-start.1
  21.1 4.9 %collective-permute-start.1 = (bf16[4,512,128]{2,1,0:T(8,128)(2,1)S(1)}, bf16[4,512,128]{2,1,0:T(8,128)(2,1)}, u32[]{:S(2)}, u32[]{:S(2)}) collective-permute-start(bf16[4,512,128]{2,1,0:T(8,128)(2,1)S(1)} %get-tuple-element.13.refs_2_.refs_1_), channel_id=1, source_target_pairs={{0,4},{4,8},{8,12},{1,5},{5,9},{9,13},{2,6},{6,10},{10,14},{3,7},{... | collective-permute-start | bytes 1572872 | tf_op jit(solution)/shard_map/ppermute | solution.py:13
  26.1 0.0 copy-done.2
  26.1 0.0 copy-done.3
  26.2 4.1 %collective-permute-start.3 = (bf16[3,1,512,128]{3,2,1,0:T(8,128)(2,1)S(1)}, bf16[3,1,512,128]{3,2,1,0:T(8,128)(2,1)S(1)}, u32[]{:S(2)}, u32[]{:S(2)}) collective-permute-start(bf16[3,1,512,128]{3,2,1,0:T(8,128)(2,1)S(1)} %pad_maximum_fusion.2), channel_id=1, source_target_pairs={{1,0},{2,1},{3,2},{5,4},{6,5},{7,6},{9,8},{10,9},{11,10},{13,12},{... | collective-permute-start | bytes 1179656 | tf_op jit(solution)/shard_map/ppermute | solution.py:123
  30.3 0.0 copy-done.1
  30.3 3.0 %collective-permute-start.2 = (bf16[3,1,512,128]{3,2,1,0:T(8,128)(2,1)S(1)}, bf16[3,1,512,128]{3,2,1,0:T(8,128)(2,1)S(1)}, u32[]{:S(2)}, u32[]{:S(2)}) collective-permute-start(bf16[3,1,512,128]{3,2,1,0:T(8,128)(2,1)S(1)} %pad_maximum_fusion.1), channel_id=1, source_target_pairs={{0,1},{1,2},{2,3},{4,5},{5,6},{6,7},{8,9},{9,10},{10,11},{12,13},{... | collective-permute-start | bytes 1179656 | tf_op jit(solution)/shard_map/ppermute | solution.py:122
  33.4 0.0 collective-permute-done.7
  33.4 1.1 %broadcast_select_fusion.3 = (bf16[576,384]{1,0:T(8,128)(2,1)S(1)}, bf16[576,384]{1,0:T(8,128)(2,1)S(1)}) fusion(bf16[576,384]{1,0:T(8,128)(2,1)} %collective-permute-done.6, bf16[576,384]{1,0:T(8,128)(2,1)S(1)} %collective-permute-done.7, pred[]{:T(512)S(6)} %eq.11), kind=kLoop, calls=%fused_computation.25 | loop fusion | flops 442368 | bytes 1769473 | tf_op jit(solution)/shard_map/jit(_where)/select_n | solution.py:144
  34.5 1.5 %broadcast_select_fusion = (bf16[1152,384]{1,0:T(8,128)(2,1)}, bf16[1152,384]{1,0:T(8,128)(2,1)}) fusion(pred[]{:T(512)S(6)} %eq.10, bf16[576,384]{1,0:T(8,128)(2,1)S(1)} %get-tuple-element.28, bf16[576,384]{1,0:T(8,128)(2,1)S(1)} %get-tuple-element.27, bf16[144,8,3,128]{3,2,1,0:T(4,128)(2,1)S(1)} %bitcast.51), kind=kLoop, calls=%fused_computation.20 | loop fusion | flops 2654208 | bytes 3538945 | tf_op jit(solution)/shard_map/jit(_where)/select_n | solution.py:148
  36.0 0.8 collective-permute-done.3.refs_4_
  36.8 1.2 %collective-permute-done.2.refs_3_ = bf16[3,1,512,128]{3,2,1,0:T(8,128)(2,1)S(1)} collective-permute-done((bf16[3,1,512,128]{3,2,1,0:T(8,128)(2,1)S(1)}, bf16[3,1,512,128]{3,2,1,0:T(8,128)(2,1)S(1)}, u32[]{:S(2)}, u32[]{:S(2)}) %collective-permute-start.2) | collective-permute-done | bytes 393248 | tf_op jit(solution)/shard_map/ppermute | solution.py:122
  38.1 0.0 copy-done.6
  38.1 0.7 copy-done.7
  38.8 5.8 %shard_map.29 = (bf16[4,512,128]{2,1,0:T(8,128)(2,1)}, bf16[4,512,128]{2,1,0:T(8,128)(2,1)}) custom-call(bf16[4,512,128]{2,1,0:T(8,128)(2,1)} %copy-done.1, bf16[4,512,128]{2,1,0:T(8,128)(2,1)} %copy-done.3, bf16[4,512,128]{2,1,0:T(8,128)(2,1)} %copy-done.2, bf16[3,1,512,128]{3,2,1,0:T(8,128)(2,1)} %copy-done.7, bf16[3,1,512,128]{3,2,1,0:T(8,128)(2,1)} %copy-done.6, ...), custom_call_target="tpu_custom_call" | custom-call | flops 1811939328 | bytes 4816896 | tf_op jit(solution)/shard_map/pallas_call | solution.py:92
  44.7 2.4 %collective-permute-start.8 = (bf16[4,512,128]{2,1,0:T(8,128)(2,1)}, bf16[4,512,128]{2,1,0:T(8,128)(2,1)S(1)}, u32[]{:S(2)}, u32[]{:S(2)}) collective-permute-start(bf16[4,512,128]{2,1,0:T(8,128)(2,1)} %get-tuple-element.16.a1_ref), channel_id=1, source_target_pairs={{0,4},{4,8},{8,12},{1,5},{5,9},{9,13},{2,6},{6,10},{10,14},{3,7},{... | collective-permute-start | bytes 1572872 | tf_op jit(solution)/shard_map/ppermute | solution.py:13
  47.1 0.0 collective-permute-done.1.refs_0_
  47.1 1.0 %slice_bitcast_fusion.4 = (bf16[1,1,512,128]{3,2,1,0:T(8,128)(2,1)S(1)}, bf16[1,1,512,128]{3,2,1,0:T(8,128)(2,1)S(1)}) fusion(bf16[4,512,128]{2,1,0:T(8,128)(2,1)} %collective-permute-done.1.refs_0_), kind=kLoop, calls=%fused_computation.32 | loop fusion | bytes 524288 | tf_op jit(solution)/shard_map/broadcast_in_dim | solution.py:130
  48.1 4.7 %collective-permute-start.4 = (bf16[1,1,512,128]{3,2,1,0:T(8,128)(2,1)S(1)}, bf16[1,1,512,128]{3,2,1,0:T(8,128)(2,1)S(1)}, u32[]{:S(2)}, u32[]{:S(2)}) collective-permute-start(bf16[1,1,512,128]{3,2,1,0:T(8,128)(2,1)S(1)} %get-tuple-element.38), channel_id=1, source_target_pairs={{0,1},{1,2},{2,3},{4,5},{5,6},{6,7},{8,9},{9,10},{10,11},{12,13},{... | collective-permute-start | bytes 393224 | tf_op jit(solution)/shard_map/ppermute | solution.py:129
  52.7 1.9 %collective-permute-start.5 = (bf16[1,1,512,128]{3,2,1,0:T(8,128)(2,1)S(1)}, bf16[1,1,512,128]{3,2,1,0:T(8,128)(2,1)S(1)}, u32[]{:S(2)}, u32[]{:S(2)}) collective-permute-start(bf16[1,1,512,128]{3,2,1,0:T(8,128)(2,1)S(1)} %get-tuple-element.37), channel_id=1, source_target_pairs={{1,0},{2,1},{3,2},{5,4},{6,5},{7,6},{9,8},{10,9},{11,10},{13,12},{... | collective-permute-start | bytes 393224 | tf_op jit(solution)/shard_map/ppermute | solution.py:130
  54.7 1.0 %slice_bitcast_fusion.8 = (bf16[1,1,512,128]{3,2,1,0:T(8,128)(2,1)S(1)}, bf16[1,1,512,128]{3,2,1,0:T(8,128)(2,1)S(1)}) fusion(bf16[4,512,128]{2,1,0:T(8,128)(2,1)} %get-tuple-element.16.a1_ref), kind=kLoop, calls=%fused_computation.36 | loop fusion | bytes 524288 | tf_op jit(solution)/shard_map/stack | solution.py:123
  55.7 0.0 collective-permute-done.4.refs_5_
  55.7 0.0 copy-start.12
  55.7 3.3 %collective-permute-done.5.refs_6_ = bf16[1,1,512,128]{3,2,1,0:T(8,128)(2,1)S(1)} collective-permute-done((bf16[1,1,512,128]{3,2,1,0:T(8,128)(2,1)S(1)}, bf16[1,1,512,128]{3,2,1,0:T(8,128)(2,1)S(1)}, u32[]{:S(2)}, u32[]{:S(2)}) %collective-permute-start.5) | collective-permute-done | bytes 131104 | tf_op jit(solution)/shard_map/ppermute | solution.py:130
  59.0 0.0 copy-done.12
  59.0 0.6 copy-done.13
  59.7 5.9 %shard_map.28 = (bf16[4,512,128]{2,1,0:T(8,128)(2,1)}, bf16[4,512,128]{2,1,0:T(8,128)(2,1)}) custom-call(bf16[4,512,128]{2,1,0:T(8,128)(2,1)} %collective-permute-done.1.refs_0_, bf16[4,512,128]{2,1,0:T(8,128)(2,1)} %copy-done.1, bf16[4,512,128]{2,1,0:T(8,128)(2,1)} %copy-done.3, bf16[3,1,512,128]{3,2,1,0:T(8,128)(2,1)} %copy-done.7, ...), custom_call_target="tpu_custom_call" | custom-call | flops 1811939328 | bytes 5079040 | tf_op jit(solution)/shard_map/pallas_call | solution.py:92
  65.6 0.0 collective-permute-done.8.c1_ref
  65.6 3.2 %collective-permute-start.9 = (bf16[4,512,128]{2,1,0:T(8,128)(2,1)}, bf16[4,512,128]{2,1,0:T(8,128)(2,1)S(1)}, u32[]{:S(2)}, u32[]{:S(2)}) collective-permute-start(bf16[4,512,128]{2,1,0:T(8,128)(2,1)} %get-tuple-element.17.a0_ref), channel_id=1, source_target_pairs={{0,4},{4,8},{8,12},{1,5},{5,9},{9,13},{2,6},{6,10},{10,14},{3,7},{... | collective-permute-start | bytes 1572872 | tf_op jit(solution)/shard_map/ppermute | solution.py:13
  68.8 1.0 %slice_bitcast_fusion.9 = (bf16[1,1,512,128]{3,2,1,0:T(8,128)(2,1)S(1)}, bf16[1,1,512,128]{3,2,1,0:T(8,128)(2,1)S(1)}) fusion(bf16[4,512,128]{2,1,0:T(8,128)(2,1)} %get-tuple-element.17.a0_ref), kind=kLoop, calls=%fused_computation.37 | loop fusion | bytes 524288 | tf_op jit(solution)/shard_map/stack | solution.py:123
  69.9 1.9 %collective-permute-start.11 = (bf16[3,1,512,128]{3,2,1,0:T(8,128)(2,1)S(1)}, bf16[3,1,512,128]{3,2,1,0:T(8,128)(2,1)S(1)}, u32[]{:S(2)}, u32[]{:S(2)}) collective-permute-start(bf16[3,1,512,128]{3,2,1,0:T(8,128)(2,1)S(1)} %pad_maximum_fusion.4), channel_id=1, source_target_pairs={{1,0},{2,1},{3,2},{5,4},{6,5},{7,6},{9,8},{10,9},{11,10},{13,12},{... | collective-permute-start | bytes 1179656 | tf_op jit(solution)/shard_map/ppermute | solution.py:123
  71.9 0.0 copy-done.4
  71.9 3.6 %collective-permute-start.10 = (bf16[3,1,512,128]{3,2,1,0:T(8,128)(2,1)S(1)}, bf16[3,1,512,128]{3,2,1,0:T(8,128)(2,1)S(1)}, u32[]{:S(2)}, u32[]{:S(2)}) collective-permute-start(bf16[3,1,512,128]{3,2,1,0:T(8,128)(2,1)S(1)} %pad_maximum_fusion.3), channel_id=1, source_target_pairs={{0,1},{1,2},{2,3},{4,5},{5,6},{6,7},{8,9},{9,10},{10,11},{12,13},{... | collective-permute-start | bytes 1179656 | tf_op jit(solution)/shard_map/ppermute | solution.py:122
  75.6 2.7 %collective-permute-done.9.c2_ref = bf16[4,512,128]{2,1,0:T(8,128)(2,1)S(1)} collective-permute-done((bf16[4,512,128]{2,1,0:T(8,128)(2,1)}, bf16[4,512,128]{2,1,0:T(8,128)(2,1)S(1)}, u32[]{:S(2)}, u32[]{:S(2)}) %collective-permute-start.9) | collective-permute-done | bytes 524320 | tf_op jit(solution)/shard_map/ppermute | solution.py:13
  78.3 1.9 %collective-permute-start.12 = (bf16[1,1,512,128]{3,2,1,0:T(8,128)(2,1)S(1)}, bf16[1,1,512,128]{3,2,1,0:T(8,128)(2,1)S(1)}, u32[]{:S(2)}, u32[]{:S(2)}) collective-permute-start(bf16[1,1,512,128]{3,2,1,0:T(8,128)(2,1)S(1)} %get-tuple-element.30), channel_id=1, source_target_pairs={{0,1},{1,2},{2,3},{4,5},{5,6},{6,7},{8,9},{9,10},{10,11},{12,13},{... | collective-permute-start | bytes 393224 | tf_op jit(solution)/shard_map/ppermute | solution.py:125
  80.2 2.6 %collective-permute-start.13 = (bf16[1,1,512,128]{3,2,1,0:T(8,128)(2,1)S(1)}, bf16[1,1,512,128]{3,2,1,0:T(8,128)(2,1)S(1)}, u32[]{:S(2)}, u32[]{:S(2)}) collective-permute-start(bf16[1,1,512,128]{3,2,1,0:T(8,128)(2,1)S(1)} %get-tuple-element.29), channel_id=1, source_target_pairs={{1,0},{2,1},{3,2},{5,4},{6,5},{7,6},{9,8},{10,9},{11,10},{13,12},{... | collective-permute-start | bytes 393224 | tf_op jit(solution)/shard_map/ppermute | solution.py:126
  82.8 0.0 collective-permute-done.11.bot_a
  82.8 0.0 copy-start.8
  82.8 0.0 collective-permute-done.10.top_a
  82.9 0.0 copy-start.9
  82.9 0.0 collective-permute-done.12.top_b
  82.9 0.0 copy-start.10
  82.9 3.6 %collective-permute-done.13.bot_b = bf16[1,1,512,128]{3,2,1,0:T(8,128)(2,1)S(1)} collective-permute-done((bf16[1,1,512,128]{3,2,1,0:T(8,128)(2,1)S(1)}, bf16[1,1,512,128]{3,2,1,0:T(8,128)(2,1)S(1)}, u32[]{:S(2)}, u32[]{:S(2)}) %collective-permute-start.13) | collective-permute-done | bytes 131104 | tf_op jit(solution)/shard_map/ppermute | solution.py:126
  86.5 0.0 copy-done.5
  86.5 0.0 copy-done.8
  86.5 0.0 copy-done.9
  86.5 0.0 copy-done.10
  86.5 0.7 copy-done.11
  87.2 8.7 %shard_map.30 = bf16[2,4,512,128]{3,2,1,0:T(8,128)(2,1)} custom-call(bf16[4,512,128]{2,1,0:T(8,128)(2,1)} %copy-done.5, bf16[4,512,128]{2,1,0:T(8,128)(2,1)} %copy-done.4, bf16[4,512,128]{2,1,0:T(8,128)(2,1)} %get-tuple-element.17.a0_ref, bf16[4,512,128]{2,1,0:T(8,128)(2,1)} %get-tuple-element.16.a1_ref, bf16[3,1,512,128]{3,2,1,0:T(8,128)(2,1)} %copy-done.9, ...), custom_call_target="tpu_custom_call" | custom-call | flops 3623878656 | bytes 6127616 | tf_op jit(solution)/shard_map/pallas_call | solution.py:103
  (14 shorter events, 0.3 us)
Async XLA Ops:
  1.9 3.0 %copy-start = (bf16[1,2,4,512,128]{4,3,2,1,0:T(8,128)(2,1)S(1)}, bf16[1,2,4,512,128]{4,3,2,1,0:T(8,128)(2,1)}, u32[]{:S(2)}) copy-start(bf16[1,2,4,512,128]{4,3,2,1,0:T(8,128)(2,1)} %param.2) | copy-start | bytes 3145732
  2.9 12.2 %collective-permute-start.6 = (bf16[576,384]{1,0:T(8,128)(2,1)}, bf16[576,384]{1,0:T(8,128)(2,1)}, u32[]{:S(2)}, u32[]{:S(2)}) collective-permute-start(bf16[576,384]{1,0:T(8,128)(2,1)} %constant_dynamic-slice_fusion), channel_id=1, source_target_pairs={{0,16},{16,0},{1,17},{17,1},{2,18},{18,2},{3,19},{19,3},{4,20},{20... | collective-permute-start | bytes 1327112 | tf_op jit(solution)/shard_map/ppermute | solution.py:142
  6.0 13.8 %collective-permute-start = (bf16[4,512,128]{2,1,0:T(8,128)(2,1)}, bf16[4,512,128]{2,1,0:T(8,128)(2,1)}, u32[]{:S(2)}, u32[]{:S(2)}) collective-permute-start(bf16[4,512,128]{2,1,0:T(8,128)(2,1)} %get-tuple-element.24.refs_5_), channel_id=1, source_target_pairs={{0,4},{4,8},{8,12},{1,5},{5,9},{9,13},{2,6},{6,10},{10,14},{3,7},{... | collective-permute-start | bytes 1572872 | tf_op jit(solution)/shard_map/ppermute | solution.py:13
  10.6 15.5 %copy-start.2 = (bf16[4,512,128]{2,1,0:T(8,128)(2,1)}, bf16[4,512,128]{2,1,0:T(8,128)(2,1)S(1)}, u32[]{:S(2)}) copy-start(bf16[4,512,128]{2,1,0:T(8,128)(2,1)S(1)} %get-tuple-element.25.refs_2_) | copy-start | bytes 1572868
  10.6 15.5 %copy-start.3 = (bf16[4,512,128]{2,1,0:T(8,128)(2,1)}, bf16[4,512,128]{2,1,0:T(8,128)(2,1)S(1)}, u32[]{:S(2)}) copy-start(bf16[4,512,128]{2,1,0:T(8,128)(2,1)S(1)} %get-tuple-element.13.refs_2_.refs_1_) | copy-start | bytes 1572868
  15.2 18.2 %collective-permute-start.7 = (bf16[576,384]{1,0:T(8,128)(2,1)}, bf16[576,384]{1,0:T(8,128)(2,1)S(1)}, u32[]{:S(2)}, u32[]{:S(2)}) collective-permute-start(bf16[576,384]{1,0:T(8,128)(2,1)} %collective-permute-done.6), channel_id=1, source_target_pairs={{0,1},{1,0},{2,3},{3,2},{4,5},{5,4},{6,7},{7,6},{8,9},{9,8},{10,11... | collective-permute-start | bytes 1327112 | tf_op jit(solution)/shard_map/ppermute | solution.py:143
  21.1 9.2 %copy-start.1 = (bf16[4,512,128]{2,1,0:T(8,128)(2,1)}, bf16[4,512,128]{2,1,0:T(8,128)(2,1)S(1)}, u32[]{:S(2)}) copy-start(bf16[4,512,128]{2,1,0:T(8,128)(2,1)S(1)} %fusion.7.refs_1_.refs_0_) | copy-start | bytes 1572868
  21.1 25.9 %collective-permute-start.1 = (bf16[4,512,128]{2,1,0:T(8,128)(2,1)S(1)}, bf16[4,512,128]{2,1,0:T(8,128)(2,1)}, u32[]{:S(2)}, u32[]{:S(2)}) collective-permute-start(bf16[4,512,128]{2,1,0:T(8,128)(2,1)S(1)} %get-tuple-element.13.refs_2_.refs_1_), channel_id=1, source_target_pairs={{0,4},{4,8},{8,12},{1,5},{5,9},{9,13},{2,6},{6,10},{10,14},{3,7},{... | collective-permute-start | bytes 1572872 | tf_op jit(solution)/shard_map/ppermute | solution.py:13
  26.2 10.6 %collective-permute-start.3 = (bf16[3,1,512,128]{3,2,1,0:T(8,128)(2,1)S(1)}, bf16[3,1,512,128]{3,2,1,0:T(8,128)(2,1)S(1)}, u32[]{:S(2)}, u32[]{:S(2)}) collective-permute-start(bf16[3,1,512,128]{3,2,1,0:T(8,128)(2,1)S(1)} %pad_maximum_fusion.2), channel_id=1, source_target_pairs={{1,0},{2,1},{3,2},{5,4},{6,5},{7,6},{9,8},{10,9},{11,10},{13,12},{... | collective-permute-start | bytes 1179656 | tf_op jit(solution)/shard_map/ppermute | solution.py:123
  30.3 7.8 %collective-permute-start.2 = (bf16[3,1,512,128]{3,2,1,0:T(8,128)(2,1)S(1)}, bf16[3,1,512,128]{3,2,1,0:T(8,128)(2,1)S(1)}, u32[]{:S(2)}, u32[]{:S(2)}) collective-permute-start(bf16[3,1,512,128]{3,2,1,0:T(8,128)(2,1)S(1)} %pad_maximum_fusion.1), channel_id=1, source_target_pairs={{0,1},{1,2},{2,3},{4,5},{5,6},{6,7},{8,9},{9,10},{10,11},{12,13},{... | collective-permute-start | bytes 1179656 | tf_op jit(solution)/shard_map/ppermute | solution.py:122
  36.8 1.2 %copy-start.6 = (bf16[3,1,512,128]{3,2,1,0:T(8,128)(2,1)}, bf16[3,1,512,128]{3,2,1,0:T(8,128)(2,1)S(1)}, u32[]{:S(2)}) copy-start(bf16[3,1,512,128]{3,2,1,0:T(8,128)(2,1)S(1)} %collective-permute-done.3.refs_4_) | copy-start | bytes 1179652
  38.1 0.7 copy-start.7
  44.7 21.0 %collective-permute-start.8 = (bf16[4,512,128]{2,1,0:T(8,128)(2,1)}, bf16[4,512,128]{2,1,0:T(8,128)(2,1)S(1)}, u32[]{:S(2)}, u32[]{:S(2)}) collective-permute-start(bf16[4,512,128]{2,1,0:T(8,128)(2,1)} %get-tuple-element.16.a1_ref), channel_id=1, source_target_pairs={{0,4},{4,8},{8,12},{1,5},{5,9},{9,13},{2,6},{6,10},{10,14},{3,7},{... | collective-permute-start | bytes 1572872 | tf_op jit(solution)/shard_map/ppermute | solution.py:13
  48.1 7.6 %collective-permute-start.4 = (bf16[1,1,512,128]{3,2,1,0:T(8,128)(2,1)S(1)}, bf16[1,1,512,128]{3,2,1,0:T(8,128)(2,1)S(1)}, u32[]{:S(2)}, u32[]{:S(2)}) collective-permute-start(bf16[1,1,512,128]{3,2,1,0:T(8,128)(2,1)S(1)} %get-tuple-element.38), channel_id=1, source_target_pairs={{0,1},{1,2},{2,3},{4,5},{5,6},{6,7},{8,9},{9,10},{10,11},{12,13},{... | collective-permute-start | bytes 393224 | tf_op jit(solution)/shard_map/ppermute | solution.py:129
  52.7 6.3 %collective-permute-start.5 = (bf16[1,1,512,128]{3,2,1,0:T(8,128)(2,1)S(1)}, bf16[1,1,512,128]{3,2,1,0:T(8,128)(2,1)S(1)}, u32[]{:S(2)}, u32[]{:S(2)}) collective-permute-start(bf16[1,1,512,128]{3,2,1,0:T(8,128)(2,1)S(1)} %get-tuple-element.37), channel_id=1, source_target_pairs={{1,0},{2,1},{3,2},{5,4},{6,5},{7,6},{9,8},{10,9},{11,10},{13,12},{... | collective-permute-start | bytes 393224 | tf_op jit(solution)/shard_map/ppermute | solution.py:130
  55.7 3.4 %copy-start.12 = (bf16[1,1,512,128]{3,2,1,0:T(8,128)(2,1)}, bf16[1,1,512,128]{3,2,1,0:T(8,128)(2,1)S(1)}, u32[]{:S(2)}) copy-start(bf16[1,1,512,128]{3,2,1,0:T(8,128)(2,1)S(1)} %collective-permute-done.4.refs_5_) | copy-start | bytes 393220
  59.0 0.7 copy-start.13
  65.6 6.3 %copy-start.4 = (bf16[4,512,128]{2,1,0:T(8,128)(2,1)}, bf16[4,512,128]{2,1,0:T(8,128)(2,1)S(1)}, u32[]{:S(2)}) copy-start(bf16[4,512,128]{2,1,0:T(8,128)(2,1)S(1)} %collective-permute-done.8.c1_ref) | copy-start | bytes 1572868
  65.6 12.6 %collective-permute-start.9 = (bf16[4,512,128]{2,1,0:T(8,128)(2,1)}, bf16[4,512,128]{2,1,0:T(8,128)(2,1)S(1)}, u32[]{:S(2)}, u32[]{:S(2)}) collective-permute-start(bf16[4,512,128]{2,1,0:T(8,128)(2,1)} %get-tuple-element.17.a0_ref), channel_id=1, source_target_pairs={{0,4},{4,8},{8,12},{1,5},{5,9},{9,13},{2,6},{6,10},{10,14},{3,7},{... | collective-permute-start | bytes 1572872 | tf_op jit(solution)/shard_map/ppermute | solution.py:13
  69.9 12.9 %collective-permute-start.11 = (bf16[3,1,512,128]{3,2,1,0:T(8,128)(2,1)S(1)}, bf16[3,1,512,128]{3,2,1,0:T(8,128)(2,1)S(1)}, u32[]{:S(2)}, u32[]{:S(2)}) collective-permute-start(bf16[3,1,512,128]{3,2,1,0:T(8,128)(2,1)S(1)} %pad_maximum_fusion.4), channel_id=1, source_target_pairs={{1,0},{2,1},{3,2},{5,4},{6,5},{7,6},{9,8},{10,9},{11,10},{13,12},{... | collective-permute-start | bytes 1179656 | tf_op jit(solution)/shard_map/ppermute | solution.py:123
  71.9 10.9 %collective-permute-start.10 = (bf16[3,1,512,128]{3,2,1,0:T(8,128)(2,1)S(1)}, bf16[3,1,512,128]{3,2,1,0:T(8,128)(2,1)S(1)}, u32[]{:S(2)}, u32[]{:S(2)}) collective-permute-start(bf16[3,1,512,128]{3,2,1,0:T(8,128)(2,1)S(1)} %pad_maximum_fusion.3), channel_id=1, source_target_pairs={{0,1},{1,2},{2,3},{4,5},{5,6},{6,7},{8,9},{9,10},{10,11},{12,13},{... | collective-permute-start | bytes 1179656 | tf_op jit(solution)/shard_map/ppermute | solution.py:122
  78.3 8.2 %copy-start.5 = (bf16[4,512,128]{2,1,0:T(8,128)(2,1)}, bf16[4,512,128]{2,1,0:T(8,128)(2,1)S(1)}, u32[]{:S(2)}) copy-start(bf16[4,512,128]{2,1,0:T(8,128)(2,1)S(1)} %collective-permute-done.9.c2_ref) | copy-start | bytes 1572868
  78.3 4.6 %collective-permute-start.12 = (bf16[1,1,512,128]{3,2,1,0:T(8,128)(2,1)S(1)}, bf16[1,1,512,128]{3,2,1,0:T(8,128)(2,1)S(1)}, u32[]{:S(2)}, u32[]{:S(2)}) collective-permute-start(bf16[1,1,512,128]{3,2,1,0:T(8,128)(2,1)S(1)} %get-tuple-element.30), channel_id=1, source_target_pairs={{0,1},{1,2},{2,3},{4,5},{5,6},{6,7},{8,9},{9,10},{10,11},{12,13},{... | collective-permute-start | bytes 393224 | tf_op jit(solution)/shard_map/ppermute | solution.py:125
  80.2 6.3 %collective-permute-start.13 = (bf16[1,1,512,128]{3,2,1,0:T(8,128)(2,1)S(1)}, bf16[1,1,512,128]{3,2,1,0:T(8,128)(2,1)S(1)}, u32[]{:S(2)}, u32[]{:S(2)}) collective-permute-start(bf16[1,1,512,128]{3,2,1,0:T(8,128)(2,1)S(1)} %get-tuple-element.29), channel_id=1, source_target_pairs={{1,0},{2,1},{3,2},{5,4},{6,5},{7,6},{9,8},{10,9},{11,10},{13,12},{... | collective-permute-start | bytes 393224 | tf_op jit(solution)/shard_map/ppermute | solution.py:126
  82.8 3.7 %copy-start.8 = (bf16[3,1,512,128]{3,2,1,0:T(8,128)(2,1)}, bf16[3,1,512,128]{3,2,1,0:T(8,128)(2,1)S(1)}, u32[]{:S(2)}) copy-start(bf16[3,1,512,128]{3,2,1,0:T(8,128)(2,1)S(1)} %collective-permute-done.11.bot_a) | copy-start | bytes 1179652
  82.9 3.7 %copy-start.9 = (bf16[3,1,512,128]{3,2,1,0:T(8,128)(2,1)}, bf16[3,1,512,128]{3,2,1,0:T(8,128)(2,1)S(1)}, u32[]{:S(2)}) copy-start(bf16[3,1,512,128]{3,2,1,0:T(8,128)(2,1)S(1)} %collective-permute-done.10.top_a) | copy-start | bytes 1179652
  82.9 3.7 %copy-start.10 = (bf16[1,1,512,128]{3,2,1,0:T(8,128)(2,1)}, bf16[1,1,512,128]{3,2,1,0:T(8,128)(2,1)S(1)}, u32[]{:S(2)}) copy-start(bf16[1,1,512,128]{3,2,1,0:T(8,128)(2,1)S(1)} %collective-permute-done.12.top_b) | copy-start | bytes 393220
  86.5 0.7 copy-start.11

commit v13 on v10

--- a/solution.py
+++ b/solution.py
@@ -46,12 +46,39 @@
     return [(c2_ref, top_b, bot_b, 0), (c1_ref, top_a, bot_a, 0), (a0_ref, top_a, bot_a, 1)]
 
 
-def frame_kernel(t, with_act, *refs):
+def assemble(first, local_ref, got_ref, other_ref, buf):
+    section = lax.axis_index("section")
+    core = lax.axis_index("space") % 2
+    half = got_ref.shape[0]
+    use_local = section == 0 if first else section != 0
+
+    @pl.when(use_local)
+    def _():
+        buf[...] = local_ref[...]
+
+    @pl.when(jnp.logical_and(jnp.logical_not(use_local), core == 0))
+    def _():
+        buf[:half] = got_ref[...]
+        buf[half:] = other_ref[...]
+
+    @pl.when(jnp.logical_and(jnp.logical_not(use_local), core != 0))
+    def _():
+        buf[:half] = other_ref[...]
+        buf[half:] = got_ref[...]
+
+    return buf
+
+
+def frame_kernel(t, with_act, first, *refs):
+    buf = refs[-1]
+    refs = refs[:-1]
     if t == 1:
-        c1_ref, a0_ref, a1_ref, top_a, bot_a, base_ref, w_ref = refs[:7]
+        c1_ref, a0_ref, a1_ref, top_a, bot_a, base_ref = refs[:6]
+        w_ref = assemble(first, *refs[6:9], buf)
         sources = frame_sources(1, None, c1_ref, a0_ref, a1_ref, top_a, bot_a, None, None)
     else:
-        c2_ref, c1_ref, a0_ref, top_a, bot_a, top_b, bot_b, base_ref, w_ref = refs[:9]
+        c2_ref, c1_ref, a0_ref, top_a, bot_a, top_b, bot_b, base_ref = refs[:8]
+        w_ref = assemble(first, *refs[8:11], buf)
         sources = frame_sources(0, c2_ref, c1_ref, a0_ref, None, top_a, bot_a, top_b, bot_b)
     outs = refs[len(refs) - (2 if with_act else 1) :]
 
@@ -65,7 +92,8 @@
     conv_rows(sources, base_ref, w_ref, store)
 
 
-def pair_kernel(c2_ref, c1_ref, a0_ref, a1_ref, top_a, bot_a, top_b, bot_b, x0_ref, x1_ref, w_ref, out_ref):
+def pair_kernel(first, c2_ref, c1_ref, a0_ref, a1_ref, top_a, bot_a, top_b, bot_b, x0_ref, x1_ref, local_ref, got_ref, other_ref, out_ref, buf):
+    w_ref = assemble(first, local_ref, got_ref, other_ref, buf)
     for t, base_ref in ((1, x1_ref), (0, x0_ref)):
         sources = frame_sources(t, c2_ref, c1_ref, a0_ref, a1_ref, top_a, bot_a, top_b, bot_b)
 
@@ -84,27 +112,31 @@
     )
 
 
-def frame_conv(t, operands, base, w_mat, with_act):
+def frame_conv(t, operands, base, w_parts, with_act):
     rows, width, chans = base.shape
-    flops = 2 * rows * width * w_mat.shape[0] * w_mat.shape[1]
-    nbytes = sum(x.size * x.dtype.itemsize for x in operands) + 3 * base.size * 2 + w_mat.size * 2
+    first, local, got, other = w_parts
+    flops = 2 * rows * width * local.shape[0] * local.shape[1]
+    nbytes = sum(x.size * x.dtype.itemsize for x in operands) + 3 * base.size * 2 + local.size * 4
     shape = jax.ShapeDtypeStruct(base.shape, base.dtype)
     return pl.pallas_call(
-        functools.partial(frame_kernel, t, with_act),
+        functools.partial(frame_kernel, t, with_act, first),
         out_shape=(shape, shape) if with_act else (shape,),
+        scratch_shapes=[pltpu.VMEM(local.shape, local.dtype)],
         cost_estimate=pl.CostEstimate(flops=flops, bytes_accessed=nbytes, transcendentals=0),
-    )(*operands, base, w_mat)
+    )(*operands, base, local, got, other)
 
 
-def pair_conv(operands, x0, x1, w_mat):
+def pair_conv(operands, x0, x1, w_parts):
     rows, width, chans = x0.shape
-    flops = 4 * rows * width * w_mat.shape[0] * w_mat.shape[1]
-    nbytes = sum(x.size * x.dtype.itemsize for x in operands) + 4 * x0.size * 2 + w_mat.size * 2
+    first, local, got, other = w_parts
+    flops = 4 * rows * width * local.shape[0] * local.shape[1]
+    nbytes = sum(x.size * x.dtype.itemsize for x in operands) + 4 * x0.size * 2 + local.size * 4
     return pl.pallas_call(
-        pair_kernel,
+        functools.partial(pair_kernel, first),
         out_shape=jax.ShapeDtypeStruct((2,) + x0.shape, x0.dtype),
+        scratch_shapes=[pltpu.VMEM(local.shape, local.dtype)],
         cost_estimate=pl.CostEstimate(flops=flops, bytes_accessed=nbytes, transcendentals=0),
-    )(*operands, x0, x1, w_mat)
+    )(*operands, x0, x1, local, got, other)
 
 
 def conv_block(frames_in, acts, w_mat, with_act, merge):
@@ -138,12 +170,7 @@
     mine = lax.dynamic_slice_in_dim(local, core * half, half, axis=0)
     got = lax.ppermute(mine, "section", [(0, 1), (1, 0)])
     other = lax.ppermute(got, "space", [(i, i ^ 1) for i in range(n_space)])
-    low = jnp.where(core == 0, got, other)
-    high = jnp.where(core == 0, other, got)
-    remote = jnp.concatenate([low, high], axis=0)
-    first = jnp.where(section == 0, local, remote)
-    second = jnp.where(section == 0, remote, local)
-    return first, second
+    return (True, local, got, other), (False, local, got, other)
 
 
 def body(video, weights):

time: 92.8 us -> 88.8 us (0.957)
  other arithmetic: 5.63 us -> 2.02 us
  local copies, waits for them, and re-layouts: 8.19 us -> 6.19 us
  starting transfers between devices: 38.3 us -> 39.9 us
  waiting for transfers between devices: 19.3 us -> 17.8 us
  Pallas kernels: 20.5 us -> 21.7 us
    ppermute x2, waiting for transfers between devices: 6.97 us -> 0.67 us  [conv_block(): bot_b = lax.ppermute(c2[None, :1], 'space', up)]
    select_n x2 -> x0, other arithmetic: 2.63 us -> none  [the longest x1 1.53 us: both_taps(): second = jnp.where(section == 0, remote, local)]
    ppermute x2, waiting for transfers between devices: 0.01 us -> 2.13 us  [conv_block(): top_b = lax.ppermute(c2[None, -1:], 'space', down)]
    ppermute x2, waiting for transfers between devices: 0.82 us -> 2.86 us  [conv_block(): bot_a = lax.ppermute(jnp.stack([c1[:1], a0[:1], a1[:1]]), 'space', up)]
    ppermute x1, waiting for transfers between devices: 7.5 us -> 9.48 us  [both_taps(): got = lax.ppermute(mine, 'section', [(0, 1), (1, 0)])]
    another operation x5, local copies, waits for them, and re-layouts: 3.98 us -> 2.05 us  [conv_block(): bot_a = lax.ppermute(jnp.stack([c1[:1], a0[:1], a1[:1]]), 'space', up)]
    ppermute x2, waiting for transfers between devices: 1.24 us -> 0.01 us  [conv_block(): top_a = lax.ppermute(jnp.stack([c1[-1:], a0[-1:], a1[-1:]]), 'space', down)]
    pallas_call x3, Pallas kernels: 20.5 us -> 21.7 us  [the longest x2 12.4 us: frame_conv(): pl.pallas_call(functools.partial(frame_kernel, t, with_act, first), out_s...]
  transfers between devices with their start and end apart: 14 -> 14, of which waited for: 6 -> 6; matrix products, arithmetic and copies ran while one was open for 10% -> 5% of each run, Pallas kernels for 13% -> 14%
where the time goes in v13:
time: 88.8 us; the launch traced here: 88 us
  starting transfers between devices  39.9 us (45%)
  Pallas kernels  21.7 us (24%)
  waiting for transfers between devices  17.8 us (20%)
  local copies, waits for them, and re-layouts  6.19 us (7%)
  other arithmetic  2.02 us (2%)
    ppermute x4, starting transfers between devices, shift_tm(): return lax.ppermute(x, 'tm', [(i, i + 1) for i in range(n - 1)])  14 us
    pallas_call x2, Pallas kernels, frame_conv(): pl.pallas_call(functools.partial(frame_kernel, t, with_act, first), out_s...  12.4 us
    ppermute x1, waiting for transfers between devices, both_taps(): got = lax.ppermute(mine, 'section', [(0, 1), (1, 0)])  9.48 us
    pallas_call x1, Pallas kernels, pair_conv(): pl.pallas_call(functools.partial(pair_kernel, first), out_shape=jax.Shape...  9.22 us
    ppermute x2, starting transfers between devices, conv_block(): top_a = lax.ppermute(jnp.stack([c1[-1:], a0[-1:], a1[-1:]]), 'space', down)  7.83 us
    ppermute x2, starting transfers between devices, conv_block(): top_b = lax.ppermute(c2[None, -1:], 'space', down)  7.28 us
    ppermute x2, starting transfers between devices, conv_block(): bot_b = lax.ppermute(c2[None, :1], 'space', up)  3.84 us
    ppermute x2, starting transfers between devices, conv_block(): bot_a = lax.ppermute(jnp.stack([c1[:1], a0[:1], a1[:1]]), 'space', up)  3.84 us
  transfers between devices with their start and end apart: 14, of which 6 were waited for; matrix products, arithmetic and copies ran while one was open for 5% of the time, Pallas kernels for 14%

profile of v13, /device:TPU:1, one launch (start us, length us, event | category | flops | bytes accessed | tf_op | source)
XLA Modules:
  0.0 88.0 jit_solution(11345580215020742967)
XLA Ops:
  0.0 1.8 %fusion.7 = (bf16[4,512,128]{2,1,0:T(8,128)(2,1)S(1)}, bf16[4,512,128]{2,1,0:T(8,128)(2,1)S(1)}) fusion(bf16[1,2,4,512,128]{4,3,2,1,0:T(8,128)(2,1)} %param.2), kind=kLoop, calls=%fused_computation.11 | loop fusion | flops 3145728 | bytes 2097152 | tf_op jit(solution)/shard_map/convert_element_type | solution.py:17
  1.8 0.0 copy-start.2
  1.8 0.0 copy-start.3
  1.9 4.1 %collective-permute-start = (bf16[4,512,128]{2,1,0:T(8,128)(2,1)S(1)}, bf16[4,512,128]{2,1,0:T(8,128)(2,1)S(1)}, u32[]{:S(2)}, u32[]{:S(2)}) collective-permute-start(bf16[4,512,128]{2,1,0:T(8,128)(2,1)S(1)} %get-tuple-element.23.refs_2_), channel_id=1, source_target_pairs={{0,4},{4,8},{8,12},{1,5},{5,9},{9,13},{2,6},{6,10},{10,14},{3,7},{... | collective-permute-start | bytes 1572872 | tf_op jit(solution)/shard_map/ppermute | solution.py:13
  5.9 0.0 copy-done.4
  6.0 0.8 copy.4
  6.7 0.1 copy.7
  6.9 0.0 copy-start.1
  6.9 0.1 constant_dynamic-slice_fusion
  7.0 1.3 %collective-permute-start.6 = (bf16[576,384]{1,0:T(8,128)(2,1)S(1)}, bf16[576,384]{1,0:T(8,128)(2,1)S(1)}, u32[]{:S(2)}, u32[]{:S(2)}) collective-permute-start(bf16[576,384]{1,0:T(8,128)(2,1)S(1)} %constant_dynamic-slice_fusion), channel_id=1, source_target_pairs={{0,16},{16,0},{1,17},{17,1},{2,18},{18,2},{3,19},{19,3},{4,20},{20... | collective-permute-start | bytes 1327112 | tf_op jit(solution)/shard_map/ppermute | solution.py:171
  8.2 0.0 copy-done.2
  8.3 9.5 %collective-permute-done.6.refs_9_.refs_7_.got_ref = bf16[576,384]{1,0:T(8,128)(2,1)S(1)} collective-permute-done((bf16[576,384]{1,0:T(8,128)(2,1)S(1)}, bf16[576,384]{1,0:T(8,128)(2,1)S(1)}, u32[]{:S(2)}, u32[]{:S(2)}) %collective-permute-start.6) | collective-permute-done | bytes 442400 | tf_op jit(solution)/shard_map/ppermute | solution.py:171
  17.7 1.9 %collective-permute-start.7 = (bf16[576,384]{1,0:T(8,128)(2,1)S(1)}, bf16[576,384]{1,0:T(8,128)(2,1)S(1)}, u32[]{:S(2)}, u32[]{:S(2)}) collective-permute-start(bf16[576,384]{1,0:T(8,128)(2,1)S(1)} %collective-permute-done.6.refs_9_.refs_7_.got_ref), channel_id=1, source_target_pairs={{0,1},{1,0},{2,3},{3,2},{4,5},{5,4},{6,7},{7,6},{8,9},{9,8},{10,11... | collective-permute-start | bytes 1327112 | tf_op jit(solution)/shard_map/ppermute | solution.py:172
  19.6 0.0 collective-permute-done.refs_1_.refs_0_
  19.6 0.0 copy-done.1
  19.7 3.2 %collective-permute-start.2 = (bf16[3,1,512,128]{3,2,1,0:T(8,128)(2,1)S(1)}, bf16[3,1,512,128]{3,2,1,0:T(8,128)(2,1)S(1)}, u32[]{:S(2)}, u32[]{:S(2)}) collective-permute-start(bf16[3,1,512,128]{3,2,1,0:T(8,128)(2,1)S(1)} %pad_maximum_fusion), channel_id=1, source_target_pairs={{0,1},{1,2},{2,3},{4,5},{5,6},{6,7},{8,9},{9,10},{10,11},{12,13},{... | collective-permute-start | bytes 1179656 | tf_op jit(solution)/shard_map/ppermute | solution.py:151
  23.0 0.0 copy-done.9
  23.0 0.0 copy-done.8
  23.0 1.9 %collective-permute-start.3 = (bf16[3,1,512,128]{3,2,1,0:T(8,128)(2,1)S(1)}, bf16[3,1,512,128]{3,2,1,0:T(8,128)(2,1)S(1)}, u32[]{:S(2)}, u32[]{:S(2)}) collective-permute-start(bf16[3,1,512,128]{3,2,1,0:T(8,128)(2,1)S(1)} %pad_maximum_fusion.1), channel_id=1, source_target_pairs={{1,0},{2,1},{3,2},{5,4},{6,5},{7,6},{9,8},{10,9},{11,10},{13,12},{... | collective-permute-start | bytes 1179656 | tf_op jit(solution)/shard_map/ppermute | solution.py:152
  24.9 0.0 copy-done.3
  24.9 3.2 %collective-permute-start.1 = (bf16[4,512,128]{2,1,0:T(8,128)(2,1)S(1)}, bf16[4,512,128]{2,1,0:T(8,128)(2,1)S(1)}, u32[]{:S(2)}, u32[]{:S(2)}) collective-permute-start(bf16[4,512,128]{2,1,0:T(8,128)(2,1)S(1)} %get-tuple-element.13.refs_2_.refs_1_), channel_id=1, source_target_pairs={{0,4},{4,8},{8,12},{1,5},{5,9},{9,13},{2,6},{6,10},{10,14},{3,7},{... | collective-permute-start | bytes 1572872 | tf_op jit(solution)/shard_map/ppermute | solution.py:13
  28.1 0.0 copy-done
  28.2 1.1 %slice_bitcast_fusion = (bf16[4,512,128]{2,1,0:T(8,128)(2,1)}, bf16[4,512,128]{2,1,0:T(8,128)(2,1)}) fusion(bf16[1,2,4,512,128]{4,3,2,1,0:T(8,128)(2,1)S(1)} %copy-done), kind=kLoop, calls=%fused_computation.13 | loop fusion | bytes 2097152 | tf_op jit(solution)/shard_map/squeeze | solution.py:180
  29.2 0.0 collective-permute-done.7.refs_10_.refs_8_.other_ref
  29.2 0.0 collective-permute-done.2.refs_3_
  29.2 0.0 copy-start.11
  29.2 2.9 %collective-permute-done.3.refs_4_ = bf16[3,1,512,128]{3,2,1,0:T(8,128)(2,1)S(1)} collective-permute-done((bf16[3,1,512,128]{3,2,1,0:T(8,128)(2,1)S(1)}, bf16[3,1,512,128]{3,2,1,0:T(8,128)(2,1)S(1)}, u32[]{:S(2)}, u32[]{:S(2)}) %collective-permute-start.3) | collective-permute-done | bytes 393248 | tf_op jit(solution)/shard_map/ppermute | solution.py:152
  32.1 0.0 copy-done.10
  32.1 0.0 copy-done.11
  32.1 0.8 copy-done.12
  32.9 6.2 %shard_map.29 = (bf16[4,512,128]{2,1,0:T(8,128)(2,1)}, bf16[4,512,128]{2,1,0:T(8,128)(2,1)}) custom-call(bf16[4,512,128]{2,1,0:T(8,128)(2,1)} %copy-done.8, bf16[4,512,128]{2,1,0:T(8,128)(2,1)} %copy-done.3, bf16[4,512,128]{2,1,0:T(8,128)(2,1)} %copy-done.2, bf16[3,1,512,128]{3,2,1,0:T(8,128)(2,1)} %copy-done.11, bf16[3,1,512,128]{3,2,1,0:T(8,128)(2,1)} %copy-done.12, ...), custom_call_target="tpu_custom_call" | custom-call | flops 1811939328 | bytes 5701632 | tf_op jit(solution)/shard_map/pallas_call | solution.py:121
  39.0 3.5 %collective-permute-start.8 = (bf16[4,512,128]{2,1,0:T(8,128)(2,1)}, bf16[4,512,128]{2,1,0:T(8,128)(2,1)S(1)}, u32[]{:S(2)}, u32[]{:S(2)}) collective-permute-start(bf16[4,512,128]{2,1,0:T(8,128)(2,1)} %get-tuple-element.16.a1_ref), channel_id=1, source_target_pairs={{0,4},{4,8},{8,12},{1,5},{5,9},{9,13},{2,6},{6,10},{10,14},{3,7},{... | collective-permute-start | bytes 1572872 | tf_op jit(solution)/shard_map/ppermute | solution.py:13
  42.5 0.0 collective-permute-done.1.refs_0_
  42.5 0.0 copy-start.7
  42.6 1.9 %collective-permute-start.5 = (bf16[1,1,512,128]{3,2,1,0:T(8,128)(2,1)S(1)}, bf16[1,1,512,128]{3,2,1,0:T(8,128)(2,1)S(1)}, u32[]{:S(2)}, u32[]{:S(2)}) collective-permute-start(bf16[1,1,512,128]{3,2,1,0:T(8,128)(2,1)S(1)} %get-tuple-element.33), channel_id=1, source_target_pairs={{1,0},{2,1},{3,2},{5,4},{6,5},{7,6},{9,8},{10,9},{11,10},{13,12},{... | collective-permute-start | bytes 393224 | tf_op jit(solution)/shard_map/ppermute | solution.py:159
  44.5 3.6 %collective-permute-start.4 = (bf16[1,1,512,128]{3,2,1,0:T(8,128)(2,1)S(1)}, bf16[1,1,512,128]{3,2,1,0:T(8,128)(2,1)S(1)}, u32[]{:S(2)}, u32[]{:S(2)}) collective-permute-start(bf16[1,1,512,128]{3,2,1,0:T(8,128)(2,1)S(1)} %get-tuple-element.34), channel_id=1, source_target_pairs={{0,1},{1,2},{2,3},{4,5},{5,6},{6,7},{8,9},{9,10},{10,11},{12,13},{... | collective-permute-start | bytes 393224 | tf_op jit(solution)/shard_map/ppermute | solution.py:158
  48.2 1.0 %slice_bitcast_fusion.8 = (bf16[1,1,512,128]{3,2,1,0:T(8,128)(2,1)S(1)}, bf16[1,1,512,128]{3,2,1,0:T(8,128)(2,1)S(1)}) fusion(bf16[4,512,128]{2,1,0:T(8,128)(2,1)} %get-tuple-element.16.a1_ref), kind=kLoop, calls=%fused_computation.25 | loop fusion | bytes 524288 | tf_op jit(solution)/shard_map/stack | solution.py:152
  49.1 0.0 collective-permute-done.5.refs_6_
  49.2 0.0 copy-start.17
  49.2 0.9 %collective-permute-done.4.refs_5_ = bf16[1,1,512,128]{3,2,1,0:T(8,128)(2,1)S(1)} collective-permute-done((bf16[1,1,512,128]{3,2,1,0:T(8,128)(2,1)S(1)}, bf16[1,1,512,128]{3,2,1,0:T(8,128)(2,1)S(1)}, u32[]{:S(2)}, u32[]{:S(2)}) %collective-permute-start.4) | collective-permute-done | bytes 131104 | tf_op jit(solution)/shard_map/ppermute | solution.py:158
  50.1 0.0 copy-done.7
  50.1 0.0 copy-done.17
  50.1 0.6 copy-done.18
  50.7 6.3 %shard_map.28 = (bf16[4,512,128]{2,1,0:T(8,128)(2,1)}, bf16[4,512,128]{2,1,0:T(8,128)(2,1)}) custom-call(bf16[4,512,128]{2,1,0:T(8,128)(2,1)} %copy-done.7, bf16[4,512,128]{2,1,0:T(8,128)(2,1)} %copy-done.8, bf16[4,512,128]{2,1,0:T(8,128)(2,1)} %copy-done.3, bf16[3,1,512,128]{3,2,1,0:T(8,128)(2,1)} %copy-done.11, bf16[3,1,512,128]{3,2,1,0:T(8,128)(2,1)} %copy-done.12, ...), custom_call_target="tpu_custom_call" | custom-call | flops 1811939328 | bytes 5963776 | tf_op jit(solution)/shard_map/pallas_call | solution.py:121
  57.0 0.0 collective-permute-done.8.c1_ref
  57.0 3.2 %collective-permute-start.9 = (bf16[4,512,128]{2,1,0:T(8,128)(2,1)}, bf16[4,512,128]{2,1,0:T(8,128)(2,1)S(1)}, u32[]{:S(2)}, u32[]{:S(2)}) collective-permute-start(bf16[4,512,128]{2,1,0:T(8,128)(2,1)} %get-tuple-element.17.a0_ref), channel_id=1, source_target_pairs={{0,4},{4,8},{8,12},{1,5},{5,9},{9,13},{2,6},{6,10},{10,14},{3,7},{... | collective-permute-start | bytes 1572872 | tf_op jit(solution)/shard_map/ppermute | solution.py:13
  60.2 1.0 %slice_bitcast_fusion.9 = (bf16[1,1,512,128]{3,2,1,0:T(8,128)(2,1)S(1)}, bf16[1,1,512,128]{3,2,1,0:T(8,128)(2,1)S(1)}) fusion(bf16[4,512,128]{2,1,0:T(8,128)(2,1)} %get-tuple-element.17.a0_ref), kind=kLoop, calls=%fused_computation.26 | loop fusion | bytes 524288 | tf_op jit(solution)/shard_map/stack | solution.py:152
  61.3 4.6 %collective-permute-start.10 = (bf16[3,1,512,128]{3,2,1,0:T(8,128)(2,1)S(1)}, bf16[3,1,512,128]{3,2,1,0:T(8,128)(2,1)S(1)}, u32[]{:S(2)}, u32[]{:S(2)}) collective-permute-start(bf16[3,1,512,128]{3,2,1,0:T(8,128)(2,1)S(1)} %pad_maximum_fusion.2), channel_id=1, source_target_pairs={{0,1},{1,2},{2,3},{4,5},{5,6},{6,7},{8,9},{9,10},{10,11},{12,13},{... | collective-permute-start | bytes 1179656 | tf_op jit(solution)/shard_map/ppermute | solution.py:151
  66.0 0.0 copy-done.5
  66.0 1.9 %collective-permute-start.11 = (bf16[3,1,512,128]{3,2,1,0:T(8,128)(2,1)S(1)}, bf16[3,1,512,128]{3,2,1,0:T(8,128)(2,1)S(1)}, u32[]{:S(2)}, u32[]{:S(2)}) collective-permute-start(bf16[3,1,512,128]{3,2,1,0:T(8,128)(2,1)S(1)} %pad_maximum_fusion.3), channel_id=1, source_target_pairs={{1,0},{2,1},{3,2},{5,4},{6,5},{7,6},{9,8},{10,9},{11,10},{13,12},{... | collective-permute-start | bytes 1179656 | tf_op jit(solution)/shard_map/ppermute | solution.py:152
  67.9 2.7 %collective-permute-done.9.c2_ref = bf16[4,512,128]{2,1,0:T(8,128)(2,1)S(1)} collective-permute-done((bf16[4,512,128]{2,1,0:T(8,128)(2,1)}, bf16[4,512,128]{2,1,0:T(8,128)(2,1)S(1)}, u32[]{:S(2)}, u32[]{:S(2)}) %collective-permute-start.9) | collective-permute-done | bytes 524320 | tf_op jit(solution)/shard_map/ppermute | solution.py:13
  70.6 1.9 %collective-permute-start.13 = (bf16[1,1,512,128]{3,2,1,0:T(8,128)(2,1)S(1)}, bf16[1,1,512,128]{3,2,1,0:T(8,128)(2,1)S(1)}, u32[]{:S(2)}, u32[]{:S(2)}) collective-permute-start(bf16[1,1,512,128]{3,2,1,0:T(8,128)(2,1)S(1)} %get-tuple-element.25), channel_id=1, source_target_pairs={{1,0},{2,1},{3,2},{5,4},{6,5},{7,6},{9,8},{10,9},{11,10},{13,12},{... | collective-permute-start | bytes 393224 | tf_op jit(solution)/shard_map/ppermute | solution.py:155
  72.6 3.6 %collective-permute-start.12 = (bf16[1,1,512,128]{3,2,1,0:T(8,128)(2,1)S(1)}, bf16[1,1,512,128]{3,2,1,0:T(8,128)(2,1)S(1)}, u32[]{:S(2)}, u32[]{:S(2)}) collective-permute-start(bf16[1,1,512,128]{3,2,1,0:T(8,128)(2,1)S(1)} %get-tuple-element.26), channel_id=1, source_target_pairs={{0,1},{1,2},{2,3},{4,5},{5,6},{6,7},{8,9},{9,10},{10,11},{12,13},{... | collective-permute-start | bytes 393224 | tf_op jit(solution)/shard_map/ppermute | solution.py:154
  76.2 0.0 collective-permute-done.10.top_a
  76.2 0.0 copy-start.13
  76.2 0.0 collective-permute-done.11.bot_a
  76.2 0.0 copy-start.14
  76.3 0.7 collective-permute-done.13.bot_b
  76.9 1.2 %collective-permute-done.12.top_b = bf16[1,1,512,128]{3,2,1,0:T(8,128)(2,1)S(1)} collective-permute-done((bf16[1,1,512,128]{3,2,1,0:T(8,128)(2,1)S(1)}, bf16[1,1,512,128]{3,2,1,0:T(8,128)(2,1)S(1)}, u32[]{:S(2)}, u32[]{:S(2)}) %collective-permute-start.12) | collective-permute-done | bytes 131104 | tf_op jit(solution)/shard_map/ppermute | solution.py:154
  78.1 0.0 copy-done.6
  78.1 0.0 copy-done.13
  78.1 0.0 copy-done.14
  78.2 0.6 copy-done.16
  78.8 9.2 %shard_map.30 = bf16[2,4,512,128]{3,2,1,0:T(8,128)(2,1)} custom-call(bf16[4,512,128]{2,1,0:T(8,128)(2,1)} %copy-done.6, bf16[4,512,128]{2,1,0:T(8,128)(2,1)} %copy-done.5, bf16[4,512,128]{2,1,0:T(8,128)(2,1)} %get-tuple-element.17.a0_ref, bf16[4,512,128]{2,1,0:T(8,128)(2,1)} %get-tuple-element.16.a1_ref, bf16[3,1,512,128]{3,2,1,0:T(8,128)(2,1)} %copy-done.13, ...), custom_call_target="tpu_custom_call" | custom-call | flops 3623878656 | bytes 7012352 | tf_op jit(solution)/shard_map/pallas_call | solution.py:134
  (21 shorter events, 0.3 us)
Async XLA Ops:
  0.0 5.9 %copy-start.4 = (bf16[1,9,384,128]{3,2,1,0:T(8,128)(2,1)S(1)}, bf16[1,9,384,128]{3,2,1,0:T(8,128)(2,1)}, u32[]{:S(2)}) copy-start(bf16[1,9,384,128]{3,2,1,0:T(8,128)(2,1)} %param.3) | copy-start | bytes 2654212
  1.8 6.4 %copy-start.2 = (bf16[4,512,128]{2,1,0:T(8,128)(2,1)}, bf16[4,512,128]{2,1,0:T(8,128)(2,1)S(1)}, u32[]{:S(2)}) copy-start(bf16[4,512,128]{2,1,0:T(8,128)(2,1)S(1)} %get-tuple-element.23.refs_2_) | copy-start | bytes 1572868
  1.8 23.1 %copy-start.3 = (bf16[4,512,128]{2,1,0:T(8,128)(2,1)}, bf16[4,512,128]{2,1,0:T(8,128)(2,1)S(1)}, u32[]{:S(2)}) copy-start(bf16[4,512,128]{2,1,0:T(8,128)(2,1)S(1)} %get-tuple-element.13.refs_2_.refs_1_) | copy-start | bytes 1572868
  1.9 17.8 %collective-permute-start = (bf16[4,512,128]{2,1,0:T(8,128)(2,1)S(1)}, bf16[4,512,128]{2,1,0:T(8,128)(2,1)S(1)}, u32[]{:S(2)}, u32[]{:S(2)}) collective-permute-start(bf16[4,512,128]{2,1,0:T(8,128)(2,1)S(1)} %get-tuple-element.23.refs_2_), channel_id=1, source_target_pairs={{0,4},{4,8},{8,12},{1,5},{5,9},{9,13},{2,6},{6,10},{10,14},{3,7},{... | collective-permute-start | bytes 1572872 | tf_op jit(solution)/shard_map/ppermute | solution.py:13
  6.9 12.8 %copy-start.1 = (bf16[144,8,3,128]{3,1,2,0:T(8,128)(2,1)}, bf16[144,8,3,128]{3,1,2,0:T(8,128)(2,1)S(1)}, u32[]{:S(2)}) copy-start(bf16[144,8,3,128]{3,1,2,0:T(8,128)(2,1)S(1)} %copy.7) | copy-start | bytes 2654212
  7.0 10.8 %collective-permute-start.6 = (bf16[576,384]{1,0:T(8,128)(2,1)S(1)}, bf16[576,384]{1,0:T(8,128)(2,1)S(1)}, u32[]{:S(2)}, u32[]{:S(2)}) collective-permute-start(bf16[576,384]{1,0:T(8,128)(2,1)S(1)} %constant_dynamic-slice_fusion), channel_id=1, source_target_pairs={{0,16},{16,0},{1,17},{17,1},{2,18},{18,2},{3,19},{19,3},{4,20},{20... | collective-permute-start | bytes 1327112 | tf_op jit(solution)/shard_map/ppermute | solution.py:171
  17.7 5.2 %copy-start.9 = (bf16[576,384]{1,0:T(8,128)(2,1)}, bf16[576,384]{1,0:T(8,128)(2,1)S(1)}, u32[]{:S(2)}) copy-start(bf16[576,384]{1,0:T(8,128)(2,1)S(1)} %collective-permute-done.6.refs_9_.refs_7_.got_ref) | copy-start | bytes 1327108
  17.7 11.5 %collective-permute-start.7 = (bf16[576,384]{1,0:T(8,128)(2,1)S(1)}, bf16[576,384]{1,0:T(8,128)(2,1)S(1)}, u32[]{:S(2)}, u32[]{:S(2)}) collective-permute-start(bf16[576,384]{1,0:T(8,128)(2,1)S(1)} %collective-permute-done.6.refs_9_.refs_7_.got_ref), channel_id=1, source_target_pairs={{0,1},{1,0},{2,3},{3,2},{4,5},{5,4},{6,7},{7,6},{8,9},{9,8},{10,11... | collective-permute-start | bytes 1327112 | tf_op jit(solution)/shard_map/ppermute | solution.py:172
  19.6 3.4 %copy-start.8 = (bf16[4,512,128]{2,1,0:T(8,128)(2,1)}, bf16[4,512,128]{2,1,0:T(8,128)(2,1)S(1)}, u32[]{:S(2)}) copy-start(bf16[4,512,128]{2,1,0:T(8,128)(2,1)S(1)} %collective-permute-done.refs_1_.refs_0_) | copy-start | bytes 1572868
  19.6 8.5 %copy-start = (bf16[1,2,4,512,128]{4,3,2,1,0:T(8,128)(2,1)S(1)}, bf16[1,2,4,512,128]{4,3,2,1,0:T(8,128)(2,1)}, u32[]{:S(2)}) copy-start(bf16[1,2,4,512,128]{4,3,2,1,0:T(8,128)(2,1)} %param.2) | copy-start | bytes 3145732
  19.7 9.5 %collective-permute-start.2 = (bf16[3,1,512,128]{3,2,1,0:T(8,128)(2,1)S(1)}, bf16[3,1,512,128]{3,2,1,0:T(8,128)(2,1)S(1)}, u32[]{:S(2)}, u32[]{:S(2)}) collective-permute-start(bf16[3,1,512,128]{3,2,1,0:T(8,128)(2,1)S(1)} %pad_maximum_fusion), channel_id=1, source_target_pairs={{0,1},{1,2},{2,3},{4,5},{5,6},{6,7},{8,9},{9,10},{10,11},{12,13},{... | collective-permute-start | bytes 1179656 | tf_op jit(solution)/shard_map/ppermute | solution.py:151
  23.0 9.1 %collective-permute-start.3 = (bf16[3,1,512,128]{3,2,1,0:T(8,128)(2,1)S(1)}, bf16[3,1,512,128]{3,2,1,0:T(8,128)(2,1)S(1)}, u32[]{:S(2)}, u32[]{:S(2)}) collective-permute-start(bf16[3,1,512,128]{3,2,1,0:T(8,128)(2,1)S(1)} %pad_maximum_fusion.1), channel_id=1, source_target_pairs={{1,0},{2,1},{3,2},{5,4},{6,5},{7,6},{9,8},{10,9},{11,10},{13,12},{... | collective-permute-start | bytes 1179656 | tf_op jit(solution)/shard_map/ppermute | solution.py:152
  24.9 17.6 %collective-permute-start.1 = (bf16[4,512,128]{2,1,0:T(8,128)(2,1)S(1)}, bf16[4,512,128]{2,1,0:T(8,128)(2,1)S(1)}, u32[]{:S(2)}, u32[]{:S(2)}) collective-permute-start(bf16[4,512,128]{2,1,0:T(8,128)(2,1)S(1)} %get-tuple-element.13.refs_2_.refs_1_), channel_id=1, source_target_pairs={{0,4},{4,8},{8,12},{1,5},{5,9},{9,13},{2,6},{6,10},{10,14},{3,7},{... | collective-permute-start | bytes 1572872 | tf_op jit(solution)/shard_map/ppermute | solution.py:13
  29.2 2.9 %copy-start.10 = (bf16[576,384]{1,0:T(8,128)(2,1)}, bf16[576,384]{1,0:T(8,128)(2,1)S(1)}, u32[]{:S(2)}) copy-start(bf16[576,384]{1,0:T(8,128)(2,1)S(1)} %collective-permute-done.7.refs_10_.refs_8_.other_ref) | copy-start | bytes 1327108
  29.2 2.9 %copy-start.11 = (bf16[3,1,512,128]{3,2,1,0:T(8,128)(2,1)}, bf16[3,1,512,128]{3,2,1,0:T(8,128)(2,1)S(1)}, u32[]{:S(2)}) copy-start(bf16[3,1,512,128]{3,2,1,0:T(8,128)(2,1)S(1)} %collective-permute-done.2.refs_3_) | copy-start | bytes 1179652
  32.1 0.8 copy-start.12
  39.0 18.0 %collective-permute-start.8 = (bf16[4,512,128]{2,1,0:T(8,128)(2,1)}, bf16[4,512,128]{2,1,0:T(8,128)(2,1)S(1)}, u32[]{:S(2)}, u32[]{:S(2)}) collective-permute-start(bf16[4,512,128]{2,1,0:T(8,128)(2,1)} %get-tuple-element.16.a1_ref), channel_id=1, source_target_pairs={{0,4},{4,8},{8,12},{1,5},{5,9},{9,13},{2,6},{6,10},{10,14},{3,7},{... | collective-permute-start | bytes 1572872 | tf_op jit(solution)/shard_map/ppermute | solution.py:13
  42.5 7.5 %copy-start.7 = (bf16[4,512,128]{2,1,0:T(8,128)(2,1)}, bf16[4,512,128]{2,1,0:T(8,128)(2,1)S(1)}, u32[]{:S(2)}) copy-start(bf16[4,512,128]{2,1,0:T(8,128)(2,1)S(1)} %collective-permute-done.1.refs_0_) | copy-start | bytes 1572868
  42.6 6.6 %collective-permute-start.5 = (bf16[1,1,512,128]{3,2,1,0:T(8,128)(2,1)S(1)}, bf16[1,1,512,128]{3,2,1,0:T(8,128)(2,1)S(1)}, u32[]{:S(2)}, u32[]{:S(2)}) collective-permute-start(bf16[1,1,512,128]{3,2,1,0:T(8,128)(2,1)S(1)} %get-tuple-element.33), channel_id=1, source_target_pairs={{1,0},{2,1},{3,2},{5,4},{6,5},{7,6},{9,8},{10,9},{11,10},{13,12},{... | collective-permute-start | bytes 393224 | tf_op jit(solution)/shard_map/ppermute | solution.py:159
  44.5 5.6 %collective-permute-start.4 = (bf16[1,1,512,128]{3,2,1,0:T(8,128)(2,1)S(1)}, bf16[1,1,512,128]{3,2,1,0:T(8,128)(2,1)S(1)}, u32[]{:S(2)}, u32[]{:S(2)}) collective-permute-start(bf16[1,1,512,128]{3,2,1,0:T(8,128)(2,1)S(1)} %get-tuple-element.34), channel_id=1, source_target_pairs={{0,1},{1,2},{2,3},{4,5},{5,6},{6,7},{8,9},{9,10},{10,11},{12,13},{... | collective-permute-start | bytes 393224 | tf_op jit(solution)/shard_map/ppermute | solution.py:158
  49.2 0.9 %copy-start.17 = (bf16[1,1,512,128]{3,2,1,0:T(8,128)(2,1)}, bf16[1,1,512,128]{3,2,1,0:T(8,128)(2,1)S(1)}, u32[]{:S(2)}) copy-start(bf16[1,1,512,128]{3,2,1,0:T(8,128)(2,1)S(1)} %collective-permute-done.5.refs_6_) | copy-start | bytes 393220
  50.1 0.7 copy-start.18
  57.0 9.0 %copy-start.5 = (bf16[4,512,128]{2,1,0:T(8,128)(2,1)}, bf16[4,512,128]{2,1,0:T(8,128)(2,1)S(1)}, u32[]{:S(2)}) copy-start(bf16[4,512,128]{2,1,0:T(8,128)(2,1)S(1)} %collective-permute-done.8.c1_ref) | copy-start | bytes 1572868
  57.0 13.6 %collective-permute-start.9 = (bf16[4,512,128]{2,1,0:T(8,128)(2,1)}, bf16[4,512,128]{2,1,0:T(8,128)(2,1)S(1)}, u32[]{:S(2)}, u32[]{:S(2)}) collective-permute-start(bf16[4,512,128]{2,1,0:T(8,128)(2,1)} %get-tuple-element.17.a0_ref), channel_id=1, source_target_pairs={{0,4},{4,8},{8,12},{1,5},{5,9},{9,13},{2,6},{6,10},{10,14},{3,7},{... | collective-permute-start | bytes 1572872 | tf_op jit(solution)/shard_map/ppermute | solution.py:13
  61.3 14.9 %collective-permute-start.10 = (bf16[3,1,512,128]{3,2,1,0:T(8,128)(2,1)S(1)}, bf16[3,1,512,128]{3,2,1,0:T(8,128)(2,1)S(1)}, u32[]{:S(2)}, u32[]{:S(2)}) collective-permute-start(bf16[3,1,512,128]{3,2,1,0:T(8,128)(2,1)S(1)} %pad_maximum_fusion.2), channel_id=1, source_target_pairs={{0,1},{1,2},{2,3},{4,5},{5,6},{6,7},{8,9},{9,10},{10,11},{12,13},{... | collective-permute-start | bytes 1179656 | tf_op jit(solution)/shard_map/ppermute | solution.py:151
  66.0 10.2 %collective-permute-start.11 = (bf16[3,1,512,128]{3,2,1,0:T(8,128)(2,1)S(1)}, bf16[3,1,512,128]{3,2,1,0:T(8,128)(2,1)S(1)}, u32[]{:S(2)}, u32[]{:S(2)}) collective-permute-start(bf16[3,1,512,128]{3,2,1,0:T(8,128)(2,1)S(1)} %pad_maximum_fusion.3), channel_id=1, source_target_pairs={{1,0},{2,1},{3,2},{5,4},{6,5},{7,6},{9,8},{10,9},{11,10},{13,12},{... | collective-permute-start | bytes 1179656 | tf_op jit(solution)/shard_map/ppermute | solution.py:152
  70.6 7.5 %copy-start.6 = (bf16[4,512,128]{2,1,0:T(8,128)(2,1)}, bf16[4,512,128]{2,1,0:T(8,128)(2,1)S(1)}, u32[]{:S(2)}) copy-start(bf16[4,512,128]{2,1,0:T(8,128)(2,1)S(1)} %collective-permute-done.9.c2_ref) | copy-start | bytes 1572868
  70.6 6.3 %collective-permute-start.13 = (bf16[1,1,512,128]{3,2,1,0:T(8,128)(2,1)S(1)}, bf16[1,1,512,128]{3,2,1,0:T(8,128)(2,1)S(1)}, u32[]{:S(2)}, u32[]{:S(2)}) collective-permute-start(bf16[1,1,512,128]{3,2,1,0:T(8,128)(2,1)S(1)} %get-tuple-element.25), channel_id=1, source_target_pairs={{1,0},{2,1},{3,2},{5,4},{6,5},{7,6},{9,8},{10,9},{11,10},{13,12},{... | collective-permute-start | bytes 393224 | tf_op jit(solution)/shard_map/ppermute | solution.py:155
  72.6 5.6 %collective-permute-start.12 = (bf16[1,1,512,128]{3,2,1,0:T(8,128)(2,1)S(1)}, bf16[1,1,512,128]{3,2,1,0:T(8,128)(2,1)S(1)}, u32[]{:S(2)}, u32[]{:S(2)}) collective-permute-start(bf16[1,1,512,128]{3,2,1,0:T(8,128)(2,1)S(1)} %get-tuple-element.26), channel_id=1, source_target_pairs={{0,1},{1,2},{2,3},{4,5},{5,6},{6,7},{8,9},{9,10},{10,11},{12,13},{... | collective-permute-start | bytes 393224 | tf_op jit(solution)/shard_map/ppermute | solution.py:154
  76.2 1.9 %copy-start.13 = (bf16[3,1,512,128]{3,2,1,0:T(8,128)(2,1)}, bf16[3,1,512,128]{3,2,1,0:T(8,128)(2,1)S(1)}, u32[]{:S(2)}) copy-start(bf16[3,1,512,128]{3,2,1,0:T(8,128)(2,1)S(1)} %collective-permute-done.10.top_a) | copy-start | bytes 1179652
  76.2 1.9 %copy-start.14 = (bf16[3,1,512,128]{3,2,1,0:T(8,128)(2,1)}, bf16[3,1,512,128]{3,2,1,0:T(8,128)(2,1)S(1)}, u32[]{:S(2)}) copy-start(bf16[3,1,512,128]{3,2,1,0:T(8,128)(2,1)S(1)} %collective-permute-done.11.bot_a) | copy-start | bytes 1179652
  76.9 1.2 %copy-start.15 = (bf16[1,1,512,128]{3,2,1,0:T(8,128)(2,1)}, bf16[1,1,512,128]{3,2,1,0:T(8,128)(2,1)S(1)}, u32[]{:S(2)}) copy-start(bf16[1,1,512,128]{3,2,1,0:T(8,128)(2,1)S(1)} %collective-permute-done.13.bot_b) | copy-start | bytes 393220
  78.1 0.6 copy-start.16

commit v14 on v13

--- a/solution.py
+++ b/solution.py
@@ -69,7 +69,7 @@
     return buf
 
 
-def frame_kernel(t, with_act, first, *refs):
+def frame_kernel(t, with_act, first, indexed, *refs):
     buf = refs[-1]
     refs = refs[:-1]
     if t == 1:
@@ -81,6 +81,8 @@
         w_ref = assemble(first, *refs[8:11], buf)
         sources = frame_sources(0, c2_ref, c1_ref, a0_ref, None, top_a, bot_a, top_b, bot_b)
     outs = refs[len(refs) - (2 if with_act else 1) :]
+    if indexed:
+        base_ref = base_ref.at[t]
 
     def store(h, value):
         out = value.astype(outs[0].dtype)
@@ -112,14 +114,14 @@
     )
 
 
-def frame_conv(t, operands, base, w_parts, with_act):
-    rows, width, chans = base.shape
+def frame_conv(t, operands, base, w_parts, with_act, indexed=False):
+    rows, width, chans = base.shape[-3:]
     first, local, got, other = w_parts
     flops = 2 * rows * width * local.shape[0] * local.shape[1]
     nbytes = sum(x.size * x.dtype.itemsize for x in operands) + 3 * base.size * 2 + local.size * 4
-    shape = jax.ShapeDtypeStruct(base.shape, base.dtype)
+    shape = jax.ShapeDtypeStruct(base.shape[-3:], base.dtype)
     return pl.pallas_call(
-        functools.partial(frame_kernel, t, with_act, first),
+        functools.partial(frame_kernel, t, with_act, first, indexed),
         out_shape=(shape, shape) if with_act else (shape,),
         scratch_shapes=[pltpu.VMEM(local.shape, local.dtype)],
         cost_estimate=pl.CostEstimate(flops=flops, bytes_accessed=nbytes, transcendentals=0),
@@ -139,7 +141,7 @@
     )(*operands, x0, x1, local, got, other)
 
 
-def conv_block(frames_in, acts, w_mat, with_act, merge):
+def conv_block(frames_in, acts, w_mat, with_act, merge, whole=None):
     x0, x1 = frames_in
     a0, a1 = acts
     n = lax.axis_size("space")
@@ -154,10 +156,10 @@
         top_b = lax.ppermute(c2[None, -1:], "space", down)
         bot_b = lax.ppermute(c2[None, :1], "space", up)
         return pair_conv((c2, c1, a0, a1, top_a, bot_a, top_b, bot_b), x0, x1, w_mat)
-    outs1 = frame_conv(1, (c1, a0, a1, top_a, bot_a), x1, w_mat, with_act)
+    outs1 = frame_conv(1, (c1, a0, a1, top_a, bot_a), whole, w_mat, with_act, True)
     top_b = lax.ppermute(c2[None, -1:], "space", down)
     bot_b = lax.ppermute(c2[None, :1], "space", up)
-    outs0 = frame_conv(0, (c2, c1, a0, top_a, bot_a, top_b, bot_b), x0, w_mat, with_act)
+    outs0 = frame_conv(0, (c2, c1, a0, top_a, bot_a, top_b, bot_b), whole, w_mat, with_act, True)
     return outs0, outs1
 
 
@@ -180,7 +182,7 @@
     x0, x1 = clip[0], clip[1]
     a1 = silu(x1)
     a0 = silu(x0)
-    (h0, s0), (h1, s1) = conv_block((x0, x1), (a0, a1), first, True, False)
+    (h0, s0), (h1, s1) = conv_block((x0, x1), (a0, a1), first, True, False, clip)
     whole = conv_block((h0, h1), (s0, s1), second, False, True)
     return whole[None]
 

time: 88.8 us -> 89.5 us (level)
  waiting for transfers between devices: 17.8 us -> 19.5 us
  local copies, waits for them, and re-layouts: 6.19 us -> 5.12 us
    squeeze x1 -> x0, local copies, waits for them, and re-layouts: 1.06 us -> none  [body(): x0, x1 = (clip[0], clip[1])]
    ppermute x2, waiting for transfers between devices: 2.86 us -> 3.91 us  [conv_block(): bot_a = lax.ppermute(jnp.stack([c1[:1], a0[:1], a1[:1]]), 'space', up)]
    unnamed x39 -> x37, local copies, waits for them, and re-layouts: 2.23 us -> 2.22 us
  transfers between devices with their start and end apart: 14 -> 14, of which waited for: 6 -> 6; matrix products, arithmetic and copies ran while one was open for 5% -> 4% of each run, Pallas kernels for 14% -> 14%
where the time goes in v14:
time: 89.5 us; the launch traced here: 88.7 us
  starting transfers between devices  39.8 us (44%)
  Pallas kernels  22 us (25%)
  waiting for transfers between devices  19.5 us (22%)
  local copies, waits for them, and re-layouts  5.12 us (6%)
  other arithmetic  2.02 us (2%)
    ppermute x4, starting transfers between devices, shift_tm(): return lax.ppermute(x, 'tm', [(i, i + 1) for i in range(n - 1)])  14 us
    pallas_call x2, Pallas kernels, frame_conv(): pl.pallas_call(functools.partial(frame_kernel, t, with_act, first, indexe...  12.8 us
    ppermute x1, waiting for transfers between devices, both_taps(): got = lax.ppermute(mine, 'section', [(0, 1), (1, 0)])  9.48 us
    pallas_call x1, Pallas kernels, pair_conv(): pl.pallas_call(functools.partial(pair_kernel, first), out_shape=jax.Shape...  9.22 us
    ppermute x2, starting transfers between devices, conv_block(): top_a = lax.ppermute(jnp.stack([c1[-1:], a0[-1:], a1[-1:]]), 'space', down)  7.69 us
    ppermute x2, starting transfers between devices, conv_block(): top_b = lax.ppermute(c2[None, -1:], 'space', down)  7.28 us
    ppermute x2, waiting for transfers between devices, conv_block(): bot_a = lax.ppermute(jnp.stack([c1[:1], a0[:1], a1[:1]]), 'space', up)  3.91 us
    ppermute x2, starting transfers between devices, conv_block(): bot_a = lax.ppermute(jnp.stack([c1[:1], a0[:1], a1[:1]]), 'space', up)  3.84 us
  transfers between devices with their start and end apart: 14, of which 6 were waited for; matrix products, arithmetic and copies ran while one was open for 4% of the time, Pallas kernels for 14%

profile of v14, /device:TPU:1, one launch (start us, length us, event | category | flops | bytes accessed | tf_op | source)
XLA Modules:
  0.0 88.7 jit_solution(17489872646190539878)
XLA Ops:
  0.0 1.8 %fusion.7 = (bf16[4,512,128]{2,1,0:T(8,128)(2,1)S(1)}, bf16[4,512,128]{2,1,0:T(8,128)(2,1)S(1)}) fusion(bf16[1,2,4,512,128]{4,3,2,1,0:T(8,128)(2,1)} %param.2), kind=kLoop, calls=%fused_computation.11 | loop fusion | flops 3145728 | bytes 2097152 | tf_op jit(solution)/shard_map/convert_element_type | solution.py:17
  1.8 0.0 copy-start.1
  1.8 0.0 copy-start.2
  1.9 4.1 %collective-permute-start = (bf16[4,512,128]{2,1,0:T(8,128)(2,1)S(1)}, bf16[4,512,128]{2,1,0:T(8,128)(2,1)S(1)}, u32[]{:S(2)}, u32[]{:S(2)}) collective-permute-start(bf16[4,512,128]{2,1,0:T(8,128)(2,1)S(1)} %get-tuple-element.21.refs_2_), channel_id=1, source_target_pairs={{0,4},{4,8},{8,12},{1,5},{5,9},{9,13},{2,6},{6,10},{10,14},{3,7},{... | collective-permute-start | bytes 1572872 | tf_op jit(solution)/shard_map/ppermute | solution.py:13
  5.9 0.0 copy-done.3
  6.0 0.8 copy.4
  6.7 0.1 copy.7
  6.9 0.0 copy-start
  6.9 0.1 constant_dynamic-slice_fusion
  7.0 1.3 %collective-permute-start.6 = (bf16[576,384]{1,0:T(8,128)(2,1)S(1)}, bf16[576,384]{1,0:T(8,128)(2,1)S(1)}, u32[]{:S(2)}, u32[]{:S(2)}) collective-permute-start(bf16[576,384]{1,0:T(8,128)(2,1)S(1)} %constant_dynamic-slice_fusion), channel_id=1, source_target_pairs={{0,16},{16,0},{1,17},{17,1},{2,18},{18,2},{3,19},{19,3},{4,20},{20... | collective-permute-start | bytes 1327112 | tf_op jit(solution)/shard_map/ppermute | solution.py:173
  8.2 0.0 copy-done.1
  8.3 9.5 %collective-permute-done.6.refs_9_.refs_7_.got_ref = bf16[576,384]{1,0:T(8,128)(2,1)S(1)} collective-permute-done((bf16[576,384]{1,0:T(8,128)(2,1)S(1)}, bf16[576,384]{1,0:T(8,128)(2,1)S(1)}, u32[]{:S(2)}, u32[]{:S(2)}) %collective-permute-start.6) | collective-permute-done | bytes 442400 | tf_op jit(solution)/shard_map/ppermute | solution.py:173
  17.7 1.9 %collective-permute-start.7 = (bf16[576,384]{1,0:T(8,128)(2,1)S(1)}, bf16[576,384]{1,0:T(8,128)(2,1)S(1)}, u32[]{:S(2)}, u32[]{:S(2)}) collective-permute-start(bf16[576,384]{1,0:T(8,128)(2,1)S(1)} %collective-permute-done.6.refs_9_.refs_7_.got_ref), channel_id=1, source_target_pairs={{0,1},{1,0},{2,3},{3,2},{4,5},{5,4},{6,7},{7,6},{8,9},{9,8},{10,11... | collective-permute-start | bytes 1327112 | tf_op jit(solution)/shard_map/ppermute | solution.py:174
  19.6 0.0 collective-permute-done.refs_1_.refs_0_
  19.6 0.0 copy-done
  19.7 3.1 %collective-permute-start.2 = (bf16[3,1,512,128]{3,2,1,0:T(8,128)(2,1)S(1)}, bf16[3,1,512,128]{3,2,1,0:T(8,128)(2,1)S(1)}, u32[]{:S(2)}, u32[]{:S(2)}) collective-permute-start(bf16[3,1,512,128]{3,2,1,0:T(8,128)(2,1)S(1)} %pad_maximum_fusion), channel_id=1, source_target_pairs={{0,1},{1,2},{2,3},{4,5},{5,6},{6,7},{8,9},{9,10},{10,11},{12,13},{... | collective-permute-start | bytes 1179656 | tf_op jit(solution)/shard_map/ppermute | solution.py:153
  22.8 0.0 copy-done.8
  22.8 0.0 copy-done.7
  22.8 1.9 %collective-permute-start.3 = (bf16[3,1,512,128]{3,2,1,0:T(8,128)(2,1)S(1)}, bf16[3,1,512,128]{3,2,1,0:T(8,128)(2,1)S(1)}, u32[]{:S(2)}, u32[]{:S(2)}) collective-permute-start(bf16[3,1,512,128]{3,2,1,0:T(8,128)(2,1)S(1)} %pad_maximum_fusion.1), channel_id=1, source_target_pairs={{1,0},{2,1},{3,2},{5,4},{6,5},{7,6},{9,8},{10,9},{11,10},{13,12},{... | collective-permute-start | bytes 1179656 | tf_op jit(solution)/shard_map/ppermute | solution.py:154
  24.8 0.0 copy-done.2
  24.8 3.2 %collective-permute-start.1 = (bf16[4,512,128]{2,1,0:T(8,128)(2,1)S(1)}, bf16[4,512,128]{2,1,0:T(8,128)(2,1)S(1)}, u32[]{:S(2)}, u32[]{:S(2)}) collective-permute-start(bf16[4,512,128]{2,1,0:T(8,128)(2,1)S(1)} %get-tuple-element.13.refs_2_.refs_1_), channel_id=1, source_target_pairs={{0,4},{4,8},{8,12},{1,5},{5,9},{9,13},{2,6},{6,10},{10,14},{3,7},{... | collective-permute-start | bytes 1572872 | tf_op jit(solution)/shard_map/ppermute | solution.py:13
  28.0 0.0 collective-permute-done.7.refs_10_.refs_8_.other_ref
  28.0 0.0 copy-start.9
  28.0 0.0 collective-permute-done.2.refs_3_
  28.0 0.0 copy-start.10
  28.0 3.9 %collective-permute-done.3.refs_4_ = bf16[3,1,512,128]{3,2,1,0:T(8,128)(2,1)S(1)} collective-permute-done((bf16[3,1,512,128]{3,2,1,0:T(8,128)(2,1)S(1)}, bf16[3,1,512,128]{3,2,1,0:T(8,128)(2,1)S(1)}, u32[]{:S(2)}, u32[]{:S(2)}) %collective-permute-start.3) | collective-permute-done | bytes 393248 | tf_op jit(solution)/shard_map/ppermute | solution.py:154
  31.9 0.0 copy-done.9
  32.0 0.0 copy-done.10
  32.0 0.7 copy-done.11
  32.7 6.3 %shard_map.29 = (bf16[4,512,128]{2,1,0:T(8,128)(2,1)}, bf16[4,512,128]{2,1,0:T(8,128)(2,1)}) custom-call(bf16[4,512,128]{2,1,0:T(8,128)(2,1)} %copy-done.7, bf16[4,512,128]{2,1,0:T(8,128)(2,1)} %copy-done.2, bf16[4,512,128]{2,1,0:T(8,128)(2,1)} %copy-done.1, bf16[3,1,512,128]{3,2,1,0:T(8,128)(2,1)} %copy-done.10, bf16[3,1,512,128]{3,2,1,0:T(8,128)(2,1)} %copy-done.11, ...), custom_call_target="tpu_custom_call" | custom-call | flops 1811939328 | bytes 7274496 | tf_op jit(solution)/shard_map/pallas_call | solution.py:123
  39.0 3.5 %collective-permute-start.8 = (bf16[4,512,128]{2,1,0:T(8,128)(2,1)}, bf16[4,512,128]{2,1,0:T(8,128)(2,1)S(1)}, u32[]{:S(2)}, u32[]{:S(2)}) collective-permute-start(bf16[4,512,128]{2,1,0:T(8,128)(2,1)} %get-tuple-element.16.a1_ref), channel_id=1, source_target_pairs={{0,4},{4,8},{8,12},{1,5},{5,9},{9,13},{2,6},{6,10},{10,14},{3,7},{... | collective-permute-start | bytes 1572872 | tf_op jit(solution)/shard_map/ppermute | solution.py:13
  42.5 0.0 collective-permute-done.1.refs_0_
  42.5 0.0 copy-start.6
  42.6 1.9 %collective-permute-start.5 = (bf16[1,1,512,128]{3,2,1,0:T(8,128)(2,1)S(1)}, bf16[1,1,512,128]{3,2,1,0:T(8,128)(2,1)S(1)}, u32[]{:S(2)}, u32[]{:S(2)}) collective-permute-start(bf16[1,1,512,128]{3,2,1,0:T(8,128)(2,1)S(1)} %get-tuple-element.31), channel_id=1, source_target_pairs={{1,0},{2,1},{3,2},{5,4},{6,5},{7,6},{9,8},{10,9},{11,10},{13,12},{... | collective-permute-start | bytes 393224 | tf_op jit(solution)/shard_map/ppermute | solution.py:161
  44.5 3.6 %collective-permute-start.4 = (bf16[1,1,512,128]{3,2,1,0:T(8,128)(2,1)S(1)}, bf16[1,1,512,128]{3,2,1,0:T(8,128)(2,1)S(1)}, u32[]{:S(2)}, u32[]{:S(2)}) collective-permute-start(bf16[1,1,512,128]{3,2,1,0:T(8,128)(2,1)S(1)} %get-tuple-element.32), channel_id=1, source_target_pairs={{0,1},{1,2},{2,3},{4,5},{5,6},{6,7},{8,9},{9,10},{10,11},{12,13},{... | collective-permute-start | bytes 393224 | tf_op jit(solution)/shard_map/ppermute | solution.py:160
  48.1 1.0 %slice_bitcast_fusion.6 = (bf16[1,1,512,128]{3,2,1,0:T(8,128)(2,1)S(1)}, bf16[1,1,512,128]{3,2,1,0:T(8,128)(2,1)S(1)}) fusion(bf16[4,512,128]{2,1,0:T(8,128)(2,1)} %get-tuple-element.16.a1_ref), kind=kLoop, calls=%fused_computation.23 | loop fusion | bytes 524288 | tf_op jit(solution)/shard_map/stack | solution.py:154
  49.1 0.0 collective-permute-done.5.refs_6_
  49.1 0.0 copy-start.16
  49.1 0.9 %collective-permute-done.4.refs_5_ = bf16[1,1,512,128]{3,2,1,0:T(8,128)(2,1)S(1)} collective-permute-done((bf16[1,1,512,128]{3,2,1,0:T(8,128)(2,1)S(1)}, bf16[1,1,512,128]{3,2,1,0:T(8,128)(2,1)S(1)}, u32[]{:S(2)}, u32[]{:S(2)}) %collective-permute-start.4) | collective-permute-done | bytes 131104 | tf_op jit(solution)/shard_map/ppermute | solution.py:160
  50.1 0.0 copy-done.6
  50.1 0.0 copy-done.16
  50.1 0.6 copy-done.17
  50.7 6.4 %shard_map.28 = (bf16[4,512,128]{2,1,0:T(8,128)(2,1)}, bf16[4,512,128]{2,1,0:T(8,128)(2,1)}) custom-call(bf16[4,512,128]{2,1,0:T(8,128)(2,1)} %copy-done.6, bf16[4,512,128]{2,1,0:T(8,128)(2,1)} %copy-done.7, bf16[4,512,128]{2,1,0:T(8,128)(2,1)} %copy-done.2, bf16[3,1,512,128]{3,2,1,0:T(8,128)(2,1)} %copy-done.10, bf16[3,1,512,128]{3,2,1,0:T(8,128)(2,1)} %copy-done.11, ...), custom_call_target="tpu_custom_call" | custom-call | flops 1811939328 | bytes 7536640 | tf_op jit(solution)/shard_map/pallas_call | solution.py:123
  57.2 0.0 collective-permute-done.8.c1_ref
  57.2 3.2 %collective-permute-start.9 = (bf16[4,512,128]{2,1,0:T(8,128)(2,1)}, bf16[4,512,128]{2,1,0:T(8,128)(2,1)S(1)}, u32[]{:S(2)}, u32[]{:S(2)}) collective-permute-start(bf16[4,512,128]{2,1,0:T(8,128)(2,1)} %get-tuple-element.17.a0_ref), channel_id=1, source_target_pairs={{0,4},{4,8},{8,12},{1,5},{5,9},{9,13},{2,6},{6,10},{10,14},{3,7},{... | collective-permute-start | bytes 1572872 | tf_op jit(solution)/shard_map/ppermute | solution.py:13
  60.4 1.0 %slice_bitcast_fusion.7 = (bf16[1,1,512,128]{3,2,1,0:T(8,128)(2,1)S(1)}, bf16[1,1,512,128]{3,2,1,0:T(8,128)(2,1)S(1)}) fusion(bf16[4,512,128]{2,1,0:T(8,128)(2,1)} %get-tuple-element.17.a0_ref), kind=kLoop, calls=%fused_computation.24 | loop fusion | bytes 524288 | tf_op jit(solution)/shard_map/stack | solution.py:154
  61.4 4.6 %collective-permute-start.10 = (bf16[3,1,512,128]{3,2,1,0:T(8,128)(2,1)S(1)}, bf16[3,1,512,128]{3,2,1,0:T(8,128)(2,1)S(1)}, u32[]{:S(2)}, u32[]{:S(2)}) collective-permute-start(bf16[3,1,512,128]{3,2,1,0:T(8,128)(2,1)S(1)} %pad_maximum_fusion.2), channel_id=1, source_target_pairs={{0,1},{1,2},{2,3},{4,5},{5,6},{6,7},{8,9},{9,10},{10,11},{12,13},{... | collective-permute-start | bytes 1179656 | tf_op jit(solution)/shard_map/ppermute | solution.py:153
  66.1 0.0 copy-done.4
  66.2 1.9 %collective-permute-start.11 = (bf16[3,1,512,128]{3,2,1,0:T(8,128)(2,1)S(1)}, bf16[3,1,512,128]{3,2,1,0:T(8,128)(2,1)S(1)}, u32[]{:S(2)}, u32[]{:S(2)}) collective-permute-start(bf16[3,1,512,128]{3,2,1,0:T(8,128)(2,1)S(1)} %pad_maximum_fusion.3), channel_id=1, source_target_pairs={{1,0},{2,1},{3,2},{5,4},{6,5},{7,6},{9,8},{10,9},{11,10},{13,12},{... | collective-permute-start | bytes 1179656 | tf_op jit(solution)/shard_map/ppermute | solution.py:154
  68.1 3.3 %collective-permute-done.9.c2_ref = bf16[4,512,128]{2,1,0:T(8,128)(2,1)S(1)} collective-permute-done((bf16[4,512,128]{2,1,0:T(8,128)(2,1)}, bf16[4,512,128]{2,1,0:T(8,128)(2,1)S(1)}, u32[]{:S(2)}, u32[]{:S(2)}) %collective-permute-start.9) | collective-permute-done | bytes 524320 | tf_op jit(solution)/shard_map/ppermute | solution.py:13
  71.4 1.9 %collective-permute-start.13 = (bf16[1,1,512,128]{3,2,1,0:T(8,128)(2,1)S(1)}, bf16[1,1,512,128]{3,2,1,0:T(8,128)(2,1)S(1)}, u32[]{:S(2)}, u32[]{:S(2)}) collective-permute-start(bf16[1,1,512,128]{3,2,1,0:T(8,128)(2,1)S(1)} %get-tuple-element.23), channel_id=1, source_target_pairs={{1,0},{2,1},{3,2},{5,4},{6,5},{7,6},{9,8},{10,9},{11,10},{13,12},{... | collective-permute-start | bytes 393224 | tf_op jit(solution)/shard_map/ppermute | solution.py:157
  73.3 3.6 %collective-permute-start.12 = (bf16[1,1,512,128]{3,2,1,0:T(8,128)(2,1)S(1)}, bf16[1,1,512,128]{3,2,1,0:T(8,128)(2,1)S(1)}, u32[]{:S(2)}, u32[]{:S(2)}) collective-permute-start(bf16[1,1,512,128]{3,2,1,0:T(8,128)(2,1)S(1)} %get-tuple-element.24), channel_id=1, source_target_pairs={{0,1},{1,2},{2,3},{4,5},{5,6},{6,7},{8,9},{9,10},{10,11},{12,13},{... | collective-permute-start | bytes 393224 | tf_op jit(solution)/shard_map/ppermute | solution.py:156
  76.9 0.0 collective-permute-done.10.top_a
  76.9 0.0 copy-start.12
  77.0 0.0 collective-permute-done.11.bot_a
  77.0 0.0 copy-start.13
  77.0 0.7 collective-permute-done.13.bot_b
  77.6 1.2 %collective-permute-done.12.top_b = bf16[1,1,512,128]{3,2,1,0:T(8,128)(2,1)S(1)} collective-permute-done((bf16[1,1,512,128]{3,2,1,0:T(8,128)(2,1)S(1)}, bf16[1,1,512,128]{3,2,1,0:T(8,128)(2,1)S(1)}, u32[]{:S(2)}, u32[]{:S(2)}) %collective-permute-start.12) | collective-permute-done | bytes 131104 | tf_op jit(solution)/shard_map/ppermute | solution.py:156
  78.9 0.0 copy-done.5
  78.9 0.0 copy-done.12
  78.9 0.0 copy-done.13
  78.9 0.0 copy-done.14
  78.9 0.6 copy-done.15
  79.5 9.2 %shard_map.30 = bf16[2,4,512,128]{3,2,1,0:T(8,128)(2,1)} custom-call(bf16[4,512,128]{2,1,0:T(8,128)(2,1)} %copy-done.5, bf16[4,512,128]{2,1,0:T(8,128)(2,1)} %copy-done.4, bf16[4,512,128]{2,1,0:T(8,128)(2,1)} %get-tuple-element.17.a0_ref, bf16[4,512,128]{2,1,0:T(8,128)(2,1)} %get-tuple-element.16.a1_ref, bf16[3,1,512,128]{3,2,1,0:T(8,128)(2,1)} %copy-done.12, ...), custom_call_target="tpu_custom_call" | custom-call | flops 3623878656 | bytes 7012352 | tf_op jit(solution)/shard_map/pallas_call | solution.py:136
  (18 shorter events, 0.3 us)
Async XLA Ops:
  0.0 5.9 %copy-start.3 = (bf16[1,9,384,128]{3,2,1,0:T(8,128)(2,1)S(1)}, bf16[1,9,384,128]{3,2,1,0:T(8,128)(2,1)}, u32[]{:S(2)}) copy-start(bf16[1,9,384,128]{3,2,1,0:T(8,128)(2,1)} %param.3) | copy-start | bytes 2654212
  1.8 6.4 %copy-start.1 = (bf16[4,512,128]{2,1,0:T(8,128)(2,1)}, bf16[4,512,128]{2,1,0:T(8,128)(2,1)S(1)}, u32[]{:S(2)}) copy-start(bf16[4,512,128]{2,1,0:T(8,128)(2,1)S(1)} %get-tuple-element.21.refs_2_) | copy-start | bytes 1572868
  1.8 22.9 %copy-start.2 = (bf16[4,512,128]{2,1,0:T(8,128)(2,1)}, bf16[4,512,128]{2,1,0:T(8,128)(2,1)S(1)}, u32[]{:S(2)}) copy-start(bf16[4,512,128]{2,1,0:T(8,128)(2,1)S(1)} %get-tuple-element.13.refs_2_.refs_1_) | copy-start | bytes 1572868
  1.9 17.8 %collective-permute-start = (bf16[4,512,128]{2,1,0:T(8,128)(2,1)S(1)}, bf16[4,512,128]{2,1,0:T(8,128)(2,1)S(1)}, u32[]{:S(2)}, u32[]{:S(2)}) collective-permute-start(bf16[4,512,128]{2,1,0:T(8,128)(2,1)S(1)} %get-tuple-element.21.refs_2_), channel_id=1, source_target_pairs={{0,4},{4,8},{8,12},{1,5},{5,9},{9,13},{2,6},{6,10},{10,14},{3,7},{... | collective-permute-start | bytes 1572872 | tf_op jit(solution)/shard_map/ppermute | solution.py:13
  6.9 12.8 %copy-start = (bf16[144,8,3,128]{3,1,2,0:T(8,128)(2,1)}, bf16[144,8,3,128]{3,1,2,0:T(8,128)(2,1)S(1)}, u32[]{:S(2)}) copy-start(bf16[144,8,3,128]{3,1,2,0:T(8,128)(2,1)S(1)} %copy.7) | copy-start | bytes 2654212
  7.0 10.8 %collective-permute-start.6 = (bf16[576,384]{1,0:T(8,128)(2,1)S(1)}, bf16[576,384]{1,0:T(8,128)(2,1)S(1)}, u32[]{:S(2)}, u32[]{:S(2)}) collective-permute-start(bf16[576,384]{1,0:T(8,128)(2,1)S(1)} %constant_dynamic-slice_fusion), channel_id=1, source_target_pairs={{0,16},{16,0},{1,17},{17,1},{2,18},{18,2},{3,19},{19,3},{4,20},{20... | collective-permute-start | bytes 1327112 | tf_op jit(solution)/shard_map/ppermute | solution.py:173
  17.7 5.1 %copy-start.8 = (bf16[576,384]{1,0:T(8,128)(2,1)}, bf16[576,384]{1,0:T(8,128)(2,1)S(1)}, u32[]{:S(2)}) copy-start(bf16[576,384]{1,0:T(8,128)(2,1)S(1)} %collective-permute-done.6.refs_9_.refs_7_.got_ref) | copy-start | bytes 1327108
  17.7 10.3 %collective-permute-start.7 = (bf16[576,384]{1,0:T(8,128)(2,1)S(1)}, bf16[576,384]{1,0:T(8,128)(2,1)S(1)}, u32[]{:S(2)}, u32[]{:S(2)}) collective-permute-start(bf16[576,384]{1,0:T(8,128)(2,1)S(1)} %collective-permute-done.6.refs_9_.refs_7_.got_ref), channel_id=1, source_target_pairs={{0,1},{1,0},{2,3},{3,2},{4,5},{5,4},{6,7},{7,6},{8,9},{9,8},{10,11... | collective-permute-start | bytes 1327112 | tf_op jit(solution)/shard_map/ppermute | solution.py:174
  19.6 3.2 %copy-start.7 = (bf16[4,512,128]{2,1,0:T(8,128)(2,1)}, bf16[4,512,128]{2,1,0:T(8,128)(2,1)S(1)}, u32[]{:S(2)}) copy-start(bf16[4,512,128]{2,1,0:T(8,128)(2,1)S(1)} %collective-permute-done.refs_1_.refs_0_) | copy-start | bytes 1572868
  19.7 8.3 %collective-permute-start.2 = (bf16[3,1,512,128]{3,2,1,0:T(8,128)(2,1)S(1)}, bf16[3,1,512,128]{3,2,1,0:T(8,128)(2,1)S(1)}, u32[]{:S(2)}, u32[]{:S(2)}) collective-permute-start(bf16[3,1,512,128]{3,2,1,0:T(8,128)(2,1)S(1)} %pad_maximum_fusion), channel_id=1, source_target_pairs={{0,1},{1,2},{2,3},{4,5},{5,6},{6,7},{8,9},{9,10},{10,11},{12,13},{... | collective-permute-start | bytes 1179656 | tf_op jit(solution)/shard_map/ppermute | solution.py:153
  22.8 9.1 %collective-permute-start.3 = (bf16[3,1,512,128]{3,2,1,0:T(8,128)(2,1)S(1)}, bf16[3,1,512,128]{3,2,1,0:T(8,128)(2,1)S(1)}, u32[]{:S(2)}, u32[]{:S(2)}) collective-permute-start(bf16[3,1,512,128]{3,2,1,0:T(8,128)(2,1)S(1)} %pad_maximum_fusion.1), channel_id=1, source_target_pairs={{1,0},{2,1},{3,2},{5,4},{6,5},{7,6},{9,8},{10,9},{11,10},{13,12},{... | collective-permute-start | bytes 1179656 | tf_op jit(solution)/shard_map/ppermute | solution.py:154
  24.8 17.7 %collective-permute-start.1 = (bf16[4,512,128]{2,1,0:T(8,128)(2,1)S(1)}, bf16[4,512,128]{2,1,0:T(8,128)(2,1)S(1)}, u32[]{:S(2)}, u32[]{:S(2)}) collective-permute-start(bf16[4,512,128]{2,1,0:T(8,128)(2,1)S(1)} %get-tuple-element.13.refs_2_.refs_1_), channel_id=1, source_target_pairs={{0,4},{4,8},{8,12},{1,5},{5,9},{9,13},{2,6},{6,10},{10,14},{3,7},{... | collective-permute-start | bytes 1572872 | tf_op jit(solution)/shard_map/ppermute | solution.py:13
  28.0 3.9 %copy-start.9 = (bf16[576,384]{1,0:T(8,128)(2,1)}, bf16[576,384]{1,0:T(8,128)(2,1)S(1)}, u32[]{:S(2)}) copy-start(bf16[576,384]{1,0:T(8,128)(2,1)S(1)} %collective-permute-done.7.refs_10_.refs_8_.other_ref) | copy-start | bytes 1327108
  28.0 3.9 %copy-start.10 = (bf16[3,1,512,128]{3,2,1,0:T(8,128)(2,1)}, bf16[3,1,512,128]{3,2,1,0:T(8,128)(2,1)S(1)}, u32[]{:S(2)}) copy-start(bf16[3,1,512,128]{3,2,1,0:T(8,128)(2,1)S(1)} %collective-permute-done.2.refs_3_) | copy-start | bytes 1179652
  31.9 0.7 copy-start.11
  39.0 18.1 %collective-permute-start.8 = (bf16[4,512,128]{2,1,0:T(8,128)(2,1)}, bf16[4,512,128]{2,1,0:T(8,128)(2,1)S(1)}, u32[]{:S(2)}, u32[]{:S(2)}) collective-permute-start(bf16[4,512,128]{2,1,0:T(8,128)(2,1)} %get-tuple-element.16.a1_ref), channel_id=1, source_target_pairs={{0,4},{4,8},{8,12},{1,5},{5,9},{9,13},{2,6},{6,10},{10,14},{3,7},{... | collective-permute-start | bytes 1572872 | tf_op jit(solution)/shard_map/ppermute | solution.py:13
  42.5 7.5 %copy-start.6 = (bf16[4,512,128]{2,1,0:T(8,128)(2,1)}, bf16[4,512,128]{2,1,0:T(8,128)(2,1)S(1)}, u32[]{:S(2)}) copy-start(bf16[4,512,128]{2,1,0:T(8,128)(2,1)S(1)} %collective-permute-done.1.refs_0_) | copy-start | bytes 1572868
  42.6 6.6 %collective-permute-start.5 = (bf16[1,1,512,128]{3,2,1,0:T(8,128)(2,1)S(1)}, bf16[1,1,512,128]{3,2,1,0:T(8,128)(2,1)S(1)}, u32[]{:S(2)}, u32[]{:S(2)}) collective-permute-start(bf16[1,1,512,128]{3,2,1,0:T(8,128)(2,1)S(1)} %get-tuple-element.31), channel_id=1, source_target_pairs={{1,0},{2,1},{3,2},{5,4},{6,5},{7,6},{9,8},{10,9},{11,10},{13,12},{... | collective-permute-start | bytes 393224 | tf_op jit(solution)/shard_map/ppermute | solution.py:161
  44.5 5.6 %collective-permute-start.4 = (bf16[1,1,512,128]{3,2,1,0:T(8,128)(2,1)S(1)}, bf16[1,1,512,128]{3,2,1,0:T(8,128)(2,1)S(1)}, u32[]{:S(2)}, u32[]{:S(2)}) collective-permute-start(bf16[1,1,512,128]{3,2,1,0:T(8,128)(2,1)S(1)} %get-tuple-element.32), channel_id=1, source_target_pairs={{0,1},{1,2},{2,3},{4,5},{5,6},{6,7},{8,9},{9,10},{10,11},{12,13},{... | collective-permute-start | bytes 393224 | tf_op jit(solution)/shard_map/ppermute | solution.py:160
  49.1 0.9 %copy-start.16 = (bf16[1,1,512,128]{3,2,1,0:T(8,128)(2,1)}, bf16[1,1,512,128]{3,2,1,0:T(8,128)(2,1)S(1)}, u32[]{:S(2)}) copy-start(bf16[1,1,512,128]{3,2,1,0:T(8,128)(2,1)S(1)} %collective-permute-done.5.refs_6_) | copy-start | bytes 393220
  50.1 0.7 copy-start.17
  57.2 9.0 %copy-start.4 = (bf16[4,512,128]{2,1,0:T(8,128)(2,1)}, bf16[4,512,128]{2,1,0:T(8,128)(2,1)S(1)}, u32[]{:S(2)}) copy-start(bf16[4,512,128]{2,1,0:T(8,128)(2,1)S(1)} %collective-permute-done.8.c1_ref) | copy-start | bytes 1572868
  57.2 14.2 %collective-permute-start.9 = (bf16[4,512,128]{2,1,0:T(8,128)(2,1)}, bf16[4,512,128]{2,1,0:T(8,128)(2,1)S(1)}, u32[]{:S(2)}, u32[]{:S(2)}) collective-permute-start(bf16[4,512,128]{2,1,0:T(8,128)(2,1)} %get-tuple-element.17.a0_ref), channel_id=1, source_target_pairs={{0,4},{4,8},{8,12},{1,5},{5,9},{9,13},{2,6},{6,10},{10,14},{3,7},{... | collective-permute-start | bytes 1572872 | tf_op jit(solution)/shard_map/ppermute | solution.py:13
  61.4 15.5 %collective-permute-start.10 = (bf16[3,1,512,128]{3,2,1,0:T(8,128)(2,1)S(1)}, bf16[3,1,512,128]{3,2,1,0:T(8,128)(2,1)S(1)}, u32[]{:S(2)}, u32[]{:S(2)}) collective-permute-start(bf16[3,1,512,128]{3,2,1,0:T(8,128)(2,1)S(1)} %pad_maximum_fusion.2), channel_id=1, source_target_pairs={{0,1},{1,2},{2,3},{4,5},{5,6},{6,7},{8,9},{9,10},{10,11},{12,13},{... | collective-permute-start | bytes 1179656 | tf_op jit(solution)/shard_map/ppermute | solution.py:153
  66.2 10.8 %collective-permute-start.11 = (bf16[3,1,512,128]{3,2,1,0:T(8,128)(2,1)S(1)}, bf16[3,1,512,128]{3,2,1,0:T(8,128)(2,1)S(1)}, u32[]{:S(2)}, u32[]{:S(2)}) collective-permute-start(bf16[3,1,512,128]{3,2,1,0:T(8,128)(2,1)S(1)} %pad_maximum_fusion.3), channel_id=1, source_target_pairs={{1,0},{2,1},{3,2},{5,4},{6,5},{7,6},{9,8},{10,9},{11,10},{13,12},{... | collective-permute-start | bytes 1179656 | tf_op jit(solution)/shard_map/ppermute | solution.py:154
  71.3 7.5 %copy-start.5 = (bf16[4,512,128]{2,1,0:T(8,128)(2,1)}, bf16[4,512,128]{2,1,0:T(8,128)(2,1)S(1)}, u32[]{:S(2)}) copy-start(bf16[4,512,128]{2,1,0:T(8,128)(2,1)S(1)} %collective-permute-done.9.c2_ref) | copy-start | bytes 1572868
  71.4 6.3 %collective-permute-start.13 = (bf16[1,1,512,128]{3,2,1,0:T(8,128)(2,1)S(1)}, bf16[1,1,512,128]{3,2,1,0:T(8,128)(2,1)S(1)}, u32[]{:S(2)}, u32[]{:S(2)}) collective-permute-start(bf16[1,1,512,128]{3,2,1,0:T(8,128)(2,1)S(1)} %get-tuple-element.23), channel_id=1, source_target_pairs={{1,0},{2,1},{3,2},{5,4},{6,5},{7,6},{9,8},{10,9},{11,10},{13,12},{... | collective-permute-start | bytes 393224 | tf_op jit(solution)/shard_map/ppermute | solution.py:157
  73.3 5.6 %collective-permute-start.12 = (bf16[1,1,512,128]{3,2,1,0:T(8,128)(2,1)S(1)}, bf16[1,1,512,128]{3,2,1,0:T(8,128)(2,1)S(1)}, u32[]{:S(2)}, u32[]{:S(2)}) collective-permute-start(bf16[1,1,512,128]{3,2,1,0:T(8,128)(2,1)S(1)} %get-tuple-element.24), channel_id=1, source_target_pairs={{0,1},{1,2},{2,3},{4,5},{5,6},{6,7},{8,9},{9,10},{10,11},{12,13},{... | collective-permute-start | bytes 393224 | tf_op jit(solution)/shard_map/ppermute | solution.py:156
  76.9 1.9 %copy-start.12 = (bf16[3,1,512,128]{3,2,1,0:T(8,128)(2,1)}, bf16[3,1,512,128]{3,2,1,0:T(8,128)(2,1)S(1)}, u32[]{:S(2)}) copy-start(bf16[3,1,512,128]{3,2,1,0:T(8,128)(2,1)S(1)} %collective-permute-done.10.top_a) | copy-start | bytes 1179652
  77.0 1.9 %copy-start.13 = (bf16[3,1,512,128]{3,2,1,0:T(8,128)(2,1)}, bf16[3,1,512,128]{3,2,1,0:T(8,128)(2,1)S(1)}, u32[]{:S(2)}) copy-start(bf16[3,1,512,128]{3,2,1,0:T(8,128)(2,1)S(1)} %collective-permute-done.11.bot_a) | copy-start | bytes 1179652
  77.6 1.2 %copy-start.14 = (bf16[1,1,512,128]{3,2,1,0:T(8,128)(2,1)}, bf16[1,1,512,128]{3,2,1,0:T(8,128)(2,1)S(1)}, u32[]{:S(2)}) copy-start(bf16[1,1,512,128]{3,2,1,0:T(8,128)(2,1)S(1)} %collective-permute-done.13.bot_b) | copy-start | bytes 393220
  78.9 0.6 copy-start.15

commit v15 on v13

--- a/solution.py
+++ b/solution.py
@@ -49,22 +49,34 @@
 def assemble(first, local_ref, got_ref, other_ref, buf):
     section = lax.axis_index("section")
     core = lax.axis_index("space") % 2
-    half = got_ref.shape[0]
+    nine, three_c, chans = local_ref.shape
+    half = got_ref.shape[1]
     use_local = section == 0 if first else section != 0
+
+    def fill_full(src):
+        for k in range(nine):
+            for s in range(3):
+                buf[k * chans : (k + 1) * chans, s * chans : (s + 1) * chans] = src[k, s * chans : (s + 1) * chans, :]
+
+    def fill_halves(lo, hi):
+        for k in range(nine):
+            for s in range(3):
+                for i in range(0, chans, 64):
+                    row = s * chans + i
+                    part, at = (lo, row) if row < half else (hi, row - half)
+                    buf[k * chans + i : k * chans + i + 64, s * chans : (s + 1) * chans] = part[k, at : at + 64, :]
 
     @pl.when(use_local)
     def _():
-        buf[...] = local_ref[...]
+        fill_full(local_ref)
 
     @pl.when(jnp.logical_and(jnp.logical_not(use_local), core == 0))
     def _():
-        buf[:half] = got_ref[...]
-        buf[half:] = other_ref[...]
+        fill_halves(got_ref, other_ref)
 
     @pl.when(jnp.logical_and(jnp.logical_not(use_local), core != 0))
     def _():
-        buf[:half] = other_ref[...]
-        buf[half:] = got_ref[...]
+        fill_halves(other_ref, got_ref)
 
     return buf
 
@@ -115,13 +127,14 @@
 def frame_conv(t, operands, base, w_parts, with_act):
     rows, width, chans = base.shape
     first, local, got, other = w_parts
-    flops = 2 * rows * width * local.shape[0] * local.shape[1]
+    w_shape = (local.shape[0] * local.shape[2], local.shape[1])
+    flops = 2 * rows * width * w_shape[0] * w_shape[1]
     nbytes = sum(x.size * x.dtype.itemsize for x in operands) + 3 * base.size * 2 + local.size * 4
     shape = jax.ShapeDtypeStruct(base.shape, base.dtype)
     return pl.pallas_call(
         functools.partial(frame_kernel, t, with_act, first),
         out_shape=(shape, shape) if with_act else (shape,),
-        scratch_shapes=[pltpu.VMEM(local.shape, local.dtype)],
+        scratch_shapes=[pltpu.VMEM(w_shape, local.dtype)],
         cost_estimate=pl.CostEstimate(flops=flops, bytes_accessed=nbytes, transcendentals=0),
     )(*operands, base, local, got, other)
 
@@ -129,12 +142,13 @@
 def pair_conv(operands, x0, x1, w_parts):
     rows, width, chans = x0.shape
     first, local, got, other = w_parts
-    flops = 4 * rows * width * local.shape[0] * local.shape[1]
+    w_shape = (local.shape[0] * local.shape[2], local.shape[1])
+    flops = 4 * rows * width * w_shape[0] * w_shape[1]
     nbytes = sum(x.size * x.dtype.itemsize for x in operands) + 4 * x0.size * 2 + local.size * 4
     return pl.pallas_call(
         functools.partial(pair_kernel, first),
         out_shape=jax.ShapeDtypeStruct((2,) + x0.shape, x0.dtype),
-        scratch_shapes=[pltpu.VMEM(local.shape, local.dtype)],
+        scratch_shapes=[pltpu.VMEM(w_shape, local.dtype)],
         cost_estimate=pl.CostEstimate(flops=flops, bytes_accessed=nbytes, transcendentals=0),
     )(*operands, x0, x1, local, got, other)
 
@@ -162,12 +176,12 @@
 
 
 def both_taps(weights):
-    local = tap_matrix(weights[0])
-    half = local.shape[0] // 2
+    local = weights[0]
+    half = local.shape[1] // 2
     section = lax.axis_index("section")
     core = lax.axis_index("space") % 2
     n_space = lax.axis_size("space")
-    mine = lax.dynamic_slice_in_dim(local, core * half, half, axis=0)
+    mine = lax.dynamic_slice_in_dim(local, core * half, half, axis=1)
     got = lax.ppermute(mine, "section", [(0, 1), (1, 0)])
     other = lax.ppermute(got, "space", [(i, i ^ 1) for i in range(n_space)])
     return (True, local, got, other), (False, local, got, other)

time: 88.8 us -> 89.9 us (1.012)
  waiting for transfers between devices: 17.8 us -> 24.2 us
  starting transfers between devices: 39.9 us -> 35.8 us
  local copies, waits for them, and re-layouts: 6.19 us -> 5.06 us
    ppermute x2, waiting for transfers between devices: 0.67 us -> 7.61 us  [conv_block(): bot_b = lax.ppermute(c2[None, :1], 'space', up)]
    ppermute x2, starting transfers between devices: 7.28 us -> 3.84 us  [conv_block(): top_b = lax.ppermute(c2[None, -1:], 'space', down)]
    ppermute x2, starting transfers between devices: 7.83 us -> 5.37 us  [conv_block(): top_a = lax.ppermute(jnp.stack([c1[-1:], a0[-1:], a1[-1:]]), 'space', down)]
    ppermute x2, waiting for transfers between devices: 2.13 us -> 0.01 us  [conv_block(): top_b = lax.ppermute(c2[None, -1:], 'space', down)]
    ppermute x4, waiting for transfers between devices: 2.69 us -> 4.43 us  [shift_tm(): return lax.ppermute(x, 'tm', [(i, i + 1) for i in range(n - 1)])]
    ppermute x2, starting transfers between devices: 3.84 us -> 4.82 us  [conv_block(): bot_b = lax.ppermute(c2[None, :1], 'space', up)]
    another operation x5, local copies, waits for them, and re-layouts: 2.05 us -> 1.08 us  [conv_block(): bot_a = lax.ppermute(jnp.stack([c1[:1], a0[:1], a1[:1]]), 'space', up)]
    unnamed x39 -> x38, local copies, waits for them, and re-layouts: 2.23 us -> 2.86 us
  transfers between devices with their start and end apart: 14 -> 14, of which waited for: 6 -> 5; matrix products, arithmetic and copies ran while one was open for 5% -> 3% of each run, Pallas kernels for 14% -> 14%
where the time goes in v15:
time: 89.9 us; the launch traced here: 89.4 us
  starting transfers between devices  35.8 us (40%)
  waiting for transfers between devices  24.2 us (27%)
  Pallas kernels  21.9 us (24%)
  local copies, waits for them, and re-layouts  5.06 us (6%)
  other arithmetic  2.02 us (2%)
    ppermute x4, starting transfers between devices, shift_tm(): return lax.ppermute(x, 'tm', [(i, i + 1) for i in range(n - 1)])  14.4 us
    pallas_call x2, Pallas kernels, frame_conv(): pl.pallas_call(functools.partial(frame_kernel, t, with_act, first), out_s...  12.6 us
    ppermute x1, waiting for transfers between devices, both_taps(): got = lax.ppermute(mine, 'section', [(0, 1), (1, 0)])  9.48 us
    pallas_call x1, Pallas kernels, pair_conv(): pl.pallas_call(functools.partial(pair_kernel, first), out_shape=jax.Shape...  9.29 us
    ppermute x2, waiting for transfers between devices, conv_block(): bot_b = lax.ppermute(c2[None, :1], 'space', up)  7.61 us
    ppermute x2, starting transfers between devices, conv_block(): top_a = lax.ppermute(jnp.stack([c1[-1:], a0[-1:], a1[-1:]]), 'space', down)  5.37 us
    ppermute x2, starting transfers between devices, conv_block(): bot_b = lax.ppermute(c2[None, :1], 'space', up)  4.82 us
    ppermute x4, waiting for transfers between devices, shift_tm(): return lax.ppermute(x, 'tm', [(i, i + 1) for i in range(n - 1)])  4.43 us
  transfers between devices with their start and end apart: 14, of which 5 were waited for; matrix products, arithmetic and copies ran while one was open for 3% of the time, Pallas kernels for 14%

profile of v15, /device:TPU:1, one launch (start us, length us, event | category | flops | bytes accessed | tf_op | source)
XLA Modules:
  0.0 89.4 jit_solution(6183519348684974668)
XLA Ops:
  0.0 0.0 copy-start.3
  0.0 1.8 %fusion.7 = (bf16[4,512,128]{2,1,0:T(8,128)(2,1)S(1)}, bf16[4,512,128]{2,1,0:T(8,128)(2,1)S(1)}) fusion(bf16[1,2,4,512,128]{4,3,2,1,0:T(8,128)(2,1)} %param.2), kind=kLoop, calls=%fused_computation.11 | loop fusion | flops 3145728 | bytes 2097152 | tf_op jit(solution)/shard_map/convert_element_type | solution.py:17
  1.8 0.0 copy-start.1
  1.8 0.0 copy-start.2
  1.9 4.1 %collective-permute-start = (bf16[4,512,128]{2,1,0:T(8,128)(2,1)S(1)}, bf16[4,512,128]{2,1,0:T(8,128)(2,1)S(1)}, u32[]{:S(2)}, u32[]{:S(2)}) collective-permute-start(bf16[4,512,128]{2,1,0:T(8,128)(2,1)S(1)} %get-tuple-element.23.refs_2_), channel_id=1, source_target_pairs={{0,4},{4,8},{8,12},{1,5},{5,9},{9,13},{2,6},{6,10},{10,14},{3,7},{... | collective-permute-start | bytes 1572872 | tf_op jit(solution)/shard_map/ppermute | solution.py:13
  5.9 0.0 copy-done.3
  6.0 1.3 %collective-permute-start.6 = (bf16[9,192,128]{2,1,0:T(8,128)(2,1)S(1)}, bf16[9,192,128]{2,1,0:T(8,128)(2,1)S(1)}, u32[]{:S(2)}, u32[]{:S(2)}) collective-permute-start(bf16[9,192,128]{2,1,0:T(8,128)(2,1)S(1)} %dynamic-slice_bitcast_fusion), channel_id=1, source_target_pairs={{0,16},{16,0},{1,17},{17,1},{2,18},{18,2},{3,19},{19,3},{4,20},{20... | collective-permute-start | bytes 1327112 | tf_op jit(solution)/shard_map/ppermute | solution.py:185
  7.3 0.0 copy-done.1
  7.3 9.5 %collective-permute-done.6.refs_9_.refs_7_.got_ref = bf16[9,192,128]{2,1,0:T(8,128)(2,1)S(1)} collective-permute-done((bf16[9,192,128]{2,1,0:T(8,128)(2,1)S(1)}, bf16[9,192,128]{2,1,0:T(8,128)(2,1)S(1)}, u32[]{:S(2)}, u32[]{:S(2)}) %collective-permute-start.6) | collective-permute-done | bytes 442400 | tf_op jit(solution)/shard_map/ppermute | solution.py:185
  16.8 0.0 copy-start.9
  16.8 1.9 %collective-permute-start.7 = (bf16[9,192,128]{2,1,0:T(8,128)(2,1)S(1)}, bf16[9,192,128]{2,1,0:T(8,128)(2,1)S(1)}, u32[]{:S(2)}, u32[]{:S(2)}) collective-permute-start(bf16[9,192,128]{2,1,0:T(8,128)(2,1)S(1)} %collective-permute-done.6.refs_9_.refs_7_.got_ref), channel_id=1, source_target_pairs={{0,1},{1,0},{2,3},{3,2},{4,5},{5,4},{6,7},{7,6},{8,9},{9,8},{10,11... | collective-permute-start | bytes 1327112 | tf_op jit(solution)/shard_map/ppermute | solution.py:186
  18.6 0.0 collective-permute-done.refs_1_.refs_0_
  18.7 0.0 copy-start.8
  18.7 0.0 copy-done.9
  18.7 0.8 copy-done.8
  19.5 3.3 %collective-permute-start.2 = (bf16[3,1,512,128]{3,2,1,0:T(8,128)(2,1)S(1)}, bf16[3,1,512,128]{3,2,1,0:T(8,128)(2,1)S(1)}, u32[]{:S(2)}, u32[]{:S(2)}) collective-permute-start(bf16[3,1,512,128]{3,2,1,0:T(8,128)(2,1)S(1)} %pad_maximum_fusion), channel_id=1, source_target_pairs={{0,1},{1,2},{2,3},{4,5},{5,6},{6,7},{8,9},{9,10},{10,11},{12,13},{... | collective-permute-start | bytes 1179656 | tf_op jit(solution)/shard_map/ppermute | solution.py:165
  22.9 1.9 %collective-permute-start.3 = (bf16[3,1,512,128]{3,2,1,0:T(8,128)(2,1)S(1)}, bf16[3,1,512,128]{3,2,1,0:T(8,128)(2,1)S(1)}, u32[]{:S(2)}, u32[]{:S(2)}) collective-permute-start(bf16[3,1,512,128]{3,2,1,0:T(8,128)(2,1)S(1)} %pad_maximum_fusion.1), channel_id=1, source_target_pairs={{1,0},{2,1},{3,2},{5,4},{6,5},{7,6},{9,8},{10,9},{11,10},{13,12},{... | collective-permute-start | bytes 1179656 | tf_op jit(solution)/shard_map/ppermute | solution.py:166
  24.8 0.0 copy-done.2
  24.8 3.4 %collective-permute-start.1 = (bf16[4,512,128]{2,1,0:T(8,128)(2,1)S(1)}, bf16[4,512,128]{2,1,0:T(8,128)(2,1)S(1)}, u32[]{:S(2)}, u32[]{:S(2)}) collective-permute-start(bf16[4,512,128]{2,1,0:T(8,128)(2,1)S(1)} %get-tuple-element.13.refs_2_.refs_1_), channel_id=1, source_target_pairs={{0,4},{4,8},{8,12},{1,5},{5,9},{9,13},{2,6},{6,10},{10,14},{3,7},{... | collective-permute-start | bytes 1572872 | tf_op jit(solution)/shard_map/ppermute | solution.py:13
  28.2 0.0 copy-done
  28.2 1.0 %slice_bitcast_fusion = (bf16[4,512,128]{2,1,0:T(8,128)(2,1)}, bf16[4,512,128]{2,1,0:T(8,128)(2,1)}) fusion(bf16[1,2,4,512,128]{4,3,2,1,0:T(8,128)(2,1)S(1)} %copy-done), kind=kLoop, calls=%fused_computation.12 | loop fusion | bytes 2097152 | tf_op jit(solution)/shard_map/squeeze | solution.py:194
  29.3 0.0 collective-permute-done.7.refs_10_.refs_8_.other_ref
  29.3 0.0 collective-permute-done.2.refs_3_
  29.3 0.0 copy-start.11
  29.3 2.7 %collective-permute-done.3.refs_4_ = bf16[3,1,512,128]{3,2,1,0:T(8,128)(2,1)S(1)} collective-permute-done((bf16[3,1,512,128]{3,2,1,0:T(8,128)(2,1)S(1)}, bf16[3,1,512,128]{3,2,1,0:T(8,128)(2,1)S(1)}, u32[]{:S(2)}, u32[]{:S(2)}) %collective-permute-start.3) | collective-permute-done | bytes 393248 | tf_op jit(solution)/shard_map/ppermute | solution.py:166
  32.0 0.0 copy-done.10
  32.0 0.0 copy-done.11
  32.0 0.8 copy-done.12
  32.7 6.3 %shard_map.29 = (bf16[4,512,128]{2,1,0:T(8,128)(2,1)}, bf16[4,512,128]{2,1,0:T(8,128)(2,1)}) custom-call(bf16[4,512,128]{2,1,0:T(8,128)(2,1)} %copy-done.8, bf16[4,512,128]{2,1,0:T(8,128)(2,1)} %copy-done.2, bf16[4,512,128]{2,1,0:T(8,128)(2,1)} %copy-done.1, bf16[3,1,512,128]{3,2,1,0:T(8,128)(2,1)} %copy-done.11, bf16[3,1,512,128]{3,2,1,0:T(8,128)(2,1)} %copy-done.12, ...), custom_call_target="tpu_custom_call" | custom-call | flops 1811939328 | bytes 5701632 | tf_op jit(solution)/shard_map/pallas_call | solution.py:134
  39.0 3.8 %collective-permute-start.8 = (bf16[4,512,128]{2,1,0:T(8,128)(2,1)}, bf16[4,512,128]{2,1,0:T(8,128)(2,1)S(1)}, u32[]{:S(2)}, u32[]{:S(2)}) collective-permute-start(bf16[4,512,128]{2,1,0:T(8,128)(2,1)} %get-tuple-element.16.a1_ref), channel_id=1, source_target_pairs={{0,4},{4,8},{8,12},{1,5},{5,9},{9,13},{2,6},{6,10},{10,14},{3,7},{... | collective-permute-start | bytes 1572872 | tf_op jit(solution)/shard_map/ppermute | solution.py:13
  42.8 0.0 collective-permute-done.1.refs_0_
  42.8 0.0 copy-start.7
  42.8 1.9 %collective-permute-start.4 = (bf16[1,1,512,128]{3,2,1,0:T(8,128)(2,1)S(1)}, bf16[1,1,512,128]{3,2,1,0:T(8,128)(2,1)S(1)}, u32[]{:S(2)}, u32[]{:S(2)}) collective-permute-start(bf16[1,1,512,128]{3,2,1,0:T(8,128)(2,1)S(1)} %get-tuple-element.34), channel_id=1, source_target_pairs={{0,1},{1,2},{2,3},{4,5},{5,6},{6,7},{8,9},{9,10},{10,11},{12,13},{... | collective-permute-start | bytes 393224 | tf_op jit(solution)/shard_map/ppermute | solution.py:172
  44.8 2.4 %collective-permute-start.5 = (bf16[1,1,512,128]{3,2,1,0:T(8,128)(2,1)S(1)}, bf16[1,1,512,128]{3,2,1,0:T(8,128)(2,1)S(1)}, u32[]{:S(2)}, u32[]{:S(2)}) collective-permute-start(bf16[1,1,512,128]{3,2,1,0:T(8,128)(2,1)S(1)} %get-tuple-element.33), channel_id=1, source_target_pairs={{1,0},{2,1},{3,2},{5,4},{6,5},{7,6},{9,8},{10,9},{11,10},{13,12},{... | collective-permute-start | bytes 393224 | tf_op jit(solution)/shard_map/ppermute | solution.py:173
  47.2 0.0 copy-done.4
  47.2 0.0 copy-done.7
  47.2 0.0 collective-permute-done.4.refs_5_
  47.3 0.0 copy-start.17
  47.3 3.8 %collective-permute-done.5.refs_6_ = bf16[1,1,512,128]{3,2,1,0:T(8,128)(2,1)S(1)} collective-permute-done((bf16[1,1,512,128]{3,2,1,0:T(8,128)(2,1)S(1)}, bf16[1,1,512,128]{3,2,1,0:T(8,128)(2,1)S(1)}, u32[]{:S(2)}, u32[]{:S(2)}) %collective-permute-start.5) | collective-permute-done | bytes 131104 | tf_op jit(solution)/shard_map/ppermute | solution.py:173
  51.1 0.0 copy-done.17
  51.1 0.6 copy-done.18
  51.7 6.3 %shard_map.28 = (bf16[4,512,128]{2,1,0:T(8,128)(2,1)}, bf16[4,512,128]{2,1,0:T(8,128)(2,1)}) custom-call(bf16[4,512,128]{2,1,0:T(8,128)(2,1)} %copy-done.7, bf16[4,512,128]{2,1,0:T(8,128)(2,1)} %copy-done.8, bf16[4,512,128]{2,1,0:T(8,128)(2,1)} %copy-done.2, bf16[3,1,512,128]{3,2,1,0:T(8,128)(2,1)} %copy-done.11, bf16[3,1,512,128]{3,2,1,0:T(8,128)(2,1)} %copy-done.12, ...), custom_call_target="tpu_custom_call" | custom-call | flops 1811939328 | bytes 5963776 | tf_op jit(solution)/shard_map/pallas_call | solution.py:134
  58.0 0.0 collective-permute-done.8.c1_ref
  58.0 3.2 %collective-permute-start.9 = (bf16[4,512,128]{2,1,0:T(8,128)(2,1)}, bf16[4,512,128]{2,1,0:T(8,128)(2,1)S(1)}, u32[]{:S(2)}, u32[]{:S(2)}) collective-permute-start(bf16[4,512,128]{2,1,0:T(8,128)(2,1)} %get-tuple-element.17.a0_ref), channel_id=1, source_target_pairs={{0,4},{4,8},{8,12},{1,5},{5,9},{9,13},{2,6},{6,10},{10,14},{3,7},{... | collective-permute-start | bytes 1572872 | tf_op jit(solution)/shard_map/ppermute | solution.py:13
  61.3 1.0 %slice_bitcast_fusion.9 = (bf16[1,1,512,128]{3,2,1,0:T(8,128)(2,1)S(1)}, bf16[1,1,512,128]{3,2,1,0:T(8,128)(2,1)S(1)}) fusion(bf16[4,512,128]{2,1,0:T(8,128)(2,1)} %get-tuple-element.17.a0_ref), kind=kLoop, calls=%fused_computation.26 | loop fusion | bytes 524288 | tf_op jit(solution)/shard_map/stack | solution.py:166
  62.3 0.0 copy-done.5
  62.3 2.1 %collective-permute-start.10 = (bf16[3,1,512,128]{3,2,1,0:T(8,128)(2,1)S(1)}, bf16[3,1,512,128]{3,2,1,0:T(8,128)(2,1)S(1)}, u32[]{:S(2)}, u32[]{:S(2)}) collective-permute-start(bf16[3,1,512,128]{3,2,1,0:T(8,128)(2,1)S(1)} %pad_maximum_fusion.2), channel_id=1, source_target_pairs={{0,1},{1,2},{2,3},{4,5},{5,6},{6,7},{8,9},{9,10},{10,11},{12,13},{... | collective-permute-start | bytes 1179656 | tf_op jit(solution)/shard_map/ppermute | solution.py:165
  64.5 2.3 %collective-permute-start.11 = (bf16[3,1,512,128]{3,2,1,0:T(8,128)(2,1)S(1)}, bf16[3,1,512,128]{3,2,1,0:T(8,128)(2,1)S(1)}, u32[]{:S(2)}, u32[]{:S(2)}) collective-permute-start(bf16[3,1,512,128]{3,2,1,0:T(8,128)(2,1)S(1)} %pad_maximum_fusion.3), channel_id=1, source_target_pairs={{1,0},{2,1},{3,2},{5,4},{6,5},{7,6},{9,8},{10,9},{11,10},{13,12},{... | collective-permute-start | bytes 1179656 | tf_op jit(solution)/shard_map/ppermute | solution.py:166
  66.8 4.4 %collective-permute-done.9.c2_ref = bf16[4,512,128]{2,1,0:T(8,128)(2,1)S(1)} collective-permute-done((bf16[4,512,128]{2,1,0:T(8,128)(2,1)}, bf16[4,512,128]{2,1,0:T(8,128)(2,1)S(1)}, u32[]{:S(2)}, u32[]{:S(2)}) %collective-permute-start.9) | collective-permute-done | bytes 524320 | tf_op jit(solution)/shard_map/ppermute | solution.py:13
  71.2 1.9 %collective-permute-start.12 = (bf16[1,1,512,128]{3,2,1,0:T(8,128)(2,1)S(1)}, bf16[1,1,512,128]{3,2,1,0:T(8,128)(2,1)S(1)}, u32[]{:S(2)}, u32[]{:S(2)}) collective-permute-start(bf16[1,1,512,128]{3,2,1,0:T(8,128)(2,1)S(1)} %get-tuple-element.26), channel_id=1, source_target_pairs={{0,1},{1,2},{2,3},{4,5},{5,6},{6,7},{8,9},{9,10},{10,11},{12,13},{... | collective-permute-start | bytes 393224 | tf_op jit(solution)/shard_map/ppermute | solution.py:168
  73.1 2.4 %collective-permute-start.13 = (bf16[1,1,512,128]{3,2,1,0:T(8,128)(2,1)S(1)}, bf16[1,1,512,128]{3,2,1,0:T(8,128)(2,1)S(1)}, u32[]{:S(2)}, u32[]{:S(2)}) collective-permute-start(bf16[1,1,512,128]{3,2,1,0:T(8,128)(2,1)S(1)} %get-tuple-element.25), channel_id=1, source_target_pairs={{1,0},{2,1},{3,2},{5,4},{6,5},{7,6},{9,8},{10,9},{11,10},{13,12},{... | collective-permute-start | bytes 393224 | tf_op jit(solution)/shard_map/ppermute | solution.py:169
  75.6 0.0 collective-permute-done.10.top_a
  75.6 0.0 copy-start.13
  75.6 0.0 collective-permute-done.11.bot_a
  75.6 0.0 copy-start.14
  75.6 0.0 collective-permute-done.12.top_b
  75.6 0.0 copy-start.15
  75.6 3.8 %collective-permute-done.13.bot_b = bf16[1,1,512,128]{3,2,1,0:T(8,128)(2,1)S(1)} collective-permute-done((bf16[1,1,512,128]{3,2,1,0:T(8,128)(2,1)S(1)}, bf16[1,1,512,128]{3,2,1,0:T(8,128)(2,1)S(1)}, u32[]{:S(2)}, u32[]{:S(2)}) %collective-permute-start.13) | collective-permute-done | bytes 131104 | tf_op jit(solution)/shard_map/ppermute | solution.py:169
  79.4 0.0 copy-done.6
  79.4 0.0 copy-done.13
  79.4 0.0 copy-done.14
  79.4 0.0 copy-done.15
  79.4 0.6 copy-done.16
  80.1 9.3 %shard_map.30 = bf16[2,4,512,128]{3,2,1,0:T(8,128)(2,1)} custom-call(bf16[4,512,128]{2,1,0:T(8,128)(2,1)} %copy-done.6, bf16[4,512,128]{2,1,0:T(8,128)(2,1)} %copy-done.5, bf16[4,512,128]{2,1,0:T(8,128)(2,1)} %get-tuple-element.17.a0_ref, bf16[4,512,128]{2,1,0:T(8,128)(2,1)} %get-tuple-element.16.a1_ref, bf16[3,1,512,128]{3,2,1,0:T(8,128)(2,1)} %copy-done.13, ...), custom_call_target="tpu_custom_call" | custom-call | flops 3623878656 | bytes 7012352 | tf_op jit(solution)/shard_map/pallas_call | solution.py:148
  (19 shorter events, 0.4 us)
Async XLA Ops:
  0.0 5.9 %copy-start.3 = (bf16[1,9,384,128]{3,2,1,0:T(8,128)(2,1)S(1)}, bf16[1,9,384,128]{3,2,1,0:T(8,128)(2,1)}, u32[]{:S(2)}) copy-start(bf16[1,9,384,128]{3,2,1,0:T(8,128)(2,1)} %param.3) | copy-start | bytes 2654212
  1.8 5.5 %copy-start.1 = (bf16[4,512,128]{2,1,0:T(8,128)(2,1)}, bf16[4,512,128]{2,1,0:T(8,128)(2,1)S(1)}, u32[]{:S(2)}) copy-start(bf16[4,512,128]{2,1,0:T(8,128)(2,1)S(1)} %get-tuple-element.23.refs_2_) | copy-start | bytes 1572868
  1.8 23.0 %copy-start.2 = (bf16[4,512,128]{2,1,0:T(8,128)(2,1)}, bf16[4,512,128]{2,1,0:T(8,128)(2,1)S(1)}, u32[]{:S(2)}) copy-start(bf16[4,512,128]{2,1,0:T(8,128)(2,1)S(1)} %get-tuple-element.13.refs_2_.refs_1_) | copy-start | bytes 1572868
  1.9 16.8 %collective-permute-start = (bf16[4,512,128]{2,1,0:T(8,128)(2,1)S(1)}, bf16[4,512,128]{2,1,0:T(8,128)(2,1)S(1)}, u32[]{:S(2)}, u32[]{:S(2)}) collective-permute-start(bf16[4,512,128]{2,1,0:T(8,128)(2,1)S(1)} %get-tuple-element.23.refs_2_), channel_id=1, source_target_pairs={{0,4},{4,8},{8,12},{1,5},{5,9},{9,13},{2,6},{6,10},{10,14},{3,7},{... | collective-permute-start | bytes 1572872 | tf_op jit(solution)/shard_map/ppermute | solution.py:13
  6.0 10.8 %collective-permute-start.6 = (bf16[9,192,128]{2,1,0:T(8,128)(2,1)S(1)}, bf16[9,192,128]{2,1,0:T(8,128)(2,1)S(1)}, u32[]{:S(2)}, u32[]{:S(2)}) collective-permute-start(bf16[9,192,128]{2,1,0:T(8,128)(2,1)S(1)} %dynamic-slice_bitcast_fusion), channel_id=1, source_target_pairs={{0,16},{16,0},{1,17},{17,1},{2,18},{18,2},{3,19},{19,3},{4,20},{20... | collective-permute-start | bytes 1327112 | tf_op jit(solution)/shard_map/ppermute | solution.py:185
  16.8 1.9 %copy-start.9 = (bf16[9,192,128]{2,1,0:T(8,128)(2,1)}, bf16[9,192,128]{2,1,0:T(8,128)(2,1)S(1)}, u32[]{:S(2)}) copy-start(bf16[9,192,128]{2,1,0:T(8,128)(2,1)S(1)} %collective-permute-done.6.refs_9_.refs_7_.got_ref) | copy-start | bytes 1327108
  16.8 12.5 %collective-permute-start.7 = (bf16[9,192,128]{2,1,0:T(8,128)(2,1)S(1)}, bf16[9,192,128]{2,1,0:T(8,128)(2,1)S(1)}, u32[]{:S(2)}, u32[]{:S(2)}) collective-permute-start(bf16[9,192,128]{2,1,0:T(8,128)(2,1)S(1)} %collective-permute-done.6.refs_9_.refs_7_.got_ref), channel_id=1, source_target_pairs={{0,1},{1,0},{2,3},{3,2},{4,5},{5,4},{6,7},{7,6},{8,9},{9,8},{10,11... | collective-permute-start | bytes 1327112 | tf_op jit(solution)/shard_map/ppermute | solution.py:186
  18.7 0.8 copy-start.8
  19.5 8.7 %copy-start = (bf16[1,2,4,512,128]{4,3,2,1,0:T(8,128)(2,1)S(1)}, bf16[1,2,4,512,128]{4,3,2,1,0:T(8,128)(2,1)}, u32[]{:S(2)}) copy-start(bf16[1,2,4,512,128]{4,3,2,1,0:T(8,128)(2,1)} %param.2) | copy-start | bytes 3145732
  19.5 9.7 %collective-permute-start.2 = (bf16[3,1,512,128]{3,2,1,0:T(8,128)(2,1)S(1)}, bf16[3,1,512,128]{3,2,1,0:T(8,128)(2,1)S(1)}, u32[]{:S(2)}, u32[]{:S(2)}) collective-permute-start(bf16[3,1,512,128]{3,2,1,0:T(8,128)(2,1)S(1)} %pad_maximum_fusion), channel_id=1, source_target_pairs={{0,1},{1,2},{2,3},{4,5},{5,6},{6,7},{8,9},{9,10},{10,11},{12,13},{... | collective-permute-start | bytes 1179656 | tf_op jit(solution)/shard_map/ppermute | solution.py:165
  22.9 9.1 %collective-permute-start.3 = (bf16[3,1,512,128]{3,2,1,0:T(8,128)(2,1)S(1)}, bf16[3,1,512,128]{3,2,1,0:T(8,128)(2,1)S(1)}, u32[]{:S(2)}, u32[]{:S(2)}) collective-permute-start(bf16[3,1,512,128]{3,2,1,0:T(8,128)(2,1)S(1)} %pad_maximum_fusion.1), channel_id=1, source_target_pairs={{1,0},{2,1},{3,2},{5,4},{6,5},{7,6},{9,8},{10,9},{11,10},{13,12},{... | collective-permute-start | bytes 1179656 | tf_op jit(solution)/shard_map/ppermute | solution.py:166
  24.8 18.0 %collective-permute-start.1 = (bf16[4,512,128]{2,1,0:T(8,128)(2,1)S(1)}, bf16[4,512,128]{2,1,0:T(8,128)(2,1)S(1)}, u32[]{:S(2)}, u32[]{:S(2)}) collective-permute-start(bf16[4,512,128]{2,1,0:T(8,128)(2,1)S(1)} %get-tuple-element.13.refs_2_.refs_1_), channel_id=1, source_target_pairs={{0,4},{4,8},{8,12},{1,5},{5,9},{9,13},{2,6},{6,10},{10,14},{3,7},{... | collective-permute-start | bytes 1572872 | tf_op jit(solution)/shard_map/ppermute | solution.py:13
  29.3 2.7 %copy-start.10 = (bf16[9,192,128]{2,1,0:T(8,128)(2,1)}, bf16[9,192,128]{2,1,0:T(8,128)(2,1)S(1)}, u32[]{:S(2)}) copy-start(bf16[9,192,128]{2,1,0:T(8,128)(2,1)S(1)} %collective-permute-done.7.refs_10_.refs_8_.other_ref) | copy-start | bytes 1327108
  29.3 2.7 %copy-start.11 = (bf16[3,1,512,128]{3,2,1,0:T(8,128)(2,1)}, bf16[3,1,512,128]{3,2,1,0:T(8,128)(2,1)S(1)}, u32[]{:S(2)}) copy-start(bf16[3,1,512,128]{3,2,1,0:T(8,128)(2,1)S(1)} %collective-permute-done.2.refs_3_) | copy-start | bytes 1179652
  32.0 0.8 copy-start.12
  39.0 8.2 %copy-start.4 = (bf16[4,512,128]{2,1,0:T(8,128)(2,1)S(1)}, bf16[4,512,128]{2,1,0:T(8,128)(2,1)}, u32[]{:S(2)}) copy-start(bf16[4,512,128]{2,1,0:T(8,128)(2,1)} %get-tuple-element.16.a1_ref) | copy-start | bytes 1572868
  39.0 19.0 %collective-permute-start.8 = (bf16[4,512,128]{2,1,0:T(8,128)(2,1)}, bf16[4,512,128]{2,1,0:T(8,128)(2,1)S(1)}, u32[]{:S(2)}, u32[]{:S(2)}) collective-permute-start(bf16[4,512,128]{2,1,0:T(8,128)(2,1)} %get-tuple-element.16.a1_ref), channel_id=1, source_target_pairs={{0,4},{4,8},{8,12},{1,5},{5,9},{9,13},{2,6},{6,10},{10,14},{3,7},{... | collective-permute-start | bytes 1572872 | tf_op jit(solution)/shard_map/ppermute | solution.py:13
  42.8 4.4 %copy-start.7 = (bf16[4,512,128]{2,1,0:T(8,128)(2,1)}, bf16[4,512,128]{2,1,0:T(8,128)(2,1)S(1)}, u32[]{:S(2)}) copy-start(bf16[4,512,128]{2,1,0:T(8,128)(2,1)S(1)} %collective-permute-done.1.refs_0_) | copy-start | bytes 1572868
  42.8 4.4 %collective-permute-start.4 = (bf16[1,1,512,128]{3,2,1,0:T(8,128)(2,1)S(1)}, bf16[1,1,512,128]{3,2,1,0:T(8,128)(2,1)S(1)}, u32[]{:S(2)}, u32[]{:S(2)}) collective-permute-start(bf16[1,1,512,128]{3,2,1,0:T(8,128)(2,1)S(1)} %get-tuple-element.34), channel_id=1, source_target_pairs={{0,1},{1,2},{2,3},{4,5},{5,6},{6,7},{8,9},{9,10},{10,11},{12,13},{... | collective-permute-start | bytes 393224 | tf_op jit(solution)/shard_map/ppermute | solution.py:172
  44.8 6.3 %collective-permute-start.5 = (bf16[1,1,512,128]{3,2,1,0:T(8,128)(2,1)S(1)}, bf16[1,1,512,128]{3,2,1,0:T(8,128)(2,1)S(1)}, u32[]{:S(2)}, u32[]{:S(2)}) collective-permute-start(bf16[1,1,512,128]{3,2,1,0:T(8,128)(2,1)S(1)} %get-tuple-element.33), channel_id=1, source_target_pairs={{1,0},{2,1},{3,2},{5,4},{6,5},{7,6},{9,8},{10,9},{11,10},{13,12},{... | collective-permute-start | bytes 393224 | tf_op jit(solution)/shard_map/ppermute | solution.py:173
  47.3 3.8 %copy-start.17 = (bf16[1,1,512,128]{3,2,1,0:T(8,128)(2,1)}, bf16[1,1,512,128]{3,2,1,0:T(8,128)(2,1)S(1)}, u32[]{:S(2)}) copy-start(bf16[1,1,512,128]{3,2,1,0:T(8,128)(2,1)S(1)} %collective-permute-done.4.refs_5_) | copy-start | bytes 393220
  51.1 0.6 copy-start.18
  58.0 4.2 %copy-start.5 = (bf16[4,512,128]{2,1,0:T(8,128)(2,1)}, bf16[4,512,128]{2,1,0:T(8,128)(2,1)S(1)}, u32[]{:S(2)}) copy-start(bf16[4,512,128]{2,1,0:T(8,128)(2,1)S(1)} %collective-permute-done.8.c1_ref) | copy-start | bytes 1572868
  58.0 13.1 %collective-permute-start.9 = (bf16[4,512,128]{2,1,0:T(8,128)(2,1)}, bf16[4,512,128]{2,1,0:T(8,128)(2,1)S(1)}, u32[]{:S(2)}, u32[]{:S(2)}) collective-permute-start(bf16[4,512,128]{2,1,0:T(8,128)(2,1)} %get-tuple-element.17.a0_ref), channel_id=1, source_target_pairs={{0,4},{4,8},{8,12},{1,5},{5,9},{9,13},{2,6},{6,10},{10,14},{3,7},{... | collective-permute-start | bytes 1572872 | tf_op jit(solution)/shard_map/ppermute | solution.py:13
  62.3 13.2 %collective-permute-start.10 = (bf16[3,1,512,128]{3,2,1,0:T(8,128)(2,1)S(1)}, bf16[3,1,512,128]{3,2,1,0:T(8,128)(2,1)S(1)}, u32[]{:S(2)}, u32[]{:S(2)}) collective-permute-start(bf16[3,1,512,128]{3,2,1,0:T(8,128)(2,1)S(1)} %pad_maximum_fusion.2), channel_id=1, source_target_pairs={{0,1},{1,2},{2,3},{4,5},{5,6},{6,7},{8,9},{9,10},{10,11},{12,13},{... | collective-permute-start | bytes 1179656 | tf_op jit(solution)/shard_map/ppermute | solution.py:165
  64.5 11.1 %collective-permute-start.11 = (bf16[3,1,512,128]{3,2,1,0:T(8,128)(2,1)S(1)}, bf16[3,1,512,128]{3,2,1,0:T(8,128)(2,1)S(1)}, u32[]{:S(2)}, u32[]{:S(2)}) collective-permute-start(bf16[3,1,512,128]{3,2,1,0:T(8,128)(2,1)S(1)} %pad_maximum_fusion.3), channel_id=1, source_target_pairs={{1,0},{2,1},{3,2},{5,4},{6,5},{7,6},{9,8},{10,9},{11,10},{13,12},{... | collective-permute-start | bytes 1179656 | tf_op jit(solution)/shard_map/ppermute | solution.py:166
  71.2 8.2 %copy-start.6 = (bf16[4,512,128]{2,1,0:T(8,128)(2,1)}, bf16[4,512,128]{2,1,0:T(8,128)(2,1)S(1)}, u32[]{:S(2)}) copy-start(bf16[4,512,128]{2,1,0:T(8,128)(2,1)S(1)} %collective-permute-done.9.c2_ref) | copy-start | bytes 1572868
  71.2 4.4 %collective-permute-start.12 = (bf16[1,1,512,128]{3,2,1,0:T(8,128)(2,1)S(1)}, bf16[1,1,512,128]{3,2,1,0:T(8,128)(2,1)S(1)}, u32[]{:S(2)}, u32[]{:S(2)}) collective-permute-start(bf16[1,1,512,128]{3,2,1,0:T(8,128)(2,1)S(1)} %get-tuple-element.26), channel_id=1, source_target_pairs={{0,1},{1,2},{2,3},{4,5},{5,6},{6,7},{8,9},{9,10},{10,11},{12,13},{... | collective-permute-start | bytes 393224 | tf_op jit(solution)/shard_map/ppermute | solution.py:168
  73.1 6.3 %collective-permute-start.13 = (bf16[1,1,512,128]{3,2,1,0:T(8,128)(2,1)S(1)}, bf16[1,1,512,128]{3,2,1,0:T(8,128)(2,1)S(1)}, u32[]{:S(2)}, u32[]{:S(2)}) collective-permute-start(bf16[1,1,512,128]{3,2,1,0:T(8,128)(2,1)S(1)} %get-tuple-element.25), channel_id=1, source_target_pairs={{1,0},{2,1},{3,2},{5,4},{6,5},{7,6},{9,8},{10,9},{11,10},{13,12},{... | collective-permute-start | bytes 393224 | tf_op jit(solution)/shard_map/ppermute | solution.py:169
  75.6 3.9 %copy-start.13 = (bf16[3,1,512,128]{3,2,1,0:T(8,128)(2,1)}, bf16[3,1,512,128]{3,2,1,0:T(8,128)(2,1)S(1)}, u32[]{:S(2)}) copy-start(bf16[3,1,512,128]{3,2,1,0:T(8,128)(2,1)S(1)} %collective-permute-done.10.top_a) | copy-start | bytes 1179652
  75.6 3.8 %copy-start.14 = (bf16[3,1,512,128]{3,2,1,0:T(8,128)(2,1)}, bf16[3,1,512,128]{3,2,1,0:T(8,128)(2,1)S(1)}, u32[]{:S(2)}) copy-start(bf16[3,1,512,128]{3,2,1,0:T(8,128)(2,1)S(1)} %collective-permute-done.11.bot_a) | copy-start | bytes 1179652
  75.6 3.8 %copy-start.15 = (bf16[1,1,512,128]{3,2,1,0:T(8,128)(2,1)}, bf16[1,1,512,128]{3,2,1,0:T(8,128)(2,1)S(1)}, u32[]{:S(2)}) copy-start(bf16[1,1,512,128]{3,2,1,0:T(8,128)(2,1)S(1)} %collective-permute-done.12.top_b) | copy-start | bytes 393220
  79.4 0.7 copy-start.16

commit v16 on v13

--- a/solution.py
+++ b/solution.py
@@ -179,6 +179,7 @@
     assert clip.shape[0] == 2
     x0, x1 = clip[0], clip[1]
     a1 = silu(x1)
+    x0, a1 = lax.optimization_barrier((x0, a1))
     a0 = silu(x0)
     (h0, s0), (h1, s1) = conv_block((x0, x1), (a0, a1), first, True, False)
     whole = conv_block((h0, h1), (s0, s1), second, False, True)

time: 88.8 us -> 89.7 us (1.010)
  waiting for transfers between devices: 17.8 us -> 19.1 us
    ppermute x2, waiting for transfers between devices: 2.86 us -> 3.91 us  [conv_block(): bot_a = lax.ppermute(jnp.stack([c1[:1], a0[:1], a1[:1]]), 'space', up)]
    convert_element_type x1 -> x2, other arithmetic: 1.83 us -> 1.69 us  [silu(): return jax.nn.silu(x.astype(jnp.float32)).astype(jnp.bfloat16)]
    unnamed x39 -> x41, local copies, waits for them, and re-layouts: 2.23 us -> 2.25 us
  transfers between devices with their start and end apart: 14 -> 14, of which waited for: 6 -> 6; matrix products, arithmetic and copies ran while one was open for 5% -> 4% of each run, Pallas kernels for 14% -> 14%
where the time goes in v16:
time: 89.7 us; the launch traced here: 88.9 us
  starting transfers between devices  39.7 us (44%)
  Pallas kernels  21.7 us (24%)
  waiting for transfers between devices  19.1 us (21%)
  local copies, waits for them, and re-layouts  6.01 us (7%)
  other arithmetic  1.88 us (2%)
    ppermute x4, starting transfers between devices, shift_tm(): return lax.ppermute(x, 'tm', [(i, i + 1) for i in range(n - 1)])  13.9 us
    pallas_call x2, Pallas kernels, frame_conv(): pl.pallas_call(functools.partial(frame_kernel, t, with_act, first), out_s...  12.4 us
    pallas_call x1, Pallas kernels, pair_conv(): pl.pallas_call(functools.partial(pair_kernel, first), out_shape=jax.Shape...  9.22 us
    ppermute x1, waiting for transfers between devices, both_taps(): got = lax.ppermute(mine, 'section', [(0, 1), (1, 0)])  9.16 us
    ppermute x2, starting transfers between devices, conv_block(): top_a = lax.ppermute(jnp.stack([c1[-1:], a0[-1:], a1[-1:]]), 'space', down)  7.69 us
    ppermute x2, starting transfers between devices, conv_block(): top_b = lax.ppermute(c2[None, -1:], 'space', down)  7.28 us
    ppermute x2, waiting for transfers between devices, conv_block(): bot_a = lax.ppermute(jnp.stack([c1[:1], a0[:1], a1[:1]]), 'space', up)  3.91 us
    ppermute x2, starting transfers between devices, conv_block(): bot_b = lax.ppermute(c2[None, :1], 'space', up)  3.84 us
  transfers between devices with their start and end apart: 14, of which 6 were waited for; matrix products, arithmetic and copies ran while one was open for 4% of the time, Pallas kernels for 14%

profile of v16, /device:TPU:1, one launch (start us, length us, event | category | flops | bytes accessed | tf_op | source)
XLA Modules:
  0.0 88.9 jit_solution(9840585371868870116)
XLA Ops:
  0.0 1.4 %fusion.3.refs_2_ = bf16[4,512,128]{2,1,0:T(8,128)(2,1)S(1)} fusion(bf16[1,2,4,512,128]{4,3,2,1,0:T(8,128)(2,1)} %param.2), kind=kLoop, calls=%fused_computation.7 | loop fusion | flops 1572864 | bytes 1048576 | tf_op jit(solution)/shard_map/convert_element_type | solution.py:17
  1.4 0.0 copy-done
  1.4 0.0 copy-start.3
  1.4 0.0 copy-start.5
  1.4 0.9 slice_bitcast_fusion
  2.3 4.1 %collective-permute-start = (bf16[4,512,128]{2,1,0:T(8,128)(2,1)S(1)}, bf16[4,512,128]{2,1,0:T(8,128)(2,1)S(1)}, u32[]{:S(2)}, u32[]{:S(2)}) collective-permute-start(bf16[4,512,128]{2,1,0:T(8,128)(2,1)S(1)} %fusion.3.refs_2_), channel_id=1, source_target_pairs={{0,4},{4,8},{8,12},{1,5},{5,9},{9,13},{2,6},{6,10},{10,14},{3,7},{... | collective-permute-start | bytes 1572872 | tf_op jit(solution)/shard_map/ppermute | solution.py:13
  6.4 0.0 copy-done.5
  6.4 0.8 copy.4
  7.2 0.1 copy.7
  7.3 0.0 copy-start.2
  7.3 0.1 constant_dynamic-slice_fusion
  7.4 1.3 %collective-permute-start.6 = (bf16[576,384]{1,0:T(8,128)(2,1)S(1)}, bf16[576,384]{1,0:T(8,128)(2,1)S(1)}, u32[]{:S(2)}, u32[]{:S(2)}) collective-permute-start(bf16[576,384]{1,0:T(8,128)(2,1)S(1)} %constant_dynamic-slice_fusion), channel_id=1, source_target_pairs={{0,16},{16,0},{1,17},{17,1},{2,18},{18,2},{3,19},{19,3},{4,20},{20... | collective-permute-start | bytes 1327112 | tf_op jit(solution)/shard_map/ppermute | solution.py:171
  8.7 0.0 copy-done.3
  8.7 0.0 copy-done.1
  8.7 0.3 fusion.7.refs_2_.refs_1_
  9.0 0.0 copy-done.2
  9.0 0.0 copy-start.4
  9.0 9.2 %collective-permute-done.6.refs_9_.refs_7_.got_ref = bf16[576,384]{1,0:T(8,128)(2,1)S(1)} collective-permute-done((bf16[576,384]{1,0:T(8,128)(2,1)S(1)}, bf16[576,384]{1,0:T(8,128)(2,1)S(1)}, u32[]{:S(2)}, u32[]{:S(2)}) %collective-permute-start.6) | collective-permute-done | bytes 442400 | tf_op jit(solution)/shard_map/ppermute | solution.py:171
  18.2 1.9 %collective-permute-start.7 = (bf16[576,384]{1,0:T(8,128)(2,1)S(1)}, bf16[576,384]{1,0:T(8,128)(2,1)S(1)}, u32[]{:S(2)}, u32[]{:S(2)}) collective-permute-start(bf16[576,384]{1,0:T(8,128)(2,1)S(1)} %collective-permute-done.6.refs_9_.refs_7_.got_ref), channel_id=1, source_target_pairs={{0,1},{1,0},{2,3},{3,2},{4,5},{5,4},{6,7},{7,6},{8,9},{9,8},{10,11... | collective-permute-start | bytes 1327112 | tf_op jit(solution)/shard_map/ppermute | solution.py:172
  20.1 0.0 collective-permute-done.refs_1_.refs_0_
  20.1 3.1 %collective-permute-start.2 = (bf16[3,1,512,128]{3,2,1,0:T(8,128)(2,1)S(1)}, bf16[3,1,512,128]{3,2,1,0:T(8,128)(2,1)S(1)}, u32[]{:S(2)}, u32[]{:S(2)}) collective-permute-start(bf16[3,1,512,128]{3,2,1,0:T(8,128)(2,1)S(1)} %pad_maximum_fusion), channel_id=1, source_target_pairs={{0,1},{1,2},{2,3},{4,5},{5,6},{6,7},{8,9},{9,10},{10,11},{12,13},{... | collective-permute-start | bytes 1179656 | tf_op jit(solution)/shard_map/ppermute | solution.py:151
  23.3 0.0 copy-done.10
  23.3 0.0 copy-done.9
  23.3 1.9 %collective-permute-start.3 = (bf16[3,1,512,128]{3,2,1,0:T(8,128)(2,1)S(1)}, bf16[3,1,512,128]{3,2,1,0:T(8,128)(2,1)S(1)}, u32[]{:S(2)}, u32[]{:S(2)}) collective-permute-start(bf16[3,1,512,128]{3,2,1,0:T(8,128)(2,1)S(1)} %pad_maximum_fusion.1), channel_id=1, source_target_pairs={{1,0},{2,1},{3,2},{5,4},{6,5},{7,6},{9,8},{10,9},{11,10},{13,12},{... | collective-permute-start | bytes 1179656 | tf_op jit(solution)/shard_map/ppermute | solution.py:152
  25.2 0.0 copy-done.4
  25.2 3.2 %collective-permute-start.1 = (bf16[4,512,128]{2,1,0:T(8,128)(2,1)S(1)}, bf16[4,512,128]{2,1,0:T(8,128)(2,1)S(1)}, u32[]{:S(2)}, u32[]{:S(2)}) collective-permute-start(bf16[4,512,128]{2,1,0:T(8,128)(2,1)S(1)} %fusion.7.refs_2_.refs_1_), channel_id=1, source_target_pairs={{0,4},{4,8},{8,12},{1,5},{5,9},{9,13},{2,6},{6,10},{10,14},{3,7},{... | collective-permute-start | bytes 1572872 | tf_op jit(solution)/shard_map/ppermute | solution.py:13
  28.4 0.0 collective-permute-done.7.refs_10_.refs_8_.other_ref
  28.4 0.0 copy-start.11
  28.5 0.0 collective-permute-done.2.refs_3_
  28.5 0.0 copy-start.12
  28.5 3.9 %collective-permute-done.3.refs_4_ = bf16[3,1,512,128]{3,2,1,0:T(8,128)(2,1)S(1)} collective-permute-done((bf16[3,1,512,128]{3,2,1,0:T(8,128)(2,1)S(1)}, bf16[3,1,512,128]{3,2,1,0:T(8,128)(2,1)S(1)}, u32[]{:S(2)}, u32[]{:S(2)}) %collective-permute-start.3) | collective-permute-done | bytes 393248 | tf_op jit(solution)/shard_map/ppermute | solution.py:152
  32.4 0.8 copy-done.13
  33.1 0.0 copy-done.11
  33.2 0.0 copy-done.12
  33.2 6.2 %shard_map.29 = (bf16[4,512,128]{2,1,0:T(8,128)(2,1)}, bf16[4,512,128]{2,1,0:T(8,128)(2,1)}) custom-call(bf16[4,512,128]{2,1,0:T(8,128)(2,1)} %copy-done.9, bf16[4,512,128]{2,1,0:T(8,128)(2,1)} %copy-done.4, bf16[4,512,128]{2,1,0:T(8,128)(2,1)} %copy-done.3, bf16[3,1,512,128]{3,2,1,0:T(8,128)(2,1)} %copy-done.12, bf16[3,1,512,128]{3,2,1,0:T(8,128)(2,1)} %copy-done.13, ...), custom_call_target="tpu_custom_call" | custom-call | flops 1811939328 | bytes 5701632 | tf_op jit(solution)/shard_map/pallas_call | solution.py:121
  39.3 3.5 %collective-permute-start.8 = (bf16[4,512,128]{2,1,0:T(8,128)(2,1)}, bf16[4,512,128]{2,1,0:T(8,128)(2,1)S(1)}, u32[]{:S(2)}, u32[]{:S(2)}) collective-permute-start(bf16[4,512,128]{2,1,0:T(8,128)(2,1)} %get-tuple-element.20.a1_ref), channel_id=1, source_target_pairs={{0,4},{4,8},{8,12},{1,5},{5,9},{9,13},{2,6},{6,10},{10,14},{3,7},{... | collective-permute-start | bytes 1572872 | tf_op jit(solution)/shard_map/ppermute | solution.py:13
  42.8 0.0 collective-permute-done.1.refs_0_
  42.8 0.0 copy-start.8
  42.9 1.9 %collective-permute-start.5 = (bf16[1,1,512,128]{3,2,1,0:T(8,128)(2,1)S(1)}, bf16[1,1,512,128]{3,2,1,0:T(8,128)(2,1)S(1)}, u32[]{:S(2)}, u32[]{:S(2)}) collective-permute-start(bf16[1,1,512,128]{3,2,1,0:T(8,128)(2,1)S(1)} %get-tuple-element.35), channel_id=1, source_target_pairs={{1,0},{2,1},{3,2},{5,4},{6,5},{7,6},{9,8},{10,9},{11,10},{13,12},{... | collective-permute-start | bytes 393224 | tf_op jit(solution)/shard_map/ppermute | solution.py:159
  44.8 3.6 %collective-permute-start.4 = (bf16[1,1,512,128]{3,2,1,0:T(8,128)(2,1)S(1)}, bf16[1,1,512,128]{3,2,1,0:T(8,128)(2,1)S(1)}, u32[]{:S(2)}, u32[]{:S(2)}) collective-permute-start(bf16[1,1,512,128]{3,2,1,0:T(8,128)(2,1)S(1)} %get-tuple-element.36), channel_id=1, source_target_pairs={{0,1},{1,2},{2,3},{4,5},{5,6},{6,7},{8,9},{9,10},{10,11},{12,13},{... | collective-permute-start | bytes 393224 | tf_op jit(solution)/shard_map/ppermute | solution.py:158
  48.5 1.0 %slice_bitcast_fusion.6 = (bf16[1,1,512,128]{3,2,1,0:T(8,128)(2,1)S(1)}, bf16[1,1,512,128]{3,2,1,0:T(8,128)(2,1)S(1)}) fusion(bf16[4,512,128]{2,1,0:T(8,128)(2,1)} %get-tuple-element.20.a1_ref), kind=kLoop, calls=%fused_computation.23 | loop fusion | bytes 524288 | tf_op jit(solution)/shard_map/stack | solution.py:152
  49.4 0.0 collective-permute-done.5.refs_6_
  49.5 0.0 copy-start.18
  49.5 0.9 %collective-permute-done.4.refs_5_ = bf16[1,1,512,128]{3,2,1,0:T(8,128)(2,1)S(1)} collective-permute-done((bf16[1,1,512,128]{3,2,1,0:T(8,128)(2,1)S(1)}, bf16[1,1,512,128]{3,2,1,0:T(8,128)(2,1)S(1)}, u32[]{:S(2)}, u32[]{:S(2)}) %collective-permute-start.4) | collective-permute-done | bytes 131104 | tf_op jit(solution)/shard_map/ppermute | solution.py:158
  50.4 0.0 copy-done.8
  50.4 0.6 copy-done.19
  51.0 6.3 %shard_map.28 = (bf16[4,512,128]{2,1,0:T(8,128)(2,1)}, bf16[4,512,128]{2,1,0:T(8,128)(2,1)}) custom-call(bf16[4,512,128]{2,1,0:T(8,128)(2,1)} %copy-done.8, bf16[4,512,128]{2,1,0:T(8,128)(2,1)} %copy-done.9, bf16[4,512,128]{2,1,0:T(8,128)(2,1)} %copy-done.4, bf16[3,1,512,128]{3,2,1,0:T(8,128)(2,1)} %copy-done.12, bf16[3,1,512,128]{3,2,1,0:T(8,128)(2,1)} %copy-done.13, ...), custom_call_target="tpu_custom_call" | custom-call | flops 1811939328 | bytes 5963776 | tf_op jit(solution)/shard_map/pallas_call | solution.py:121
  57.3 0.0 collective-permute-done.8.c1_ref
  57.3 3.2 %collective-permute-start.9 = (bf16[4,512,128]{2,1,0:T(8,128)(2,1)}, bf16[4,512,128]{2,1,0:T(8,128)(2,1)S(1)}, u32[]{:S(2)}, u32[]{:S(2)}) collective-permute-start(bf16[4,512,128]{2,1,0:T(8,128)(2,1)} %get-tuple-element.21.a0_ref), channel_id=1, source_target_pairs={{0,4},{4,8},{8,12},{1,5},{5,9},{9,13},{2,6},{6,10},{10,14},{3,7},{... | collective-permute-start | bytes 1572872 | tf_op jit(solution)/shard_map/ppermute | solution.py:13
  60.5 1.0 %slice_bitcast_fusion.7 = (bf16[1,1,512,128]{3,2,1,0:T(8,128)(2,1)S(1)}, bf16[1,1,512,128]{3,2,1,0:T(8,128)(2,1)S(1)}) fusion(bf16[4,512,128]{2,1,0:T(8,128)(2,1)} %get-tuple-element.21.a0_ref), kind=kLoop, calls=%fused_computation.24 | loop fusion | bytes 524288 | tf_op jit(solution)/shard_map/stack | solution.py:152
  61.6 4.6 %collective-permute-start.10 = (bf16[3,1,512,128]{3,2,1,0:T(8,128)(2,1)S(1)}, bf16[3,1,512,128]{3,2,1,0:T(8,128)(2,1)S(1)}, u32[]{:S(2)}, u32[]{:S(2)}) collective-permute-start(bf16[3,1,512,128]{3,2,1,0:T(8,128)(2,1)S(1)} %pad_maximum_fusion.2), channel_id=1, source_target_pairs={{0,1},{1,2},{2,3},{4,5},{5,6},{6,7},{8,9},{9,10},{10,11},{12,13},{... | collective-permute-start | bytes 1179656 | tf_op jit(solution)/shard_map/ppermute | solution.py:151
  66.3 0.0 copy-done.6
  66.3 1.9 %collective-permute-start.11 = (bf16[3,1,512,128]{3,2,1,0:T(8,128)(2,1)S(1)}, bf16[3,1,512,128]{3,2,1,0:T(8,128)(2,1)S(1)}, u32[]{:S(2)}, u32[]{:S(2)}) collective-permute-start(bf16[3,1,512,128]{3,2,1,0:T(8,128)(2,1)S(1)} %pad_maximum_fusion.3), channel_id=1, source_target_pairs={{1,0},{2,1},{3,2},{5,4},{6,5},{7,6},{9,8},{10,9},{11,10},{13,12},{... | collective-permute-start | bytes 1179656 | tf_op jit(solution)/shard_map/ppermute | solution.py:152
  68.2 3.3 %collective-permute-done.9.c2_ref = bf16[4,512,128]{2,1,0:T(8,128)(2,1)S(1)} collective-permute-done((bf16[4,512,128]{2,1,0:T(8,128)(2,1)}, bf16[4,512,128]{2,1,0:T(8,128)(2,1)S(1)}, u32[]{:S(2)}, u32[]{:S(2)}) %collective-permute-start.9) | collective-permute-done | bytes 524320 | tf_op jit(solution)/shard_map/ppermute | solution.py:13
  71.5 1.9 %collective-permute-start.13 = (bf16[1,1,512,128]{3,2,1,0:T(8,128)(2,1)S(1)}, bf16[1,1,512,128]{3,2,1,0:T(8,128)(2,1)S(1)}, u32[]{:S(2)}, u32[]{:S(2)}) collective-permute-start(bf16[1,1,512,128]{3,2,1,0:T(8,128)(2,1)S(1)} %get-tuple-element.27), channel_id=1, source_target_pairs={{1,0},{2,1},{3,2},{5,4},{6,5},{7,6},{9,8},{10,9},{11,10},{13,12},{... | collective-permute-start | bytes 393224 | tf_op jit(solution)/shard_map/ppermute | solution.py:155
  73.4 3.6 %collective-permute-start.12 = (bf16[1,1,512,128]{3,2,1,0:T(8,128)(2,1)S(1)}, bf16[1,1,512,128]{3,2,1,0:T(8,128)(2,1)S(1)}, u32[]{:S(2)}, u32[]{:S(2)}) collective-permute-start(bf16[1,1,512,128]{3,2,1,0:T(8,128)(2,1)S(1)} %get-tuple-element.28), channel_id=1, source_target_pairs={{0,1},{1,2},{2,3},{4,5},{5,6},{6,7},{8,9},{9,10},{10,11},{12,13},{... | collective-permute-start | bytes 393224 | tf_op jit(solution)/shard_map/ppermute | solution.py:154
  77.1 0.0 collective-permute-done.10.top_a
  77.1 0.0 copy-start.14
  77.1 0.0 collective-permute-done.11.bot_a
  77.1 0.7 collective-permute-done.13.bot_b
  77.8 1.2 %collective-permute-done.12.top_b = bf16[1,1,512,128]{3,2,1,0:T(8,128)(2,1)S(1)} collective-permute-done((bf16[1,1,512,128]{3,2,1,0:T(8,128)(2,1)S(1)}, bf16[1,1,512,128]{3,2,1,0:T(8,128)(2,1)S(1)}, u32[]{:S(2)}, u32[]{:S(2)}) %collective-permute-start.12) | collective-permute-done | bytes 131104 | tf_op jit(solution)/shard_map/ppermute | solution.py:154
  79.0 0.0 copy-done.16
  79.0 0.6 copy-done.17
  79.7 9.2 %shard_map.30 = bf16[2,4,512,128]{3,2,1,0:T(8,128)(2,1)} custom-call(bf16[4,512,128]{2,1,0:T(8,128)(2,1)} %copy-done.7, bf16[4,512,128]{2,1,0:T(8,128)(2,1)} %copy-done.6, bf16[4,512,128]{2,1,0:T(8,128)(2,1)} %get-tuple-element.21.a0_ref, bf16[4,512,128]{2,1,0:T(8,128)(2,1)} %get-tuple-element.20.a1_ref, bf16[3,1,512,128]{3,2,1,0:T(8,128)(2,1)} %copy-done.14, ...), custom_call_target="tpu_custom_call" | custom-call | flops 3623878656 | bytes 7012352 | tf_op jit(solution)/shard_map/pallas_call | solution.py:134
  (24 shorter events, 0.3 us)
Async XLA Ops:
  0.0 1.4 %copy-start = (bf16[1,2,4,512,128]{4,3,2,1,0:T(8,128)(2,1)S(1)}, bf16[1,2,4,512,128]{4,3,2,1,0:T(8,128)(2,1)}, u32[]{:S(2)}) copy-start(bf16[1,2,4,512,128]{4,3,2,1,0:T(8,128)(2,1)} %param.2) | copy-start | bytes 3145732
  1.4 7.2 %copy-start.3 = (bf16[4,512,128]{2,1,0:T(8,128)(2,1)}, bf16[4,512,128]{2,1,0:T(8,128)(2,1)S(1)}, u32[]{:S(2)}) copy-start(bf16[4,512,128]{2,1,0:T(8,128)(2,1)S(1)} %fusion.3.refs_2_) | copy-start | bytes 1572868
  1.4 5.0 %copy-start.5 = (bf16[1,9,384,128]{3,2,1,0:T(8,128)(2,1)S(1)}, bf16[1,9,384,128]{3,2,1,0:T(8,128)(2,1)}, u32[]{:S(2)}) copy-start(bf16[1,9,384,128]{3,2,1,0:T(8,128)(2,1)} %param.3) | copy-start | bytes 2654212
  2.3 6.4 %copy-start.1 = (bf16[4,512,128]{2,1,0:T(8,128)(2,1)}, bf16[4,512,128]{2,1,0:T(8,128)(2,1)S(1)}, u32[]{:S(2)}) copy-start(bf16[4,512,128]{2,1,0:T(8,128)(2,1)S(1)} %get-tuple-element.15.refs_7_) | copy-start | bytes 1572868
  2.3 17.7 %collective-permute-start = (bf16[4,512,128]{2,1,0:T(8,128)(2,1)S(1)}, bf16[4,512,128]{2,1,0:T(8,128)(2,1)S(1)}, u32[]{:S(2)}, u32[]{:S(2)}) collective-permute-start(bf16[4,512,128]{2,1,0:T(8,128)(2,1)S(1)} %fusion.3.refs_2_), channel_id=1, source_target_pairs={{0,4},{4,8},{8,12},{1,5},{5,9},{9,13},{2,6},{6,10},{10,14},{3,7},{... | collective-permute-start | bytes 1572872 | tf_op jit(solution)/shard_map/ppermute | solution.py:13
  7.3 1.7 %copy-start.2 = (bf16[144,8,3,128]{3,1,2,0:T(8,128)(2,1)}, bf16[144,8,3,128]{3,1,2,0:T(8,128)(2,1)S(1)}, u32[]{:S(2)}) copy-start(bf16[144,8,3,128]{3,1,2,0:T(8,128)(2,1)S(1)} %copy.7) | copy-start | bytes 2654212
  7.4 10.8 %collective-permute-start.6 = (bf16[576,384]{1,0:T(8,128)(2,1)S(1)}, bf16[576,384]{1,0:T(8,128)(2,1)S(1)}, u32[]{:S(2)}, u32[]{:S(2)}) collective-permute-start(bf16[576,384]{1,0:T(8,128)(2,1)S(1)} %constant_dynamic-slice_fusion), channel_id=1, source_target_pairs={{0,16},{16,0},{1,17},{17,1},{2,18},{18,2},{3,19},{19,3},{4,20},{20... | collective-permute-start | bytes 1327112 | tf_op jit(solution)/shard_map/ppermute | solution.py:171
  9.0 16.2 %copy-start.4 = (bf16[4,512,128]{2,1,0:T(8,128)(2,1)}, bf16[4,512,128]{2,1,0:T(8,128)(2,1)S(1)}, u32[]{:S(2)}) copy-start(bf16[4,512,128]{2,1,0:T(8,128)(2,1)S(1)} %fusion.7.refs_2_.refs_1_) | copy-start | bytes 1572868
  18.2 5.1 %copy-start.10 = (bf16[576,384]{1,0:T(8,128)(2,1)}, bf16[576,384]{1,0:T(8,128)(2,1)S(1)}, u32[]{:S(2)}) copy-start(bf16[576,384]{1,0:T(8,128)(2,1)S(1)} %collective-permute-done.6.refs_9_.refs_7_.got_ref) | copy-start | bytes 1327108
  18.2 10.3 %collective-permute-start.7 = (bf16[576,384]{1,0:T(8,128)(2,1)S(1)}, bf16[576,384]{1,0:T(8,128)(2,1)S(1)}, u32[]{:S(2)}, u32[]{:S(2)}) collective-permute-start(bf16[576,384]{1,0:T(8,128)(2,1)S(1)} %collective-permute-done.6.refs_9_.refs_7_.got_ref), channel_id=1, source_target_pairs={{0,1},{1,0},{2,3},{3,2},{4,5},{5,4},{6,7},{7,6},{8,9},{9,8},{10,11... | collective-permute-start | bytes 1327112 | tf_op jit(solution)/shard_map/ppermute | solution.py:172
  20.1 3.2 %copy-start.9 = (bf16[4,512,128]{2,1,0:T(8,128)(2,1)}, bf16[4,512,128]{2,1,0:T(8,128)(2,1)S(1)}, u32[]{:S(2)}) copy-start(bf16[4,512,128]{2,1,0:T(8,128)(2,1)S(1)} %collective-permute-done.refs_1_.refs_0_) | copy-start | bytes 1572868
  20.1 8.3 %collective-permute-start.2 = (bf16[3,1,512,128]{3,2,1,0:T(8,128)(2,1)S(1)}, bf16[3,1,512,128]{3,2,1,0:T(8,128)(2,1)S(1)}, u32[]{:S(2)}, u32[]{:S(2)}) collective-permute-start(bf16[3,1,512,128]{3,2,1,0:T(8,128)(2,1)S(1)} %pad_maximum_fusion), channel_id=1, source_target_pairs={{0,1},{1,2},{2,3},{4,5},{5,6},{6,7},{8,9},{9,10},{10,11},{12,13},{... | collective-permute-start | bytes 1179656 | tf_op jit(solution)/shard_map/ppermute | solution.py:151
  23.3 9.1 %collective-permute-start.3 = (bf16[3,1,512,128]{3,2,1,0:T(8,128)(2,1)S(1)}, bf16[3,1,512,128]{3,2,1,0:T(8,128)(2,1)S(1)}, u32[]{:S(2)}, u32[]{:S(2)}) collective-permute-start(bf16[3,1,512,128]{3,2,1,0:T(8,128)(2,1)S(1)} %pad_maximum_fusion.1), channel_id=1, source_target_pairs={{1,0},{2,1},{3,2},{5,4},{6,5},{7,6},{9,8},{10,9},{11,10},{13,12},{... | collective-permute-start | bytes 1179656 | tf_op jit(solution)/shard_map/ppermute | solution.py:152
  25.2 17.6 %collective-permute-start.1 = (bf16[4,512,128]{2,1,0:T(8,128)(2,1)S(1)}, bf16[4,512,128]{2,1,0:T(8,128)(2,1)S(1)}, u32[]{:S(2)}, u32[]{:S(2)}) collective-permute-start(bf16[4,512,128]{2,1,0:T(8,128)(2,1)S(1)} %fusion.7.refs_2_.refs_1_), channel_id=1, source_target_pairs={{0,4},{4,8},{8,12},{1,5},{5,9},{9,13},{2,6},{6,10},{10,14},{3,7},{... | collective-permute-start | bytes 1572872 | tf_op jit(solution)/shard_map/ppermute | solution.py:13
  28.4 4.7 %copy-start.11 = (bf16[576,384]{1,0:T(8,128)(2,1)}, bf16[576,384]{1,0:T(8,128)(2,1)S(1)}, u32[]{:S(2)}) copy-start(bf16[576,384]{1,0:T(8,128)(2,1)S(1)} %collective-permute-done.7.refs_10_.refs_8_.other_ref) | copy-start | bytes 1327108
  28.5 4.7 %copy-start.12 = (bf16[3,1,512,128]{3,2,1,0:T(8,128)(2,1)}, bf16[3,1,512,128]{3,2,1,0:T(8,128)(2,1)S(1)}, u32[]{:S(2)}) copy-start(bf16[3,1,512,128]{3,2,1,0:T(8,128)(2,1)S(1)} %collective-permute-done.2.refs_3_) | copy-start | bytes 1179652
  32.4 0.8 copy-start.13
  39.3 18.0 %collective-permute-start.8 = (bf16[4,512,128]{2,1,0:T(8,128)(2,1)}, bf16[4,512,128]{2,1,0:T(8,128)(2,1)S(1)}, u32[]{:S(2)}, u32[]{:S(2)}) collective-permute-start(bf16[4,512,128]{2,1,0:T(8,128)(2,1)} %get-tuple-element.20.a1_ref), channel_id=1, source_target_pairs={{0,4},{4,8},{8,12},{1,5},{5,9},{9,13},{2,6},{6,10},{10,14},{3,7},{... | collective-permute-start | bytes 1572872 | tf_op jit(solution)/shard_map/ppermute | solution.py:13
  42.8 7.5 %copy-start.8 = (bf16[4,512,128]{2,1,0:T(8,128)(2,1)}, bf16[4,512,128]{2,1,0:T(8,128)(2,1)S(1)}, u32[]{:S(2)}) copy-start(bf16[4,512,128]{2,1,0:T(8,128)(2,1)S(1)} %collective-permute-done.1.refs_0_) | copy-start | bytes 1572868
  42.9 6.6 %collective-permute-start.5 = (bf16[1,1,512,128]{3,2,1,0:T(8,128)(2,1)S(1)}, bf16[1,1,512,128]{3,2,1,0:T(8,128)(2,1)S(1)}, u32[]{:S(2)}, u32[]{:S(2)}) collective-permute-start(bf16[1,1,512,128]{3,2,1,0:T(8,128)(2,1)S(1)} %get-tuple-element.35), channel_id=1, source_target_pairs={{1,0},{2,1},{3,2},{5,4},{6,5},{7,6},{9,8},{10,9},{11,10},{13,12},{... | collective-permute-start | bytes 393224 | tf_op jit(solution)/shard_map/ppermute | solution.py:159
  44.8 5.6 %collective-permute-start.4 = (bf16[1,1,512,128]{3,2,1,0:T(8,128)(2,1)S(1)}, bf16[1,1,512,128]{3,2,1,0:T(8,128)(2,1)S(1)}, u32[]{:S(2)}, u32[]{:S(2)}) collective-permute-start(bf16[1,1,512,128]{3,2,1,0:T(8,128)(2,1)S(1)} %get-tuple-element.36), channel_id=1, source_target_pairs={{0,1},{1,2},{2,3},{4,5},{5,6},{6,7},{8,9},{9,10},{10,11},{12,13},{... | collective-permute-start | bytes 393224 | tf_op jit(solution)/shard_map/ppermute | solution.py:158
  49.5 0.9 %copy-start.18 = (bf16[1,1,512,128]{3,2,1,0:T(8,128)(2,1)}, bf16[1,1,512,128]{3,2,1,0:T(8,128)(2,1)S(1)}, u32[]{:S(2)}) copy-start(bf16[1,1,512,128]{3,2,1,0:T(8,128)(2,1)S(1)} %collective-permute-done.5.refs_6_) | copy-start | bytes 393220
  50.4 0.7 copy-start.19
  57.3 9.0 %copy-start.6 = (bf16[4,512,128]{2,1,0:T(8,128)(2,1)}, bf16[4,512,128]{2,1,0:T(8,128)(2,1)S(1)}, u32[]{:S(2)}) copy-start(bf16[4,512,128]{2,1,0:T(8,128)(2,1)S(1)} %collective-permute-done.8.c1_ref) | copy-start | bytes 1572868
  57.3 14.2 %collective-permute-start.9 = (bf16[4,512,128]{2,1,0:T(8,128)(2,1)}, bf16[4,512,128]{2,1,0:T(8,128)(2,1)S(1)}, u32[]{:S(2)}, u32[]{:S(2)}) collective-permute-start(bf16[4,512,128]{2,1,0:T(8,128)(2,1)} %get-tuple-element.21.a0_ref), channel_id=1, source_target_pairs={{0,4},{4,8},{8,12},{1,5},{5,9},{9,13},{2,6},{6,10},{10,14},{3,7},{... | collective-permute-start | bytes 1572872 | tf_op jit(solution)/shard_map/ppermute | solution.py:13
  61.6 15.5 %collective-permute-start.10 = (bf16[3,1,512,128]{3,2,1,0:T(8,128)(2,1)S(1)}, bf16[3,1,512,128]{3,2,1,0:T(8,128)(2,1)S(1)}, u32[]{:S(2)}, u32[]{:S(2)}) collective-permute-start(bf16[3,1,512,128]{3,2,1,0:T(8,128)(2,1)S(1)} %pad_maximum_fusion.2), channel_id=1, source_target_pairs={{0,1},{1,2},{2,3},{4,5},{5,6},{6,7},{8,9},{9,10},{10,11},{12,13},{... | collective-permute-start | bytes 1179656 | tf_op jit(solution)/shard_map/ppermute | solution.py:151
  66.3 10.8 %collective-permute-start.11 = (bf16[3,1,512,128]{3,2,1,0:T(8,128)(2,1)S(1)}, bf16[3,1,512,128]{3,2,1,0:T(8,128)(2,1)S(1)}, u32[]{:S(2)}, u32[]{:S(2)}) collective-permute-start(bf16[3,1,512,128]{3,2,1,0:T(8,128)(2,1)S(1)} %pad_maximum_fusion.3), channel_id=1, source_target_pairs={{1,0},{2,1},{3,2},{5,4},{6,5},{7,6},{9,8},{10,9},{11,10},{13,12},{... | collective-permute-start | bytes 1179656 | tf_op jit(solution)/shard_map/ppermute | solution.py:152
  71.5 7.5 %copy-start.7 = (bf16[4,512,128]{2,1,0:T(8,128)(2,1)}, bf16[4,512,128]{2,1,0:T(8,128)(2,1)S(1)}, u32[]{:S(2)}) copy-start(bf16[4,512,128]{2,1,0:T(8,128)(2,1)S(1)} %collective-permute-done.9.c2_ref) | copy-start | bytes 1572868
  71.5 6.3 %collective-permute-start.13 = (bf16[1,1,512,128]{3,2,1,0:T(8,128)(2,1)S(1)}, bf16[1,1,512,128]{3,2,1,0:T(8,128)(2,1)S(1)}, u32[]{:S(2)}, u32[]{:S(2)}) collective-permute-start(bf16[1,1,512,128]{3,2,1,0:T(8,128)(2,1)S(1)} %get-tuple-element.27), channel_id=1, source_target_pairs={{1,0},{2,1},{3,2},{5,4},{6,5},{7,6},{9,8},{10,9},{11,10},{13,12},{... | collective-permute-start | bytes 393224 | tf_op jit(solution)/shard_map/ppermute | solution.py:155
  73.4 5.6 %collective-permute-start.12 = (bf16[1,1,512,128]{3,2,1,0:T(8,128)(2,1)S(1)}, bf16[1,1,512,128]{3,2,1,0:T(8,128)(2,1)S(1)}, u32[]{:S(2)}, u32[]{:S(2)}) collective-permute-start(bf16[1,1,512,128]{3,2,1,0:T(8,128)(2,1)S(1)} %get-tuple-element.28), channel_id=1, source_target_pairs={{0,1},{1,2},{2,3},{4,5},{5,6},{6,7},{8,9},{9,10},{10,11},{12,13},{... | collective-permute-start | bytes 393224 | tf_op jit(solution)/shard_map/ppermute | solution.py:154
  77.1 1.9 %copy-start.14 = (bf16[3,1,512,128]{3,2,1,0:T(8,128)(2,1)}, bf16[3,1,512,128]{3,2,1,0:T(8,128)(2,1)S(1)}, u32[]{:S(2)}) copy-start(bf16[3,1,512,128]{3,2,1,0:T(8,128)(2,1)S(1)} %collective-permute-done.10.top_a) | copy-start | bytes 1179652
  77.1 1.9 %copy-start.15 = (bf16[3,1,512,128]{3,2,1,0:T(8,128)(2,1)}, bf16[3,1,512,128]{3,2,1,0:T(8,128)(2,1)S(1)}, u32[]{:S(2)}) copy-start(bf16[3,1,512,128]{3,2,1,0:T(8,128)(2,1)S(1)} %collective-permute-done.11.bot_a) | copy-start | bytes 1179652
  77.8 1.2 %copy-start.16 = (bf16[1,1,512,128]{3,2,1,0:T(8,128)(2,1)}, bf16[1,1,512,128]{3,2,1,0:T(8,128)(2,1)S(1)}, u32[]{:S(2)}) copy-start(bf16[1,1,512,128]{3,2,1,0:T(8,128)(2,1)S(1)} %collective-permute-done.13.bot_b) | copy-start | bytes 393220
  79.0 0.6 copy-start.17
